TPU v7x, 128 devices: a whole 4x4x4 slice. The times are simulated.
128 devices in a mesh: seq: 32 (over y, x, core), mp: 4 (over z).
Axes of the slice: x: 4, y: 4, z: 4, core: 2. Of those that a mesh axis runs over, the one named last changes fastest.
Arguments:
- states: bfloat16 [4, 16, 2048], P(None, None, 'mp'), may hold values from -4 to 4
- query_weight: bfloat16 [2048, 2048], P('seq', 'mp'), may hold values from -5 to 5
- key_weight: bfloat16 [2048, 2048], P('seq', 'mp'), may hold values from -5 to 5
- value_weight: bfloat16 [2048, 2048], P('seq', 'mp'), may hold values from -5 to 5
- output_weight: bfloat16 [2048, 2048], P('seq', 'mp'), may hold values from -5 to 5
- gate_weight: bfloat16 [2048, 8192], P('seq', 'mp'), may hold values from -5 to 5
- up_weight: bfloat16 [2048, 8192], P('seq', 'mp'), may hold values from -5 to 5
- down_weight: bfloat16 [8192, 2048], P('seq', 'mp'), may hold values from -5 to 5
- query_gain: float32 [2048], P('mp'), may hold values from 0.5 to 2
- key_gain: float32 [2048], P('mp'), may hold values from 0.5 to 2
- attention_gain: float32 [2048], P('mp'), may hold values from 0.1 to 1.9
- feedforward_gain: float32 [2048], P('mp'), may hold values from 0.1 to 1.9
- key_cache: bfloat16 [512, 256, 2048], P('seq', None, 'mp'), may hold values from -500 to 500
- value_cache: bfloat16 [512, 256, 2048], P('seq', None, 'mp'), may hold values from -6 to 6
- lengths: int32 [16], replicated, may hold values from 1 to 32768, as said below
- page_owner: int32 [512], P('seq'), may hold values from -1 to 15, as said below
- page_index: int32 [512], P('seq'), may hold values from 0 to 127, as said below
Outputs:
- decoded: bfloat16 [4, 16, 2048], P(None, None, 'mp')
Inputs may be any that keep to these rules, and one draw needn't show every extreme that they name: Request r owns exactly ceil(lengths[r] / 256) pages. `page_owner`: on each device of seq the used pages come before the unused ones. `page_index`: the pages of one request carry the numbers 0, 1, 2 and so on, once each; unused pages carry 0.
All inputs are finite; a program needn't handle non-finite values.
Results may differ from a plain program's by a relative error of at most 0.015.
Values may be sent and summed in bfloat16 or wider, within the bound.
No kernel may reach another device: no remote copies, remote signals or barrier semaphores. Data moves between devices by JAX's collectives and lax.ppermute only.
A program may use at most 64 MiB of HBM per device.

v0:
```python
import jax
import jax.numpy as jnp
from jax import lax
from jax.sharding import PartitionSpec as P

D = 2048
HD = 128
R = 16
STEPS = 4
PAGE = 256


epsilon = 1e-06
rope_base = 500000.0
very_low = -1e30
SEQ_SIZE = 32
MP_SIZE = 4
SEQ_FACTORS = (2, 4, 4)


def rotary(values, positions):
    half_width = HD // 2
    frequencies = rope_base ** (-2.0 * jnp.arange(half_width, dtype=jnp.float32) / HD)
    angles = positions.astype(jnp.float32)[:, None] * frequencies[None, :]
    cosine = jnp.cos(angles)[:, None, :]
    sine_part = jnp.sin(angles)[:, None, :]
    first_half = values[..., :half_width]
    second_half = values[..., half_width:]
    return jnp.concatenate(
        [
            first_half * cosine - second_half * sine_part,
            second_half * cosine + first_half * sine_part,
        ],
        axis=-1,
    )


def seq_columns(block, width):
    per = block.shape[1] // width
    seq = lax.axis_index("seq")
    mp = lax.axis_index("mp")
    piece = lax.dynamic_slice_in_dim(block, (seq % per) * width, width, 1)
    result = piece
    for shift in range(1, MP_SIZE):
        pairs = [
            (i * MP_SIZE + i // per, i * MP_SIZE + (i // per + shift) % MP_SIZE) for i in range(SEQ_SIZE)
        ]
        received = lax.ppermute(piece, ("seq", "mp"), pairs)
        result = jnp.where(mp == (seq // per + shift) % MP_SIZE, received, result)
    return result


def seq_groups():
    groups = []
    stride = 1
    for size in SEQ_FACTORS:
        groups.append((stride, size))
        stride *= size
    return groups


def digit_pairs(count, stride, size, shift):
    return [
        (i, i + (((i // stride) % size + shift) % size - (i // stride) % size) * stride)
        for i in range(count)
    ]


def exchange(value, axis, count, stride, size):
    digit = (lax.axis_index(axis) // stride) % size
    stack = jnp.zeros((size,) + value.shape, value.dtype)
    stack = lax.dynamic_update_index_in_dim(stack, value, digit, 0)
    for shift in range(1, size):
        received = lax.ppermute(value, axis, digit_pairs(count, stride, size, shift))
        stack = lax.dynamic_update_index_in_dim(stack, received, (digit - shift) % size, 0)
    return stack


def scatter_digit(current, stride, size):
    me = lax.axis_index("seq")
    digit = (me // stride) % size
    part = current.shape[1] // size
    total = lax.dynamic_slice_in_dim(current, digit * part, part, 1)
    for shift in range(1, size):
        send = lax.dynamic_slice_in_dim(current, ((digit + shift) % size) * part, part, 1)
        total = total + lax.ppermute(send, "seq", digit_pairs(SEQ_SIZE, stride, size, shift))
    return total


def gather_digit(current, stride, size):
    me = lax.axis_index("seq")
    digit = (me // stride) % size
    part = current.shape[1]
    whole = jnp.zeros((current.shape[0], part * size), current.dtype)
    whole = lax.dynamic_update_slice_in_dim(whole, current, digit * part, 1)
    for shift in range(1, size):
        received = lax.ppermute(current, "seq", digit_pairs(SEQ_SIZE, stride, size, shift))
        whole = lax.dynamic_update_slice_in_dim(whole, received, ((digit - shift) % size) * part, 1)
    return whole


def seq_total(partial_value, ladder=False):
    groups = seq_groups()
    current = partial_value
    if ladder:
        for stride, size in groups:
            current = scatter_digit(current, stride, size)
        for stride, size in reversed(groups):
            current = gather_digit(current, stride, size)
        return current
    stride, size = groups[0]
    current = scatter_digit(current, stride, size)
    for other_stride, other_size in groups[1:]:
        current = jnp.sum(exchange(current, "seq", SEQ_SIZE, other_stride, other_size), axis=0)
    return gather_digit(current, stride, size)


def merge_stack(stack):
    member_max = stack[..., HD]
    highest = jnp.max(member_max, axis=0)
    scale = jnp.exp(member_max - highest[None])
    totals = jnp.sum(stack[..., HD + 1] * scale, axis=0)
    running = jnp.sum(stack[..., :HD] * scale[..., None], axis=0)
    return jnp.concatenate([running, highest[..., None], totals[..., None]], axis=-1)


def feature_sums(squares):
    return jnp.sum(exchange(squares, "mp", MP_SIZE, 1, MP_SIZE), axis=0)


def inverse_rms(square_total):
    return lax.rsqrt(square_total / D + epsilon)[:, None]


def local(
    states,
    query_weight,
    key_weight,
    value_weight,
    output_weight,
    gate_weight,
    up_weight,
    down_weight,
    query_gain,
    key_gain,
    attention_gain,
    feedforward_gain,
    key_cache,
    value_cache,
    lengths,
    page_owner,
    page_index,
):
    local_width = query_weight.shape[1]
    local_heads = local_width // HD
    rows = STEPS * R
    score_scale = HD ** (-0.5)
    token_rows = states.reshape(rows, local_width)
    positions = (lengths[None, :] + jnp.arange(STEPS, dtype=jnp.int32)[:, None]).reshape(rows)

    sliced = seq_columns(token_rows, query_weight.shape[0])
    summed = seq_total(
        jnp.concatenate(
            [
                jnp.dot(sliced, query_weight, preferred_element_type=jnp.float32),
                jnp.dot(sliced, key_weight, preferred_element_type=jnp.float32),
                jnp.dot(sliced, value_weight, preferred_element_type=jnp.float32),
            ],
            axis=1,
        )
    )
    query_raw = summed[:, :local_width]
    key_raw = summed[:, local_width : 2 * local_width]
    value_raw = summed[:, 2 * local_width :]
    squares = feature_sums(
        jnp.stack([jnp.sum(query_raw * query_raw, axis=1), jnp.sum(key_raw * key_raw, axis=1)], axis=1)
    )
    queries = rotary(
        (query_raw * inverse_rms(squares[:, 0]) * query_gain).reshape(rows, local_heads, HD), positions
    ).astype(jnp.bfloat16)
    new_keys = rotary(
        (key_raw * inverse_rms(squares[:, 1]) * key_gain).reshape(rows, local_heads, HD), positions
    ).astype(jnp.bfloat16)
    new_values = value_raw.astype(jnp.bfloat16).reshape(rows, local_heads, HD)

    pages = key_cache.shape[0]
    tokens = pages * PAGE
    keys = key_cache.reshape(tokens, local_width)
    values = value_cache.reshape(tokens, local_width)
    token_owner = jnp.repeat(page_owner, PAGE)
    token_spot = (page_index[:, None] * PAGE + jnp.arange(PAGE, dtype=jnp.int32)[None, :]).reshape(tokens)
    request_of_row = jnp.tile(jnp.arange(R, dtype=jnp.int32), STEPS)
    length_of_row = jnp.tile(lengths, STEPS)
    validity = (token_owner[None, :] == request_of_row[:, None]) & (
        token_spot[None, :] < length_of_row[:, None]
    )
    flat_queries = queries.reshape(rows, local_width)
    scores = jnp.stack(
        [
            lax.dot_general(
                flat_queries[:, h * HD : (h + 1) * HD],
                keys[:, h * HD : (h + 1) * HD],
                (((1,), (1,)), ((), ())),
                preferred_element_type=jnp.float32,
            )
            for h in range(local_heads)
        ]
    ) * score_scale
    masked = jnp.where(validity[None], scores, very_low)
    maxima = jnp.max(masked, axis=2)
    weights = jnp.where(validity[None], jnp.exp(masked - maxima[..., None]), 0.0)
    totals = jnp.sum(weights, axis=2)
    rounded = weights.astype(jnp.bfloat16)
    running = jnp.stack(
        [
            jnp.dot(rounded[h], values[:, h * HD : (h + 1) * HD], preferred_element_type=jnp.float32)
            for h in range(local_heads)
        ]
    )

    stats = jnp.concatenate([running, maxima[..., None], totals[..., None]], axis=2)
    for stride, size in seq_groups():
        stats = merge_stack(exchange(stats, "seq", SEQ_SIZE, stride, size))
    cache_running = stats[..., :HD]
    cache_highest = stats[..., HD]
    cache_totals = stats[..., HD + 1]

    q4 = queries.reshape(STEPS, R, local_heads, HD)
    k4 = new_keys.reshape(STEPS, R, local_heads, HD)
    v4 = new_values.reshape(STEPS, R, local_heads, HD)
    fresh_scores = (
        jnp.einsum("srhd,trhd->hsrt", q4, k4, preferred_element_type=jnp.float32) * score_scale
    )
    allowed = (jnp.arange(STEPS)[None, :] <= jnp.arange(STEPS)[:, None])[None, :, None, :]
    fresh_scores = jnp.where(allowed, fresh_scores, very_low)
    cache_highest = cache_highest.reshape(local_heads, STEPS, R)
    highest = jnp.maximum(cache_highest, jnp.max(fresh_scores, axis=-1))
    fresh_weights = jnp.where(allowed, jnp.exp(fresh_scores - highest[..., None]), 0.0)
    factor = jnp.exp(cache_highest - highest)
    final_totals = cache_totals.reshape(local_heads, STEPS, R) * factor + jnp.sum(fresh_weights, axis=-1)
    final_running = cache_running.reshape(local_heads, STEPS, R, HD) * factor[..., None] + jnp.einsum(
        "hsrt,trhd->hsrd", fresh_weights.astype(jnp.bfloat16), v4, preferred_element_type=jnp.float32
    )
    attended = (final_running / final_totals[..., None]).astype(jnp.bfloat16)
    attended = jnp.transpose(attended, (1, 2, 0, 3)).reshape(rows, local_width)

    sliced = seq_columns(attended, output_weight.shape[0])
    attention_out = seq_total(jnp.dot(sliced, output_weight, preferred_element_type=jnp.float32))
    attention_squares = feature_sums(jnp.sum(attention_out * attention_out, axis=1))
    hidden = (
        token_rows.astype(jnp.float32) + attention_out * inverse_rms(attention_squares) * attention_gain
    ).astype(jnp.bfloat16)

    hidden_cols = seq_columns(hidden, gate_weight.shape[0])
    hidden_units = gate_weight.shape[1]
    summed_both = seq_total(
        jnp.concatenate(
            [
                jnp.dot(hidden_cols, gate_weight, preferred_element_type=jnp.float32),
                jnp.dot(hidden_cols, up_weight, preferred_element_type=jnp.float32),
            ],
            axis=1,
        ),
        ladder=True,
    )
    active = (jax.nn.silu(summed_both[:, :hidden_units]) * summed_both[:, hidden_units:]).astype(
        jnp.bfloat16
    )
    active_cols = seq_columns(active, down_weight.shape[0])
    mlp_out = seq_total(jnp.dot(active_cols, down_weight, preferred_element_type=jnp.float32))
    mlp_squares = feature_sums(jnp.sum(mlp_out * mlp_out, axis=1))
    decoded = (
        hidden.astype(jnp.float32) + mlp_out * inverse_rms(mlp_squares) * feedforward_gain
    ).astype(jnp.bfloat16)
    return decoded.reshape(STEPS, R, local_width)


def solution(mesh):
    global SEQ_SIZE, MP_SIZE, SEQ_FACTORS
    SEQ_SIZE = mesh.shape["seq"]
    MP_SIZE = mesh.shape["mp"]
    factors = []
    left = SEQ_SIZE
    if left % 2 == 0:
        factors.append(2)
        left //= 2
    while left % 4 == 0:
        factors.append(4)
        left //= 4
    if left > 1:
        factors.append(left)
    SEQ_FACTORS = tuple(factors)
    in_specs = (
        P(None, None, "mp"),
        P("seq", "mp"),
        P("seq", "mp"),
        P("seq", "mp"),
        P("seq", "mp"),
        P("seq", "mp"),
        P("seq", "mp"),
        P("seq", "mp"),
        P("mp"),
        P("mp"),
        P("mp"),
        P("mp"),
        P("seq", None, "mp"),
        P("seq", None, "mp"),
        P(),
        P("seq"),
        P("seq"),
    )
    out_specs = P(None, None, "mp")
    return jax.shard_map(local, mesh=mesh, in_specs=in_specs, out_specs=out_specs, check_vma=False)
```

profile of v0, /device:TPU:0, one launch (start us, length us, event | category | flops | bytes accessed | tf_op | source)
XLA Modules:
  0.0 218.5 jit_solution(11966179286981091920)
XLA Ops:
  0.8 6.0 %collective-permute-start = (bf16[64,64]{1,0:T(8,128)(2,1)S(1)}, bf16[64,64]{1,0:T(8,128)(2,1)S(1)}, u32[]{:S(2)}, u32[]{:S(2)}) collective-permute-start(bf16[64,64]{1,0:T(8,128)(2,1)S(1)} %constant_dynamic-slice_fusion.11), channel_id=1, source_target_pairs={{0,3},{4,7},{8,11},{12,15},{16,19},{20,23},{24,27},{28,31},{33,32}... | collective-permute-start | bytes 24584 | tf_op jit(solution)/shard_map/ppermute | solution.py:48
  6.9 1.3 collective-permute-start.1
  8.2 1.3 collective-permute-start.2
  16.6 1.4 collective-permute-done.3
  18.1 1.6 collective-permute-start.4
  19.9 2.8 %collective-permute-start.5 = (f32[64,768]{1,0:T(8,128)S(1)}, f32[64,768]{1,0:T(8,128)S(1)}, u32[]{:S(2)}, u32[]{:S(2)}) collective-permute-start(f32[64,768]{1,0:T(8,128)S(1)} %get-tuple-element.16), channel_id=1, source_target_pairs={{0,16},{4,20},{8,24},{12,28},{16,0},{20,4},{24,8},{28,12},{32,48},... | collective-permute-start | bytes 589832 | tf_op jit(solution)/shard_map/ppermute | solution.py:74
  22.7 1.4 collective-permute-start.6
  24.1 2.2 %collective-permute-done.4 = f32[64,768]{1,0:T(8,128)S(1)} collective-permute-done((f32[64,768]{1,0:T(8,128)S(1)}, f32[64,768]{1,0:T(8,128)S(1)}, u32[]{:S(2)}, u32[]{:S(2)}) %collective-permute-start.4) | collective-permute-done | bytes 196640 | tf_op jit(solution)/shard_map/ppermute | solution.py:74
  26.4 5.2 %collective-permute-done.5 = f32[64,768]{1,0:T(8,128)S(1)} collective-permute-done((f32[64,768]{1,0:T(8,128)S(1)}, f32[64,768]{1,0:T(8,128)S(1)}, u32[]{:S(2)}, u32[]{:S(2)}) %collective-permute-start.5) | collective-permute-done | bytes 196640 | tf_op jit(solution)/shard_map/ppermute | solution.py:74
  31.7 3.4 %collective-permute-start.8 = (f32[64,768]{1,0:T(8,128)S(1)}, f32[64,768]{1,0:T(8,128)S(1)}, u32[]{:S(2)}, u32[]{:S(2)}) collective-permute-start(f32[64,768]{1,0:T(8,128)S(1)} %reduce_sum.189), channel_id=1, source_target_pairs={{0,64},{4,68},{8,72},{12,76},{16,80},{20,84},{24,88},{28,92},{32,9... | collective-permute-start | bytes 589832 | tf_op jit(solution)/shard_map/ppermute | solution.py:74
  35.2 5.3 %collective-permute-done.7 = f32[64,768]{1,0:T(8,128)S(1)} collective-permute-done((f32[64,768]{1,0:T(8,128)S(1)}, f32[64,768]{1,0:T(8,128)S(1)}, u32[]{:S(2)}, u32[]{:S(2)}) %collective-permute-start.7) | collective-permute-done | bytes 196640 | tf_op jit(solution)/shard_map/ppermute | solution.py:74
  40.6 2.8 %collective-permute-done.8 = f32[64,768]{1,0:T(8,128)S(1)} collective-permute-done((f32[64,768]{1,0:T(8,128)S(1)}, f32[64,768]{1,0:T(8,128)S(1)}, u32[]{:S(2)}, u32[]{:S(2)}) %collective-permute-start.8) | collective-permute-done | bytes 196640 | tf_op jit(solution)/shard_map/ppermute | solution.py:74
  44.1 1.4 collective-permute-done.10
  46.2 2.0 collective-permute-start.12
  49.1 1.4 collective-permute-done.11
  52.4 1.9 convolution_bitcast_fusion
  54.3 1.7 convolution_bitcast_fusion.1
  57.7 1.4 fusion.2
  63.8 1.7 collective-permute-start.15
  65.9 3.3 %collective-permute-start.16 = (f32[4,64,130]{1,0,2:T(4,128)S(1)}, f32[4,64,130]{1,0,2:T(4,128)S(1)}, u32[]{:S(2)}, u32[]{:S(2)}) collective-permute-start(f32[4,64,130]{1,0,2:T(4,128)S(1)} %pad_maximum_fusion.1), channel_id=1, source_target_pairs={{0,16},{4,20},{8,24},{12,28},{16,0},{20,4},{24,8},{28,12},{32,48},... | collective-permute-start | bytes 399368 | tf_op jit(solution)/shard_map/ppermute | solution.py:74
  70.1 3.7 %collective-permute-done.15 = f32[4,64,130]{1,0,2:T(4,128)S(1)} collective-permute-done((f32[4,64,130]{1,0,2:T(4,128)S(1)}, f32[4,64,130]{1,0,2:T(4,128)S(1)}, u32[]{:S(2)}, u32[]{:S(2)}) %collective-permute-start.15) | collective-permute-done | bytes 133152 | tf_op jit(solution)/shard_map/ppermute | solution.py:74
  73.8 6.8 %collective-permute-done.16 = f32[4,64,130]{1,0,2:T(4,128)S(1)} collective-permute-done((f32[4,64,130]{1,0,2:T(4,128)S(1)}, f32[4,64,130]{1,0,2:T(4,128)S(1)}, u32[]{:S(2)}, u32[]{:S(2)}) %collective-permute-start.16) | collective-permute-done | bytes 133152 | tf_op jit(solution)/shard_map/ppermute | solution.py:74
  82.4 2.9 %collective-permute-start.19 = (f32[4,64,130]{1,0,2:T(4,128)S(1)}, f32[4,64,130]{1,0,2:T(4,128)S(1)}, u32[]{:S(2)}, u32[]{:S(2)}) collective-permute-start(f32[4,64,130]{1,0,2:T(4,128)S(1)} %pad_maximum_fusion.2), channel_id=1, source_target_pairs={{0,64},{4,68},{8,72},{12,76},{16,80},{20,84},{24,88},{28,92},{32,9... | collective-permute-start | bytes 399368 | tf_op jit(solution)/shard_map/ppermute | solution.py:74
  86.0 5.5 %collective-permute-done.18 = f32[4,64,130]{1,0,2:T(4,128)S(1)} collective-permute-done((f32[4,64,130]{1,0,2:T(4,128)S(1)}, f32[4,64,130]{1,0,2:T(4,128)S(1)}, u32[]{:S(2)}, u32[]{:S(2)}) %collective-permute-start.18) | collective-permute-done | bytes 133152 | tf_op jit(solution)/shard_map/ppermute | solution.py:74
  91.6 4.7 %collective-permute-done.19 = f32[4,64,130]{1,0,2:T(4,128)S(1)} collective-permute-done((f32[4,64,130]{1,0,2:T(4,128)S(1)}, f32[4,64,130]{1,0,2:T(4,128)S(1)}, u32[]{:S(2)}, u32[]{:S(2)}) %collective-permute-start.19) | collective-permute-done | bytes 133152 | tf_op jit(solution)/shard_map/ppermute | solution.py:74
  98.7 4.1 %collective-permute-start.21 = (bf16[64,64]{1,0:T(8,128)(2,1)S(1)}, bf16[64,64]{1,0:T(8,128)(2,1)S(1)}, u32[]{:S(2)}, u32[]{:S(2)}) collective-permute-start(bf16[64,64]{1,0:T(8,128)(2,1)S(1)} %constant_dynamic-slice_fusion.9), channel_id=1, source_target_pairs={{0,3},{4,7},{8,11},{12,15},{16,19},{20,23},{24,27},{28,31},{33,32}... | collective-permute-start | bytes 24584 | tf_op jit(solution)/shard_map/ppermute | solution.py:48
  102.8 1.3 collective-permute-start.22
  104.1 1.3 collective-permute-start.23
  105.6 1.3 collective-permute-done.23
  108.4 2.5 %collective-permute-start.25 = (f32[64,256]{1,0:T(8,128)S(1)}, f32[64,256]{1,0:T(8,128)S(1)}, u32[]{:S(2)}, u32[]{:S(2)}) collective-permute-start(f32[64,256]{1,0:T(8,128)S(1)} %get-tuple-element.12), channel_id=1, source_target_pairs={{0,8},{4,12},{8,16},{12,20},{16,24},{20,28},{24,0},{28,4},{32,40},... | collective-permute-start | bytes 196616 | tf_op jit(solution)/shard_map/ppermute | solution.py:74
  110.9 2.4 %collective-permute-start.26 = (f32[64,256]{1,0:T(8,128)S(1)}, f32[64,256]{1,0:T(8,128)S(1)}, u32[]{:S(2)}, u32[]{:S(2)}) collective-permute-start(f32[64,256]{1,0:T(8,128)S(1)} %get-tuple-element.12), channel_id=1, source_target_pairs={{0,16},{4,20},{8,24},{12,28},{16,0},{20,4},{24,8},{28,12},{32,48},... | collective-permute-start | bytes 196616 | tf_op jit(solution)/shard_map/ppermute | solution.py:74
  114.3 2.7 %collective-permute-done.26 = f32[64,256]{1,0:T(8,128)S(1)} collective-permute-done((f32[64,256]{1,0:T(8,128)S(1)}, f32[64,256]{1,0:T(8,128)S(1)}, u32[]{:S(2)}, u32[]{:S(2)}) %collective-permute-start.26) | collective-permute-done | bytes 65568 | tf_op jit(solution)/shard_map/ppermute | solution.py:74
  117.7 5.7 %collective-permute-start.29 = (f32[64,256]{1,0:T(8,128)S(1)}, f32[64,256]{1,0:T(8,128)S(1)}, u32[]{:S(2)}, u32[]{:S(2)}) collective-permute-start(f32[64,256]{1,0:T(8,128)S(1)} %reduce_sum.202), channel_id=1, source_target_pairs={{0,64},{4,68},{8,72},{12,76},{16,80},{20,84},{24,88},{28,92},{32,9... | collective-permute-start | bytes 196616 | tf_op jit(solution)/shard_map/ppermute | solution.py:74
  123.5 1.4 collective-permute-done.28
  124.9 1.4 collective-permute-done.29
  126.4 1.3 collective-permute-done.30
  130.5 2.0 collective-permute-start.34
  132.5 1.5 collective-permute-done.32
  135.2 4.6 %collective-permute-start.35 = (bf16[64,64]{1,0:T(8,128)(2,1)S(1)}, bf16[64,64]{1,0:T(8,128)(2,1)S(1)}, u32[]{:S(2)}, u32[]{:S(2)}) collective-permute-start(bf16[64,64]{1,0:T(8,128)(2,1)S(1)} %constant_dynamic-slice_fusion.7), channel_id=1, source_target_pairs={{0,3},{4,7},{8,11},{12,15},{16,19},{20,23},{24,27},{28,31},{33,32}... | collective-permute-start | bytes 24584 | tf_op jit(solution)/shard_map/ppermute | solution.py:48
  142.5 1.3 collective-permute-done.37
  144.6 1.8 collective-permute-done.38
  147.1 2.5 %collective-permute-start.40 = (f32[64,512]{1,0:T(8,128)S(1)}, f32[64,512]{1,0:T(8,128)S(1)}, u32[]{:S(2)}, u32[]{:S(2)}) collective-permute-start(f32[64,512]{1,0:T(8,128)S(1)} %get-tuple-element.24), channel_id=1, source_target_pairs={{0,16},{4,20},{8,24},{12,28},{16,0},{20,4},{24,8},{28,12},{32,48},... | collective-permute-start | bytes 393224 | tf_op jit(solution)/shard_map/ppermute | solution.py:86
  150.8 5.4 %collective-permute-done.39 = f32[64,512]{1,0:T(8,128)S(1)} collective-permute-done((f32[64,512]{1,0:T(8,128)S(1)}, f32[64,512]{1,0:T(8,128)S(1)}, u32[]{:S(2)}, u32[]{:S(2)}) %collective-permute-start.39) | collective-permute-done | bytes 131104 | tf_op jit(solution)/shard_map/ppermute | solution.py:86
  157.0 4.5 %collective-permute-start.43 = (f32[64,128]{1,0:T(8,128)S(1)}, f32[64,128]{1,0:T(8,128)S(1)}, u32[]{:S(2)}, u32[]{:S(2)}) collective-permute-start(f32[64,128]{1,0:T(8,128)S(1)} %get-tuple-element.33), channel_id=1, source_target_pairs={{0,64},{4,68},{8,72},{12,76},{16,80},{20,84},{24,88},{28,92},{32,9... | collective-permute-start | bytes 98312 | tf_op jit(solution)/shard_map/ppermute | solution.py:86
  162.1 1.6 collective-permute-done.43
  163.7 1.7 collective-permute-done.44
  165.7 2.7 %collective-permute-start.46 = (f32[64,128]{1,0:T(8,128)S(1)}, f32[64,128]{1,0:T(8,128)S(1)}, u32[]{:S(2)}, u32[]{:S(2)}) collective-permute-start(f32[64,128]{1,0:T(8,128)S(1)} %get-tuple-element.10), channel_id=1, source_target_pairs={{0,64},{4,68},{8,72},{12,76},{16,80},{20,84},{24,88},{28,92},{32,9... | collective-permute-start | bytes 98312 | tf_op jit(solution)/shard_map/ppermute | solution.py:97
  168.4 1.4 collective-permute-start.47
  173.2 3.2 %collective-permute-start.49 = (f32[64,512]{1,0:T(8,128)S(1)}, f32[64,512]{1,0:T(8,128)S(1)}, u32[]{:S(2)}, u32[]{:S(2)}) collective-permute-start(f32[64,512]{1,0:T(8,128)S(1)} %constant_dynamic-update-slice_fusion.8), channel_id=1, source_target_pairs={{0,16},{4,20},{8,24},{12,28},{16,0},{20,4},{24,8},{28,12},{32,48},... | collective-permute-start | bytes 393224 | tf_op jit(solution)/shard_map/ppermute | solution.py:97
  176.5 1.9 collective-permute-done.48
  178.5 2.3 %collective-permute-done.49 = f32[64,512]{1,0:T(8,128)S(1)} collective-permute-done((f32[64,512]{1,0:T(8,128)S(1)}, f32[64,512]{1,0:T(8,128)S(1)}, u32[]{:S(2)}, u32[]{:S(2)}) %collective-permute-start.49) | collective-permute-done | bytes 131104 | tf_op jit(solution)/shard_map/ppermute | solution.py:97
  181.7 1.7 collective-permute-done.51
  183.7 3.8 %collective-permute-start.52 = (bf16[64,256]{1,0:T(8,128)(2,1)S(1)}, bf16[64,256]{1,0:T(8,128)(2,1)S(1)}, u32[]{:S(2)}, u32[]{:S(2)}) collective-permute-start(bf16[64,256]{1,0:T(8,128)(2,1)S(1)} %fusion.21), channel_id=1, source_target_pairs={{0,3},{4,7},{8,11},{12,15},{16,19},{20,23},{24,27},{28,31},{33,32}... | collective-permute-start | bytes 98312 | tf_op jit(solution)/shard_map/ppermute | solution.py:48
  187.4 1.3 collective-permute-start.53
  188.7 1.3 collective-permute-start.54
  190.3 1.3 collective-permute-done.54
  193.5 3.2 %collective-permute-start.57 = (f32[64,256]{1,0:T(8,128)S(1)}, f32[64,256]{1,0:T(8,128)S(1)}, u32[]{:S(2)}, u32[]{:S(2)}) collective-permute-start(f32[64,256]{1,0:T(8,128)S(1)} %get-tuple-element.8), channel_id=1, source_target_pairs={{0,16},{4,20},{8,24},{12,28},{16,0},{20,4},{24,8},{28,12},{32,48},... | collective-permute-start | bytes 196616 | tf_op jit(solution)/shard_map/ppermute | solution.py:74
  197.4 2.0 collective-permute-done.56
  201.1 5.1 %collective-permute-start.60 = (f32[64,256]{1,0:T(8,128)S(1)}, f32[64,256]{1,0:T(8,128)S(1)}, u32[]{:S(2)}, u32[]{:S(2)}) collective-permute-start(f32[64,256]{1,0:T(8,128)S(1)} %reduce_sum.206), channel_id=1, source_target_pairs={{0,64},{4,68},{8,72},{12,76},{16,80},{20,84},{24,88},{28,92},{32,9... | collective-permute-start | bytes 196616 | tf_op jit(solution)/shard_map/ppermute | solution.py:74
  206.3 1.4 collective-permute-done.59
  207.7 1.4 collective-permute-done.60
  209.2 1.3 collective-permute-done.61
  213.2 2.1 collective-permute-start.65
  215.3 1.5 collective-permute-done.63
  (287 shorter events, 52.1 us)
Async XLA Ops:
  0.8 11.8 %collective-permute-start = (bf16[64,64]{1,0:T(8,128)(2,1)S(1)}, bf16[64,64]{1,0:T(8,128)(2,1)S(1)}, u32[]{:S(2)}, u32[]{:S(2)}) collective-permute-start(bf16[64,64]{1,0:T(8,128)(2,1)S(1)} %constant_dynamic-slice_fusion.11), channel_id=1, source_target_pairs={{0,3},{4,7},{8,11},{12,15},{16,19},{20,23},{24,27},{28,31},{33,32}... | collective-permute-start | bytes 24584 | tf_op jit(solution)/shard_map/ppermute | solution.py:48
  6.9 5.7 %collective-permute-start.1 = (bf16[64,64]{1,0:T(8,128)(2,1)S(1)}, bf16[64,64]{1,0:T(8,128)(2,1)S(1)}, u32[]{:S(2)}, u32[]{:S(2)}) collective-permute-start(bf16[64,64]{1,0:T(8,128)(2,1)S(1)} %constant_dynamic-slice_fusion.11), channel_id=1, source_target_pairs={{0,2},{4,6},{8,10},{12,14},{16,18},{20,22},{24,26},{28,30},{33,35}... | collective-permute-start | bytes 24584 | tf_op jit(solution)/shard_map/ppermute | solution.py:48
  8.2 4.5 %collective-permute-start.2 = (bf16[64,64]{1,0:T(8,128)(2,1)S(1)}, bf16[64,64]{1,0:T(8,128)(2,1)S(1)}, u32[]{:S(2)}, u32[]{:S(2)}) collective-permute-start(bf16[64,64]{1,0:T(8,128)(2,1)S(1)} %constant_dynamic-slice_fusion.11), channel_id=1, source_target_pairs={{0,1},{4,5},{8,9},{12,13},{16,17},{20,21},{24,25},{28,29},{33,34},... | collective-permute-start | bytes 24584 | tf_op jit(solution)/shard_map/ppermute | solution.py:48
  16.5 1.5 collective-permute-start.3
  18.1 8.2 %collective-permute-start.4 = (f32[64,768]{1,0:T(8,128)S(1)}, f32[64,768]{1,0:T(8,128)S(1)}, u32[]{:S(2)}, u32[]{:S(2)}) collective-permute-start(f32[64,768]{1,0:T(8,128)S(1)} %get-tuple-element.16), channel_id=1, source_target_pairs={{0,8},{4,12},{8,16},{12,20},{16,24},{20,28},{24,0},{28,4},{32,40},... | collective-permute-start | bytes 589832 | tf_op jit(solution)/shard_map/ppermute | solution.py:74
  19.9 11.7 %collective-permute-start.5 = (f32[64,768]{1,0:T(8,128)S(1)}, f32[64,768]{1,0:T(8,128)S(1)}, u32[]{:S(2)}, u32[]{:S(2)}) collective-permute-start(f32[64,768]{1,0:T(8,128)S(1)} %get-tuple-element.16), channel_id=1, source_target_pairs={{0,16},{4,20},{8,24},{12,28},{16,0},{20,4},{24,8},{28,12},{32,48},... | collective-permute-start | bytes 589832 | tf_op jit(solution)/shard_map/ppermute | solution.py:74
  22.7 8.9 %collective-permute-start.6 = (f32[64,768]{1,0:T(8,128)S(1)}, f32[64,768]{1,0:T(8,128)S(1)}, u32[]{:S(2)}, u32[]{:S(2)}) collective-permute-start(f32[64,768]{1,0:T(8,128)S(1)} %get-tuple-element.16), channel_id=1, source_target_pairs={{0,24},{4,28},{8,0},{12,4},{16,8},{20,12},{24,16},{28,20},{32,56},... | collective-permute-start | bytes 589832 | tf_op jit(solution)/shard_map/ppermute | solution.py:74
  31.7 8.9 %collective-permute-start.7 = (f32[64,768]{1,0:T(8,128)S(1)}, f32[64,768]{1,0:T(8,128)S(1)}, u32[]{:S(2)}, u32[]{:S(2)}) collective-permute-start(f32[64,768]{1,0:T(8,128)S(1)} %reduce_sum.189), channel_id=1, source_target_pairs={{0,32},{4,36},{8,40},{12,44},{16,48},{20,52},{24,56},{28,60},{32,6... | collective-permute-start | bytes 589832 | tf_op jit(solution)/shard_map/ppermute | solution.py:74
  31.7 11.7 %collective-permute-start.8 = (f32[64,768]{1,0:T(8,128)S(1)}, f32[64,768]{1,0:T(8,128)S(1)}, u32[]{:S(2)}, u32[]{:S(2)}) collective-permute-start(f32[64,768]{1,0:T(8,128)S(1)} %reduce_sum.189), channel_id=1, source_target_pairs={{0,64},{4,68},{8,72},{12,76},{16,80},{20,84},{24,88},{28,92},{32,9... | collective-permute-start | bytes 589832 | tf_op jit(solution)/shard_map/ppermute | solution.py:74
  35.1 8.7 %collective-permute-start.9 = (f32[64,768]{1,0:T(8,128)S(1)}, f32[64,768]{1,0:T(8,128)S(1)}, u32[]{:S(2)}, u32[]{:S(2)}) collective-permute-start(f32[64,768]{1,0:T(8,128)S(1)} %reduce_sum.189), channel_id=1, source_target_pairs={{0,96},{4,100},{8,104},{12,108},{16,112},{20,116},{24,120},{28,124... | collective-permute-start | bytes 589832 | tf_op jit(solution)/shard_map/ppermute | solution.py:74
  43.9 1.5 collective-permute-start.10
  45.6 4.9 %collective-permute-start.11 = (f32[64,2]{0,1:T(2,128)S(1)}, f32[64,2]{0,1:T(2,128)S(1)}, u32[]{:S(2)}, u32[]{:S(2)}) collective-permute-start(f32[64,2]{0,1:T(2,128)S(1)} %pad_maximum_fusion.5), channel_id=1, source_target_pairs={{0,1},{1,2},{2,3},{3,0},{4,5},{5,6},{6,7},{7,4},{8,9},{9,10},{10,1... | collective-permute-start | bytes 1544 | tf_op jit(solution)/shard_map/ppermute | solution.py:74
  46.2 5.1 %collective-permute-start.12 = (f32[64,2]{0,1:T(2,128)S(1)}, f32[64,2]{0,1:T(2,128)S(1)}, u32[]{:S(2)}, u32[]{:S(2)}) collective-permute-start(f32[64,2]{0,1:T(2,128)S(1)} %pad_maximum_fusion.5), channel_id=1, source_target_pairs={{0,2},{1,3},{2,0},{3,1},{4,6},{5,7},{6,4},{7,5},{8,10},{9,11},{10,... | collective-permute-start | bytes 1544 | tf_op jit(solution)/shard_map/ppermute | solution.py:74
  48.2 3.6 %collective-permute-start.13 = (f32[64,2]{0,1:T(2,128)S(1)}, f32[64,2]{0,1:T(2,128)S(1)}, u32[]{:S(2)}, u32[]{:S(2)}) collective-permute-start(f32[64,2]{0,1:T(2,128)S(1)} %pad_maximum_fusion.5), channel_id=1, source_target_pairs={{0,3},{1,0},{2,1},{3,2},{4,7},{5,4},{6,5},{7,6},{8,11},{9,8},{10,9... | collective-permute-start | bytes 1544 | tf_op jit(solution)/shard_map/ppermute | solution.py:74
  61.5 1.6 collective-permute-start.14
  63.8 10.0 %collective-permute-start.15 = (f32[4,64,130]{1,0,2:T(4,128)S(1)}, f32[4,64,130]{1,0,2:T(4,128)S(1)}, u32[]{:S(2)}, u32[]{:S(2)}) collective-permute-start(f32[4,64,130]{1,0,2:T(4,128)S(1)} %pad_maximum_fusion.1), channel_id=1, source_target_pairs={{0,8},{4,12},{8,16},{12,20},{16,24},{20,28},{24,0},{28,4},{32,40},... | collective-permute-start | bytes 399368 | tf_op jit(solution)/shard_map/ppermute | solution.py:74
  65.9 14.7 %collective-permute-start.16 = (f32[4,64,130]{1,0,2:T(4,128)S(1)}, f32[4,64,130]{1,0,2:T(4,128)S(1)}, u32[]{:S(2)}, u32[]{:S(2)}) collective-permute-start(f32[4,64,130]{1,0,2:T(4,128)S(1)} %pad_maximum_fusion.1), channel_id=1, source_target_pairs={{0,16},{4,20},{8,24},{12,28},{16,0},{20,4},{24,8},{28,12},{32,48},... | collective-permute-start | bytes 399368 | tf_op jit(solution)/shard_map/ppermute | solution.py:74
  69.2 11.6 %collective-permute-start.17 = (f32[4,64,130]{1,0,2:T(4,128)S(1)}, f32[4,64,130]{1,0,2:T(4,128)S(1)}, u32[]{:S(2)}, u32[]{:S(2)}) collective-permute-start(f32[4,64,130]{1,0,2:T(4,128)S(1)} %pad_maximum_fusion.1), channel_id=1, source_target_pairs={{0,24},{4,28},{8,0},{12,4},{16,8},{20,12},{24,16},{28,20},{32,56},... | collective-permute-start | bytes 399368 | tf_op jit(solution)/shard_map/ppermute | solution.py:74
  81.4 10.1 %collective-permute-start.18 = (f32[4,64,130]{1,0,2:T(4,128)S(1)}, f32[4,64,130]{1,0,2:T(4,128)S(1)}, u32[]{:S(2)}, u32[]{:S(2)}) collective-permute-start(f32[4,64,130]{1,0,2:T(4,128)S(1)} %pad_maximum_fusion.2), channel_id=1, source_target_pairs={{0,32},{4,36},{8,40},{12,44},{16,48},{20,52},{24,56},{28,60},{32,6... | collective-permute-start | bytes 399368 | tf_op jit(solution)/shard_map/ppermute | solution.py:74
  82.4 13.9 %collective-permute-start.19 = (f32[4,64,130]{1,0,2:T(4,128)S(1)}, f32[4,64,130]{1,0,2:T(4,128)S(1)}, u32[]{:S(2)}, u32[]{:S(2)}) collective-permute-start(f32[4,64,130]{1,0,2:T(4,128)S(1)} %pad_maximum_fusion.2), channel_id=1, source_target_pairs={{0,64},{4,68},{8,72},{12,76},{16,80},{20,84},{24,88},{28,92},{32,9... | collective-permute-start | bytes 399368 | tf_op jit(solution)/shard_map/ppermute | solution.py:74
  85.3 11.5 %collective-permute-start.20 = (f32[4,64,130]{1,0,2:T(4,128)S(1)}, f32[4,64,130]{1,0,2:T(4,128)S(1)}, u32[]{:S(2)}, u32[]{:S(2)}) collective-permute-start(f32[4,64,130]{1,0,2:T(4,128)S(1)} %pad_maximum_fusion.2), channel_id=1, source_target_pairs={{0,96},{4,100},{8,104},{12,108},{16,112},{20,116},{24,120},{28,124... | collective-permute-start | bytes 399368 | tf_op jit(solution)/shard_map/ppermute | solution.py:74
  98.7 6.7 %collective-permute-start.21 = (bf16[64,64]{1,0:T(8,128)(2,1)S(1)}, bf16[64,64]{1,0:T(8,128)(2,1)S(1)}, u32[]{:S(2)}, u32[]{:S(2)}) collective-permute-start(bf16[64,64]{1,0:T(8,128)(2,1)S(1)} %constant_dynamic-slice_fusion.9), channel_id=1, source_target_pairs={{0,3},{4,7},{8,11},{12,15},{16,19},{20,23},{24,27},{28,31},{33,32}... | collective-permute-start | bytes 24584 | tf_op jit(solution)/shard_map/ppermute | solution.py:48
  102.8 2.7 %collective-permute-start.22 = (bf16[64,64]{1,0:T(8,128)(2,1)S(1)}, bf16[64,64]{1,0:T(8,128)(2,1)S(1)}, u32[]{:S(2)}, u32[]{:S(2)}) collective-permute-start(bf16[64,64]{1,0:T(8,128)(2,1)S(1)} %constant_dynamic-slice_fusion.9), channel_id=1, source_target_pairs={{0,2},{4,6},{8,10},{12,14},{16,18},{20,22},{24,26},{28,30},{33,35}... | collective-permute-start | bytes 24584 | tf_op jit(solution)/shard_map/ppermute | solution.py:48
  104.1 2.7 %collective-permute-start.23 = (bf16[64,64]{1,0:T(8,128)(2,1)S(1)}, bf16[64,64]{1,0:T(8,128)(2,1)S(1)}, u32[]{:S(2)}, u32[]{:S(2)}) collective-permute-start(bf16[64,64]{1,0:T(8,128)(2,1)S(1)} %constant_dynamic-slice_fusion.9), channel_id=1, source_target_pairs={{0,1},{4,5},{8,9},{12,13},{16,17},{20,21},{24,25},{28,29},{33,34},... | collective-permute-start | bytes 24584 | tf_op jit(solution)/shard_map/ppermute | solution.py:48
  107.0 1.3 collective-permute-start.24
  108.4 5.9 %collective-permute-start.25 = (f32[64,256]{1,0:T(8,128)S(1)}, f32[64,256]{1,0:T(8,128)S(1)}, u32[]{:S(2)}, u32[]{:S(2)}) collective-permute-start(f32[64,256]{1,0:T(8,128)S(1)} %get-tuple-element.12), channel_id=1, source_target_pairs={{0,8},{4,12},{8,16},{12,20},{16,24},{20,28},{24,0},{28,4},{32,40},... | collective-permute-start | bytes 196616 | tf_op jit(solution)/shard_map/ppermute | solution.py:74
  110.9 6.1 %collective-permute-start.26 = (f32[64,256]{1,0:T(8,128)S(1)}, f32[64,256]{1,0:T(8,128)S(1)}, u32[]{:S(2)}, u32[]{:S(2)}) collective-permute-start(f32[64,256]{1,0:T(8,128)S(1)} %get-tuple-element.12), channel_id=1, source_target_pairs={{0,16},{4,20},{8,24},{12,28},{16,0},{20,4},{24,8},{28,12},{32,48},... | collective-permute-start | bytes 196616 | tf_op jit(solution)/shard_map/ppermute | solution.py:74
  113.3 4.3 %collective-permute-start.27 = (f32[64,256]{1,0:T(8,128)S(1)}, f32[64,256]{1,0:T(8,128)S(1)}, u32[]{:S(2)}, u32[]{:S(2)}) collective-permute-start(f32[64,256]{1,0:T(8,128)S(1)} %get-tuple-element.12), channel_id=1, source_target_pairs={{0,24},{4,28},{8,0},{12,4},{16,8},{20,12},{24,16},{28,20},{32,56},... | collective-permute-start | bytes 196616 | tf_op jit(solution)/shard_map/ppermute | solution.py:74
  117.6 7.3 %collective-permute-start.28 = (f32[64,256]{1,0:T(8,128)S(1)}, f32[64,256]{1,0:T(8,128)S(1)}, u32[]{:S(2)}, u32[]{:S(2)}) collective-permute-start(f32[64,256]{1,0:T(8,128)S(1)} %reduce_sum.202), channel_id=1, source_target_pairs={{0,32},{4,36},{8,40},{12,44},{16,48},{20,52},{24,56},{28,60},{32,6... | collective-permute-start | bytes 196616 | tf_op jit(solution)/shard_map/ppermute | solution.py:74
  117.7 8.7 %collective-permute-start.29 = (f32[64,256]{1,0:T(8,128)S(1)}, f32[64,256]{1,0:T(8,128)S(1)}, u32[]{:S(2)}, u32[]{:S(2)}) collective-permute-start(f32[64,256]{1,0:T(8,128)S(1)} %reduce_sum.202), channel_id=1, source_target_pairs={{0,64},{4,68},{8,72},{12,76},{16,80},{20,84},{24,88},{28,92},{32,9... | collective-permute-start | bytes 196616 | tf_op jit(solution)/shard_map/ppermute | solution.py:74
  123.4 4.3 %collective-permute-start.30 = (f32[64,256]{1,0:T(8,128)S(1)}, f32[64,256]{1,0:T(8,128)S(1)}, u32[]{:S(2)}, u32[]{:S(2)}) collective-permute-start(f32[64,256]{1,0:T(8,128)S(1)} %reduce_sum.202), channel_id=1, source_target_pairs={{0,96},{4,100},{8,104},{12,108},{16,112},{20,116},{24,120},{28,124... | collective-permute-start | bytes 196616 | tf_op jit(solution)/shard_map/ppermute | solution.py:74
  127.7 1.3 collective-permute-start.31
  129.2 4.8 %collective-permute-start.32 = (f32[64]{0:T(128)S(1)}, f32[64]{0:T(128)S(1)}, u32[]{:S(2)}, u32[]{:S(2)}) collective-permute-start(f32[64]{0:T(128)S(1)} %multiply_reduce_fusion.1), channel_id=1, source_target_pairs={{0,1},{1,2},{2,3},{3,0},{4,5},{5,6},{6,7},{7,4},{8,9},{9,10},{10,1... | collective-permute-start | bytes 776 | tf_op jit(solution)/shard_map/ppermute | solution.py:74
  129.3 5.2 %collective-permute-start.33 = (f32[64]{0:T(128)S(1)}, f32[64]{0:T(128)S(1)}, u32[]{:S(2)}, u32[]{:S(2)}) collective-permute-start(f32[64]{0:T(128)S(1)} %multiply_reduce_fusion.1), channel_id=1, source_target_pairs={{0,2},{1,3},{2,0},{3,1},{4,6},{5,7},{6,4},{7,5},{8,10},{9,11},{10,... | collective-permute-start | bytes 776 | tf_op jit(solution)/shard_map/ppermute | solution.py:74
  130.5 4.5 %collective-permute-start.34 = (f32[64]{0:T(128)S(1)}, f32[64]{0:T(128)S(1)}, u32[]{:S(2)}, u32[]{:S(2)}) collective-permute-start(f32[64]{0:T(128)S(1)} %multiply_reduce_fusion.1), channel_id=1, source_target_pairs={{0,3},{1,0},{2,1},{3,2},{4,7},{5,4},{6,5},{7,6},{8,11},{9,8},{10,9... | collective-permute-start | bytes 776 | tf_op jit(solution)/shard_map/ppermute | solution.py:74
  135.2 7.2 %collective-permute-start.35 = (bf16[64,64]{1,0:T(8,128)(2,1)S(1)}, bf16[64,64]{1,0:T(8,128)(2,1)S(1)}, u32[]{:S(2)}, u32[]{:S(2)}) collective-permute-start(bf16[64,64]{1,0:T(8,128)(2,1)S(1)} %constant_dynamic-slice_fusion.7), channel_id=1, source_target_pairs={{0,3},{4,7},{8,11},{12,15},{16,19},{20,23},{24,27},{28,31},{33,32}... | collective-permute-start | bytes 24584 | tf_op jit(solution)/shard_map/ppermute | solution.py:48
  139.8 2.7 %collective-permute-start.36 = (bf16[64,64]{1,0:T(8,128)(2,1)S(1)}, bf16[64,64]{1,0:T(8,128)(2,1)S(1)}, u32[]{:S(2)}, u32[]{:S(2)}) collective-permute-start(bf16[64,64]{1,0:T(8,128)(2,1)S(1)} %constant_dynamic-slice_fusion.7), channel_id=1, source_target_pairs={{0,2},{4,6},{8,10},{12,14},{16,18},{20,22},{24,26},{28,30},{33,35}... | collective-permute-start | bytes 24584 | tf_op jit(solution)/shard_map/ppermute | solution.py:48
  141.1 2.7 %collective-permute-start.37 = (bf16[64,64]{1,0:T(8,128)(2,1)S(1)}, bf16[64,64]{1,0:T(8,128)(2,1)S(1)}, u32[]{:S(2)}, u32[]{:S(2)}) collective-permute-start(bf16[64,64]{1,0:T(8,128)(2,1)S(1)} %constant_dynamic-slice_fusion.7), channel_id=1, source_target_pairs={{0,1},{4,5},{8,9},{12,13},{16,17},{20,21},{24,25},{28,29},{33,34},... | collective-permute-start | bytes 24584 | tf_op jit(solution)/shard_map/ppermute | solution.py:48
  144.4 2.0 collective-permute-start.38
  146.6 9.6 %collective-permute-start.39 = (f32[64,512]{1,0:T(8,128)S(1)}, f32[64,512]{1,0:T(8,128)S(1)}, u32[]{:S(2)}, u32[]{:S(2)}) collective-permute-start(f32[64,512]{1,0:T(8,128)S(1)} %get-tuple-element.22), channel_id=1, source_target_pairs={{0,8},{4,12},{8,16},{12,20},{16,24},{20,28},{24,0},{28,4},{32,40},... | collective-permute-start | bytes 393224 | tf_op jit(solution)/shard_map/ppermute | solution.py:86
  147.1 9.1 %collective-permute-start.40 = (f32[64,512]{1,0:T(8,128)S(1)}, f32[64,512]{1,0:T(8,128)S(1)}, u32[]{:S(2)}, u32[]{:S(2)}) collective-permute-start(f32[64,512]{1,0:T(8,128)S(1)} %get-tuple-element.24), channel_id=1, source_target_pairs={{0,16},{4,20},{8,24},{12,28},{16,0},{20,4},{24,8},{28,12},{32,48},... | collective-permute-start | bytes 393224 | tf_op jit(solution)/shard_map/ppermute | solution.py:86
  149.7 7.1 %collective-permute-start.41 = (f32[64,512]{1,0:T(8,128)S(1)}, f32[64,512]{1,0:T(8,128)S(1)}, u32[]{:S(2)}, u32[]{:S(2)}) collective-permute-start(f32[64,512]{1,0:T(8,128)S(1)} %get-tuple-element.23), channel_id=1, source_target_pairs={{0,24},{4,28},{8,0},{12,4},{16,8},{20,12},{24,16},{28,20},{32,56},... | collective-permute-start | bytes 393224 | tf_op jit(solution)/shard_map/ppermute | solution.py:86
  156.9 5.2 %collective-permute-start.42 = (f32[64,128]{1,0:T(8,128)S(1)}, f32[64,128]{1,0:T(8,128)S(1)}, u32[]{:S(2)}, u32[]{:S(2)}) collective-permute-start(f32[64,128]{1,0:T(8,128)S(1)} %get-tuple-element.31), channel_id=1, source_target_pairs={{0,32},{4,36},{8,40},{12,44},{16,48},{20,52},{24,56},{28,60},{32,6... | collective-permute-start | bytes 98312 | tf_op jit(solution)/shard_map/ppermute | solution.py:86
  157.0 6.7 %collective-permute-start.43 = (f32[64,128]{1,0:T(8,128)S(1)}, f32[64,128]{1,0:T(8,128)S(1)}, u32[]{:S(2)}, u32[]{:S(2)}) collective-permute-start(f32[64,128]{1,0:T(8,128)S(1)} %get-tuple-element.33), channel_id=1, source_target_pairs={{0,64},{4,68},{8,72},{12,76},{16,80},{20,84},{24,88},{28,92},{32,9... | collective-permute-start | bytes 98312 | tf_op jit(solution)/shard_map/ppermute | solution.py:86
  161.4 3.9 %collective-permute-start.44 = (f32[64,128]{1,0:T(8,128)S(1)}, f32[64,128]{1,0:T(8,128)S(1)}, u32[]{:S(2)}, u32[]{:S(2)}) collective-permute-start(f32[64,128]{1,0:T(8,128)S(1)} %get-tuple-element.32), channel_id=1, source_target_pairs={{0,96},{4,100},{8,104},{12,108},{16,112},{20,116},{24,120},{28,124... | collective-permute-start | bytes 98312 | tf_op jit(solution)/shard_map/ppermute | solution.py:86
  165.4 5.4 %collective-permute-start.45 = (f32[64,128]{1,0:T(8,128)S(1)}, f32[64,128]{1,0:T(8,128)S(1)}, u32[]{:S(2)}, u32[]{:S(2)}) collective-permute-start(f32[64,128]{1,0:T(8,128)S(1)} %get-tuple-element.10), channel_id=1, source_target_pairs={{0,32},{4,36},{8,40},{12,44},{16,48},{20,52},{24,56},{28,60},{32,6... | collective-permute-start | bytes 98312 | tf_op jit(solution)/shard_map/ppermute | solution.py:97
  165.7 5.5 %collective-permute-start.46 = (f32[64,128]{1,0:T(8,128)S(1)}, f32[64,128]{1,0:T(8,128)S(1)}, u32[]{:S(2)}, u32[]{:S(2)}) collective-permute-start(f32[64,128]{1,0:T(8,128)S(1)} %get-tuple-element.10), channel_id=1, source_target_pairs={{0,64},{4,68},{8,72},{12,76},{16,80},{20,84},{24,88},{28,92},{32,9... | collective-permute-start | bytes 98312 | tf_op jit(solution)/shard_map/ppermute | solution.py:97
  168.4 3.9 %collective-permute-start.47 = (f32[64,128]{1,0:T(8,128)S(1)}, f32[64,128]{1,0:T(8,128)S(1)}, u32[]{:S(2)}, u32[]{:S(2)}) collective-permute-start(f32[64,128]{1,0:T(8,128)S(1)} %get-tuple-element.10), channel_id=1, source_target_pairs={{0,96},{4,100},{8,104},{12,108},{16,112},{20,116},{24,120},{28,124... | collective-permute-start | bytes 98312 | tf_op jit(solution)/shard_map/ppermute | solution.py:97
  172.3 6.2 %collective-permute-start.48 = (f32[64,512]{1,0:T(8,128)S(1)}, f32[64,512]{1,0:T(8,128)S(1)}, u32[]{:S(2)}, u32[]{:S(2)}) collective-permute-start(f32[64,512]{1,0:T(8,128)S(1)} %constant_dynamic-update-slice_fusion.8), channel_id=1, source_target_pairs={{0,8},{4,12},{8,16},{12,20},{16,24},{20,28},{24,0},{28,4},{32,40},... | collective-permute-start | bytes 393224 | tf_op jit(solution)/shard_map/ppermute | solution.py:97
  173.2 7.6 %collective-permute-start.49 = (f32[64,512]{1,0:T(8,128)S(1)}, f32[64,512]{1,0:T(8,128)S(1)}, u32[]{:S(2)}, u32[]{:S(2)}) collective-permute-start(f32[64,512]{1,0:T(8,128)S(1)} %constant_dynamic-update-slice_fusion.8), channel_id=1, source_target_pairs={{0,16},{4,20},{8,24},{12,28},{16,0},{20,4},{24,8},{28,12},{32,48},... | collective-permute-start | bytes 393224 | tf_op jit(solution)/shard_map/ppermute | solution.py:97
  176.4 5.0 %collective-permute-start.50 = (f32[64,512]{1,0:T(8,128)S(1)}, f32[64,512]{1,0:T(8,128)S(1)}, u32[]{:S(2)}, u32[]{:S(2)}) collective-permute-start(f32[64,512]{1,0:T(8,128)S(1)} %constant_dynamic-update-slice_fusion.8), channel_id=1, source_target_pairs={{0,24},{4,28},{8,0},{12,4},{16,8},{20,12},{24,16},{28,20},{32,56},... | collective-permute-start | bytes 393224 | tf_op jit(solution)/shard_map/ppermute | solution.py:97
  181.4 2.0 collective-permute-start.51
  183.7 6.4 %collective-permute-start.52 = (bf16[64,256]{1,0:T(8,128)(2,1)S(1)}, bf16[64,256]{1,0:T(8,128)(2,1)S(1)}, u32[]{:S(2)}, u32[]{:S(2)}) collective-permute-start(bf16[64,256]{1,0:T(8,128)(2,1)S(1)} %fusion.21), channel_id=1, source_target_pairs={{0,3},{4,7},{8,11},{12,15},{16,19},{20,23},{24,27},{28,31},{33,32}... | collective-permute-start | bytes 98312 | tf_op jit(solution)/shard_map/ppermute | solution.py:48
  187.4 2.9 %collective-permute-start.53 = (bf16[64,256]{1,0:T(8,128)(2,1)S(1)}, bf16[64,256]{1,0:T(8,128)(2,1)S(1)}, u32[]{:S(2)}, u32[]{:S(2)}) collective-permute-start(bf16[64,256]{1,0:T(8,128)(2,1)S(1)} %fusion.21), channel_id=1, source_target_pairs={{0,2},{4,6},{8,10},{12,14},{16,18},{20,22},{24,26},{28,30},{33,35}... | collective-permute-start | bytes 98312 | tf_op jit(solution)/shard_map/ppermute | solution.py:48
  188.7 2.9 %collective-permute-start.54 = (bf16[64,256]{1,0:T(8,128)(2,1)S(1)}, bf16[64,256]{1,0:T(8,128)(2,1)S(1)}, u32[]{:S(2)}, u32[]{:S(2)}) collective-permute-start(bf16[64,256]{1,0:T(8,128)(2,1)S(1)} %fusion.21), channel_id=1, source_target_pairs={{0,1},{4,5},{8,9},{12,13},{16,17},{20,21},{24,25},{28,29},{33,34},... | collective-permute-start | bytes 98312 | tf_op jit(solution)/shard_map/ppermute | solution.py:48
  193.2 6.2 %collective-permute-start.56 = (f32[64,256]{1,0:T(8,128)S(1)}, f32[64,256]{1,0:T(8,128)S(1)}, u32[]{:S(2)}, u32[]{:S(2)}) collective-permute-start(f32[64,256]{1,0:T(8,128)S(1)} %get-tuple-element.8), channel_id=1, source_target_pairs={{0,8},{4,12},{8,16},{12,20},{16,24},{20,28},{24,0},{28,4},{32,40},... | collective-permute-start | bytes 196616 | tf_op jit(solution)/shard_map/ppermute | solution.py:74
  193.5 6.7 %collective-permute-start.57 = (f32[64,256]{1,0:T(8,128)S(1)}, f32[64,256]{1,0:T(8,128)S(1)}, u32[]{:S(2)}, u32[]{:S(2)}) collective-permute-start(f32[64,256]{1,0:T(8,128)S(1)} %get-tuple-element.8), channel_id=1, source_target_pairs={{0,16},{4,20},{8,24},{12,28},{16,0},{20,4},{24,8},{28,12},{32,48},... | collective-permute-start | bytes 196616 | tf_op jit(solution)/shard_map/ppermute | solution.py:74
  196.7 4.3 %collective-permute-start.58 = (f32[64,256]{1,0:T(8,128)S(1)}, f32[64,256]{1,0:T(8,128)S(1)}, u32[]{:S(2)}, u32[]{:S(2)}) collective-permute-start(f32[64,256]{1,0:T(8,128)S(1)} %get-tuple-element.8), channel_id=1, source_target_pairs={{0,24},{4,28},{8,0},{12,4},{16,8},{20,12},{24,16},{28,20},{32,56},... | collective-permute-start | bytes 196616 | tf_op jit(solution)/shard_map/ppermute | solution.py:74
  201.0 6.7 %collective-permute-start.59 = (f32[64,256]{1,0:T(8,128)S(1)}, f32[64,256]{1,0:T(8,128)S(1)}, u32[]{:S(2)}, u32[]{:S(2)}) collective-permute-start(f32[64,256]{1,0:T(8,128)S(1)} %reduce_sum.206), channel_id=1, source_target_pairs={{0,32},{4,36},{8,40},{12,44},{16,48},{20,52},{24,56},{28,60},{32,6... | collective-permute-start | bytes 196616 | tf_op jit(solution)/shard_map/ppermute | solution.py:74
  201.1 8.1 %collective-permute-start.60 = (f32[64,256]{1,0:T(8,128)S(1)}, f32[64,256]{1,0:T(8,128)S(1)}, u32[]{:S(2)}, u32[]{:S(2)}) collective-permute-start(f32[64,256]{1,0:T(8,128)S(1)} %reduce_sum.206), channel_id=1, source_target_pairs={{0,64},{4,68},{8,72},{12,76},{16,80},{20,84},{24,88},{28,92},{32,9... | collective-permute-start | bytes 196616 | tf_op jit(solution)/shard_map/ppermute | solution.py:74
  206.2 4.3 %collective-permute-start.61 = (f32[64,256]{1,0:T(8,128)S(1)}, f32[64,256]{1,0:T(8,128)S(1)}, u32[]{:S(2)}, u32[]{:S(2)}) collective-permute-start(f32[64,256]{1,0:T(8,128)S(1)} %reduce_sum.206), channel_id=1, source_target_pairs={{0,96},{4,100},{8,104},{12,108},{16,112},{20,116},{24,120},{28,124... | collective-permute-start | bytes 196616 | tf_op jit(solution)/shard_map/ppermute | solution.py:74
  212.0 4.8 %collective-permute-start.63 = (f32[64]{0:T(128)S(1)}, f32[64]{0:T(128)S(1)}, u32[]{:S(2)}, u32[]{:S(2)}) collective-permute-start(f32[64]{0:T(128)S(1)} %multiply_reduce_fusion), channel_id=1, source_target_pairs={{0,1},{1,2},{2,3},{3,0},{4,5},{5,6},{6,7},{7,4},{8,9},{9,10},{10,1... | collective-permute-start | bytes 776 | tf_op jit(solution)/shard_map/ppermute | solution.py:74
  212.1 5.2 %collective-permute-start.64 = (f32[64]{0:T(128)S(1)}, f32[64]{0:T(128)S(1)}, u32[]{:S(2)}, u32[]{:S(2)}) collective-permute-start(f32[64]{0:T(128)S(1)} %multiply_reduce_fusion), channel_id=1, source_target_pairs={{0,2},{1,3},{2,0},{3,1},{4,6},{5,7},{6,4},{7,5},{8,10},{9,11},{10,... | collective-permute-start | bytes 776 | tf_op jit(solution)/shard_map/ppermute | solution.py:74
  213.2 4.5 %collective-permute-start.65 = (f32[64]{0:T(128)S(1)}, f32[64]{0:T(128)S(1)}, u32[]{:S(2)}, u32[]{:S(2)}) collective-permute-start(f32[64]{0:T(128)S(1)} %multiply_reduce_fusion), channel_id=1, source_target_pairs={{0,3},{1,0},{2,1},{3,2},{4,7},{5,4},{6,5},{7,6},{8,11},{9,8},{10,9... | collective-permute-start | bytes 776 | tf_op jit(solution)/shard_map/ppermute | solution.py:74
  (13 other events, 440.5 us)
where the time goes:
time: 219 us
  starting transfers between devices  96.6 us (44%)
  waiting for transfers between devices  93.8 us (43%)
  matrix products  9.91 us (5%)
  other arithmetic  8.49 us (4%)
  local copies, waits for them, and re-layouts  7.87 us (4%)
    ppermute x34, waiting for transfers between devices, exchange(): lax.ppermute(value, axis, digit_pairs(count, stride, size, shift))  61.1 us
    ppermute x34, starting transfers between devices, exchange(): lax.ppermute(value, axis, digit_pairs(count, stride, size, shift))  49.7 us
    ppermute x12, starting transfers between devices, seq_columns(): received = lax.ppermute(piece, ('seq', 'mp'), pairs)  28.8 us
    ppermute x10, waiting for transfers between devices, scatter_digit(): lax.ppermute(send, 'seq', digit_pairs(SEQ_SIZE, stride, size, shift))  15.5 us
    ppermute x10, waiting for transfers between devices, gather_digit(): lax.ppermute(current, 'seq', digit_pairs(SEQ_SIZE, stride, size, shift))  12.8 us
    ppermute x10, starting transfers between devices, scatter_digit(): lax.ppermute(send, 'seq', digit_pairs(SEQ_SIZE, stride, size, shift))  9.16 us
    ppermute x10, starting transfers between devices, gather_digit(): lax.ppermute(current, 'seq', digit_pairs(SEQ_SIZE, stride, size, shift))  8.9 us
    dot_general x4, matrix products, local(): lax.dot_general(flat_queries[:, h * HD:(h + 1) * HD], keys[:, h * HD:(h +...  4.57 us
  transfers between devices with their start and end apart: 66, of which 58 were waited for; matrix products, arithmetic and copies ran while one was open for 3% of the time, Pallas kernels for 0%

commit v1 on v0

--- a/solution.py
+++ b/solution.py
@@ -38,16 +38,13 @@
 def seq_columns(block, width):
     per = block.shape[1] // width
     seq = lax.axis_index("seq")
-    mp = lax.axis_index("mp")
     piece = lax.dynamic_slice_in_dim(block, (seq % per) * width, width, 1)
-    result = piece
-    for shift in range(1, MP_SIZE):
-        pairs = [
-            (i * MP_SIZE + i // per, i * MP_SIZE + (i // per + shift) % MP_SIZE) for i in range(SEQ_SIZE)
-        ]
-        received = lax.ppermute(piece, ("seq", "mp"), pairs)
-        result = jnp.where(mp == (seq // per + shift) % MP_SIZE, received, result)
-    return result
+    pairs = [
+        (s * MP_SIZE + m, (m * per + s % per) * MP_SIZE + s // per)
+        for s in range(SEQ_SIZE)
+        for m in range(MP_SIZE)
+    ]
+    return lax.ppermute(piece, ("seq", "mp"), pairs)
 
 
 def seq_groups():
@@ -113,6 +110,31 @@
     for other_stride, other_size in groups[1:]:
         current = jnp.sum(exchange(current, "seq", SEQ_SIZE, other_stride, other_size), axis=0)
     return gather_digit(current, stride, size)
+
+
+def gate_up_active(gate_part, up_part):
+    rows, units = gate_part.shape
+    unit_block = units // SEQ_SIZE
+    arranged = jnp.stack(
+        [gate_part.reshape(rows, SEQ_SIZE, unit_block), up_part.reshape(rows, SEQ_SIZE, unit_block)],
+        axis=2,
+    ).reshape(rows, 2 * units)
+    groups = seq_groups()
+    for stride, size in groups:
+        arranged = scatter_digit(arranged, stride, size)
+    active = (jax.nn.silu(arranged[:, :unit_block]) * arranged[:, unit_block:]).astype(jnp.bfloat16)
+    last_stride, last_size = groups[-1]
+    active = gather_digit(active, last_stride, last_size)
+    per = SEQ_SIZE // MP_SIZE
+    pairs = []
+    for s in range(SEQ_SIZE):
+        lead = 0
+        for stride, size in groups[:-1]:
+            lead = lead * size + (s // stride) % size
+        last = (s // last_stride) % last_size
+        for m in range(MP_SIZE):
+            pairs.append((s * MP_SIZE + m, (m * per + lead) * MP_SIZE + last))
+    return lax.ppermute(active, ("seq", "mp"), pairs)
 
 
 def merge_stack(stack):
@@ -252,21 +274,10 @@
     ).astype(jnp.bfloat16)
 
     hidden_cols = seq_columns(hidden, gate_weight.shape[0])
-    hidden_units = gate_weight.shape[1]
-    summed_both = seq_total(
-        jnp.concatenate(
-            [
-                jnp.dot(hidden_cols, gate_weight, preferred_element_type=jnp.float32),
-                jnp.dot(hidden_cols, up_weight, preferred_element_type=jnp.float32),
-            ],
-            axis=1,
-        ),
-        ladder=True,
-    )
-    active = (jax.nn.silu(summed_both[:, :hidden_units]) * summed_both[:, hidden_units:]).astype(
-        jnp.bfloat16
-    )
-    active_cols = seq_columns(active, down_weight.shape[0])
+    active_cols = gate_up_active(
+        jnp.dot(hidden_cols, gate_weight, preferred_element_type=jnp.float32),
+        jnp.dot(hidden_cols, up_weight, preferred_element_type=jnp.float32),
+    )
     mlp_out = seq_total(jnp.dot(active_cols, down_weight, preferred_element_type=jnp.float32))
     mlp_squares = feature_sums(jnp.sum(mlp_out * mlp_out, axis=1))
     decoded = (
@@ -280,7 +291,7 @@
     SEQ_SIZE = mesh.shape["seq"]
     MP_SIZE = mesh.shape["mp"]
     factors = []
-    left = SEQ_SIZE
+    left = SEQ_SIZE // MP_SIZE
     if left % 2 == 0:
         factors.append(2)
         left //= 2
@@ -289,6 +300,7 @@
         left //= 4
     if left > 1:
         factors.append(left)
+    factors.append(MP_SIZE)
     SEQ_FACTORS = tuple(factors)
     in_specs = (
         P(None, None, "mp"),

time: 219 us -> 217 us (level)
  waiting for transfers between devices: 93.8 us -> 74.3 us
  starting transfers between devices: 96.6 us -> 108 us
  local copies, waits for them, and re-layouts: 7.87 us -> 12.4 us
  other arithmetic: 8.49 us -> 10.9 us
    ppermute x34, starting transfers between devices: 49.7 us -> 78.9 us  [exchange(): lax.ppermute(value, axis, digit_pairs(count, stride, size, shift))]
    ppermute x12 -> x4, starting transfers between devices: 28.8 us -> 2.84 us  [the longest x3 2.17 us: seq_columns(): return lax.ppermute(piece, ('seq', 'mp'), pairs)]
    ppermute x10, starting transfers between devices: 9.16 us -> 21.4 us  [scatter_digit(): lax.ppermute(send, 'seq', digit_pairs(SEQ_SIZE, stride, size, shift))]
    ppermute x34, waiting for transfers between devices: 61.1 us -> 53.6 us  [exchange(): lax.ppermute(value, axis, digit_pairs(count, stride, size, shift))]
    ppermute x10 -> x6, waiting for transfers between devices: 12.8 us -> 6.18 us  [gather_digit(): lax.ppermute(current, 'seq', digit_pairs(SEQ_SIZE, stride, size, shift))]
    ppermute x10 -> x6, starting transfers between devices: 8.9 us -> 4.41 us  [gather_digit(): lax.ppermute(current, 'seq', digit_pairs(SEQ_SIZE, stride, size, shift))]
    ppermute x12 -> x4, waiting for transfers between devices: 4.39 us -> 0.01 us  [the longest x3 0.01 us: seq_columns(): return lax.ppermute(piece, ('seq', 'mp'), pairs)]
    another operation x1 -> x2, other arithmetic: 0.25 us -> 3.88 us  [the longest x1 3.64 us: gate_up_active(): jnp.stack([gate_part.reshape(rows, SEQ_SIZE, unit_block), up_part.reshape...]
  transfers between devices with their start and end apart: 66 -> 54, of which waited for: 58 -> 39; matrix products, arithmetic and copies ran while one was open for 3% -> 3% of each run, Pallas kernels for 0% -> 0%
where the time goes in v1:
time: 217 us
  starting transfers between devices  108 us (50%)
  waiting for transfers between devices  74.3 us (34%)
  local copies, waits for them, and re-layouts  12.4 us (6%)
  other arithmetic  10.9 us (5%)
  matrix products  9.86 us (5%)
    ppermute x34, starting transfers between devices, exchange(): lax.ppermute(value, axis, digit_pairs(count, stride, size, shift))  78.9 us
    ppermute x34, waiting for transfers between devices, exchange(): lax.ppermute(value, axis, digit_pairs(count, stride, size, shift))  53.6 us
    ppermute x10, starting transfers between devices, scatter_digit(): lax.ppermute(send, 'seq', digit_pairs(SEQ_SIZE, stride, size, shift))  21.4 us
    ppermute x10, waiting for transfers between devices, scatter_digit(): lax.ppermute(send, 'seq', digit_pairs(SEQ_SIZE, stride, size, shift))  14.5 us
    ppermute x6, waiting for transfers between devices, gather_digit(): lax.ppermute(current, 'seq', digit_pairs(SEQ_SIZE, stride, size, shift))  6.18 us
    dot_general x4, matrix products, local(): lax.dot_general(flat_queries[:, h * HD:(h + 1) * HD], keys[:, h * HD:(h +...  4.51 us
    ppermute x6, starting transfers between devices, gather_digit(): lax.ppermute(current, 'seq', digit_pairs(SEQ_SIZE, stride, size, shift))  4.41 us
  transfers between devices with their start and end apart: 54, of which 39 were waited for; matrix products, arithmetic and copies ran while one was open for 3% of the time, Pallas kernels for 0%

profile of v1, /device:TPU:0, one launch (start us, length us, event | category | flops | bytes accessed | tf_op | source)
XLA Modules:
  0.0 216.7 jit_solution(8903536243771069855)
XLA Ops:
  7.7 1.4 collective-permute-done.1
  9.2 1.7 collective-permute-start.2
  11.1 2.8 %collective-permute-start.3 = (f32[64,768]{1,0:T(8,128)S(1)}, f32[64,768]{1,0:T(8,128)S(1)}, u32[]{:S(2)}, u32[]{:S(2)}) collective-permute-start(f32[64,768]{1,0:T(8,128)S(1)} %get-tuple-element.14), channel_id=1, source_target_pairs={{0,16},{4,20},{8,24},{12,28},{16,0},{20,4},{24,8},{28,12},{32,48},... | collective-permute-start | bytes 589832 | tf_op jit(solution)/shard_map/ppermute | solution.py:71
  13.9 1.4 collective-permute-start.4
  15.3 2.1 collective-permute-done.2
  17.5 5.3 %collective-permute-done.3 = f32[64,768]{1,0:T(8,128)S(1)} collective-permute-done((f32[64,768]{1,0:T(8,128)S(1)}, f32[64,768]{1,0:T(8,128)S(1)}, u32[]{:S(2)}, u32[]{:S(2)}) %collective-permute-start.3) | collective-permute-done | bytes 196640 | tf_op jit(solution)/shard_map/ppermute | solution.py:71
  22.9 4.7 %collective-permute-start.5 = (f32[64,768]{1,0:T(8,128)S(1)}, f32[64,768]{1,0:T(8,128)S(1)}, u32[]{:S(2)}, u32[]{:S(2)}) collective-permute-start(f32[64,768]{1,0:T(8,128)S(1)} %reduce_sum.189), channel_id=1, source_target_pairs={{0,32},{4,36},{8,40},{12,44},{16,48},{20,52},{24,56},{28,60},{32,6... | collective-permute-start | bytes 589832 | tf_op jit(solution)/shard_map/ppermute | solution.py:71
  27.6 5.0 %collective-permute-start.6 = (f32[64,768]{1,0:T(8,128)S(1)}, f32[64,768]{1,0:T(8,128)S(1)}, u32[]{:S(2)}, u32[]{:S(2)}) collective-permute-start(f32[64,768]{1,0:T(8,128)S(1)} %reduce_sum.189), channel_id=1, source_target_pairs={{0,64},{4,68},{8,72},{12,76},{16,80},{20,84},{24,88},{28,92},{32,9... | collective-permute-start | bytes 589832 | tf_op jit(solution)/shard_map/ppermute | solution.py:71
  32.6 1.9 collective-permute-start.7
  34.7 1.3 collective-permute-done.5
  36.0 4.9 %collective-permute-done.6 = f32[64,768]{1,0:T(8,128)S(1)} collective-permute-done((f32[64,768]{1,0:T(8,128)S(1)}, f32[64,768]{1,0:T(8,128)S(1)}, u32[]{:S(2)}, u32[]{:S(2)}) %collective-permute-start.6) | collective-permute-done | bytes 196640 | tf_op jit(solution)/shard_map/ppermute | solution.py:71
  41.2 1.4 collective-permute-done.8
  42.7 2.6 %collective-permute-start.9 = (f32[64,2]{0,1:T(2,128)S(1)}, f32[64,2]{0,1:T(2,128)S(1)}, u32[]{:S(2)}, u32[]{:S(2)}) collective-permute-start(f32[64,2]{0,1:T(2,128)S(1)} %pad_maximum_fusion.6), channel_id=1, source_target_pairs={{0,1},{1,2},{2,3},{3,0},{4,5},{5,6},{6,7},{7,4},{8,9},{9,10},{10,1... | collective-permute-start | bytes 1544 | tf_op jit(solution)/shard_map/ppermute | solution.py:71
  45.2 2.5 %collective-permute-start.10 = (f32[64,2]{0,1:T(2,128)S(1)}, f32[64,2]{0,1:T(2,128)S(1)}, u32[]{:S(2)}, u32[]{:S(2)}) collective-permute-start(f32[64,2]{0,1:T(2,128)S(1)} %pad_maximum_fusion.6), channel_id=1, source_target_pairs={{0,2},{1,3},{2,0},{3,1},{4,6},{5,7},{6,4},{7,5},{8,10},{9,11},{10,... | collective-permute-start | bytes 1544 | tf_op jit(solution)/shard_map/ppermute | solution.py:71
  47.7 1.5 collective-permute-start.11
  51.9 1.8 convolution_bitcast_fusion
  53.8 1.7 convolution_bitcast_fusion.1
  57.2 1.4 fusion.2
  63.2 1.7 collective-permute-start.13
  65.4 3.2 %collective-permute-start.14 = (f32[4,64,130]{1,0,2:T(4,128)S(1)}, f32[4,64,130]{1,0,2:T(4,128)S(1)}, u32[]{:S(2)}, u32[]{:S(2)}) collective-permute-start(f32[4,64,130]{1,0,2:T(4,128)S(1)} %pad_maximum_fusion.2), channel_id=1, source_target_pairs={{0,16},{4,20},{8,24},{12,28},{16,0},{20,4},{24,8},{28,12},{32,48},... | collective-permute-start | bytes 399368 | tf_op jit(solution)/shard_map/ppermute | solution.py:71
  69.4 3.9 %collective-permute-done.13 = f32[4,64,130]{1,0,2:T(4,128)S(1)} collective-permute-done((f32[4,64,130]{1,0,2:T(4,128)S(1)}, f32[4,64,130]{1,0,2:T(4,128)S(1)}, u32[]{:S(2)}, u32[]{:S(2)}) %collective-permute-start.13) | collective-permute-done | bytes 133152 | tf_op jit(solution)/shard_map/ppermute | solution.py:71
  73.3 6.8 %collective-permute-done.14 = f32[4,64,130]{1,0,2:T(4,128)S(1)} collective-permute-done((f32[4,64,130]{1,0,2:T(4,128)S(1)}, f32[4,64,130]{1,0,2:T(4,128)S(1)}, u32[]{:S(2)}, u32[]{:S(2)}) %collective-permute-start.14) | collective-permute-done | bytes 133152 | tf_op jit(solution)/shard_map/ppermute | solution.py:71
  80.8 1.8 collective-permute-start.16
  82.8 2.4 %collective-permute-start.17 = (f32[4,64,130]{1,0,2:T(4,128)S(1)}, f32[4,64,130]{1,0,2:T(4,128)S(1)}, u32[]{:S(2)}, u32[]{:S(2)}) collective-permute-start(f32[4,64,130]{1,0,2:T(4,128)S(1)} %pad_maximum_fusion.3), channel_id=1, source_target_pairs={{0,64},{4,68},{8,72},{12,76},{16,80},{20,84},{24,88},{28,92},{32,9... | collective-permute-start | bytes 399368 | tf_op jit(solution)/shard_map/ppermute | solution.py:71
  86.4 4.0 %collective-permute-done.16 = f32[4,64,130]{1,0,2:T(4,128)S(1)} collective-permute-done((f32[4,64,130]{1,0,2:T(4,128)S(1)}, f32[4,64,130]{1,0,2:T(4,128)S(1)}, u32[]{:S(2)}, u32[]{:S(2)}) %collective-permute-start.16) | collective-permute-done | bytes 133152 | tf_op jit(solution)/shard_map/ppermute | solution.py:71
  90.5 5.7 %collective-permute-done.17 = f32[4,64,130]{1,0,2:T(4,128)S(1)} collective-permute-done((f32[4,64,130]{1,0,2:T(4,128)S(1)}, f32[4,64,130]{1,0,2:T(4,128)S(1)}, u32[]{:S(2)}, u32[]{:S(2)}) %collective-permute-start.17) | collective-permute-done | bytes 133152 | tf_op jit(solution)/shard_map/ppermute | solution.py:71
  99.2 1.2 collective-permute-done.20
  100.5 2.4 %collective-permute-start.21 = (f32[64,256]{1,0:T(8,128)S(1)}, f32[64,256]{1,0:T(8,128)S(1)}, u32[]{:S(2)}, u32[]{:S(2)}) collective-permute-start(f32[64,256]{1,0:T(8,128)S(1)} %get-tuple-element.10), channel_id=1, source_target_pairs={{0,8},{4,12},{8,16},{12,20},{16,24},{20,28},{24,0},{28,4},{32,40},... | collective-permute-start | bytes 196616 | tf_op jit(solution)/shard_map/ppermute | solution.py:71
  102.8 2.4 %collective-permute-start.22 = (f32[64,256]{1,0:T(8,128)S(1)}, f32[64,256]{1,0:T(8,128)S(1)}, u32[]{:S(2)}, u32[]{:S(2)}) collective-permute-start(f32[64,256]{1,0:T(8,128)S(1)} %get-tuple-element.10), channel_id=1, source_target_pairs={{0,16},{4,20},{8,24},{12,28},{16,0},{20,4},{24,8},{28,12},{32,48},... | collective-permute-start | bytes 196616 | tf_op jit(solution)/shard_map/ppermute | solution.py:71
  106.2 2.7 %collective-permute-done.22 = f32[64,256]{1,0:T(8,128)S(1)} collective-permute-done((f32[64,256]{1,0:T(8,128)S(1)}, f32[64,256]{1,0:T(8,128)S(1)}, u32[]{:S(2)}, u32[]{:S(2)}) %collective-permute-start.22) | collective-permute-done | bytes 65568 | tf_op jit(solution)/shard_map/ppermute | solution.py:71
  109.6 7.5 %collective-permute-start.24 = (f32[64,256]{1,0:T(8,128)S(1)}, f32[64,256]{1,0:T(8,128)S(1)}, u32[]{:S(2)}, u32[]{:S(2)}) collective-permute-start(f32[64,256]{1,0:T(8,128)S(1)} %reduce_sum.202), channel_id=1, source_target_pairs={{0,32},{4,36},{8,40},{12,44},{16,48},{20,52},{24,56},{28,60},{32,6... | collective-permute-start | bytes 196616 | tf_op jit(solution)/shard_map/ppermute | solution.py:71
  117.1 5.0 %collective-permute-start.25 = (f32[64,256]{1,0:T(8,128)S(1)}, f32[64,256]{1,0:T(8,128)S(1)}, u32[]{:S(2)}, u32[]{:S(2)}) collective-permute-start(f32[64,256]{1,0:T(8,128)S(1)} %reduce_sum.202), channel_id=1, source_target_pairs={{0,64},{4,68},{8,72},{12,76},{16,80},{20,84},{24,88},{28,92},{32,9... | collective-permute-start | bytes 196616 | tf_op jit(solution)/shard_map/ppermute | solution.py:71
  122.1 1.4 collective-permute-start.26
  123.6 1.4 collective-permute-done.25
  125.0 1.3 collective-permute-done.26
  126.5 1.2 collective-permute-done.27
  128.6 1.9 collective-permute-start.29
  131.4 1.3 collective-permute-done.28
  136.1 1.4 stack_reshape.7
  137.5 3.6 %pad_maximum_fusion = f32[64,32,2,64]{3,2,1,0:T(2,128)S(1)} fusion(f32[64,32,1,64]{3,2,1,0:T(1,128)} %bitcast.246, f32[64,32,1,64]{3,2,1,0:T(1,128)S(1)} %bitcast.245), kind=kLoop, calls=%fused_computation.9 | loop fusion | flops 262144 | bytes 2097152 | tf_op jit(solution)/shard_map/stack | solution.py:118
  141.1 2.0 reshape.254
  143.3 1.8 collective-permute-done.32
  145.8 2.5 %collective-permute-start.34 = (f32[64,512]{1,0:T(8,128)S(1)}, f32[64,512]{1,0:T(8,128)S(1)}, u32[]{:S(2)}, u32[]{:S(2)}) collective-permute-start(f32[64,512]{1,0:T(8,128)S(1)} %get-tuple-element.19), channel_id=1, source_target_pairs={{0,16},{4,20},{8,24},{12,28},{16,0},{20,4},{24,8},{28,12},{32,48},... | collective-permute-start | bytes 393224 | tf_op jit(solution)/shard_map/ppermute | solution.py:83
  149.5 5.4 %collective-permute-done.33 = f32[64,512]{1,0:T(8,128)S(1)} collective-permute-done((f32[64,512]{1,0:T(8,128)S(1)}, f32[64,512]{1,0:T(8,128)S(1)}, u32[]{:S(2)}, u32[]{:S(2)}) %collective-permute-start.33) | collective-permute-done | bytes 131104 | tf_op jit(solution)/shard_map/ppermute | solution.py:83
  155.5 7.0 %collective-permute-start.36 = (f32[64,128]{1,0:T(8,128)S(1)}, f32[64,128]{1,0:T(8,128)S(1)}, u32[]{:S(2)}, u32[]{:S(2)}) collective-permute-start(f32[64,128]{1,0:T(8,128)S(1)} %get-tuple-element.26), channel_id=1, source_target_pairs={{0,32},{4,36},{8,40},{12,44},{16,48},{20,52},{24,56},{28,60},{32,6... | collective-permute-start | bytes 98312 | tf_op jit(solution)/shard_map/ppermute | solution.py:83
  162.6 5.2 %collective-permute-start.37 = (f32[64,128]{1,0:T(8,128)S(1)}, f32[64,128]{1,0:T(8,128)S(1)}, u32[]{:S(2)}, u32[]{:S(2)}) collective-permute-start(f32[64,128]{1,0:T(8,128)S(1)} %get-tuple-element.28), channel_id=1, source_target_pairs={{0,64},{4,68},{8,72},{12,76},{16,80},{20,84},{24,88},{28,92},{32,9... | collective-permute-start | bytes 98312 | tf_op jit(solution)/shard_map/ppermute | solution.py:83
  168.6 1.5 collective-permute-done.37
  170.0 1.7 collective-permute-done.38
  171.8 3.4 %collective-permute-start.40 = (bf16[64,64]{1,0:T(8,128)(2,1)S(1)}, bf16[64,64]{1,0:T(8,128)(2,1)S(1)}, u32[]{:S(2)}, u32[]{:S(2)}) collective-permute-start(bf16[64,64]{1,0:T(8,128)(2,1)S(1)} %fusion.26), channel_id=1, source_target_pairs={{0,64},{4,68},{8,72},{12,76},{16,80},{20,84},{24,88},{28,92},{32,9... | collective-permute-start | bytes 24584 | tf_op jit(solution)/shard_map/ppermute | solution.py:94
  177.3 1.7 collective-permute-done.41
  180.2 4.0 %collective-permute-start.43 = (f32[64,256]{1,0:T(8,128)S(1)}, f32[64,256]{1,0:T(8,128)S(1)}, u32[]{:S(2)}, u32[]{:S(2)}) collective-permute-start(f32[64,256]{1,0:T(8,128)S(1)} %constant_dynamic-slice_fusion), channel_id=1, source_target_pairs={{0,4},{4,0},{8,12},{12,8},{16,20},{20,16},{24,28},{28,24},{32,36},... | collective-permute-start | bytes 196616 | tf_op jit(solution)/shard_map/ppermute | solution.py:83
  185.1 2.6 %collective-permute-start.44 = (f32[64,256]{1,0:T(8,128)S(1)}, f32[64,256]{1,0:T(8,128)S(1)}, u32[]{:S(2)}, u32[]{:S(2)}) collective-permute-start(f32[64,256]{1,0:T(8,128)S(1)} %get-tuple-element.8), channel_id=1, source_target_pairs={{0,8},{4,12},{8,16},{12,20},{16,24},{20,28},{24,0},{28,4},{32,40},... | collective-permute-start | bytes 196616 | tf_op jit(solution)/shard_map/ppermute | solution.py:71
  187.8 2.6 %collective-permute-start.45 = (f32[64,256]{1,0:T(8,128)S(1)}, f32[64,256]{1,0:T(8,128)S(1)}, u32[]{:S(2)}, u32[]{:S(2)}) collective-permute-start(f32[64,256]{1,0:T(8,128)S(1)} %get-tuple-element.8), channel_id=1, source_target_pairs={{0,16},{4,20},{8,24},{12,28},{16,0},{20,4},{24,8},{28,12},{32,48},... | collective-permute-start | bytes 196616 | tf_op jit(solution)/shard_map/ppermute | solution.py:71
  190.3 1.5 collective-permute-start.46
  191.9 2.1 collective-permute-done.45
  194.6 2.6 %collective-permute-start.47 = (f32[64,256]{1,0:T(8,128)S(1)}, f32[64,256]{1,0:T(8,128)S(1)}, u32[]{:S(2)}, u32[]{:S(2)}) collective-permute-start(f32[64,256]{1,0:T(8,128)S(1)} %reduce_sum.206), channel_id=1, source_target_pairs={{0,32},{4,36},{8,40},{12,44},{16,48},{20,52},{24,56},{28,60},{32,6... | collective-permute-start | bytes 196616 | tf_op jit(solution)/shard_map/ppermute | solution.py:71
  197.2 5.2 %collective-permute-start.48 = (f32[64,256]{1,0:T(8,128)S(1)}, f32[64,256]{1,0:T(8,128)S(1)}, u32[]{:S(2)}, u32[]{:S(2)}) collective-permute-start(f32[64,256]{1,0:T(8,128)S(1)} %reduce_sum.206), channel_id=1, source_target_pairs={{0,64},{4,68},{8,72},{12,76},{16,80},{20,84},{24,88},{28,92},{32,9... | collective-permute-start | bytes 196616 | tf_op jit(solution)/shard_map/ppermute | solution.py:71
  202.4 1.7 collective-permute-start.49
  204.2 1.2 collective-permute-done.48
  205.3 1.3 collective-permute-done.49
  206.8 1.2 collective-permute-done.50
  208.2 2.6 %collective-permute-start.51 = (f32[64]{0:T(128)S(1)}, f32[64]{0:T(128)S(1)}, u32[]{:S(2)}, u32[]{:S(2)}) collective-permute-start(f32[64]{0:T(128)S(1)} %multiply_reduce_fusion), channel_id=1, source_target_pairs={{0,1},{1,2},{2,3},{3,0},{4,5},{5,6},{6,7},{7,4},{8,9},{9,10},{10,1... | collective-permute-start | bytes 776 | tf_op jit(solution)/shard_map/ppermute | solution.py:71
  211.0 2.6 %collective-permute-start.53 = (f32[64]{0:T(128)S(1)}, f32[64]{0:T(128)S(1)}, u32[]{:S(2)}, u32[]{:S(2)}) collective-permute-start(f32[64]{0:T(128)S(1)} %multiply_reduce_fusion), channel_id=1, source_target_pairs={{0,3},{1,0},{2,1},{3,2},{4,7},{5,4},{6,5},{7,6},{8,11},{9,8},{10,9... | collective-permute-start | bytes 776 | tf_op jit(solution)/shard_map/ppermute | solution.py:71
  213.6 2.2 %collective-permute-done.52 = f32[64]{0:T(128)S(1)} collective-permute-done((f32[64]{0:T(128)S(1)}, f32[64]{0:T(128)S(1)}, u32[]{:S(2)}, u32[]{:S(2)}) %collective-permute-start.52) | collective-permute-done | bytes 288 | tf_op jit(solution)/shard_map/ppermute | solution.py:71
  (257 shorter events, 39.7 us)
Async XLA Ops:
  0.0 135.2 %copy-start = (bf16[64,2048]{1,0:T(8,128)(2,1)S(1)}, bf16[64,2048]{1,0:T(8,128)(2,1)}, u32[]{:S(2)}) copy-start(bf16[64,2048]{1,0:T(8,128)(2,1)} %param.22) | copy-start | bytes 786436
  0.8 3.7 %collective-permute-start = (bf16[64,64]{1,0:T(8,128)(2,1)S(1)}, bf16[64,64]{1,0:T(8,128)(2,1)S(1)}, u32[]{:S(2)}, u32[]{:S(2)}) collective-permute-start(bf16[64,64]{1,0:T(8,128)(2,1)S(1)} %constant_dynamic-slice_fusion.12), channel_id=1, source_target_pairs={{0,0},{1,32},{2,64},{3,96},{4,4},{5,36},{6,68},{7,100},{8,8},{9,40... | collective-permute-start | bytes 24584 | tf_op jit(solution)/shard_map/ppermute | solution.py:47
  7.6 1.5 collective-permute-start.1
  9.2 8.2 %collective-permute-start.2 = (f32[64,768]{1,0:T(8,128)S(1)}, f32[64,768]{1,0:T(8,128)S(1)}, u32[]{:S(2)}, u32[]{:S(2)}) collective-permute-start(f32[64,768]{1,0:T(8,128)S(1)} %get-tuple-element.14), channel_id=1, source_target_pairs={{0,8},{4,12},{8,16},{12,20},{16,24},{20,28},{24,0},{28,4},{32,40},... | collective-permute-start | bytes 589832 | tf_op jit(solution)/shard_map/ppermute | solution.py:71
  11.1 11.7 %collective-permute-start.3 = (f32[64,768]{1,0:T(8,128)S(1)}, f32[64,768]{1,0:T(8,128)S(1)}, u32[]{:S(2)}, u32[]{:S(2)}) collective-permute-start(f32[64,768]{1,0:T(8,128)S(1)} %get-tuple-element.14), channel_id=1, source_target_pairs={{0,16},{4,20},{8,24},{12,28},{16,0},{20,4},{24,8},{28,12},{32,48},... | collective-permute-start | bytes 589832 | tf_op jit(solution)/shard_map/ppermute | solution.py:71
  13.9 8.9 %collective-permute-start.4 = (f32[64,768]{1,0:T(8,128)S(1)}, f32[64,768]{1,0:T(8,128)S(1)}, u32[]{:S(2)}, u32[]{:S(2)}) collective-permute-start(f32[64,768]{1,0:T(8,128)S(1)} %get-tuple-element.14), channel_id=1, source_target_pairs={{0,24},{4,28},{8,0},{12,4},{16,8},{20,12},{24,16},{28,20},{32,56},... | collective-permute-start | bytes 589832 | tf_op jit(solution)/shard_map/ppermute | solution.py:71
  22.9 13.1 %collective-permute-start.5 = (f32[64,768]{1,0:T(8,128)S(1)}, f32[64,768]{1,0:T(8,128)S(1)}, u32[]{:S(2)}, u32[]{:S(2)}) collective-permute-start(f32[64,768]{1,0:T(8,128)S(1)} %reduce_sum.189), channel_id=1, source_target_pairs={{0,32},{4,36},{8,40},{12,44},{16,48},{20,52},{24,56},{28,60},{32,6... | collective-permute-start | bytes 589832 | tf_op jit(solution)/shard_map/ppermute | solution.py:71
  27.6 13.3 %collective-permute-start.6 = (f32[64,768]{1,0:T(8,128)S(1)}, f32[64,768]{1,0:T(8,128)S(1)}, u32[]{:S(2)}, u32[]{:S(2)}) collective-permute-start(f32[64,768]{1,0:T(8,128)S(1)} %reduce_sum.189), channel_id=1, source_target_pairs={{0,64},{4,68},{8,72},{12,76},{16,80},{20,84},{24,88},{28,92},{32,9... | collective-permute-start | bytes 589832 | tf_op jit(solution)/shard_map/ppermute | solution.py:71
  32.6 8.3 %collective-permute-start.7 = (f32[64,768]{1,0:T(8,128)S(1)}, f32[64,768]{1,0:T(8,128)S(1)}, u32[]{:S(2)}, u32[]{:S(2)}) collective-permute-start(f32[64,768]{1,0:T(8,128)S(1)} %reduce_sum.189), channel_id=1, source_target_pairs={{0,96},{4,100},{8,104},{12,108},{16,112},{20,116},{24,120},{28,124... | collective-permute-start | bytes 589832 | tf_op jit(solution)/shard_map/ppermute | solution.py:71
  34.6 16.7 %copy-start.6 = (f32[512]{0:T(512)S(1)}, f32[512]{0:T(512)}, u32[]{:S(2)}) copy-start(f32[512]{0:T(512)} %param.26) | copy-start | bytes 6148
  34.6 16.7 %copy-start.7 = (f32[512]{0:T(512)S(1)}, f32[512]{0:T(512)}, u32[]{:S(2)}) copy-start(f32[512]{0:T(512)} %param.25) | copy-start | bytes 6148
  41.0 1.5 collective-permute-start.8
  42.7 6.6 %collective-permute-start.9 = (f32[64,2]{0,1:T(2,128)S(1)}, f32[64,2]{0,1:T(2,128)S(1)}, u32[]{:S(2)}, u32[]{:S(2)}) collective-permute-start(f32[64,2]{0,1:T(2,128)S(1)} %pad_maximum_fusion.6), channel_id=1, source_target_pairs={{0,1},{1,2},{2,3},{3,0},{4,5},{5,6},{6,7},{7,4},{8,9},{9,10},{10,1... | collective-permute-start | bytes 1544 | tf_op jit(solution)/shard_map/ppermute | solution.py:71
  45.2 5.1 %collective-permute-start.10 = (f32[64,2]{0,1:T(2,128)S(1)}, f32[64,2]{0,1:T(2,128)S(1)}, u32[]{:S(2)}, u32[]{:S(2)}) collective-permute-start(f32[64,2]{0,1:T(2,128)S(1)} %pad_maximum_fusion.6), channel_id=1, source_target_pairs={{0,2},{1,3},{2,0},{3,1},{4,6},{5,7},{6,4},{7,5},{8,10},{9,11},{10,... | collective-permute-start | bytes 1544 | tf_op jit(solution)/shard_map/ppermute | solution.py:71
  47.7 3.6 %collective-permute-start.11 = (f32[64,2]{0,1:T(2,128)S(1)}, f32[64,2]{0,1:T(2,128)S(1)}, u32[]{:S(2)}, u32[]{:S(2)}) collective-permute-start(f32[64,2]{0,1:T(2,128)S(1)} %pad_maximum_fusion.6), channel_id=1, source_target_pairs={{0,3},{1,0},{2,1},{3,2},{4,7},{5,4},{6,5},{7,6},{8,11},{9,8},{10,9... | collective-permute-start | bytes 1544 | tf_op jit(solution)/shard_map/ppermute | solution.py:71
  51.9 3.6 %copy-start.1 = (bf16[16,256,512]{2,1,0:T(8,128)(2,1)S(1)}, bf16[16,256,512]{2,1,0:T(8,128)(2,1)}, u32[]{:S(2)}) copy-start(bf16[16,256,512]{2,1,0:T(8,128)(2,1)} %param.29) | copy-start | bytes 12582916
  61.0 1.6 collective-permute-start.12
  63.2 10.0 %collective-permute-start.13 = (f32[4,64,130]{1,0,2:T(4,128)S(1)}, f32[4,64,130]{1,0,2:T(4,128)S(1)}, u32[]{:S(2)}, u32[]{:S(2)}) collective-permute-start(f32[4,64,130]{1,0,2:T(4,128)S(1)} %pad_maximum_fusion.2), channel_id=1, source_target_pairs={{0,8},{4,12},{8,16},{12,20},{16,24},{20,28},{24,0},{28,4},{32,40},... | collective-permute-start | bytes 399368 | tf_op jit(solution)/shard_map/ppermute | solution.py:71
  65.4 14.8 %collective-permute-start.14 = (f32[4,64,130]{1,0,2:T(4,128)S(1)}, f32[4,64,130]{1,0,2:T(4,128)S(1)}, u32[]{:S(2)}, u32[]{:S(2)}) collective-permute-start(f32[4,64,130]{1,0,2:T(4,128)S(1)} %pad_maximum_fusion.2), channel_id=1, source_target_pairs={{0,16},{4,20},{8,24},{12,28},{16,0},{20,4},{24,8},{28,12},{32,48},... | collective-permute-start | bytes 399368 | tf_op jit(solution)/shard_map/ppermute | solution.py:71
  68.5 11.7 %collective-permute-start.15 = (f32[4,64,130]{1,0,2:T(4,128)S(1)}, f32[4,64,130]{1,0,2:T(4,128)S(1)}, u32[]{:S(2)}, u32[]{:S(2)}) collective-permute-start(f32[4,64,130]{1,0,2:T(4,128)S(1)} %pad_maximum_fusion.2), channel_id=1, source_target_pairs={{0,24},{4,28},{8,0},{12,4},{16,8},{20,12},{24,16},{28,20},{32,56},... | collective-permute-start | bytes 399368 | tf_op jit(solution)/shard_map/ppermute | solution.py:71
  80.8 9.7 %collective-permute-start.16 = (f32[4,64,130]{1,0,2:T(4,128)S(1)}, f32[4,64,130]{1,0,2:T(4,128)S(1)}, u32[]{:S(2)}, u32[]{:S(2)}) collective-permute-start(f32[4,64,130]{1,0,2:T(4,128)S(1)} %pad_maximum_fusion.3), channel_id=1, source_target_pairs={{0,32},{4,36},{8,40},{12,44},{16,48},{20,52},{24,56},{28,60},{32,6... | collective-permute-start | bytes 399368 | tf_op jit(solution)/shard_map/ppermute | solution.py:71
  82.8 13.4 %collective-permute-start.17 = (f32[4,64,130]{1,0,2:T(4,128)S(1)}, f32[4,64,130]{1,0,2:T(4,128)S(1)}, u32[]{:S(2)}, u32[]{:S(2)}) collective-permute-start(f32[4,64,130]{1,0,2:T(4,128)S(1)} %pad_maximum_fusion.3), channel_id=1, source_target_pairs={{0,64},{4,68},{8,72},{12,76},{16,80},{20,84},{24,88},{28,92},{32,9... | collective-permute-start | bytes 399368 | tf_op jit(solution)/shard_map/ppermute | solution.py:71
  85.2 11.1 %collective-permute-start.18 = (f32[4,64,130]{1,0,2:T(4,128)S(1)}, f32[4,64,130]{1,0,2:T(4,128)S(1)}, u32[]{:S(2)}, u32[]{:S(2)}) collective-permute-start(f32[4,64,130]{1,0,2:T(4,128)S(1)} %pad_maximum_fusion.3), channel_id=1, source_target_pairs={{0,96},{4,100},{8,104},{12,108},{16,112},{20,116},{24,120},{28,124... | collective-permute-start | bytes 399368 | tf_op jit(solution)/shard_map/ppermute | solution.py:71
  96.7 2.2 %copy-start.5 = (bf16[64,512]{1,0:T(8,128)(2,1)S(1)}, bf16[64,512]{1,0:T(8,128)(2,1)}, u32[]{:S(2)}) copy-start(bf16[64,512]{1,0:T(8,128)(2,1)} %param.21) | copy-start | bytes 196612
  98.0 36.1 %copy-start.4 = (bf16[4,16,512]{2,1,0:T(8,128)(2,1)S(1)}, bf16[4,16,512]{2,1,0:T(8,128)(2,1)}, u32[]{:S(2)}) copy-start(bf16[4,16,512]{2,1,0:T(8,128)(2,1)} %param.17) | copy-start | bytes 196612
  98.1 36.1 %copy-start.8 = (f32[512]{0:T(512)S(1)}, f32[512]{0:T(512)}, u32[]{:S(2)}) copy-start(f32[512]{0:T(512)} %param.27) | copy-start | bytes 6148
  98.2 0.7 collective-permute-start.19
  99.1 1.3 collective-permute-start.20
  100.5 5.7 %collective-permute-start.21 = (f32[64,256]{1,0:T(8,128)S(1)}, f32[64,256]{1,0:T(8,128)S(1)}, u32[]{:S(2)}, u32[]{:S(2)}) collective-permute-start(f32[64,256]{1,0:T(8,128)S(1)} %get-tuple-element.10), channel_id=1, source_target_pairs={{0,8},{4,12},{8,16},{12,20},{16,24},{20,28},{24,0},{28,4},{32,40},... | collective-permute-start | bytes 196616 | tf_op jit(solution)/shard_map/ppermute | solution.py:71
  102.8 6.0 %collective-permute-start.22 = (f32[64,256]{1,0:T(8,128)S(1)}, f32[64,256]{1,0:T(8,128)S(1)}, u32[]{:S(2)}, u32[]{:S(2)}) collective-permute-start(f32[64,256]{1,0:T(8,128)S(1)} %get-tuple-element.10), channel_id=1, source_target_pairs={{0,16},{4,20},{8,24},{12,28},{16,0},{20,4},{24,8},{28,12},{32,48},... | collective-permute-start | bytes 196616 | tf_op jit(solution)/shard_map/ppermute | solution.py:71
  105.2 4.3 %collective-permute-start.23 = (f32[64,256]{1,0:T(8,128)S(1)}, f32[64,256]{1,0:T(8,128)S(1)}, u32[]{:S(2)}, u32[]{:S(2)}) collective-permute-start(f32[64,256]{1,0:T(8,128)S(1)} %get-tuple-element.10), channel_id=1, source_target_pairs={{0,24},{4,28},{8,0},{12,4},{16,8},{20,12},{24,16},{28,20},{32,56},... | collective-permute-start | bytes 196616 | tf_op jit(solution)/shard_map/ppermute | solution.py:71
  109.6 14.0 %collective-permute-start.24 = (f32[64,256]{1,0:T(8,128)S(1)}, f32[64,256]{1,0:T(8,128)S(1)}, u32[]{:S(2)}, u32[]{:S(2)}) collective-permute-start(f32[64,256]{1,0:T(8,128)S(1)} %reduce_sum.202), channel_id=1, source_target_pairs={{0,32},{4,36},{8,40},{12,44},{16,48},{20,52},{24,56},{28,60},{32,6... | collective-permute-start | bytes 196616 | tf_op jit(solution)/shard_map/ppermute | solution.py:71
  117.1 7.9 %collective-permute-start.25 = (f32[64,256]{1,0:T(8,128)S(1)}, f32[64,256]{1,0:T(8,128)S(1)}, u32[]{:S(2)}, u32[]{:S(2)}) collective-permute-start(f32[64,256]{1,0:T(8,128)S(1)} %reduce_sum.202), channel_id=1, source_target_pairs={{0,64},{4,68},{8,72},{12,76},{16,80},{20,84},{24,88},{28,92},{32,9... | collective-permute-start | bytes 196616 | tf_op jit(solution)/shard_map/ppermute | solution.py:71
  122.1 4.3 %collective-permute-start.26 = (f32[64,256]{1,0:T(8,128)S(1)}, f32[64,256]{1,0:T(8,128)S(1)}, u32[]{:S(2)}, u32[]{:S(2)}) collective-permute-start(f32[64,256]{1,0:T(8,128)S(1)} %reduce_sum.202), channel_id=1, source_target_pairs={{0,96},{4,100},{8,104},{12,108},{16,112},{20,116},{24,120},{28,124... | collective-permute-start | bytes 196616 | tf_op jit(solution)/shard_map/ppermute | solution.py:71
  123.4 12.4 %copy-start.2 = (bf16[64,2048]{1,0:T(8,128)(2,1)S(1)}, bf16[64,2048]{1,0:T(8,128)(2,1)}, u32[]{:S(2)}) copy-start(bf16[64,2048]{1,0:T(8,128)(2,1)} %param.23) | copy-start | bytes 786436
  126.4 1.3 collective-permute-start.27
  127.8 4.8 %collective-permute-start.28 = (f32[64]{0:T(128)S(1)}, f32[64]{0:T(128)S(1)}, u32[]{:S(2)}, u32[]{:S(2)}) collective-permute-start(f32[64]{0:T(128)S(1)} %multiply_reduce_fusion.1), channel_id=1, source_target_pairs={{0,1},{1,2},{2,3},{3,0},{4,5},{5,6},{6,7},{7,4},{8,9},{9,10},{10,1... | collective-permute-start | bytes 776 | tf_op jit(solution)/shard_map/ppermute | solution.py:71
  128.6 5.1 %collective-permute-start.29 = (f32[64]{0:T(128)S(1)}, f32[64]{0:T(128)S(1)}, u32[]{:S(2)}, u32[]{:S(2)}) collective-permute-start(f32[64]{0:T(128)S(1)} %multiply_reduce_fusion.1), channel_id=1, source_target_pairs={{0,2},{1,3},{2,0},{3,1},{4,6},{5,7},{6,4},{7,5},{8,10},{9,11},{10,... | collective-permute-start | bytes 776 | tf_op jit(solution)/shard_map/ppermute | solution.py:71
  130.5 3.6 %collective-permute-start.30 = (f32[64]{0:T(128)S(1)}, f32[64]{0:T(128)S(1)}, u32[]{:S(2)}, u32[]{:S(2)}) collective-permute-start(f32[64]{0:T(128)S(1)} %multiply_reduce_fusion.1), channel_id=1, source_target_pairs={{0,3},{1,0},{2,1},{3,2},{4,7},{5,4},{6,5},{7,6},{8,11},{9,8},{10,9... | collective-permute-start | bytes 776 | tf_op jit(solution)/shard_map/ppermute | solution.py:71
  134.3 0.9 collective-permute-start.31
  143.2 36.9 %copy-start.3 = (bf16[256,512]{1,0:T(8,128)(2,1)S(1)}, bf16[256,512]{1,0:T(8,128)(2,1)}, u32[]{:S(2)}) copy-start(bf16[256,512]{1,0:T(8,128)(2,1)} %param.24) | copy-start | bytes 786436
  143.2 2.0 collective-permute-start.32
  145.3 9.6 %collective-permute-start.33 = (f32[64,512]{1,0:T(8,128)S(1)}, f32[64,512]{1,0:T(8,128)S(1)}, u32[]{:S(2)}, u32[]{:S(2)}) collective-permute-start(f32[64,512]{1,0:T(8,128)S(1)} %get-tuple-element.17), channel_id=1, source_target_pairs={{0,8},{4,12},{8,16},{12,20},{16,24},{20,28},{24,0},{28,4},{32,40},... | collective-permute-start | bytes 393224 | tf_op jit(solution)/shard_map/ppermute | solution.py:83
  145.8 9.1 %collective-permute-start.34 = (f32[64,512]{1,0:T(8,128)S(1)}, f32[64,512]{1,0:T(8,128)S(1)}, u32[]{:S(2)}, u32[]{:S(2)}) collective-permute-start(f32[64,512]{1,0:T(8,128)S(1)} %get-tuple-element.19), channel_id=1, source_target_pairs={{0,16},{4,20},{8,24},{12,28},{16,0},{20,4},{24,8},{28,12},{32,48},... | collective-permute-start | bytes 393224 | tf_op jit(solution)/shard_map/ppermute | solution.py:83
  148.4 7.1 %collective-permute-start.35 = (f32[64,512]{1,0:T(8,128)S(1)}, f32[64,512]{1,0:T(8,128)S(1)}, u32[]{:S(2)}, u32[]{:S(2)}) collective-permute-start(f32[64,512]{1,0:T(8,128)S(1)} %get-tuple-element.18), channel_id=1, source_target_pairs={{0,24},{4,28},{8,0},{12,4},{16,8},{20,12},{24,16},{28,20},{32,56},... | collective-permute-start | bytes 393224 | tf_op jit(solution)/shard_map/ppermute | solution.py:83
  155.5 60.5 %copy-start.9 = (f32[512]{0:T(512)S(1)}, f32[512]{0:T(512)}, u32[]{:S(2)}) copy-start(f32[512]{0:T(512)} %param.28) | copy-start | bytes 6148
  155.5 13.0 %collective-permute-start.36 = (f32[64,128]{1,0:T(8,128)S(1)}, f32[64,128]{1,0:T(8,128)S(1)}, u32[]{:S(2)}, u32[]{:S(2)}) collective-permute-start(f32[64,128]{1,0:T(8,128)S(1)} %get-tuple-element.26), channel_id=1, source_target_pairs={{0,32},{4,36},{8,40},{12,44},{16,48},{20,52},{24,56},{28,60},{32,6... | collective-permute-start | bytes 98312 | tf_op jit(solution)/shard_map/ppermute | solution.py:83
  162.6 7.5 %collective-permute-start.37 = (f32[64,128]{1,0:T(8,128)S(1)}, f32[64,128]{1,0:T(8,128)S(1)}, u32[]{:S(2)}, u32[]{:S(2)}) collective-permute-start(f32[64,128]{1,0:T(8,128)S(1)} %get-tuple-element.28), channel_id=1, source_target_pairs={{0,64},{4,68},{8,72},{12,76},{16,80},{20,84},{24,88},{28,92},{32,9... | collective-permute-start | bytes 98312 | tf_op jit(solution)/shard_map/ppermute | solution.py:83
  167.8 3.9 %collective-permute-start.38 = (f32[64,128]{1,0:T(8,128)S(1)}, f32[64,128]{1,0:T(8,128)S(1)}, u32[]{:S(2)}, u32[]{:S(2)}) collective-permute-start(f32[64,128]{1,0:T(8,128)S(1)} %get-tuple-element.27), channel_id=1, source_target_pairs={{0,96},{4,100},{8,104},{12,108},{16,112},{20,116},{24,120},{28,124... | collective-permute-start | bytes 98312 | tf_op jit(solution)/shard_map/ppermute | solution.py:83
  171.8 5.0 %collective-permute-start.39 = (bf16[64,64]{1,0:T(8,128)(2,1)S(1)}, bf16[64,64]{1,0:T(8,128)(2,1)S(1)}, u32[]{:S(2)}, u32[]{:S(2)}) collective-permute-start(bf16[64,64]{1,0:T(8,128)(2,1)S(1)} %fusion.26), channel_id=1, source_target_pairs={{0,32},{4,36},{8,40},{12,44},{16,48},{20,52},{24,56},{28,60},{32,6... | collective-permute-start | bytes 24584 | tf_op jit(solution)/shard_map/ppermute | solution.py:94
  171.8 5.3 %collective-permute-start.40 = (bf16[64,64]{1,0:T(8,128)(2,1)S(1)}, bf16[64,64]{1,0:T(8,128)(2,1)S(1)}, u32[]{:S(2)}, u32[]{:S(2)}) collective-permute-start(bf16[64,64]{1,0:T(8,128)(2,1)S(1)} %fusion.26), channel_id=1, source_target_pairs={{0,64},{4,68},{8,72},{12,76},{16,80},{20,84},{24,88},{28,92},{32,9... | collective-permute-start | bytes 24584 | tf_op jit(solution)/shard_map/ppermute | solution.py:94
  175.3 3.7 %collective-permute-start.41 = (bf16[64,64]{1,0:T(8,128)(2,1)S(1)}, bf16[64,64]{1,0:T(8,128)(2,1)S(1)}, u32[]{:S(2)}, u32[]{:S(2)}) collective-permute-start(bf16[64,64]{1,0:T(8,128)(2,1)S(1)} %fusion.26), channel_id=1, source_target_pairs={{0,96},{4,100},{8,104},{12,108},{16,112},{20,116},{24,120},{28,124... | collective-permute-start | bytes 24584 | tf_op jit(solution)/shard_map/ppermute | solution.py:94
  179.3 0.7 collective-permute-start.42
  180.2 4.9 %collective-permute-start.43 = (f32[64,256]{1,0:T(8,128)S(1)}, f32[64,256]{1,0:T(8,128)S(1)}, u32[]{:S(2)}, u32[]{:S(2)}) collective-permute-start(f32[64,256]{1,0:T(8,128)S(1)} %constant_dynamic-slice_fusion), channel_id=1, source_target_pairs={{0,4},{4,0},{8,12},{12,8},{16,20},{20,16},{24,28},{28,24},{32,36},... | collective-permute-start | bytes 196616 | tf_op jit(solution)/shard_map/ppermute | solution.py:83
  185.1 6.8 %collective-permute-start.44 = (f32[64,256]{1,0:T(8,128)S(1)}, f32[64,256]{1,0:T(8,128)S(1)}, u32[]{:S(2)}, u32[]{:S(2)}) collective-permute-start(f32[64,256]{1,0:T(8,128)S(1)} %get-tuple-element.8), channel_id=1, source_target_pairs={{0,8},{4,12},{8,16},{12,20},{16,24},{20,28},{24,0},{28,4},{32,40},... | collective-permute-start | bytes 196616 | tf_op jit(solution)/shard_map/ppermute | solution.py:71
  187.8 6.2 %collective-permute-start.45 = (f32[64,256]{1,0:T(8,128)S(1)}, f32[64,256]{1,0:T(8,128)S(1)}, u32[]{:S(2)}, u32[]{:S(2)}) collective-permute-start(f32[64,256]{1,0:T(8,128)S(1)} %get-tuple-element.8), channel_id=1, source_target_pairs={{0,16},{4,20},{8,24},{12,28},{16,0},{20,4},{24,8},{28,12},{32,48},... | collective-permute-start | bytes 196616 | tf_op jit(solution)/shard_map/ppermute | solution.py:71
  190.3 4.3 %collective-permute-start.46 = (f32[64,256]{1,0:T(8,128)S(1)}, f32[64,256]{1,0:T(8,128)S(1)}, u32[]{:S(2)}, u32[]{:S(2)}) collective-permute-start(f32[64,256]{1,0:T(8,128)S(1)} %get-tuple-element.8), channel_id=1, source_target_pairs={{0,24},{4,28},{8,0},{12,4},{16,8},{20,12},{24,16},{28,20},{32,56},... | collective-permute-start | bytes 196616 | tf_op jit(solution)/shard_map/ppermute | solution.py:71
  194.6 9.5 %collective-permute-start.47 = (f32[64,256]{1,0:T(8,128)S(1)}, f32[64,256]{1,0:T(8,128)S(1)}, u32[]{:S(2)}, u32[]{:S(2)}) collective-permute-start(f32[64,256]{1,0:T(8,128)S(1)} %reduce_sum.206), channel_id=1, source_target_pairs={{0,32},{4,36},{8,40},{12,44},{16,48},{20,52},{24,56},{28,60},{32,6... | collective-permute-start | bytes 196616 | tf_op jit(solution)/shard_map/ppermute | solution.py:71
  197.2 8.1 %collective-permute-start.48 = (f32[64,256]{1,0:T(8,128)S(1)}, f32[64,256]{1,0:T(8,128)S(1)}, u32[]{:S(2)}, u32[]{:S(2)}) collective-permute-start(f32[64,256]{1,0:T(8,128)S(1)} %reduce_sum.206), channel_id=1, source_target_pairs={{0,64},{4,68},{8,72},{12,76},{16,80},{20,84},{24,88},{28,92},{32,9... | collective-permute-start | bytes 196616 | tf_op jit(solution)/shard_map/ppermute | solution.py:71
  202.4 4.3 %collective-permute-start.49 = (f32[64,256]{1,0:T(8,128)S(1)}, f32[64,256]{1,0:T(8,128)S(1)}, u32[]{:S(2)}, u32[]{:S(2)}) collective-permute-start(f32[64,256]{1,0:T(8,128)S(1)} %reduce_sum.206), channel_id=1, source_target_pairs={{0,96},{4,100},{8,104},{12,108},{16,112},{20,116},{24,120},{28,124... | collective-permute-start | bytes 196616 | tf_op jit(solution)/shard_map/ppermute | solution.py:71
  206.7 1.3 collective-permute-start.50
  208.2 5.4 %collective-permute-start.51 = (f32[64]{0:T(128)S(1)}, f32[64]{0:T(128)S(1)}, u32[]{:S(2)}, u32[]{:S(2)}) collective-permute-start(f32[64]{0:T(128)S(1)} %multiply_reduce_fusion), channel_id=1, source_target_pairs={{0,1},{1,2},{2,3},{3,0},{4,5},{5,6},{6,7},{7,4},{8,9},{9,10},{10,1... | collective-permute-start | bytes 776 | tf_op jit(solution)/shard_map/ppermute | solution.py:71
  210.8 5.1 %collective-permute-start.52 = (f32[64]{0:T(128)S(1)}, f32[64]{0:T(128)S(1)}, u32[]{:S(2)}, u32[]{:S(2)}) collective-permute-start(f32[64]{0:T(128)S(1)} %multiply_reduce_fusion), channel_id=1, source_target_pairs={{0,2},{1,3},{2,0},{3,1},{4,6},{5,7},{6,4},{7,5},{8,10},{9,11},{10,... | collective-permute-start | bytes 776 | tf_op jit(solution)/shard_map/ppermute | solution.py:71
  211.0 4.9 %collective-permute-start.53 = (f32[64]{0:T(128)S(1)}, f32[64]{0:T(128)S(1)}, u32[]{:S(2)}, u32[]{:S(2)}) collective-permute-start(f32[64]{0:T(128)S(1)} %multiply_reduce_fusion), channel_id=1, source_target_pairs={{0,3},{1,0},{2,1},{3,2},{4,7},{5,4},{6,5},{7,6},{8,11},{9,8},{10,9... | collective-permute-start | bytes 776 | tf_op jit(solution)/shard_map/ppermute | solution.py:71
  (1 other events, 2.2 us)

commit v2 on v1

--- a/solution.py
+++ b/solution.py
@@ -96,7 +96,7 @@
     return whole
 
 
-def seq_total(partial_value, ladder=False):
+def seq_total(partial_value, ladder=False, butterfly=False):
     groups = seq_groups()
     current = partial_value
     if ladder:
@@ -104,6 +104,10 @@
             current = scatter_digit(current, stride, size)
         for stride, size in reversed(groups):
             current = gather_digit(current, stride, size)
+        return current
+    if butterfly:
+        for stride, size in groups:
+            current = jnp.sum(exchange(current, "seq", SEQ_SIZE, stride, size), axis=0)
         return current
     stride, size = groups[0]
     current = scatter_digit(current, stride, size)
@@ -240,34 +244,62 @@
         ]
     )
 
-    stats = jnp.concatenate([running, maxima[..., None], totals[..., None]], axis=2)
-    for stride, size in seq_groups():
-        stats = merge_stack(exchange(stats, "seq", SEQ_SIZE, stride, size))
-    cache_running = stats[..., :HD]
-    cache_highest = stats[..., HD]
-    cache_totals = stats[..., HD + 1]
-
-    q4 = queries.reshape(STEPS, R, local_heads, HD)
-    k4 = new_keys.reshape(STEPS, R, local_heads, HD)
-    v4 = new_values.reshape(STEPS, R, local_heads, HD)
-    fresh_scores = (
-        jnp.einsum("srhd,trhd->hsrt", q4, k4, preferred_element_type=jnp.float32) * score_scale
-    )
-    allowed = (jnp.arange(STEPS)[None, :] <= jnp.arange(STEPS)[:, None])[None, :, None, :]
+    seq = lax.axis_index("seq")
+    slice_width = local_width // SEQ_SIZE
+    per_head = HD // slice_width
+    send = jnp.concatenate(
+        [
+            running.reshape(local_heads, rows, per_head, slice_width).transpose(0, 2, 1, 3),
+            jnp.broadcast_to(maxima[:, None, :, None], (local_heads, per_head, rows, 1)),
+            jnp.broadcast_to(totals[:, None, :, None], (local_heads, per_head, rows, 1)),
+        ],
+        axis=3,
+    ).reshape(SEQ_SIZE, rows, slice_width + 2)
+    sources = lax.all_to_all(send, "seq", 0, 0, tiled=True)
+    source_max = sources[..., slice_width]
+    cache_highest = jnp.max(source_max, axis=0)
+    scale = jnp.exp(source_max - cache_highest[None])
+    cache_totals = jnp.sum(sources[..., slice_width + 1] * scale, axis=0)
+    cache_running = jnp.sum(sources[..., :slice_width] * scale[..., None], axis=0)
+
+    head = seq // per_head
+    offset = (seq % per_head) * slice_width
+    q4 = lax.dynamic_index_in_dim(queries, head, 1, keepdims=False).reshape(STEPS, R, HD)
+    k4 = lax.dynamic_index_in_dim(new_keys, head, 1, keepdims=False).reshape(STEPS, R, HD)
+    v4 = lax.dynamic_slice_in_dim(
+        lax.dynamic_index_in_dim(new_values, head, 1, keepdims=False), offset, slice_width, 1
+    ).reshape(STEPS, R, slice_width)
+    fresh_scores = jnp.einsum("srd,trd->srt", q4, k4, preferred_element_type=jnp.float32) * score_scale
+    allowed = (jnp.arange(STEPS)[None, :] <= jnp.arange(STEPS)[:, None])[:, None, :]
     fresh_scores = jnp.where(allowed, fresh_scores, very_low)
-    cache_highest = cache_highest.reshape(local_heads, STEPS, R)
+    cache_highest = cache_highest.reshape(STEPS, R)
     highest = jnp.maximum(cache_highest, jnp.max(fresh_scores, axis=-1))
     fresh_weights = jnp.where(allowed, jnp.exp(fresh_scores - highest[..., None]), 0.0)
     factor = jnp.exp(cache_highest - highest)
-    final_totals = cache_totals.reshape(local_heads, STEPS, R) * factor + jnp.sum(fresh_weights, axis=-1)
-    final_running = cache_running.reshape(local_heads, STEPS, R, HD) * factor[..., None] + jnp.einsum(
-        "hsrt,trhd->hsrd", fresh_weights.astype(jnp.bfloat16), v4, preferred_element_type=jnp.float32
-    )
-    attended = (final_running / final_totals[..., None]).astype(jnp.bfloat16)
-    attended = jnp.transpose(attended, (1, 2, 0, 3)).reshape(rows, local_width)
-
-    sliced = seq_columns(attended, output_weight.shape[0])
-    attention_out = seq_total(jnp.dot(sliced, output_weight, preferred_element_type=jnp.float32))
+    final_totals = cache_totals.reshape(STEPS, R) * factor + jnp.sum(fresh_weights, axis=-1)
+    final_running = cache_running.reshape(STEPS, R, slice_width) * factor[..., None] + jnp.einsum(
+        "srt,trd->srd", fresh_weights.astype(jnp.bfloat16), v4, preferred_element_type=jnp.float32
+    )
+    attended = (final_running / final_totals[..., None]).astype(jnp.bfloat16).reshape(rows, slice_width)
+
+    width = output_weight.shape[0]
+    per = local_width // width
+    holders = width // slice_width
+    sliced = jnp.zeros((rows, width), jnp.bfloat16)
+    mp = lax.axis_index("mp")
+    for shift in range(MP_SIZE):
+        pairs = [
+            (s * MP_SIZE + m, (m * per + s // holders) * MP_SIZE + (s % holders + shift) % MP_SIZE)
+            for s in range(SEQ_SIZE)
+            for m in range(MP_SIZE)
+        ]
+        received = lax.ppermute(attended, ("seq", "mp"), pairs)
+        sliced = lax.dynamic_update_slice_in_dim(
+            sliced, received, ((mp - shift) % MP_SIZE) * slice_width, 1
+        )
+    attention_out = seq_total(
+        jnp.dot(sliced, output_weight, preferred_element_type=jnp.float32), butterfly=True
+    )
     attention_squares = feature_sums(jnp.sum(attention_out * attention_out, axis=1))
     hidden = (
         token_rows.astype(jnp.float32) + attention_out * inverse_rms(attention_squares) * attention_gain
@@ -278,7 +310,9 @@
         jnp.dot(hidden_cols, gate_weight, preferred_element_type=jnp.float32),
         jnp.dot(hidden_cols, up_weight, preferred_element_type=jnp.float32),
     )
-    mlp_out = seq_total(jnp.dot(active_cols, down_weight, preferred_element_type=jnp.float32))
+    mlp_out = seq_total(
+        jnp.dot(active_cols, down_weight, preferred_element_type=jnp.float32), butterfly=True
+    )
     mlp_squares = feature_sums(jnp.sum(mlp_out * mlp_out, axis=1))
     decoded = (
         hidden.astype(jnp.float32) + mlp_out * inverse_rms(mlp_squares) * feedforward_gain

time: 217 us -> 227 us (1.046)
  waiting for transfers between devices: 74.3 us -> 61.3 us
  starting transfers between devices: 108 us -> 119 us
  local copies, waits for them, and re-layouts: 12.4 us -> 21.3 us
  other arithmetic: 10.9 us -> 14.3 us
    ppermute x34 -> x29, waiting for transfers between devices: 53.6 us -> 37.3 us  [exchange(): lax.ppermute(value, axis, digit_pairs(count, stride, size, shift))]
    ppermute x0 -> x4, starting transfers between devices: none -> 13.5 us  [local(): received = lax.ppermute(attended, ('seq', 'mp'), pairs)]
    all_to_all x0 -> x1, starting transfers between devices: none -> 7.08 us  [local(): sources = lax.all_to_all(send, 'seq', 0, 0, tiled=True)]
    all_to_all x0 -> x1, waiting for transfers between devices: none -> 6.88 us  [local(): sources = lax.all_to_all(send, 'seq', 0, 0, tiled=True)]
    ppermute x34 -> x29, starting transfers between devices: 78.9 us -> 73.7 us  [exchange(): lax.ppermute(value, axis, digit_pairs(count, stride, size, shift))]
    unnamed x29 -> x46, local copies, waits for them, and re-layouts: 1.86 us -> 6.72 us
    ppermute x10 -> x8, starting transfers between devices: 21.4 us -> 17.5 us  [scatter_digit(): lax.ppermute(send, 'seq', digit_pairs(SEQ_SIZE, stride, size, shift))]
    slice x0 -> x2, local copies, waits for them, and re-layouts: none -> 3.56 us  [the longest x1 3.54 us: local(): values[:, h * HD:(h + 1) * HD]]
  transfers between devices with their start and end apart: 54 -> 49, of which waited for: 39 -> 30; matrix products, arithmetic and copies ran while one was open for 3% -> 8% of each run, Pallas kernels for 0% -> 0%
where the time goes in v2:
time: 227 us; the launch traced here: 226 us
  starting transfers between devices  119 us (52%)
  waiting for transfers between devices  61.3 us (27%)
  local copies, waits for them, and re-layouts  21.3 us (9%)
  other arithmetic  14.3 us (6%)
  matrix products  8.54 us (4%)
    ppermute x29, starting transfers between devices, exchange(): lax.ppermute(value, axis, digit_pairs(count, stride, size, shift))  73.7 us
    ppermute x29, waiting for transfers between devices, exchange(): lax.ppermute(value, axis, digit_pairs(count, stride, size, shift))  37.3 us
    ppermute x8, starting transfers between devices, scatter_digit(): lax.ppermute(send, 'seq', digit_pairs(SEQ_SIZE, stride, size, shift))  17.5 us
    ppermute x4, starting transfers between devices, local(): received = lax.ppermute(attended, ('seq', 'mp'), pairs)  13.5 us
    ppermute x8, waiting for transfers between devices, scatter_digit(): lax.ppermute(send, 'seq', digit_pairs(SEQ_SIZE, stride, size, shift))  12.2 us
    all_to_all x1, starting transfers between devices, local(): sources = lax.all_to_all(send, 'seq', 0, 0, tiled=True)  7.08 us
    all_to_all x1, waiting for transfers between devices, local(): sources = lax.all_to_all(send, 'seq', 0, 0, tiled=True)  6.88 us
    unnamed x46, local copies, waits for them, and re-layouts  6.72 us
  transfers between devices with their start and end apart: 49, of which 30 were waited for; matrix products, arithmetic and copies ran while one was open for 8% of the time, Pallas kernels for 0%

profile of v2, /device:TPU:0, one launch (start us, length us, event | category | flops | bytes accessed | tf_op | source)
XLA Modules:
  0.0 225.5 jit_solution(2606836345295814674)
XLA Ops:
  0.0 1.4 constant_dynamic-slice_fusion.10
  1.4 1.4 collective-permute-start
  5.7 3.5 %fusion.26 = (bf16[4096,128]{1,0:T(8,128)(2,1)S(1)}, bf16[4096,128]{1,0:T(8,128)(2,1)S(1)}, bf16[4096,128]{1,0:T(8,128)(2,1)S(1)}, bf16[4096,128]{1,0:T(8,128)(2,1)}) fusion(bf16[4096,512]{1,0:T(8,128)(2,1)} %bitcast.193), kind=kLoop, calls=%fused_computation.138 | loop fusion | bytes 8388608 | tf_op jit(solution)/shard_map/slice | solution.py:242
  10.9 2.3 %copy.127 = bf16[4096,128]{0,1:T(8,128)(2,1)} copy(bf16[4096,128]{1,0:T(8,128)(2,1)} %get-tuple-element.16) | data formatting | bytes 2097152
  13.2 1.3 copy.126
  18.8 1.7 collective-permute-start.2
  21.3 2.8 %collective-permute-start.3 = (f32[64,768]{1,0:T(8,128)S(1)}, f32[64,768]{1,0:T(8,128)S(1)}, u32[]{:S(2)}, u32[]{:S(2)}) collective-permute-start(f32[64,768]{1,0:T(8,128)S(1)} %get-tuple-element.10), channel_id=1, source_target_pairs={{0,16},{4,20},{8,24},{12,28},{16,0},{20,4},{24,8},{28,12},{32,48},... | collective-permute-start | bytes 589832 | tf_op jit(solution)/shard_map/ppermute | solution.py:71
  24.1 1.4 collective-permute-start.4
  25.6 1.4 collective-permute-done.2
  27.0 5.3 %collective-permute-done.3 = f32[64,768]{1,0:T(8,128)S(1)} collective-permute-done((f32[64,768]{1,0:T(8,128)S(1)}, f32[64,768]{1,0:T(8,128)S(1)}, u32[]{:S(2)}, u32[]{:S(2)}) %collective-permute-start.3) | collective-permute-done | bytes 196640 | tf_op jit(solution)/shard_map/ppermute | solution.py:71
  32.8 4.3 %collective-permute-start.5 = (f32[64,768]{1,0:T(8,128)S(1)}, f32[64,768]{1,0:T(8,128)S(1)}, u32[]{:S(2)}, u32[]{:S(2)}) collective-permute-start(f32[64,768]{1,0:T(8,128)S(1)} %reduce_sum.175), channel_id=1, source_target_pairs={{0,32},{4,36},{8,40},{12,44},{16,48},{20,52},{24,56},{28,60},{32,6... | collective-permute-start | bytes 589832 | tf_op jit(solution)/shard_map/ppermute | solution.py:71
  37.1 4.8 %collective-permute-start.6 = (f32[64,768]{1,0:T(8,128)S(1)}, f32[64,768]{1,0:T(8,128)S(1)}, u32[]{:S(2)}, u32[]{:S(2)}) collective-permute-start(f32[64,768]{1,0:T(8,128)S(1)} %reduce_sum.175), channel_id=1, source_target_pairs={{0,64},{4,68},{8,72},{12,76},{16,80},{20,84},{24,88},{28,92},{32,9... | collective-permute-start | bytes 589832 | tf_op jit(solution)/shard_map/ppermute | solution.py:71
  41.9 1.3 collective-permute-start.7
  43.3 2.0 collective-permute-done.5
  45.3 4.6 %collective-permute-done.6 = f32[64,768]{1,0:T(8,128)S(1)} collective-permute-done((f32[64,768]{1,0:T(8,128)S(1)}, f32[64,768]{1,0:T(8,128)S(1)}, u32[]{:S(2)}, u32[]{:S(2)}) %collective-permute-start.6) | collective-permute-done | bytes 196640 | tf_op jit(solution)/shard_map/ppermute | solution.py:71
  50.1 1.4 collective-permute-done.8
  51.7 1.9 collective-permute-start.9
  54.5 1.9 collective-permute-start.11
  56.8 1.9 collective-permute-done.10
  59.2 1.9 convolution_bitcast_fusion
  61.1 1.7 convolution_bitcast_fusion.1
  64.5 1.4 fusion.2
  68.7 7.1 %all-to-all-start = ((f32[32,1,1152]{2,1,0:T(1,128)}), f32[32,1,1152]{2,1,0:T(1,128)S(1)}, u32[]{:S(2)}, u32[]{:S(2)}) async-start(f32[32,1,1152]{2,1,0:T(1,128)} %reshape.362), calls=%async_computation | async-start | bytes 294912 | tf_op jit(solution)/shard_map/all_to_all | solution.py:258
  76.6 6.9 %all-to-all-done = f32[32,1,1152]{2,1,0:T(1,128)S(1)} async-done(((f32[32,1,1152]{2,1,0:T(1,128)}), f32[32,1,1152]{2,1,0:T(1,128)S(1)}, u32[]{:S(2)}, u32[]{:S(2)}) %all-to-all-start) | async-done | bytes 147488 | tf_op jit(solution)/shard_map/all_to_all | solution.py:258
  87.3 5.3 %collective-permute-start.13 = (bf16[64,16]{0,1:T(8,128)(2,1)S(1)}, bf16[64,16]{0,1:T(8,128)(2,1)S(1)}, u32[]{:S(2)}, u32[]{:S(2)}) collective-permute-start(bf16[64,16]{0,1:T(8,128)(2,1)S(1)} %copy.119), channel_id=1, source_target_pairs={{0,1},{1,33},{2,65},{3,97},{4,2},{5,34},{6,66},{7,98},{8,3},{9,35}... | collective-permute-start | bytes 6152 | tf_op jit(solution)/shard_map/ppermute | solution.py:296
  92.7 4.1 %collective-permute-start.14 = (bf16[64,16]{0,1:T(8,128)(2,1)S(1)}, bf16[64,16]{0,1:T(8,128)(2,1)S(1)}, u32[]{:S(2)}, u32[]{:S(2)}) collective-permute-start(bf16[64,16]{0,1:T(8,128)(2,1)S(1)} %copy.119), channel_id=1, source_target_pairs={{0,2},{1,34},{2,66},{3,98},{4,3},{5,35},{6,67},{7,99},{8,0},{9,32}... | collective-permute-start | bytes 6152 | tf_op jit(solution)/shard_map/ppermute | solution.py:296
  96.8 3.4 %collective-permute-start.15 = (bf16[64,16]{0,1:T(8,128)(2,1)S(1)}, bf16[64,16]{0,1:T(8,128)(2,1)S(1)}, u32[]{:S(2)}, u32[]{:S(2)}) collective-permute-start(bf16[64,16]{0,1:T(8,128)(2,1)S(1)} %copy.119), channel_id=1, source_target_pairs={{0,3},{1,35},{2,67},{3,99},{4,0},{5,32},{6,64},{7,96},{8,1},{9,33}... | collective-permute-start | bytes 6152 | tf_op jit(solution)/shard_map/ppermute | solution.py:296
  100.3 1.2 collective-permute-done.15
  101.7 2.8 %collective-permute-start.16 = (f32[64,512]{1,0:T(8,128)S(1)}, f32[64,512]{1,0:T(8,128)S(1)}, u32[]{:S(2)}, u32[]{:S(2)}) collective-permute-start(f32[64,512]{1,0:T(8,128)S(1)} %get-tuple-element.38), channel_id=1, source_target_pairs={{0,4},{4,0},{8,12},{12,8},{16,20},{20,16},{24,28},{28,24},{32,36},... | collective-permute-start | bytes 393224 | tf_op jit(solution)/shard_map/ppermute | solution.py:71
  105.6 5.1 %collective-permute-start.18 = (f32[64,512]{1,0:T(8,128)S(1)}, f32[64,512]{1,0:T(8,128)S(1)}, u32[]{:S(2)}, u32[]{:S(2)}) collective-permute-start(f32[64,512]{1,0:T(8,128)S(1)} %reduce_sum.184), channel_id=1, source_target_pairs={{0,16},{4,20},{8,24},{12,28},{16,0},{20,4},{24,8},{28,12},{32,48},... | collective-permute-start | bytes 393224 | tf_op jit(solution)/shard_map/ppermute | solution.py:71
  110.7 2.5 %collective-permute-start.19 = (f32[64,512]{1,0:T(8,128)S(1)}, f32[64,512]{1,0:T(8,128)S(1)}, u32[]{:S(2)}, u32[]{:S(2)}) collective-permute-start(f32[64,512]{1,0:T(8,128)S(1)} %reduce_sum.184), channel_id=1, source_target_pairs={{0,24},{4,28},{8,0},{12,4},{16,8},{20,12},{24,16},{28,20},{32,56},... | collective-permute-start | bytes 393224 | tf_op jit(solution)/shard_map/ppermute | solution.py:71
  113.4 3.9 %collective-permute-done.18 = f32[64,512]{1,0:T(8,128)S(1)} collective-permute-done((f32[64,512]{1,0:T(8,128)S(1)}, f32[64,512]{1,0:T(8,128)S(1)}, u32[]{:S(2)}, u32[]{:S(2)}) %collective-permute-start.18) | collective-permute-done | bytes 131104 | tf_op jit(solution)/shard_map/ppermute | solution.py:71
  117.3 1.9 collective-permute-start.20
  119.2 6.5 %collective-permute-start.21 = (f32[64,512]{1,0:T(8,128)S(1)}, f32[64,512]{1,0:T(8,128)S(1)}, u32[]{:S(2)}, u32[]{:S(2)}) collective-permute-start(f32[64,512]{1,0:T(8,128)S(1)} %reduce_sum.185), channel_id=1, source_target_pairs={{0,64},{4,68},{8,72},{12,76},{16,80},{20,84},{24,88},{28,92},{32,9... | collective-permute-start | bytes 393224 | tf_op jit(solution)/shard_map/ppermute | solution.py:71
  125.8 2.5 %collective-permute-start.22 = (f32[64,512]{1,0:T(8,128)S(1)}, f32[64,512]{1,0:T(8,128)S(1)}, u32[]{:S(2)}, u32[]{:S(2)}) collective-permute-start(f32[64,512]{1,0:T(8,128)S(1)} %reduce_sum.185), channel_id=1, source_target_pairs={{0,96},{4,100},{8,104},{12,108},{16,112},{20,116},{24,120},{28,124... | collective-permute-start | bytes 393224 | tf_op jit(solution)/shard_map/ppermute | solution.py:71
  128.4 3.0 %collective-permute-done.21 = f32[64,512]{1,0:T(8,128)S(1)} collective-permute-done((f32[64,512]{1,0:T(8,128)S(1)}, f32[64,512]{1,0:T(8,128)S(1)}, u32[]{:S(2)}, u32[]{:S(2)}) %collective-permute-start.21) | collective-permute-done | bytes 131104 | tf_op jit(solution)/shard_map/ppermute | solution.py:71
  132.1 3.7 %collective-permute-start.24 = (f32[64]{0:T(128)S(1)}, f32[64]{0:T(128)S(1)}, u32[]{:S(2)}, u32[]{:S(2)}) collective-permute-start(f32[64]{0:T(128)S(1)} %multiply_reduce_fusion.1), channel_id=1, source_target_pairs={{0,2},{1,3},{2,0},{3,1},{4,6},{5,7},{6,4},{7,5},{8,10},{9,11},{10,... | collective-permute-start | bytes 776 | tf_op jit(solution)/shard_map/ppermute | solution.py:71
  135.8 2.5 %collective-permute-start.25 = (f32[64]{0:T(128)S(1)}, f32[64]{0:T(128)S(1)}, u32[]{:S(2)}, u32[]{:S(2)}) collective-permute-start(f32[64]{0:T(128)S(1)} %multiply_reduce_fusion.1), channel_id=1, source_target_pairs={{0,3},{1,0},{2,1},{3,2},{4,7},{5,4},{6,5},{7,6},{8,11},{9,8},{10,9... | collective-permute-start | bytes 776 | tf_op jit(solution)/shard_map/ppermute | solution.py:71
  138.4 1.2 collective-permute-done.25
  142.0 1.4 stack_reshape.7
  143.5 3.6 %pad_maximum_fusion = f32[64,32,2,64]{3,2,1,0:T(2,128)S(1)} fusion(f32[64,32,1,64]{3,2,1,0:T(1,128)} %bitcast.199, f32[64,32,1,64]{3,2,1,0:T(1,128)S(1)} %bitcast.198), kind=kLoop, calls=%fused_computation.9 | loop fusion | flops 262144 | bytes 2097152 | tf_op jit(solution)/shard_map/stack | solution.py:122
  147.1 2.0 reshape.357
  149.5 1.8 collective-permute-done.27
  151.9 3.9 %collective-permute-start.29 = (f32[64,512]{1,0:T(8,128)S(1)}, f32[64,512]{1,0:T(8,128)S(1)}, u32[]{:S(2)}, u32[]{:S(2)}) collective-permute-start(f32[64,512]{1,0:T(8,128)S(1)} %get-tuple-element.19), channel_id=1, source_target_pairs={{0,16},{4,20},{8,24},{12,28},{16,0},{20,4},{24,8},{28,12},{32,48},... | collective-permute-start | bytes 393224 | tf_op jit(solution)/shard_map/ppermute | solution.py:83
  155.8 2.4 %collective-permute-done.28 = f32[64,512]{1,0:T(8,128)S(1)} collective-permute-done((f32[64,512]{1,0:T(8,128)S(1)}, f32[64,512]{1,0:T(8,128)S(1)}, u32[]{:S(2)}, u32[]{:S(2)}) %collective-permute-start.28) | collective-permute-done | bytes 131104 | tf_op jit(solution)/shard_map/ppermute | solution.py:83
  158.3 3.9 %collective-permute-done.29 = f32[64,512]{1,0:T(8,128)S(1)} collective-permute-done((f32[64,512]{1,0:T(8,128)S(1)}, f32[64,512]{1,0:T(8,128)S(1)}, u32[]{:S(2)}, u32[]{:S(2)}) %collective-permute-start.29) | collective-permute-done | bytes 131104 | tf_op jit(solution)/shard_map/ppermute | solution.py:83
  162.2 6.1 %collective-permute-start.31 = (f32[64,128]{1,0:T(8,128)S(1)}, f32[64,128]{1,0:T(8,128)S(1)}, u32[]{:S(2)}, u32[]{:S(2)}) collective-permute-start(f32[64,128]{1,0:T(8,128)S(1)} %get-tuple-element.28), channel_id=1, source_target_pairs={{0,32},{4,36},{8,40},{12,44},{16,48},{20,52},{24,56},{28,60},{32,6... | collective-permute-start | bytes 98312 | tf_op jit(solution)/shard_map/ppermute | solution.py:83
  168.4 6.0 %collective-permute-start.32 = (f32[64,128]{1,0:T(8,128)S(1)}, f32[64,128]{1,0:T(8,128)S(1)}, u32[]{:S(2)}, u32[]{:S(2)}) collective-permute-start(f32[64,128]{1,0:T(8,128)S(1)} %get-tuple-element.30), channel_id=1, source_target_pairs={{0,64},{4,68},{8,72},{12,76},{16,80},{20,84},{24,88},{28,92},{32,9... | collective-permute-start | bytes 98312 | tf_op jit(solution)/shard_map/ppermute | solution.py:83
  175.1 1.5 collective-permute-done.32
  176.6 1.7 collective-permute-done.33
  178.4 3.2 %collective-permute-start.35 = (bf16[64,64]{1,0:T(8,128)(2,1)S(1)}, bf16[64,64]{1,0:T(8,128)(2,1)S(1)}, u32[]{:S(2)}, u32[]{:S(2)}) collective-permute-start(bf16[64,64]{1,0:T(8,128)(2,1)S(1)} %fusion.9), channel_id=1, source_target_pairs={{0,64},{4,68},{8,72},{12,76},{16,80},{20,84},{24,88},{28,92},{32,9... | collective-permute-start | bytes 24584 | tf_op jit(solution)/shard_map/ppermute | solution.py:94
  183.9 1.5 collective-permute-done.36
  186.6 3.3 %collective-permute-start.38 = (f32[64,512]{1,0:T(8,128)S(1)}, f32[64,512]{1,0:T(8,128)S(1)}, u32[]{:S(2)}, u32[]{:S(2)}) collective-permute-start(f32[64,512]{1,0:T(8,128)S(1)} %get-tuple-element.40), channel_id=1, source_target_pairs={{0,4},{4,0},{8,12},{12,8},{16,20},{20,16},{24,28},{28,24},{32,36},... | collective-permute-start | bytes 393224 | tf_op jit(solution)/shard_map/ppermute | solution.py:71
  190.9 2.8 %collective-permute-start.39 = (f32[64,512]{1,0:T(8,128)S(1)}, f32[64,512]{1,0:T(8,128)S(1)}, u32[]{:S(2)}, u32[]{:S(2)}) collective-permute-start(f32[64,512]{1,0:T(8,128)S(1)} %reduce_sum.190), channel_id=1, source_target_pairs={{0,8},{4,12},{8,16},{12,20},{16,24},{20,28},{24,0},{28,4},{32,40},... | collective-permute-start | bytes 393224 | tf_op jit(solution)/shard_map/ppermute | solution.py:71
  193.8 2.6 %collective-permute-start.40 = (f32[64,512]{1,0:T(8,128)S(1)}, f32[64,512]{1,0:T(8,128)S(1)}, u32[]{:S(2)}, u32[]{:S(2)}) collective-permute-start(f32[64,512]{1,0:T(8,128)S(1)} %reduce_sum.190), channel_id=1, source_target_pairs={{0,16},{4,20},{8,24},{12,28},{16,0},{20,4},{24,8},{28,12},{32,48},... | collective-permute-start | bytes 393224 | tf_op jit(solution)/shard_map/ppermute | solution.py:71
  196.3 1.4 collective-permute-start.41
  198.7 4.0 %collective-permute-done.40 = f32[64,512]{1,0:T(8,128)S(1)} collective-permute-done((f32[64,512]{1,0:T(8,128)S(1)}, f32[64,512]{1,0:T(8,128)S(1)}, u32[]{:S(2)}, u32[]{:S(2)}) %collective-permute-start.40) | collective-permute-done | bytes 131104 | tf_op jit(solution)/shard_map/ppermute | solution.py:71
  202.8 2.5 %collective-permute-start.42 = (f32[64,512]{1,0:T(8,128)S(1)}, f32[64,512]{1,0:T(8,128)S(1)}, u32[]{:S(2)}, u32[]{:S(2)}) collective-permute-start(f32[64,512]{1,0:T(8,128)S(1)} %reduce_sum.191), channel_id=1, source_target_pairs={{0,32},{4,36},{8,40},{12,44},{16,48},{20,52},{24,56},{28,60},{32,6... | collective-permute-start | bytes 393224 | tf_op jit(solution)/shard_map/ppermute | solution.py:71
  205.3 5.2 %collective-permute-start.43 = (f32[64,512]{1,0:T(8,128)S(1)}, f32[64,512]{1,0:T(8,128)S(1)}, u32[]{:S(2)}, u32[]{:S(2)}) collective-permute-start(f32[64,512]{1,0:T(8,128)S(1)} %reduce_sum.191), channel_id=1, source_target_pairs={{0,64},{4,68},{8,72},{12,76},{16,80},{20,84},{24,88},{28,92},{32,9... | collective-permute-start | bytes 393224 | tf_op jit(solution)/shard_map/ppermute | solution.py:71
  210.4 1.5 collective-permute-start.44
  212.4 3.5 %collective-permute-done.43 = f32[64,512]{1,0:T(8,128)S(1)} collective-permute-done((f32[64,512]{1,0:T(8,128)S(1)}, f32[64,512]{1,0:T(8,128)S(1)}, u32[]{:S(2)}, u32[]{:S(2)}) %collective-permute-start.43) | collective-permute-done | bytes 131104 | tf_op jit(solution)/shard_map/ppermute | solution.py:71
  216.1 2.4 %collective-permute-start.45 = (f32[64]{0:T(128)S(1)}, f32[64]{0:T(128)S(1)}, u32[]{:S(2)}, u32[]{:S(2)}) collective-permute-start(f32[64]{0:T(128)S(1)} %multiply_reduce_fusion), channel_id=1, source_target_pairs={{0,1},{1,2},{2,3},{3,0},{4,5},{5,6},{6,7},{7,4},{8,9},{9,10},{10,1... | collective-permute-start | bytes 776 | tf_op jit(solution)/shard_map/ppermute | solution.py:71
  218.5 2.6 %collective-permute-start.46 = (f32[64]{0:T(128)S(1)}, f32[64]{0:T(128)S(1)}, u32[]{:S(2)}, u32[]{:S(2)}) collective-permute-start(f32[64]{0:T(128)S(1)} %multiply_reduce_fusion), channel_id=1, source_target_pairs={{0,2},{1,3},{2,0},{3,1},{4,6},{5,7},{6,4},{7,5},{8,10},{9,11},{10,... | collective-permute-start | bytes 776 | tf_op jit(solution)/shard_map/ppermute | solution.py:71
  221.4 2.1 collective-permute-done.46
  (251 shorter events, 36.0 us)
Async XLA Ops:
  0.0 141.2 %copy-start = (bf16[64,2048]{1,0:T(8,128)(2,1)S(1)}, bf16[64,2048]{1,0:T(8,128)(2,1)}, u32[]{:S(2)}) copy-start(bf16[64,2048]{1,0:T(8,128)(2,1)} %param.22) | copy-start | bytes 786436
  1.4 14.3 %collective-permute-start = (bf16[64,64]{1,0:T(8,128)(2,1)}, bf16[64,64]{1,0:T(8,128)(2,1)S(1)}, u32[]{:S(2)}, u32[]{:S(2)}) collective-permute-start(bf16[64,64]{1,0:T(8,128)(2,1)} %constant_dynamic-slice_fusion.10), channel_id=1, source_target_pairs={{0,0},{1,32},{2,64},{3,96},{4,4},{5,36},{6,68},{7,100},{8,8},{9,40... | collective-permute-start | bytes 24584 | tf_op jit(solution)/shard_map/ppermute | solution.py:47
  4.2 5.1 %copy-start.15 = (s32[64]{0:T(128)}, s32[64]{0:T(128)S(1)}, u32[]{:S(2)}) copy-start(s32[64]{0:T(128)S(1)} %lt.350) | copy-start | bytes 772
  10.9 4.9 %copy-start.8 = (bf16[64,512]{1,0:T(8,128)(2,1)S(1)}, bf16[64,512]{1,0:T(8,128)(2,1)}, u32[]{:S(2)}) copy-start(bf16[64,512]{1,0:T(8,128)(2,1)} %param.18) | copy-start | bytes 196612
  10.9 5.0 %copy-start.9 = (bf16[64,512]{1,0:T(8,128)(2,1)S(1)}, bf16[64,512]{1,0:T(8,128)(2,1)}, u32[]{:S(2)}) copy-start(bf16[64,512]{1,0:T(8,128)(2,1)} %param.19) | copy-start | bytes 196612
  17.1 1.5 collective-permute-start.1
  18.7 40.0 %copy-start.11 = (f32[512]{0:T(512)S(1)}, f32[512]{0:T(512)}, u32[]{:S(2)}) copy-start(f32[512]{0:T(512)} %param.26) | copy-start | bytes 6148
  18.7 40.0 %copy-start.12 = (f32[512]{0:T(512)S(1)}, f32[512]{0:T(512)}, u32[]{:S(2)}) copy-start(f32[512]{0:T(512)} %param.25) | copy-start | bytes 6148
  18.8 8.2 %collective-permute-start.2 = (f32[64,768]{1,0:T(8,128)S(1)}, f32[64,768]{1,0:T(8,128)S(1)}, u32[]{:S(2)}, u32[]{:S(2)}) collective-permute-start(f32[64,768]{1,0:T(8,128)S(1)} %get-tuple-element.10), channel_id=1, source_target_pairs={{0,8},{4,12},{8,16},{12,20},{16,24},{20,28},{24,0},{28,4},{32,40},... | collective-permute-start | bytes 589832 | tf_op jit(solution)/shard_map/ppermute | solution.py:71
  21.3 11.0 %collective-permute-start.3 = (f32[64,768]{1,0:T(8,128)S(1)}, f32[64,768]{1,0:T(8,128)S(1)}, u32[]{:S(2)}, u32[]{:S(2)}) collective-permute-start(f32[64,768]{1,0:T(8,128)S(1)} %get-tuple-element.10), channel_id=1, source_target_pairs={{0,16},{4,20},{8,24},{12,28},{16,0},{20,4},{24,8},{28,12},{32,48},... | collective-permute-start | bytes 589832 | tf_op jit(solution)/shard_map/ppermute | solution.py:71
  24.1 8.6 %collective-permute-start.4 = (f32[64,768]{1,0:T(8,128)S(1)}, f32[64,768]{1,0:T(8,128)S(1)}, u32[]{:S(2)}, u32[]{:S(2)}) collective-permute-start(f32[64,768]{1,0:T(8,128)S(1)} %get-tuple-element.10), channel_id=1, source_target_pairs={{0,24},{4,28},{8,0},{12,4},{16,8},{20,12},{24,16},{28,20},{32,56},... | collective-permute-start | bytes 589832 | tf_op jit(solution)/shard_map/ppermute | solution.py:71
  32.8 12.4 %collective-permute-start.5 = (f32[64,768]{1,0:T(8,128)S(1)}, f32[64,768]{1,0:T(8,128)S(1)}, u32[]{:S(2)}, u32[]{:S(2)}) collective-permute-start(f32[64,768]{1,0:T(8,128)S(1)} %reduce_sum.175), channel_id=1, source_target_pairs={{0,32},{4,36},{8,40},{12,44},{16,48},{20,52},{24,56},{28,60},{32,6... | collective-permute-start | bytes 589832 | tf_op jit(solution)/shard_map/ppermute | solution.py:71
  37.1 12.8 %collective-permute-start.6 = (f32[64,768]{1,0:T(8,128)S(1)}, f32[64,768]{1,0:T(8,128)S(1)}, u32[]{:S(2)}, u32[]{:S(2)}) collective-permute-start(f32[64,768]{1,0:T(8,128)S(1)} %reduce_sum.175), channel_id=1, source_target_pairs={{0,64},{4,68},{8,72},{12,76},{16,80},{20,84},{24,88},{28,92},{32,9... | collective-permute-start | bytes 589832 | tf_op jit(solution)/shard_map/ppermute | solution.py:71
  41.9 8.0 %collective-permute-start.7 = (f32[64,768]{1,0:T(8,128)S(1)}, f32[64,768]{1,0:T(8,128)S(1)}, u32[]{:S(2)}, u32[]{:S(2)}) collective-permute-start(f32[64,768]{1,0:T(8,128)S(1)} %reduce_sum.175), channel_id=1, source_target_pairs={{0,96},{4,100},{8,104},{12,108},{16,112},{20,116},{24,120},{28,124... | collective-permute-start | bytes 589832 | tf_op jit(solution)/shard_map/ppermute | solution.py:71
  50.0 1.5 collective-permute-start.8
  51.7 5.1 %collective-permute-start.9 = (f32[64,2]{0,1:T(2,128)S(1)}, f32[64,2]{0,1:T(2,128)S(1)}, u32[]{:S(2)}, u32[]{:S(2)}) collective-permute-start(f32[64,2]{0,1:T(2,128)S(1)} %pad_maximum_fusion.3), channel_id=1, source_target_pairs={{0,1},{1,2},{2,3},{3,0},{4,5},{5,6},{6,7},{7,4},{8,9},{9,10},{10,1... | collective-permute-start | bytes 1544 | tf_op jit(solution)/shard_map/ppermute | solution.py:71
  53.6 5.1 %collective-permute-start.10 = (f32[64,2]{0,1:T(2,128)S(1)}, f32[64,2]{0,1:T(2,128)S(1)}, u32[]{:S(2)}, u32[]{:S(2)}) collective-permute-start(f32[64,2]{0,1:T(2,128)S(1)} %pad_maximum_fusion.3), channel_id=1, source_target_pairs={{0,2},{1,3},{2,0},{3,1},{4,6},{5,7},{6,4},{7,5},{8,10},{9,11},{10,... | collective-permute-start | bytes 1544 | tf_op jit(solution)/shard_map/ppermute | solution.py:71
  54.5 4.2 %collective-permute-start.11 = (f32[64,2]{0,1:T(2,128)S(1)}, f32[64,2]{0,1:T(2,128)S(1)}, u32[]{:S(2)}, u32[]{:S(2)}) collective-permute-start(f32[64,2]{0,1:T(2,128)S(1)} %pad_maximum_fusion.3), channel_id=1, source_target_pairs={{0,3},{1,0},{2,1},{3,2},{4,7},{5,4},{6,5},{7,6},{8,11},{9,8},{10,9... | collective-permute-start | bytes 1544 | tf_op jit(solution)/shard_map/ppermute | solution.py:71
  58.9 3.9 %copy-start.1 = (bf16[16,256,512]{2,1,0:T(8,128)(2,1)S(1)}, bf16[16,256,512]{2,1,0:T(8,128)(2,1)}, u32[]{:S(2)}) copy-start(bf16[16,256,512]{2,1,0:T(8,128)(2,1)} %param.29) | copy-start | bytes 12582916
  59.2 4.6 %copy-start.2 = (pred[64,4096]{1,0:T(8,128)(4,1)S(1)}, pred[64,4096]{1,0:T(8,128)(4,1)}, u32[]{:S(2)}) copy-start(pred[64,4096]{1,0:T(8,128)(4,1)} %compare_and_fusion) | copy-start | bytes 786436
  64.5 1.8 copy-start.4
  67.2 34.3 %copy-start.10 = (bf16[64,512]{1,0:T(8,128)(2,1)S(1)}, bf16[64,512]{1,0:T(8,128)(2,1)}, u32[]{:S(2)}) copy-start(bf16[64,512]{1,0:T(8,128)(2,1)} %param.21) | copy-start | bytes 196612
  67.2 37.3 %copy-start.13 = (f32[512]{0:T(512)S(1)}, f32[512]{0:T(512)}, u32[]{:S(2)}) copy-start(f32[512]{0:T(512)} %param.27) | copy-start | bytes 6148
  68.7 14.8 %all-to-all-start = ((f32[32,1,1152]{2,1,0:T(1,128)}), f32[32,1,1152]{2,1,0:T(1,128)S(1)}, u32[]{:S(2)}, u32[]{:S(2)}) async-start(f32[32,1,1152]{2,1,0:T(1,128)} %reshape.362), calls=%async_computation | async-start | bytes 294912 | tf_op jit(solution)/shard_map/all_to_all | solution.py:258
  86.6 13.6 %collective-permute-start.12 = (bf16[64,16]{0,1:T(8,128)(2,1)S(1)}, bf16[64,16]{0,1:T(8,128)(2,1)S(1)}, u32[]{:S(2)}, u32[]{:S(2)}) collective-permute-start(bf16[64,16]{0,1:T(8,128)(2,1)S(1)} %copy.119), channel_id=1, source_target_pairs={{0,0},{1,32},{2,64},{3,96},{4,1},{5,33},{6,65},{7,97},{8,2},{9,34}... | collective-permute-start | bytes 6152 | tf_op jit(solution)/shard_map/ppermute | solution.py:296
  87.3 54.5 %copy-start.5 = (bf16[64,2048]{1,0:T(8,128)(2,1)S(1)}, bf16[64,2048]{1,0:T(8,128)(2,1)}, u32[]{:S(2)}) copy-start(bf16[64,2048]{1,0:T(8,128)(2,1)} %param.23) | copy-start | bytes 786436
  87.3 12.9 %collective-permute-start.13 = (bf16[64,16]{0,1:T(8,128)(2,1)S(1)}, bf16[64,16]{0,1:T(8,128)(2,1)S(1)}, u32[]{:S(2)}, u32[]{:S(2)}) collective-permute-start(bf16[64,16]{0,1:T(8,128)(2,1)S(1)} %copy.119), channel_id=1, source_target_pairs={{0,1},{1,33},{2,65},{3,97},{4,2},{5,34},{6,66},{7,98},{8,3},{9,35}... | collective-permute-start | bytes 6152 | tf_op jit(solution)/shard_map/ppermute | solution.py:296
  92.7 7.6 %collective-permute-start.14 = (bf16[64,16]{0,1:T(8,128)(2,1)S(1)}, bf16[64,16]{0,1:T(8,128)(2,1)S(1)}, u32[]{:S(2)}, u32[]{:S(2)}) collective-permute-start(bf16[64,16]{0,1:T(8,128)(2,1)S(1)} %copy.119), channel_id=1, source_target_pairs={{0,2},{1,34},{2,66},{3,98},{4,3},{5,35},{6,67},{7,99},{8,0},{9,32}... | collective-permute-start | bytes 6152 | tf_op jit(solution)/shard_map/ppermute | solution.py:296
  96.8 4.7 %collective-permute-start.15 = (bf16[64,16]{0,1:T(8,128)(2,1)S(1)}, bf16[64,16]{0,1:T(8,128)(2,1)S(1)}, u32[]{:S(2)}, u32[]{:S(2)}) collective-permute-start(bf16[64,16]{0,1:T(8,128)(2,1)S(1)} %copy.119), channel_id=1, source_target_pairs={{0,3},{1,35},{2,67},{3,99},{4,0},{5,32},{6,64},{7,96},{8,1},{9,33}... | collective-permute-start | bytes 6152 | tf_op jit(solution)/shard_map/ppermute | solution.py:296
  101.7 3.8 %collective-permute-start.16 = (f32[64,512]{1,0:T(8,128)S(1)}, f32[64,512]{1,0:T(8,128)S(1)}, u32[]{:S(2)}, u32[]{:S(2)}) collective-permute-start(f32[64,512]{1,0:T(8,128)S(1)} %get-tuple-element.38), channel_id=1, source_target_pairs={{0,4},{4,0},{8,12},{12,8},{16,20},{20,16},{24,28},{28,24},{32,36},... | collective-permute-start | bytes 393224 | tf_op jit(solution)/shard_map/ppermute | solution.py:71
  105.6 7.8 %collective-permute-start.17 = (f32[64,512]{1,0:T(8,128)S(1)}, f32[64,512]{1,0:T(8,128)S(1)}, u32[]{:S(2)}, u32[]{:S(2)}) collective-permute-start(f32[64,512]{1,0:T(8,128)S(1)} %reduce_sum.184), channel_id=1, source_target_pairs={{0,8},{4,12},{8,16},{12,20},{16,24},{20,28},{24,0},{28,4},{32,40},... | collective-permute-start | bytes 393224 | tf_op jit(solution)/shard_map/ppermute | solution.py:71
  105.6 11.6 %collective-permute-start.18 = (f32[64,512]{1,0:T(8,128)S(1)}, f32[64,512]{1,0:T(8,128)S(1)}, u32[]{:S(2)}, u32[]{:S(2)}) collective-permute-start(f32[64,512]{1,0:T(8,128)S(1)} %reduce_sum.184), channel_id=1, source_target_pairs={{0,16},{4,20},{8,24},{12,28},{16,0},{20,4},{24,8},{28,12},{32,48},... | collective-permute-start | bytes 393224 | tf_op jit(solution)/shard_map/ppermute | solution.py:71
  110.7 6.5 %collective-permute-start.19 = (f32[64,512]{1,0:T(8,128)S(1)}, f32[64,512]{1,0:T(8,128)S(1)}, u32[]{:S(2)}, u32[]{:S(2)}) collective-permute-start(f32[64,512]{1,0:T(8,128)S(1)} %reduce_sum.184), channel_id=1, source_target_pairs={{0,24},{4,28},{8,0},{12,4},{16,8},{20,12},{24,16},{28,20},{32,56},... | collective-permute-start | bytes 393224 | tf_op jit(solution)/shard_map/ppermute | solution.py:71
  117.3 11.1 %collective-permute-start.20 = (f32[64,512]{1,0:T(8,128)S(1)}, f32[64,512]{1,0:T(8,128)S(1)}, u32[]{:S(2)}, u32[]{:S(2)}) collective-permute-start(f32[64,512]{1,0:T(8,128)S(1)} %reduce_sum.185), channel_id=1, source_target_pairs={{0,32},{4,36},{8,40},{12,44},{16,48},{20,52},{24,56},{28,60},{32,6... | collective-permute-start | bytes 393224 | tf_op jit(solution)/shard_map/ppermute | solution.py:71
  119.2 12.1 %collective-permute-start.21 = (f32[64,512]{1,0:T(8,128)S(1)}, f32[64,512]{1,0:T(8,128)S(1)}, u32[]{:S(2)}, u32[]{:S(2)}) collective-permute-start(f32[64,512]{1,0:T(8,128)S(1)} %reduce_sum.185), channel_id=1, source_target_pairs={{0,64},{4,68},{8,72},{12,76},{16,80},{20,84},{24,88},{28,92},{32,9... | collective-permute-start | bytes 393224 | tf_op jit(solution)/shard_map/ppermute | solution.py:71
  125.8 5.6 %collective-permute-start.22 = (f32[64,512]{1,0:T(8,128)S(1)}, f32[64,512]{1,0:T(8,128)S(1)}, u32[]{:S(2)}, u32[]{:S(2)}) collective-permute-start(f32[64,512]{1,0:T(8,128)S(1)} %reduce_sum.185), channel_id=1, source_target_pairs={{0,96},{4,100},{8,104},{12,108},{16,112},{20,116},{24,120},{28,124... | collective-permute-start | bytes 393224 | tf_op jit(solution)/shard_map/ppermute | solution.py:71
  131.6 6.8 %collective-permute-start.23 = (f32[64]{0:T(128)S(1)}, f32[64]{0:T(128)S(1)}, u32[]{:S(2)}, u32[]{:S(2)}) collective-permute-start(f32[64]{0:T(128)S(1)} %multiply_reduce_fusion.1), channel_id=1, source_target_pairs={{0,1},{1,2},{2,3},{3,0},{4,5},{5,6},{6,7},{7,4},{8,9},{9,10},{10,1... | collective-permute-start | bytes 776 | tf_op jit(solution)/shard_map/ppermute | solution.py:71
  132.1 6.3 %collective-permute-start.24 = (f32[64]{0:T(128)S(1)}, f32[64]{0:T(128)S(1)}, u32[]{:S(2)}, u32[]{:S(2)}) collective-permute-start(f32[64]{0:T(128)S(1)} %multiply_reduce_fusion.1), channel_id=1, source_target_pairs={{0,2},{1,3},{2,0},{3,1},{4,6},{5,7},{6,4},{7,5},{8,10},{9,11},{10,... | collective-permute-start | bytes 776 | tf_op jit(solution)/shard_map/ppermute | solution.py:71
  135.8 3.8 %collective-permute-start.25 = (f32[64]{0:T(128)S(1)}, f32[64]{0:T(128)S(1)}, u32[]{:S(2)}, u32[]{:S(2)}) collective-permute-start(f32[64]{0:T(128)S(1)} %multiply_reduce_fusion.1), channel_id=1, source_target_pairs={{0,3},{1,0},{2,1},{3,2},{4,7},{5,4},{6,5},{7,6},{8,11},{9,8},{10,9... | collective-permute-start | bytes 776 | tf_op jit(solution)/shard_map/ppermute | solution.py:71
  140.5 0.7 collective-permute-start.26
  149.1 37.4 %copy-start.6 = (bf16[256,512]{1,0:T(8,128)(2,1)S(1)}, bf16[256,512]{1,0:T(8,128)(2,1)}, u32[]{:S(2)}) copy-start(bf16[256,512]{1,0:T(8,128)(2,1)} %param.24) | copy-start | bytes 786436
  149.1 2.2 collective-permute-start.27
  151.4 73.4 %copy-start.7 = (bf16[4,16,512]{2,1,0:T(8,128)(2,1)S(1)}, bf16[4,16,512]{2,1,0:T(8,128)(2,1)}, u32[]{:S(2)}) copy-start(bf16[4,16,512]{2,1,0:T(8,128)(2,1)} %param.17) | copy-start | bytes 196612
  151.4 73.4 %copy-start.14 = (f32[512]{0:T(512)S(1)}, f32[512]{0:T(512)}, u32[]{:S(2)}) copy-start(f32[512]{0:T(512)} %param.28) | copy-start | bytes 6148
  151.5 6.8 %collective-permute-start.28 = (f32[64,512]{1,0:T(8,128)S(1)}, f32[64,512]{1,0:T(8,128)S(1)}, u32[]{:S(2)}, u32[]{:S(2)}) collective-permute-start(f32[64,512]{1,0:T(8,128)S(1)} %get-tuple-element.17), channel_id=1, source_target_pairs={{0,8},{4,12},{8,16},{12,20},{16,24},{20,28},{24,0},{28,4},{32,40},... | collective-permute-start | bytes 393224 | tf_op jit(solution)/shard_map/ppermute | solution.py:83
  151.9 10.2 %collective-permute-start.29 = (f32[64,512]{1,0:T(8,128)S(1)}, f32[64,512]{1,0:T(8,128)S(1)}, u32[]{:S(2)}, u32[]{:S(2)}) collective-permute-start(f32[64,512]{1,0:T(8,128)S(1)} %get-tuple-element.19), channel_id=1, source_target_pairs={{0,16},{4,20},{8,24},{12,28},{16,0},{20,4},{24,8},{28,12},{32,48},... | collective-permute-start | bytes 393224 | tf_op jit(solution)/shard_map/ppermute | solution.py:83
  155.8 6.3 %collective-permute-start.30 = (f32[64,512]{1,0:T(8,128)S(1)}, f32[64,512]{1,0:T(8,128)S(1)}, u32[]{:S(2)}, u32[]{:S(2)}) collective-permute-start(f32[64,512]{1,0:T(8,128)S(1)} %get-tuple-element.18), channel_id=1, source_target_pairs={{0,24},{4,28},{8,0},{12,4},{16,8},{20,12},{24,16},{28,20},{32,56},... | collective-permute-start | bytes 393224 | tf_op jit(solution)/shard_map/ppermute | solution.py:83
  162.2 12.9 %collective-permute-start.31 = (f32[64,128]{1,0:T(8,128)S(1)}, f32[64,128]{1,0:T(8,128)S(1)}, u32[]{:S(2)}, u32[]{:S(2)}) collective-permute-start(f32[64,128]{1,0:T(8,128)S(1)} %get-tuple-element.28), channel_id=1, source_target_pairs={{0,32},{4,36},{8,40},{12,44},{16,48},{20,52},{24,56},{28,60},{32,6... | collective-permute-start | bytes 98312 | tf_op jit(solution)/shard_map/ppermute | solution.py:83
  168.4 8.2 %collective-permute-start.32 = (f32[64,128]{1,0:T(8,128)S(1)}, f32[64,128]{1,0:T(8,128)S(1)}, u32[]{:S(2)}, u32[]{:S(2)}) collective-permute-start(f32[64,128]{1,0:T(8,128)S(1)} %get-tuple-element.30), channel_id=1, source_target_pairs={{0,64},{4,68},{8,72},{12,76},{16,80},{20,84},{24,88},{28,92},{32,9... | collective-permute-start | bytes 98312 | tf_op jit(solution)/shard_map/ppermute | solution.py:83
  174.4 3.9 %collective-permute-start.33 = (f32[64,128]{1,0:T(8,128)S(1)}, f32[64,128]{1,0:T(8,128)S(1)}, u32[]{:S(2)}, u32[]{:S(2)}) collective-permute-start(f32[64,128]{1,0:T(8,128)S(1)} %get-tuple-element.29), channel_id=1, source_target_pairs={{0,96},{4,100},{8,104},{12,108},{16,112},{20,116},{24,120},{28,124... | collective-permute-start | bytes 98312 | tf_op jit(solution)/shard_map/ppermute | solution.py:83
  178.4 5.0 %collective-permute-start.34 = (bf16[64,64]{1,0:T(8,128)(2,1)S(1)}, bf16[64,64]{1,0:T(8,128)(2,1)S(1)}, u32[]{:S(2)}, u32[]{:S(2)}) collective-permute-start(bf16[64,64]{1,0:T(8,128)(2,1)S(1)} %fusion.9), channel_id=1, source_target_pairs={{0,32},{4,36},{8,40},{12,44},{16,48},{20,52},{24,56},{28,60},{32,6... | collective-permute-start | bytes 24584 | tf_op jit(solution)/shard_map/ppermute | solution.py:94
  178.4 5.3 %collective-permute-start.35 = (bf16[64,64]{1,0:T(8,128)(2,1)S(1)}, bf16[64,64]{1,0:T(8,128)(2,1)S(1)}, u32[]{:S(2)}, u32[]{:S(2)}) collective-permute-start(bf16[64,64]{1,0:T(8,128)(2,1)S(1)} %fusion.9), channel_id=1, source_target_pairs={{0,64},{4,68},{8,72},{12,76},{16,80},{20,84},{24,88},{28,92},{32,9... | collective-permute-start | bytes 24584 | tf_op jit(solution)/shard_map/ppermute | solution.py:94
  181.6 3.7 %collective-permute-start.36 = (bf16[64,64]{1,0:T(8,128)(2,1)S(1)}, bf16[64,64]{1,0:T(8,128)(2,1)S(1)}, u32[]{:S(2)}, u32[]{:S(2)}) collective-permute-start(bf16[64,64]{1,0:T(8,128)(2,1)S(1)} %fusion.9), channel_id=1, source_target_pairs={{0,96},{4,100},{8,104},{12,108},{16,112},{20,116},{24,120},{28,124... | collective-permute-start | bytes 24584 | tf_op jit(solution)/shard_map/ppermute | solution.py:94
  185.7 0.7 collective-permute-start.37
  186.6 4.3 %collective-permute-start.38 = (f32[64,512]{1,0:T(8,128)S(1)}, f32[64,512]{1,0:T(8,128)S(1)}, u32[]{:S(2)}, u32[]{:S(2)}) collective-permute-start(f32[64,512]{1,0:T(8,128)S(1)} %get-tuple-element.40), channel_id=1, source_target_pairs={{0,4},{4,0},{8,12},{12,8},{16,20},{20,16},{24,28},{28,24},{32,36},... | collective-permute-start | bytes 393224 | tf_op jit(solution)/shard_map/ppermute | solution.py:71
  190.9 7.7 %collective-permute-start.39 = (f32[64,512]{1,0:T(8,128)S(1)}, f32[64,512]{1,0:T(8,128)S(1)}, u32[]{:S(2)}, u32[]{:S(2)}) collective-permute-start(f32[64,512]{1,0:T(8,128)S(1)} %reduce_sum.190), channel_id=1, source_target_pairs={{0,8},{4,12},{8,16},{12,20},{16,24},{20,28},{24,0},{28,4},{32,40},... | collective-permute-start | bytes 393224 | tf_op jit(solution)/shard_map/ppermute | solution.py:71
  193.8 8.9 %collective-permute-start.40 = (f32[64,512]{1,0:T(8,128)S(1)}, f32[64,512]{1,0:T(8,128)S(1)}, u32[]{:S(2)}, u32[]{:S(2)}) collective-permute-start(f32[64,512]{1,0:T(8,128)S(1)} %reduce_sum.190), channel_id=1, source_target_pairs={{0,16},{4,20},{8,24},{12,28},{16,0},{20,4},{24,8},{28,12},{32,48},... | collective-permute-start | bytes 393224 | tf_op jit(solution)/shard_map/ppermute | solution.py:71
  196.3 6.4 %collective-permute-start.41 = (f32[64,512]{1,0:T(8,128)S(1)}, f32[64,512]{1,0:T(8,128)S(1)}, u32[]{:S(2)}, u32[]{:S(2)}) collective-permute-start(f32[64,512]{1,0:T(8,128)S(1)} %reduce_sum.190), channel_id=1, source_target_pairs={{0,24},{4,28},{8,0},{12,4},{16,8},{20,12},{24,16},{28,20},{32,56},... | collective-permute-start | bytes 393224 | tf_op jit(solution)/shard_map/ppermute | solution.py:71
  202.8 9.6 %collective-permute-start.42 = (f32[64,512]{1,0:T(8,128)S(1)}, f32[64,512]{1,0:T(8,128)S(1)}, u32[]{:S(2)}, u32[]{:S(2)}) collective-permute-start(f32[64,512]{1,0:T(8,128)S(1)} %reduce_sum.191), channel_id=1, source_target_pairs={{0,32},{4,36},{8,40},{12,44},{16,48},{20,52},{24,56},{28,60},{32,6... | collective-permute-start | bytes 393224 | tf_op jit(solution)/shard_map/ppermute | solution.py:71
  205.3 10.6 %collective-permute-start.43 = (f32[64,512]{1,0:T(8,128)S(1)}, f32[64,512]{1,0:T(8,128)S(1)}, u32[]{:S(2)}, u32[]{:S(2)}) collective-permute-start(f32[64,512]{1,0:T(8,128)S(1)} %reduce_sum.191), channel_id=1, source_target_pairs={{0,64},{4,68},{8,72},{12,76},{16,80},{20,84},{24,88},{28,92},{32,9... | collective-permute-start | bytes 393224 | tf_op jit(solution)/shard_map/ppermute | solution.py:71
  210.4 5.5 %collective-permute-start.44 = (f32[64,512]{1,0:T(8,128)S(1)}, f32[64,512]{1,0:T(8,128)S(1)}, u32[]{:S(2)}, u32[]{:S(2)}) collective-permute-start(f32[64,512]{1,0:T(8,128)S(1)} %reduce_sum.191), channel_id=1, source_target_pairs={{0,96},{4,100},{8,104},{12,108},{16,112},{20,116},{24,120},{28,124... | collective-permute-start | bytes 393224 | tf_op jit(solution)/shard_map/ppermute | solution.py:71
  216.1 5.3 %collective-permute-start.45 = (f32[64]{0:T(128)S(1)}, f32[64]{0:T(128)S(1)}, u32[]{:S(2)}, u32[]{:S(2)}) collective-permute-start(f32[64]{0:T(128)S(1)} %multiply_reduce_fusion), channel_id=1, source_target_pairs={{0,1},{1,2},{2,3},{3,0},{4,5},{5,6},{6,7},{7,4},{8,9},{9,10},{10,1... | collective-permute-start | bytes 776 | tf_op jit(solution)/shard_map/ppermute | solution.py:71
  218.5 5.1 %collective-permute-start.46 = (f32[64]{0:T(128)S(1)}, f32[64]{0:T(128)S(1)}, u32[]{:S(2)}, u32[]{:S(2)}) collective-permute-start(f32[64]{0:T(128)S(1)} %multiply_reduce_fusion), channel_id=1, source_target_pairs={{0,2},{1,3},{2,0},{3,1},{4,6},{5,7},{6,4},{7,5},{8,10},{9,11},{10,... | collective-permute-start | bytes 776 | tf_op jit(solution)/shard_map/ppermute | solution.py:71
  221.1 3.6 %collective-permute-start.47 = (f32[64]{0:T(128)S(1)}, f32[64]{0:T(128)S(1)}, u32[]{:S(2)}, u32[]{:S(2)}) collective-permute-start(f32[64]{0:T(128)S(1)} %multiply_reduce_fusion), channel_id=1, source_target_pairs={{0,3},{1,0},{2,1},{3,2},{4,7},{5,4},{6,5},{7,6},{8,11},{9,8},{10,9... | collective-permute-start | bytes 776 | tf_op jit(solution)/shard_map/ppermute | solution.py:71
  (1 other events, 1.4 us)

commit v3 on v2

--- a/solution.py
+++ b/solution.py
@@ -298,7 +298,7 @@
             sliced, received, ((mp - shift) % MP_SIZE) * slice_width, 1
         )
     attention_out = seq_total(
-        jnp.dot(sliced, output_weight, preferred_element_type=jnp.float32), butterfly=True
+        jnp.dot(sliced, output_weight, preferred_element_type=jnp.float32)
     )
     attention_squares = feature_sums(jnp.sum(attention_out * attention_out, axis=1))
     hidden = (
@@ -311,7 +311,7 @@
         jnp.dot(hidden_cols, up_weight, preferred_element_type=jnp.float32),
     )
     mlp_out = seq_total(
-        jnp.dot(active_cols, down_weight, preferred_element_type=jnp.float32), butterfly=True
+        jnp.dot(active_cols, down_weight, preferred_element_type=jnp.float32)
     )
     mlp_squares = feature_sums(jnp.sum(mlp_out * mlp_out, axis=1))
     decoded = (

time: 227 us -> 219 us (0.965)
  waiting for transfers between devices: 61.3 us -> 56.6 us
    ppermute x29 -> x27, waiting for transfers between devices: 37.3 us -> 28.8 us  [exchange(): lax.ppermute(value, axis, digit_pairs(count, stride, size, shift))]
    ppermute x29 -> x27, starting transfers between devices: 73.7 us -> 66.6 us  [exchange(): lax.ppermute(value, axis, digit_pairs(count, stride, size, shift))]
    ppermute x8 -> x10, starting transfers between devices: 17.5 us -> 24 us  [scatter_digit(): lax.ppermute(send, 'seq', digit_pairs(SEQ_SIZE, stride, size, shift))]
    ppermute x4 -> x6, waiting for transfers between devices: 3.59 us -> 5.9 us  [gather_digit(): lax.ppermute(current, 'seq', digit_pairs(SEQ_SIZE, stride, size, shift))]
    ppermute x8 -> x10, waiting for transfers between devices: 12.2 us -> 13.8 us  [scatter_digit(): lax.ppermute(send, 'seq', digit_pairs(SEQ_SIZE, stride, size, shift))]
  transfers between devices with their start and end apart: 49 -> 51, of which waited for: 30 -> 34; matrix products, arithmetic and copies ran while one was open for 8% -> 8% of each run, Pallas kernels for 0% -> 0%
where the time goes in v3:
time: 219 us
  starting transfers between devices  118 us (54%)
  waiting for transfers between devices  56.6 us (26%)
  local copies, waits for them, and re-layouts  20.9 us (10%)
  other arithmetic  13.5 us (6%)
  matrix products  8.51 us (4%)
    ppermute x27, starting transfers between devices, exchange(): lax.ppermute(value, axis, digit_pairs(count, stride, size, shift))  66.6 us
    ppermute x27, waiting for transfers between devices, exchange(): lax.ppermute(value, axis, digit_pairs(count, stride, size, shift))  28.8 us
    ppermute x10, starting transfers between devices, scatter_digit(): lax.ppermute(send, 'seq', digit_pairs(SEQ_SIZE, stride, size, shift))  24 us
    ppermute x10, waiting for transfers between devices, scatter_digit(): lax.ppermute(send, 'seq', digit_pairs(SEQ_SIZE, stride, size, shift))  13.8 us
    ppermute x4, starting transfers between devices, local(): received = lax.ppermute(attended, ('seq', 'mp'), pairs)  13.4 us
    all_to_all x1, starting transfers between devices, local(): sources = lax.all_to_all(send, 'seq', 0, 0, tiled=True)  7.09 us
    all_to_all x1, waiting for transfers between devices, local(): sources = lax.all_to_all(send, 'seq', 0, 0, tiled=True)  6.86 us
    unnamed x46, local copies, waits for them, and re-layouts  6.71 us
  transfers between devices with their start and end apart: 51, of which 34 were waited for; matrix products, arithmetic and copies ran while one was open for 8% of the time, Pallas kernels for 0%

profile of v3, /device:TPU:0, one launch (start us, length us, event | category | flops | bytes accessed | tf_op | source)
XLA Modules:
  0.0 218.9 jit_solution(7109659521425354562)
XLA Ops:
  0.0 1.4 constant_dynamic-slice_fusion.13
  1.4 1.4 collective-permute-start
  5.7 3.5 %fusion.23 = (bf16[4096,128]{1,0:T(8,128)(2,1)S(1)}, bf16[4096,128]{1,0:T(8,128)(2,1)S(1)}, bf16[4096,128]{1,0:T(8,128)(2,1)S(1)}, bf16[4096,128]{1,0:T(8,128)(2,1)}) fusion(bf16[4096,512]{1,0:T(8,128)(2,1)} %bitcast.185), kind=kLoop, calls=%fused_computation.139 | loop fusion | bytes 8388608 | tf_op jit(solution)/shard_map/slice | solution.py:242
  10.8 2.3 %copy.110 = bf16[4096,128]{0,1:T(8,128)(2,1)} copy(bf16[4096,128]{1,0:T(8,128)(2,1)} %get-tuple-element.20) | data formatting | bytes 2097152
  13.2 1.3 copy.109
  18.7 1.7 collective-permute-start.2
  21.2 2.8 %collective-permute-start.3 = (f32[64,768]{1,0:T(8,128)S(1)}, f32[64,768]{1,0:T(8,128)S(1)}, u32[]{:S(2)}, u32[]{:S(2)}) collective-permute-start(f32[64,768]{1,0:T(8,128)S(1)} %get-tuple-element.14), channel_id=1, source_target_pairs={{0,16},{4,20},{8,24},{12,28},{16,0},{20,4},{24,8},{28,12},{32,48},... | collective-permute-start | bytes 589832 | tf_op jit(solution)/shard_map/ppermute | solution.py:71
  24.0 1.4 collective-permute-start.4
  25.5 1.4 collective-permute-done.2
  26.9 5.3 %collective-permute-done.3 = f32[64,768]{1,0:T(8,128)S(1)} collective-permute-done((f32[64,768]{1,0:T(8,128)S(1)}, f32[64,768]{1,0:T(8,128)S(1)}, u32[]{:S(2)}, u32[]{:S(2)}) %collective-permute-start.3) | collective-permute-done | bytes 196640 | tf_op jit(solution)/shard_map/ppermute | solution.py:71
  32.7 4.3 %collective-permute-start.5 = (f32[64,768]{1,0:T(8,128)S(1)}, f32[64,768]{1,0:T(8,128)S(1)}, u32[]{:S(2)}, u32[]{:S(2)}) collective-permute-start(f32[64,768]{1,0:T(8,128)S(1)} %reduce_sum.153), channel_id=1, source_target_pairs={{0,32},{4,36},{8,40},{12,44},{16,48},{20,52},{24,56},{28,60},{32,6... | collective-permute-start | bytes 589832 | tf_op jit(solution)/shard_map/ppermute | solution.py:71
  37.0 4.8 %collective-permute-start.6 = (f32[64,768]{1,0:T(8,128)S(1)}, f32[64,768]{1,0:T(8,128)S(1)}, u32[]{:S(2)}, u32[]{:S(2)}) collective-permute-start(f32[64,768]{1,0:T(8,128)S(1)} %reduce_sum.153), channel_id=1, source_target_pairs={{0,64},{4,68},{8,72},{12,76},{16,80},{20,84},{24,88},{28,92},{32,9... | collective-permute-start | bytes 589832 | tf_op jit(solution)/shard_map/ppermute | solution.py:71
  41.8 1.3 collective-permute-start.7
  43.2 2.0 collective-permute-done.5
  45.2 4.6 %collective-permute-done.6 = f32[64,768]{1,0:T(8,128)S(1)} collective-permute-done((f32[64,768]{1,0:T(8,128)S(1)}, f32[64,768]{1,0:T(8,128)S(1)}, u32[]{:S(2)}, u32[]{:S(2)}) %collective-permute-start.6) | collective-permute-done | bytes 196640 | tf_op jit(solution)/shard_map/ppermute | solution.py:71
  50.0 1.4 collective-permute-done.8
  51.6 1.9 collective-permute-start.9
  54.4 1.9 collective-permute-start.11
  56.7 1.9 collective-permute-done.10
  59.1 1.9 convolution_bitcast_fusion
  61.0 1.7 convolution_bitcast_fusion.1
  64.4 1.4 fusion.2
  68.6 7.1 %all-to-all-start = ((f32[32,1,1152]{2,1,0:T(1,128)}), f32[32,1,1152]{2,1,0:T(1,128)S(1)}, u32[]{:S(2)}, u32[]{:S(2)}) async-start(f32[32,1,1152]{2,1,0:T(1,128)} %reshape.331), calls=%async_computation | async-start | bytes 294912 | tf_op jit(solution)/shard_map/all_to_all | solution.py:258
  76.5 6.9 %all-to-all-done = f32[32,1,1152]{2,1,0:T(1,128)S(1)} async-done(((f32[32,1,1152]{2,1,0:T(1,128)}), f32[32,1,1152]{2,1,0:T(1,128)S(1)}, u32[]{:S(2)}, u32[]{:S(2)}) %all-to-all-start) | async-done | bytes 147488 | tf_op jit(solution)/shard_map/all_to_all | solution.py:258
  87.2 5.2 %collective-permute-start.13 = (bf16[64,16]{0,1:T(8,128)(2,1)S(1)}, bf16[64,16]{0,1:T(8,128)(2,1)S(1)}, u32[]{:S(2)}, u32[]{:S(2)}) collective-permute-start(bf16[64,16]{0,1:T(8,128)(2,1)S(1)} %copy.102), channel_id=1, source_target_pairs={{0,1},{1,33},{2,65},{3,97},{4,2},{5,34},{6,66},{7,98},{8,3},{9,35}... | collective-permute-start | bytes 6152 | tf_op jit(solution)/shard_map/ppermute | solution.py:296
  92.4 4.1 %collective-permute-start.14 = (bf16[64,16]{0,1:T(8,128)(2,1)S(1)}, bf16[64,16]{0,1:T(8,128)(2,1)S(1)}, u32[]{:S(2)}, u32[]{:S(2)}) collective-permute-start(bf16[64,16]{0,1:T(8,128)(2,1)S(1)} %copy.102), channel_id=1, source_target_pairs={{0,2},{1,34},{2,66},{3,98},{4,3},{5,35},{6,67},{7,99},{8,0},{9,32}... | collective-permute-start | bytes 6152 | tf_op jit(solution)/shard_map/ppermute | solution.py:296
  96.5 3.4 %collective-permute-start.15 = (bf16[64,16]{0,1:T(8,128)(2,1)S(1)}, bf16[64,16]{0,1:T(8,128)(2,1)S(1)}, u32[]{:S(2)}, u32[]{:S(2)}) collective-permute-start(bf16[64,16]{0,1:T(8,128)(2,1)S(1)} %copy.102), channel_id=1, source_target_pairs={{0,3},{1,35},{2,67},{3,99},{4,0},{5,32},{6,64},{7,96},{8,1},{9,33}... | collective-permute-start | bytes 6152 | tf_op jit(solution)/shard_map/ppermute | solution.py:296
  100.1 1.2 collective-permute-done.15
  101.5 2.8 %collective-permute-start.16 = (f32[64,256]{1,0:T(8,128)S(1)}, f32[64,256]{1,0:T(8,128)S(1)}, u32[]{:S(2)}, u32[]{:S(2)}) collective-permute-start(f32[64,256]{1,0:T(8,128)S(1)} %constant_dynamic-slice_fusion.9), channel_id=1, source_target_pairs={{0,4},{4,0},{8,12},{12,8},{16,20},{20,16},{24,28},{28,24},{32,36},... | collective-permute-start | bytes 196616 | tf_op jit(solution)/shard_map/ppermute | solution.py:83
  105.3 5.0 %collective-permute-start.18 = (f32[64,256]{1,0:T(8,128)S(1)}, f32[64,256]{1,0:T(8,128)S(1)}, u32[]{:S(2)}, u32[]{:S(2)}) collective-permute-start(f32[64,256]{1,0:T(8,128)S(1)} %get-tuple-element.10), channel_id=1, source_target_pairs={{0,16},{4,20},{8,24},{12,28},{16,0},{20,4},{24,8},{28,12},{32,48},... | collective-permute-start | bytes 196616 | tf_op jit(solution)/shard_map/ppermute | solution.py:71
  110.4 2.5 %collective-permute-start.19 = (f32[64,256]{1,0:T(8,128)S(1)}, f32[64,256]{1,0:T(8,128)S(1)}, u32[]{:S(2)}, u32[]{:S(2)}) collective-permute-start(f32[64,256]{1,0:T(8,128)S(1)} %get-tuple-element.10), channel_id=1, source_target_pairs={{0,24},{4,28},{8,0},{12,4},{16,8},{20,12},{24,16},{28,20},{32,56},... | collective-permute-start | bytes 196616 | tf_op jit(solution)/shard_map/ppermute | solution.py:71
  114.8 1.7 collective-permute-start.20
  116.6 6.0 %collective-permute-start.21 = (f32[64,256]{1,0:T(8,128)S(1)}, f32[64,256]{1,0:T(8,128)S(1)}, u32[]{:S(2)}, u32[]{:S(2)}) collective-permute-start(f32[64,256]{1,0:T(8,128)S(1)} %reduce_sum.162), channel_id=1, source_target_pairs={{0,64},{4,68},{8,72},{12,76},{16,80},{20,84},{24,88},{28,92},{32,9... | collective-permute-start | bytes 196616 | tf_op jit(solution)/shard_map/ppermute | solution.py:71
  122.6 2.5 %collective-permute-start.22 = (f32[64,256]{1,0:T(8,128)S(1)}, f32[64,256]{1,0:T(8,128)S(1)}, u32[]{:S(2)}, u32[]{:S(2)}) collective-permute-start(f32[64,256]{1,0:T(8,128)S(1)} %reduce_sum.162), channel_id=1, source_target_pairs={{0,96},{4,100},{8,104},{12,108},{16,112},{20,116},{24,120},{28,124... | collective-permute-start | bytes 196616 | tf_op jit(solution)/shard_map/ppermute | solution.py:71
  125.4 1.6 collective-permute-done.22
  127.2 1.2 collective-permute-done.23
  129.0 3.4 %collective-permute-start.25 = (f32[64]{0:T(128)S(1)}, f32[64]{0:T(128)S(1)}, u32[]{:S(2)}, u32[]{:S(2)}) collective-permute-start(f32[64]{0:T(128)S(1)} %multiply_reduce_fusion.1), channel_id=1, source_target_pairs={{0,2},{1,3},{2,0},{3,1},{4,6},{5,7},{6,4},{7,5},{8,10},{9,11},{10,... | collective-permute-start | bytes 776 | tf_op jit(solution)/shard_map/ppermute | solution.py:71
  132.3 2.5 %collective-permute-start.26 = (f32[64]{0:T(128)S(1)}, f32[64]{0:T(128)S(1)}, u32[]{:S(2)}, u32[]{:S(2)}) collective-permute-start(f32[64]{0:T(128)S(1)} %multiply_reduce_fusion.1), channel_id=1, source_target_pairs={{0,3},{1,0},{2,1},{3,2},{4,7},{5,4},{6,5},{7,6},{8,11},{9,8},{10,9... | collective-permute-start | bytes 776 | tf_op jit(solution)/shard_map/ppermute | solution.py:71
  138.0 1.4 stack_reshape.7
  139.4 3.6 %pad_maximum_fusion = f32[64,32,2,64]{3,2,1,0:T(2,128)S(1)} fusion(f32[64,32,1,64]{3,2,1,0:T(1,128)} %bitcast.191, f32[64,32,1,64]{3,2,1,0:T(1,128)S(1)} %bitcast.190), kind=kLoop, calls=%fused_computation.9 | loop fusion | flops 262144 | bytes 2097152 | tf_op jit(solution)/shard_map/stack | solution.py:122
  143.0 2.0 reshape.325
  145.4 1.8 collective-permute-done.28
  147.5 3.0 %collective-permute-start.30 = (f32[64,512]{1,0:T(8,128)S(1)}, f32[64,512]{1,0:T(8,128)S(1)}, u32[]{:S(2)}, u32[]{:S(2)}) collective-permute-start(f32[64,512]{1,0:T(8,128)S(1)} %get-tuple-element.23), channel_id=1, source_target_pairs={{0,16},{4,20},{8,24},{12,28},{16,0},{20,4},{24,8},{28,12},{32,48},... | collective-permute-start | bytes 393224 | tf_op jit(solution)/shard_map/ppermute | solution.py:83
  151.6 5.4 %collective-permute-done.29 = f32[64,512]{1,0:T(8,128)S(1)} collective-permute-done((f32[64,512]{1,0:T(8,128)S(1)}, f32[64,512]{1,0:T(8,128)S(1)}, u32[]{:S(2)}, u32[]{:S(2)}) %collective-permute-start.29) | collective-permute-done | bytes 131104 | tf_op jit(solution)/shard_map/ppermute | solution.py:83
  157.7 7.2 %collective-permute-start.32 = (f32[64,128]{1,0:T(8,128)S(1)}, f32[64,128]{1,0:T(8,128)S(1)}, u32[]{:S(2)}, u32[]{:S(2)}) collective-permute-start(f32[64,128]{1,0:T(8,128)S(1)} %get-tuple-element.32), channel_id=1, source_target_pairs={{0,32},{4,36},{8,40},{12,44},{16,48},{20,52},{24,56},{28,60},{32,6... | collective-permute-start | bytes 98312 | tf_op jit(solution)/shard_map/ppermute | solution.py:83
  164.9 4.9 %collective-permute-start.33 = (f32[64,128]{1,0:T(8,128)S(1)}, f32[64,128]{1,0:T(8,128)S(1)}, u32[]{:S(2)}, u32[]{:S(2)}) collective-permute-start(f32[64,128]{1,0:T(8,128)S(1)} %get-tuple-element.34), channel_id=1, source_target_pairs={{0,64},{4,68},{8,72},{12,76},{16,80},{20,84},{24,88},{28,92},{32,9... | collective-permute-start | bytes 98312 | tf_op jit(solution)/shard_map/ppermute | solution.py:83
  170.4 1.6 collective-permute-done.33
  172.1 1.7 collective-permute-done.34
  173.9 3.1 %collective-permute-start.36 = (bf16[64,64]{1,0:T(8,128)(2,1)S(1)}, bf16[64,64]{1,0:T(8,128)(2,1)S(1)}, u32[]{:S(2)}, u32[]{:S(2)}) collective-permute-start(bf16[64,64]{1,0:T(8,128)(2,1)S(1)} %fusion.9), channel_id=1, source_target_pairs={{0,64},{4,68},{8,72},{12,76},{16,80},{20,84},{24,88},{28,92},{32,9... | collective-permute-start | bytes 24584 | tf_op jit(solution)/shard_map/ppermute | solution.py:94
  179.3 1.4 collective-permute-done.37
  182.0 4.0 %collective-permute-start.39 = (f32[64,256]{1,0:T(8,128)S(1)}, f32[64,256]{1,0:T(8,128)S(1)}, u32[]{:S(2)}, u32[]{:S(2)}) collective-permute-start(f32[64,256]{1,0:T(8,128)S(1)} %constant_dynamic-slice_fusion), channel_id=1, source_target_pairs={{0,4},{4,0},{8,12},{12,8},{16,20},{20,16},{24,28},{28,24},{32,36},... | collective-permute-start | bytes 196616 | tf_op jit(solution)/shard_map/ppermute | solution.py:83
  186.9 2.6 %collective-permute-start.40 = (f32[64,256]{1,0:T(8,128)S(1)}, f32[64,256]{1,0:T(8,128)S(1)}, u32[]{:S(2)}, u32[]{:S(2)}) collective-permute-start(f32[64,256]{1,0:T(8,128)S(1)} %get-tuple-element.8), channel_id=1, source_target_pairs={{0,8},{4,12},{8,16},{12,20},{16,24},{20,28},{24,0},{28,4},{32,40},... | collective-permute-start | bytes 196616 | tf_op jit(solution)/shard_map/ppermute | solution.py:71
  189.5 2.6 %collective-permute-start.41 = (f32[64,256]{1,0:T(8,128)S(1)}, f32[64,256]{1,0:T(8,128)S(1)}, u32[]{:S(2)}, u32[]{:S(2)}) collective-permute-start(f32[64,256]{1,0:T(8,128)S(1)} %get-tuple-element.8), channel_id=1, source_target_pairs={{0,16},{4,20},{8,24},{12,28},{16,0},{20,4},{24,8},{28,12},{32,48},... | collective-permute-start | bytes 196616 | tf_op jit(solution)/shard_map/ppermute | solution.py:71
  192.1 1.5 collective-permute-start.42
  193.7 2.1 collective-permute-done.41
  196.4 2.6 %collective-permute-start.43 = (f32[64,256]{1,0:T(8,128)S(1)}, f32[64,256]{1,0:T(8,128)S(1)}, u32[]{:S(2)}, u32[]{:S(2)}) collective-permute-start(f32[64,256]{1,0:T(8,128)S(1)} %reduce_sum.166), channel_id=1, source_target_pairs={{0,32},{4,36},{8,40},{12,44},{16,48},{20,52},{24,56},{28,60},{32,6... | collective-permute-start | bytes 196616 | tf_op jit(solution)/shard_map/ppermute | solution.py:71
  199.0 5.2 %collective-permute-start.44 = (f32[64,256]{1,0:T(8,128)S(1)}, f32[64,256]{1,0:T(8,128)S(1)}, u32[]{:S(2)}, u32[]{:S(2)}) collective-permute-start(f32[64,256]{1,0:T(8,128)S(1)} %reduce_sum.166), channel_id=1, source_target_pairs={{0,64},{4,68},{8,72},{12,76},{16,80},{20,84},{24,88},{28,92},{32,9... | collective-permute-start | bytes 196616 | tf_op jit(solution)/shard_map/ppermute | solution.py:71
  204.2 1.5 collective-permute-start.45
  205.8 1.4 collective-permute-done.44
  207.1 1.3 collective-permute-done.45
  208.6 1.2 collective-permute-done.46
  209.9 2.5 %collective-permute-start.47 = (f32[64]{0:T(128)S(1)}, f32[64]{0:T(128)S(1)}, u32[]{:S(2)}, u32[]{:S(2)}) collective-permute-start(f32[64]{0:T(128)S(1)} %multiply_reduce_fusion), channel_id=1, source_target_pairs={{0,1},{1,2},{2,3},{3,0},{4,5},{5,6},{6,7},{7,4},{8,9},{9,10},{10,1... | collective-permute-start | bytes 776 | tf_op jit(solution)/shard_map/ppermute | solution.py:71
  212.4 2.2 collective-permute-start.48
  215.3 2.2 %collective-permute-done.48 = f32[64]{0:T(128)S(1)} collective-permute-done((f32[64]{0:T(128)S(1)}, f32[64]{0:T(128)S(1)}, u32[]{:S(2)}, u32[]{:S(2)}) %collective-permute-start.48) | collective-permute-done | bytes 288 | tf_op jit(solution)/shard_map/ppermute | solution.py:71
  (255 shorter events, 38.7 us)
Async XLA Ops:
  0.0 137.1 %copy-start = (bf16[64,2048]{1,0:T(8,128)(2,1)S(1)}, bf16[64,2048]{1,0:T(8,128)(2,1)}, u32[]{:S(2)}) copy-start(bf16[64,2048]{1,0:T(8,128)(2,1)} %param.22) | copy-start | bytes 786436
  1.4 14.2 %collective-permute-start = (bf16[64,64]{1,0:T(8,128)(2,1)}, bf16[64,64]{1,0:T(8,128)(2,1)S(1)}, u32[]{:S(2)}, u32[]{:S(2)}) collective-permute-start(bf16[64,64]{1,0:T(8,128)(2,1)} %constant_dynamic-slice_fusion.13), channel_id=1, source_target_pairs={{0,0},{1,32},{2,64},{3,96},{4,4},{5,36},{6,68},{7,100},{8,8},{9,40... | collective-permute-start | bytes 24584 | tf_op jit(solution)/shard_map/ppermute | solution.py:47
  4.2 5.1 %copy-start.15 = (s32[64]{0:T(128)}, s32[64]{0:T(128)S(1)}, u32[]{:S(2)}) copy-start(s32[64]{0:T(128)S(1)} %lt.363) | copy-start | bytes 772
  10.8 4.9 %copy-start.8 = (bf16[64,512]{1,0:T(8,128)(2,1)S(1)}, bf16[64,512]{1,0:T(8,128)(2,1)}, u32[]{:S(2)}) copy-start(bf16[64,512]{1,0:T(8,128)(2,1)} %param.18) | copy-start | bytes 196612
  10.8 5.0 %copy-start.9 = (bf16[64,512]{1,0:T(8,128)(2,1)S(1)}, bf16[64,512]{1,0:T(8,128)(2,1)}, u32[]{:S(2)}) copy-start(bf16[64,512]{1,0:T(8,128)(2,1)} %param.19) | copy-start | bytes 196612
  17.0 1.5 collective-permute-start.1
  18.6 40.0 %copy-start.11 = (f32[512]{0:T(512)S(1)}, f32[512]{0:T(512)}, u32[]{:S(2)}) copy-start(f32[512]{0:T(512)} %param.26) | copy-start | bytes 6148
  18.6 40.0 %copy-start.12 = (f32[512]{0:T(512)S(1)}, f32[512]{0:T(512)}, u32[]{:S(2)}) copy-start(f32[512]{0:T(512)} %param.25) | copy-start | bytes 6148
  18.7 8.2 %collective-permute-start.2 = (f32[64,768]{1,0:T(8,128)S(1)}, f32[64,768]{1,0:T(8,128)S(1)}, u32[]{:S(2)}, u32[]{:S(2)}) collective-permute-start(f32[64,768]{1,0:T(8,128)S(1)} %get-tuple-element.14), channel_id=1, source_target_pairs={{0,8},{4,12},{8,16},{12,20},{16,24},{20,28},{24,0},{28,4},{32,40},... | collective-permute-start | bytes 589832 | tf_op jit(solution)/shard_map/ppermute | solution.py:71
  21.2 11.0 %collective-permute-start.3 = (f32[64,768]{1,0:T(8,128)S(1)}, f32[64,768]{1,0:T(8,128)S(1)}, u32[]{:S(2)}, u32[]{:S(2)}) collective-permute-start(f32[64,768]{1,0:T(8,128)S(1)} %get-tuple-element.14), channel_id=1, source_target_pairs={{0,16},{4,20},{8,24},{12,28},{16,0},{20,4},{24,8},{28,12},{32,48},... | collective-permute-start | bytes 589832 | tf_op jit(solution)/shard_map/ppermute | solution.py:71
  24.0 8.6 %collective-permute-start.4 = (f32[64,768]{1,0:T(8,128)S(1)}, f32[64,768]{1,0:T(8,128)S(1)}, u32[]{:S(2)}, u32[]{:S(2)}) collective-permute-start(f32[64,768]{1,0:T(8,128)S(1)} %get-tuple-element.14), channel_id=1, source_target_pairs={{0,24},{4,28},{8,0},{12,4},{16,8},{20,12},{24,16},{28,20},{32,56},... | collective-permute-start | bytes 589832 | tf_op jit(solution)/shard_map/ppermute | solution.py:71
  32.7 12.4 %collective-permute-start.5 = (f32[64,768]{1,0:T(8,128)S(1)}, f32[64,768]{1,0:T(8,128)S(1)}, u32[]{:S(2)}, u32[]{:S(2)}) collective-permute-start(f32[64,768]{1,0:T(8,128)S(1)} %reduce_sum.153), channel_id=1, source_target_pairs={{0,32},{4,36},{8,40},{12,44},{16,48},{20,52},{24,56},{28,60},{32,6... | collective-permute-start | bytes 589832 | tf_op jit(solution)/shard_map/ppermute | solution.py:71
  37.0 12.8 %collective-permute-start.6 = (f32[64,768]{1,0:T(8,128)S(1)}, f32[64,768]{1,0:T(8,128)S(1)}, u32[]{:S(2)}, u32[]{:S(2)}) collective-permute-start(f32[64,768]{1,0:T(8,128)S(1)} %reduce_sum.153), channel_id=1, source_target_pairs={{0,64},{4,68},{8,72},{12,76},{16,80},{20,84},{24,88},{28,92},{32,9... | collective-permute-start | bytes 589832 | tf_op jit(solution)/shard_map/ppermute | solution.py:71
  41.8 8.0 %collective-permute-start.7 = (f32[64,768]{1,0:T(8,128)S(1)}, f32[64,768]{1,0:T(8,128)S(1)}, u32[]{:S(2)}, u32[]{:S(2)}) collective-permute-start(f32[64,768]{1,0:T(8,128)S(1)} %reduce_sum.153), channel_id=1, source_target_pairs={{0,96},{4,100},{8,104},{12,108},{16,112},{20,116},{24,120},{28,124... | collective-permute-start | bytes 589832 | tf_op jit(solution)/shard_map/ppermute | solution.py:71
  49.9 1.5 collective-permute-start.8
  51.6 5.1 %collective-permute-start.9 = (f32[64,2]{0,1:T(2,128)S(1)}, f32[64,2]{0,1:T(2,128)S(1)}, u32[]{:S(2)}, u32[]{:S(2)}) collective-permute-start(f32[64,2]{0,1:T(2,128)S(1)} %pad_maximum_fusion.3), channel_id=1, source_target_pairs={{0,1},{1,2},{2,3},{3,0},{4,5},{5,6},{6,7},{7,4},{8,9},{9,10},{10,1... | collective-permute-start | bytes 1544 | tf_op jit(solution)/shard_map/ppermute | solution.py:71
  53.5 5.1 %collective-permute-start.10 = (f32[64,2]{0,1:T(2,128)S(1)}, f32[64,2]{0,1:T(2,128)S(1)}, u32[]{:S(2)}, u32[]{:S(2)}) collective-permute-start(f32[64,2]{0,1:T(2,128)S(1)} %pad_maximum_fusion.3), channel_id=1, source_target_pairs={{0,2},{1,3},{2,0},{3,1},{4,6},{5,7},{6,4},{7,5},{8,10},{9,11},{10,... | collective-permute-start | bytes 1544 | tf_op jit(solution)/shard_map/ppermute | solution.py:71
  54.4 4.2 %collective-permute-start.11 = (f32[64,2]{0,1:T(2,128)S(1)}, f32[64,2]{0,1:T(2,128)S(1)}, u32[]{:S(2)}, u32[]{:S(2)}) collective-permute-start(f32[64,2]{0,1:T(2,128)S(1)} %pad_maximum_fusion.3), channel_id=1, source_target_pairs={{0,3},{1,0},{2,1},{3,2},{4,7},{5,4},{6,5},{7,6},{8,11},{9,8},{10,9... | collective-permute-start | bytes 1544 | tf_op jit(solution)/shard_map/ppermute | solution.py:71
  59.1 4.6 %copy-start.2 = (pred[64,4096]{1,0:T(8,128)(4,1)S(1)}, pred[64,4096]{1,0:T(8,128)(4,1)}, u32[]{:S(2)}) copy-start(pred[64,4096]{1,0:T(8,128)(4,1)} %compare_and_fusion) | copy-start | bytes 786436
  67.1 34.2 %copy-start.10 = (bf16[64,512]{1,0:T(8,128)(2,1)S(1)}, bf16[64,512]{1,0:T(8,128)(2,1)}, u32[]{:S(2)}) copy-start(bf16[64,512]{1,0:T(8,128)(2,1)} %param.21) | copy-start | bytes 196612
  67.6 68.7 %copy-start.7 = (bf16[4,16,512]{2,1,0:T(8,128)(2,1)S(1)}, bf16[4,16,512]{2,1,0:T(8,128)(2,1)}, u32[]{:S(2)}) copy-start(bf16[4,16,512]{2,1,0:T(8,128)(2,1)} %param.17) | copy-start | bytes 196612
  67.6 68.7 %copy-start.13 = (f32[512]{0:T(512)S(1)}, f32[512]{0:T(512)}, u32[]{:S(2)}) copy-start(f32[512]{0:T(512)} %param.27) | copy-start | bytes 6148
  68.6 14.8 %all-to-all-start = ((f32[32,1,1152]{2,1,0:T(1,128)}), f32[32,1,1152]{2,1,0:T(1,128)S(1)}, u32[]{:S(2)}, u32[]{:S(2)}) async-start(f32[32,1,1152]{2,1,0:T(1,128)} %reshape.331), calls=%async_computation | async-start | bytes 294912 | tf_op jit(solution)/shard_map/all_to_all | solution.py:258
  75.9 61.9 %copy-start.5 = (bf16[64,2048]{1,0:T(8,128)(2,1)S(1)}, bf16[64,2048]{1,0:T(8,128)(2,1)}, u32[]{:S(2)}) copy-start(bf16[64,2048]{1,0:T(8,128)(2,1)} %param.23) | copy-start | bytes 786436
  86.5 13.5 %collective-permute-start.12 = (bf16[64,16]{0,1:T(8,128)(2,1)S(1)}, bf16[64,16]{0,1:T(8,128)(2,1)S(1)}, u32[]{:S(2)}, u32[]{:S(2)}) collective-permute-start(bf16[64,16]{0,1:T(8,128)(2,1)S(1)} %copy.102), channel_id=1, source_target_pairs={{0,0},{1,32},{2,64},{3,96},{4,1},{5,33},{6,65},{7,97},{8,2},{9,34}... | collective-permute-start | bytes 6152 | tf_op jit(solution)/shard_map/ppermute | solution.py:296
  87.2 12.8 %collective-permute-start.13 = (bf16[64,16]{0,1:T(8,128)(2,1)S(1)}, bf16[64,16]{0,1:T(8,128)(2,1)S(1)}, u32[]{:S(2)}, u32[]{:S(2)}) collective-permute-start(bf16[64,16]{0,1:T(8,128)(2,1)S(1)} %copy.102), channel_id=1, source_target_pairs={{0,1},{1,33},{2,65},{3,97},{4,2},{5,34},{6,66},{7,98},{8,3},{9,35}... | collective-permute-start | bytes 6152 | tf_op jit(solution)/shard_map/ppermute | solution.py:296
  92.4 7.6 %collective-permute-start.14 = (bf16[64,16]{0,1:T(8,128)(2,1)S(1)}, bf16[64,16]{0,1:T(8,128)(2,1)S(1)}, u32[]{:S(2)}, u32[]{:S(2)}) collective-permute-start(bf16[64,16]{0,1:T(8,128)(2,1)S(1)} %copy.102), channel_id=1, source_target_pairs={{0,2},{1,34},{2,66},{3,98},{4,3},{5,35},{6,67},{7,99},{8,0},{9,32}... | collective-permute-start | bytes 6152 | tf_op jit(solution)/shard_map/ppermute | solution.py:296
  96.5 4.7 %collective-permute-start.15 = (bf16[64,16]{0,1:T(8,128)(2,1)S(1)}, bf16[64,16]{0,1:T(8,128)(2,1)S(1)}, u32[]{:S(2)}, u32[]{:S(2)}) collective-permute-start(bf16[64,16]{0,1:T(8,128)(2,1)S(1)} %copy.102), channel_id=1, source_target_pairs={{0,3},{1,35},{2,67},{3,99},{4,0},{5,32},{6,64},{7,96},{8,1},{9,33}... | collective-permute-start | bytes 6152 | tf_op jit(solution)/shard_map/ppermute | solution.py:296
  101.5 3.7 %collective-permute-start.16 = (f32[64,256]{1,0:T(8,128)S(1)}, f32[64,256]{1,0:T(8,128)S(1)}, u32[]{:S(2)}, u32[]{:S(2)}) collective-permute-start(f32[64,256]{1,0:T(8,128)S(1)} %constant_dynamic-slice_fusion.9), channel_id=1, source_target_pairs={{0,4},{4,0},{8,12},{12,8},{16,20},{20,16},{24,28},{28,24},{32,36},... | collective-permute-start | bytes 196616 | tf_op jit(solution)/shard_map/ppermute | solution.py:83
  105.2 7.7 %collective-permute-start.17 = (f32[64,256]{1,0:T(8,128)S(1)}, f32[64,256]{1,0:T(8,128)S(1)}, u32[]{:S(2)}, u32[]{:S(2)}) collective-permute-start(f32[64,256]{1,0:T(8,128)S(1)} %get-tuple-element.10), channel_id=1, source_target_pairs={{0,8},{4,12},{8,16},{12,20},{16,24},{20,28},{24,0},{28,4},{32,40},... | collective-permute-start | bytes 196616 | tf_op jit(solution)/shard_map/ppermute | solution.py:71
  105.3 8.8 %collective-permute-start.18 = (f32[64,256]{1,0:T(8,128)S(1)}, f32[64,256]{1,0:T(8,128)S(1)}, u32[]{:S(2)}, u32[]{:S(2)}) collective-permute-start(f32[64,256]{1,0:T(8,128)S(1)} %get-tuple-element.10), channel_id=1, source_target_pairs={{0,16},{4,20},{8,24},{12,28},{16,0},{20,4},{24,8},{28,12},{32,48},... | collective-permute-start | bytes 196616 | tf_op jit(solution)/shard_map/ppermute | solution.py:71
  110.4 4.4 %collective-permute-start.19 = (f32[64,256]{1,0:T(8,128)S(1)}, f32[64,256]{1,0:T(8,128)S(1)}, u32[]{:S(2)}, u32[]{:S(2)}) collective-permute-start(f32[64,256]{1,0:T(8,128)S(1)} %get-tuple-element.10), channel_id=1, source_target_pairs={{0,24},{4,28},{8,0},{12,4},{16,8},{20,12},{24,16},{28,20},{32,56},... | collective-permute-start | bytes 196616 | tf_op jit(solution)/shard_map/ppermute | solution.py:71
  114.8 10.3 %collective-permute-start.20 = (f32[64,256]{1,0:T(8,128)S(1)}, f32[64,256]{1,0:T(8,128)S(1)}, u32[]{:S(2)}, u32[]{:S(2)}) collective-permute-start(f32[64,256]{1,0:T(8,128)S(1)} %reduce_sum.162), channel_id=1, source_target_pairs={{0,32},{4,36},{8,40},{12,44},{16,48},{20,52},{24,56},{28,60},{32,6... | collective-permute-start | bytes 196616 | tf_op jit(solution)/shard_map/ppermute | solution.py:71
  116.6 8.8 %collective-permute-start.21 = (f32[64,256]{1,0:T(8,128)S(1)}, f32[64,256]{1,0:T(8,128)S(1)}, u32[]{:S(2)}, u32[]{:S(2)}) collective-permute-start(f32[64,256]{1,0:T(8,128)S(1)} %reduce_sum.162), channel_id=1, source_target_pairs={{0,64},{4,68},{8,72},{12,76},{16,80},{20,84},{24,88},{28,92},{32,9... | collective-permute-start | bytes 196616 | tf_op jit(solution)/shard_map/ppermute | solution.py:71
  122.6 4.4 %collective-permute-start.22 = (f32[64,256]{1,0:T(8,128)S(1)}, f32[64,256]{1,0:T(8,128)S(1)}, u32[]{:S(2)}, u32[]{:S(2)}) collective-permute-start(f32[64,256]{1,0:T(8,128)S(1)} %reduce_sum.162), channel_id=1, source_target_pairs={{0,96},{4,100},{8,104},{12,108},{16,112},{20,116},{24,120},{28,124... | collective-permute-start | bytes 196616 | tf_op jit(solution)/shard_map/ppermute | solution.py:71
  127.0 1.3 collective-permute-start.23
  128.5 6.4 %collective-permute-start.24 = (f32[64]{0:T(128)S(1)}, f32[64]{0:T(128)S(1)}, u32[]{:S(2)}, u32[]{:S(2)}) collective-permute-start(f32[64]{0:T(128)S(1)} %multiply_reduce_fusion.1), channel_id=1, source_target_pairs={{0,1},{1,2},{2,3},{3,0},{4,5},{5,6},{6,7},{7,4},{8,9},{9,10},{10,1... | collective-permute-start | bytes 776 | tf_op jit(solution)/shard_map/ppermute | solution.py:71
  129.0 6.0 %collective-permute-start.25 = (f32[64]{0:T(128)S(1)}, f32[64]{0:T(128)S(1)}, u32[]{:S(2)}, u32[]{:S(2)}) collective-permute-start(f32[64]{0:T(128)S(1)} %multiply_reduce_fusion.1), channel_id=1, source_target_pairs={{0,2},{1,3},{2,0},{3,1},{4,6},{5,7},{6,4},{7,5},{8,10},{9,11},{10,... | collective-permute-start | bytes 776 | tf_op jit(solution)/shard_map/ppermute | solution.py:71
  132.3 3.8 %collective-permute-start.26 = (f32[64]{0:T(128)S(1)}, f32[64]{0:T(128)S(1)}, u32[]{:S(2)}, u32[]{:S(2)}) collective-permute-start(f32[64]{0:T(128)S(1)} %multiply_reduce_fusion.1), channel_id=1, source_target_pairs={{0,3},{1,0},{2,1},{3,2},{4,7},{5,4},{6,5},{7,6},{8,11},{9,8},{10,9... | collective-permute-start | bytes 776 | tf_op jit(solution)/shard_map/ppermute | solution.py:71
  136.4 0.7 collective-permute-start.27
  145.0 36.8 %copy-start.6 = (bf16[256,512]{1,0:T(8,128)(2,1)S(1)}, bf16[256,512]{1,0:T(8,128)(2,1)}, u32[]{:S(2)}) copy-start(bf16[256,512]{1,0:T(8,128)(2,1)} %param.24) | copy-start | bytes 786436
  145.0 73.2 %copy-start.14 = (f32[512]{0:T(512)S(1)}, f32[512]{0:T(512)}, u32[]{:S(2)}) copy-start(f32[512]{0:T(512)} %param.28) | copy-start | bytes 6148
  145.1 2.2 %collective-permute-start.28 = (f32[64,2048]{1,0:T(8,128)S(1)}, f32[64,2048]{1,0:T(8,128)S(1)}, u32[]{:S(2)}, u32[]{:S(2)}) collective-permute-start(f32[64,2048]{1,0:T(8,128)S(1)} %constant_dynamic-slice_fusion.7), channel_id=1, source_target_pairs={{0,4},{4,0},{8,12},{12,8},{16,20},{20,16},{24,28},{28,24},{32,36},... | collective-permute-start | bytes 1572872 | tf_op jit(solution)/shard_map/ppermute | solution.py:83
  147.4 9.6 %collective-permute-start.29 = (f32[64,512]{1,0:T(8,128)S(1)}, f32[64,512]{1,0:T(8,128)S(1)}, u32[]{:S(2)}, u32[]{:S(2)}) collective-permute-start(f32[64,512]{1,0:T(8,128)S(1)} %get-tuple-element.21), channel_id=1, source_target_pairs={{0,8},{4,12},{8,16},{12,20},{16,24},{20,28},{24,0},{28,4},{32,40},... | collective-permute-start | bytes 393224 | tf_op jit(solution)/shard_map/ppermute | solution.py:83
  147.5 9.5 %collective-permute-start.30 = (f32[64,512]{1,0:T(8,128)S(1)}, f32[64,512]{1,0:T(8,128)S(1)}, u32[]{:S(2)}, u32[]{:S(2)}) collective-permute-start(f32[64,512]{1,0:T(8,128)S(1)} %get-tuple-element.23), channel_id=1, source_target_pairs={{0,16},{4,20},{8,24},{12,28},{16,0},{20,4},{24,8},{28,12},{32,48},... | collective-permute-start | bytes 393224 | tf_op jit(solution)/shard_map/ppermute | solution.py:83
  150.4 7.1 %collective-permute-start.31 = (f32[64,512]{1,0:T(8,128)S(1)}, f32[64,512]{1,0:T(8,128)S(1)}, u32[]{:S(2)}, u32[]{:S(2)}) collective-permute-start(f32[64,512]{1,0:T(8,128)S(1)} %get-tuple-element.22), channel_id=1, source_target_pairs={{0,24},{4,28},{8,0},{12,4},{16,8},{20,12},{24,16},{28,20},{32,56},... | collective-permute-start | bytes 393224 | tf_op jit(solution)/shard_map/ppermute | solution.py:83
  157.7 12.8 %collective-permute-start.32 = (f32[64,128]{1,0:T(8,128)S(1)}, f32[64,128]{1,0:T(8,128)S(1)}, u32[]{:S(2)}, u32[]{:S(2)}) collective-permute-start(f32[64,128]{1,0:T(8,128)S(1)} %get-tuple-element.32), channel_id=1, source_target_pairs={{0,32},{4,36},{8,40},{12,44},{16,48},{20,52},{24,56},{28,60},{32,6... | collective-permute-start | bytes 98312 | tf_op jit(solution)/shard_map/ppermute | solution.py:83
  164.9 7.2 %collective-permute-start.33 = (f32[64,128]{1,0:T(8,128)S(1)}, f32[64,128]{1,0:T(8,128)S(1)}, u32[]{:S(2)}, u32[]{:S(2)}) collective-permute-start(f32[64,128]{1,0:T(8,128)S(1)} %get-tuple-element.34), channel_id=1, source_target_pairs={{0,64},{4,68},{8,72},{12,76},{16,80},{20,84},{24,88},{28,92},{32,9... | collective-permute-start | bytes 98312 | tf_op jit(solution)/shard_map/ppermute | solution.py:83
  169.8 3.9 %collective-permute-start.34 = (f32[64,128]{1,0:T(8,128)S(1)}, f32[64,128]{1,0:T(8,128)S(1)}, u32[]{:S(2)}, u32[]{:S(2)}) collective-permute-start(f32[64,128]{1,0:T(8,128)S(1)} %get-tuple-element.33), channel_id=1, source_target_pairs={{0,96},{4,100},{8,104},{12,108},{16,112},{20,116},{24,120},{28,124... | collective-permute-start | bytes 98312 | tf_op jit(solution)/shard_map/ppermute | solution.py:83
  173.8 5.0 %collective-permute-start.35 = (bf16[64,64]{1,0:T(8,128)(2,1)S(1)}, bf16[64,64]{1,0:T(8,128)(2,1)S(1)}, u32[]{:S(2)}, u32[]{:S(2)}) collective-permute-start(bf16[64,64]{1,0:T(8,128)(2,1)S(1)} %fusion.9), channel_id=1, source_target_pairs={{0,32},{4,36},{8,40},{12,44},{16,48},{20,52},{24,56},{28,60},{32,6... | collective-permute-start | bytes 24584 | tf_op jit(solution)/shard_map/ppermute | solution.py:94
  173.9 5.3 %collective-permute-start.36 = (bf16[64,64]{1,0:T(8,128)(2,1)S(1)}, bf16[64,64]{1,0:T(8,128)(2,1)S(1)}, u32[]{:S(2)}, u32[]{:S(2)}) collective-permute-start(bf16[64,64]{1,0:T(8,128)(2,1)S(1)} %fusion.9), channel_id=1, source_target_pairs={{0,64},{4,68},{8,72},{12,76},{16,80},{20,84},{24,88},{28,92},{32,9... | collective-permute-start | bytes 24584 | tf_op jit(solution)/shard_map/ppermute | solution.py:94
  177.0 3.7 %collective-permute-start.37 = (bf16[64,64]{1,0:T(8,128)(2,1)S(1)}, bf16[64,64]{1,0:T(8,128)(2,1)S(1)}, u32[]{:S(2)}, u32[]{:S(2)}) collective-permute-start(bf16[64,64]{1,0:T(8,128)(2,1)S(1)} %fusion.9), channel_id=1, source_target_pairs={{0,96},{4,100},{8,104},{12,108},{16,112},{20,116},{24,120},{28,124... | collective-permute-start | bytes 24584 | tf_op jit(solution)/shard_map/ppermute | solution.py:94
  181.1 0.7 collective-permute-start.38
  182.0 4.9 %collective-permute-start.39 = (f32[64,256]{1,0:T(8,128)S(1)}, f32[64,256]{1,0:T(8,128)S(1)}, u32[]{:S(2)}, u32[]{:S(2)}) collective-permute-start(f32[64,256]{1,0:T(8,128)S(1)} %constant_dynamic-slice_fusion), channel_id=1, source_target_pairs={{0,4},{4,0},{8,12},{12,8},{16,20},{20,16},{24,28},{28,24},{32,36},... | collective-permute-start | bytes 196616 | tf_op jit(solution)/shard_map/ppermute | solution.py:83
  186.9 6.8 %collective-permute-start.40 = (f32[64,256]{1,0:T(8,128)S(1)}, f32[64,256]{1,0:T(8,128)S(1)}, u32[]{:S(2)}, u32[]{:S(2)}) collective-permute-start(f32[64,256]{1,0:T(8,128)S(1)} %get-tuple-element.8), channel_id=1, source_target_pairs={{0,8},{4,12},{8,16},{12,20},{16,24},{20,28},{24,0},{28,4},{32,40},... | collective-permute-start | bytes 196616 | tf_op jit(solution)/shard_map/ppermute | solution.py:71
  189.5 6.2 %collective-permute-start.41 = (f32[64,256]{1,0:T(8,128)S(1)}, f32[64,256]{1,0:T(8,128)S(1)}, u32[]{:S(2)}, u32[]{:S(2)}) collective-permute-start(f32[64,256]{1,0:T(8,128)S(1)} %get-tuple-element.8), channel_id=1, source_target_pairs={{0,16},{4,20},{8,24},{12,28},{16,0},{20,4},{24,8},{28,12},{32,48},... | collective-permute-start | bytes 196616 | tf_op jit(solution)/shard_map/ppermute | solution.py:71
  192.1 4.3 %collective-permute-start.42 = (f32[64,256]{1,0:T(8,128)S(1)}, f32[64,256]{1,0:T(8,128)S(1)}, u32[]{:S(2)}, u32[]{:S(2)}) collective-permute-start(f32[64,256]{1,0:T(8,128)S(1)} %get-tuple-element.8), channel_id=1, source_target_pairs={{0,24},{4,28},{8,0},{12,4},{16,8},{20,12},{24,16},{28,20},{32,56},... | collective-permute-start | bytes 196616 | tf_op jit(solution)/shard_map/ppermute | solution.py:71
  196.4 9.3 %collective-permute-start.43 = (f32[64,256]{1,0:T(8,128)S(1)}, f32[64,256]{1,0:T(8,128)S(1)}, u32[]{:S(2)}, u32[]{:S(2)}) collective-permute-start(f32[64,256]{1,0:T(8,128)S(1)} %reduce_sum.166), channel_id=1, source_target_pairs={{0,32},{4,36},{8,40},{12,44},{16,48},{20,52},{24,56},{28,60},{32,6... | collective-permute-start | bytes 196616 | tf_op jit(solution)/shard_map/ppermute | solution.py:71
  199.0 8.1 %collective-permute-start.44 = (f32[64,256]{1,0:T(8,128)S(1)}, f32[64,256]{1,0:T(8,128)S(1)}, u32[]{:S(2)}, u32[]{:S(2)}) collective-permute-start(f32[64,256]{1,0:T(8,128)S(1)} %reduce_sum.166), channel_id=1, source_target_pairs={{0,64},{4,68},{8,72},{12,76},{16,80},{20,84},{24,88},{28,92},{32,9... | collective-permute-start | bytes 196616 | tf_op jit(solution)/shard_map/ppermute | solution.py:71
  204.2 4.3 %collective-permute-start.45 = (f32[64,256]{1,0:T(8,128)S(1)}, f32[64,256]{1,0:T(8,128)S(1)}, u32[]{:S(2)}, u32[]{:S(2)}) collective-permute-start(f32[64,256]{1,0:T(8,128)S(1)} %reduce_sum.166), channel_id=1, source_target_pairs={{0,96},{4,100},{8,104},{12,108},{16,112},{20,116},{24,120},{28,124... | collective-permute-start | bytes 196616 | tf_op jit(solution)/shard_map/ppermute | solution.py:71
  208.5 1.3 collective-permute-start.46
  209.9 5.3 %collective-permute-start.47 = (f32[64]{0:T(128)S(1)}, f32[64]{0:T(128)S(1)}, u32[]{:S(2)}, u32[]{:S(2)}) collective-permute-start(f32[64]{0:T(128)S(1)} %multiply_reduce_fusion), channel_id=1, source_target_pairs={{0,1},{1,2},{2,3},{3,0},{4,5},{5,6},{6,7},{7,4},{8,9},{9,10},{10,1... | collective-permute-start | bytes 776 | tf_op jit(solution)/shard_map/ppermute | solution.py:71
  212.4 5.1 %collective-permute-start.48 = (f32[64]{0:T(128)S(1)}, f32[64]{0:T(128)S(1)}, u32[]{:S(2)}, u32[]{:S(2)}) collective-permute-start(f32[64]{0:T(128)S(1)} %multiply_reduce_fusion), channel_id=1, source_target_pairs={{0,2},{1,3},{2,0},{3,1},{4,6},{5,7},{6,4},{7,5},{8,10},{9,11},{10,... | collective-permute-start | bytes 776 | tf_op jit(solution)/shard_map/ppermute | solution.py:71
  214.6 3.6 %collective-permute-start.49 = (f32[64]{0:T(128)S(1)}, f32[64]{0:T(128)S(1)}, u32[]{:S(2)}, u32[]{:S(2)}) collective-permute-start(f32[64]{0:T(128)S(1)} %multiply_reduce_fusion), channel_id=1, source_target_pairs={{0,3},{1,0},{2,1},{3,2},{4,7},{5,4},{6,5},{7,6},{8,11},{9,8},{10,9... | collective-permute-start | bytes 776 | tf_op jit(solution)/shard_map/ppermute | solution.py:71
  (3 other events, 7.1 us)

commit v4 on v3

--- a/solution.py
+++ b/solution.py
@@ -215,34 +215,32 @@
     values = value_cache.reshape(tokens, local_width)
     token_owner = jnp.repeat(page_owner, PAGE)
     token_spot = (page_index[:, None] * PAGE + jnp.arange(PAGE, dtype=jnp.int32)[None, :]).reshape(tokens)
-    request_of_row = jnp.tile(jnp.arange(R, dtype=jnp.int32), STEPS)
-    length_of_row = jnp.tile(lengths, STEPS)
-    validity = (token_owner[None, :] == request_of_row[:, None]) & (
-        token_spot[None, :] < length_of_row[:, None]
-    )
+    validity = (token_owner[None, :] == jnp.arange(R, dtype=jnp.int32)[:, None]) & (
+        token_spot[None, :] < lengths[:, None]
+    )
+    head_of_feature = jnp.arange(local_width, dtype=jnp.int32) // HD
     flat_queries = queries.reshape(rows, local_width)
-    scores = jnp.stack(
-        [
-            lax.dot_general(
-                flat_queries[:, h * HD : (h + 1) * HD],
-                keys[:, h * HD : (h + 1) * HD],
-                (((1,), (1,)), ((), ())),
-                preferred_element_type=jnp.float32,
-            )
-            for h in range(local_heads)
-        ]
-    ) * score_scale
-    masked = jnp.where(validity[None], scores, very_low)
-    maxima = jnp.max(masked, axis=2)
-    weights = jnp.where(validity[None], jnp.exp(masked - maxima[..., None]), 0.0)
-    totals = jnp.sum(weights, axis=2)
-    rounded = weights.astype(jnp.bfloat16)
-    running = jnp.stack(
-        [
-            jnp.dot(rounded[h], values[:, h * HD : (h + 1) * HD], preferred_element_type=jnp.float32)
-            for h in range(local_heads)
-        ]
-    )
+    block_queries = jnp.where(
+        head_of_feature[None, None, :] == jnp.arange(local_heads, dtype=jnp.int32)[:, None, None],
+        flat_queries[None],
+        jnp.zeros((), jnp.bfloat16),
+    ).reshape(local_heads * rows, local_width)
+    scores = lax.dot_general(
+        block_queries, keys, (((1,), (1,)), ((), ())), preferred_element_type=jnp.float32
+    ).reshape(local_heads, STEPS, R, tokens) * score_scale
+    valid = validity[None, None]
+    masked = jnp.where(valid, scores, very_low)
+    maxima = jnp.max(masked, axis=3)
+    weights = jnp.where(valid, jnp.exp(masked - maxima[..., None]), 0.0)
+    totals = jnp.sum(weights, axis=3).reshape(local_heads, rows)
+    maxima = maxima.reshape(local_heads, rows)
+    all_heads = lax.dot_general(
+        values,
+        weights.astype(jnp.bfloat16).reshape(local_heads * rows, tokens),
+        (((0,), (1,)), ((), ())),
+        preferred_element_type=jnp.float32,
+    ).reshape(local_heads, HD, local_heads, rows)
+    running = jnp.stack([all_heads[h, :, h].T for h in range(local_heads)])
 
     seq = lax.axis_index("seq")
     slice_width = local_width // SEQ_SIZE

time: 219 us -> 215 us (0.982)
  local copies, waits for them, and re-layouts: 20.9 us -> 11.7 us
    unnamed x46 -> x33, local copies, waits for them, and re-layouts: 6.71 us -> 2.42 us
    slice x1, local copies, waits for them, and re-layouts: 3.51 us -> 0.14 us  [local(): running = jnp.stack([all_heads[h, :, h].T for h in range(local_heads)])]
    ppermute x27, starting transfers between devices: 66.6 us -> 69 us  [exchange(): lax.ppermute(value, axis, digit_pairs(count, stride, size, shift))]
    dot_general x8 -> x2, matrix products: 6.29 us -> 6.76 us  [the longest x1 5.52 us: local(): lax.dot_general(block_queries, keys, (((1,), (1,)), ((), ())), preferred_...]
  transfers between devices with their start and end apart: 51 -> 51, of which waited for: 34 -> 34; matrix products, arithmetic and copies ran while one was open for 8% -> 3% of each run, Pallas kernels for 0% -> 0%
where the time goes in v4:
time: 215 us; the launch traced here: 214 us
  starting transfers between devices  120 us (56%)
  waiting for transfers between devices  57.6 us (27%)
  other arithmetic  13.3 us (6%)
  local copies, waits for them, and re-layouts  11.7 us (5%)
  matrix products  10.7 us (5%)
    ppermute x27, starting transfers between devices, exchange(): lax.ppermute(value, axis, digit_pairs(count, stride, size, shift))  69 us
    ppermute x27, waiting for transfers between devices, exchange(): lax.ppermute(value, axis, digit_pairs(count, stride, size, shift))  29.2 us
    ppermute x10, starting transfers between devices, scatter_digit(): lax.ppermute(send, 'seq', digit_pairs(SEQ_SIZE, stride, size, shift))  23.8 us
    ppermute x10, waiting for transfers between devices, scatter_digit(): lax.ppermute(send, 'seq', digit_pairs(SEQ_SIZE, stride, size, shift))  14.3 us
    ppermute x4, starting transfers between devices, local(): received = lax.ppermute(attended, ('seq', 'mp'), pairs)  13.6 us
    all_to_all x1, waiting for transfers between devices, local(): sources = lax.all_to_all(send, 'seq', 0, 0, tiled=True)  7.05 us
    all_to_all x1, starting transfers between devices, local(): sources = lax.all_to_all(send, 'seq', 0, 0, tiled=True)  6.75 us
    ppermute x6, waiting for transfers between devices, gather_digit(): lax.ppermute(current, 'seq', digit_pairs(SEQ_SIZE, stride, size, shift))  5.9 us
  transfers between devices with their start and end apart: 51, of which 34 were waited for; matrix products, arithmetic and copies ran while one was open for 3% of the time, Pallas kernels for 0%

profile of v4, /device:TPU:0, one launch (start us, length us, event | category | flops | bytes accessed | tf_op | source)
XLA Modules:
  0.0 214.4 jit_solution(13240435894023900272)
XLA Ops:
  8.2 1.2 collective-permute-done.1
  9.6 1.7 collective-permute-start.2
  11.3 2.7 %collective-permute-start.3 = (f32[64,768]{1,0:T(8,128)S(1)}, f32[64,768]{1,0:T(8,128)S(1)}, u32[]{:S(2)}, u32[]{:S(2)}) collective-permute-start(f32[64,768]{1,0:T(8,128)S(1)} %get-tuple-element.14), channel_id=1, source_target_pairs={{0,16},{4,20},{8,24},{12,28},{16,0},{20,4},{24,8},{28,12},{32,48},... | collective-permute-start | bytes 589832 | tf_op jit(solution)/shard_map/ppermute | solution.py:71
  14.0 1.4 collective-permute-start.4
  15.4 2.4 %collective-permute-done.2 = f32[64,768]{1,0:T(8,128)S(1)} collective-permute-done((f32[64,768]{1,0:T(8,128)S(1)}, f32[64,768]{1,0:T(8,128)S(1)}, u32[]{:S(2)}, u32[]{:S(2)}) %collective-permute-start.2) | collective-permute-done | bytes 196640 | tf_op jit(solution)/shard_map/ppermute | solution.py:71
  17.8 5.3 %collective-permute-done.3 = f32[64,768]{1,0:T(8,128)S(1)} collective-permute-done((f32[64,768]{1,0:T(8,128)S(1)}, f32[64,768]{1,0:T(8,128)S(1)}, u32[]{:S(2)}, u32[]{:S(2)}) %collective-permute-start.3) | collective-permute-done | bytes 196640 | tf_op jit(solution)/shard_map/ppermute | solution.py:71
  23.2 4.7 %collective-permute-start.5 = (f32[64,768]{1,0:T(8,128)S(1)}, f32[64,768]{1,0:T(8,128)S(1)}, u32[]{:S(2)}, u32[]{:S(2)}) collective-permute-start(f32[64,768]{1,0:T(8,128)S(1)} %reduce_sum.153), channel_id=1, source_target_pairs={{0,32},{4,36},{8,40},{12,44},{16,48},{20,52},{24,56},{28,60},{32,6... | collective-permute-start | bytes 589832 | tf_op jit(solution)/shard_map/ppermute | solution.py:71
  27.9 4.8 %collective-permute-start.6 = (f32[64,768]{1,0:T(8,128)S(1)}, f32[64,768]{1,0:T(8,128)S(1)}, u32[]{:S(2)}, u32[]{:S(2)}) collective-permute-start(f32[64,768]{1,0:T(8,128)S(1)} %reduce_sum.153), channel_id=1, source_target_pairs={{0,64},{4,68},{8,72},{12,76},{16,80},{20,84},{24,88},{28,92},{32,9... | collective-permute-start | bytes 589832 | tf_op jit(solution)/shard_map/ppermute | solution.py:71
  32.7 1.9 collective-permute-start.7
  34.7 1.4 collective-permute-done.5
  36.1 4.9 %collective-permute-done.6 = f32[64,768]{1,0:T(8,128)S(1)} collective-permute-done((f32[64,768]{1,0:T(8,128)S(1)}, f32[64,768]{1,0:T(8,128)S(1)}, u32[]{:S(2)}, u32[]{:S(2)}) %collective-permute-start.6) | collective-permute-done | bytes 196640 | tf_op jit(solution)/shard_map/ppermute | solution.py:71
  41.3 1.4 collective-permute-done.8
  42.8 2.5 %collective-permute-start.9 = (f32[64,2]{0,1:T(2,128)S(1)}, f32[64,2]{0,1:T(2,128)S(1)}, u32[]{:S(2)}, u32[]{:S(2)}) collective-permute-start(f32[64,2]{0,1:T(2,128)S(1)} %pad_maximum_fusion.3), channel_id=1, source_target_pairs={{0,1},{1,2},{2,3},{3,0},{4,5},{5,6},{6,7},{7,4},{8,9},{9,10},{10,1... | collective-permute-start | bytes 1544 | tf_op jit(solution)/shard_map/ppermute | solution.py:71
  45.3 2.5 %collective-permute-start.10 = (f32[64,2]{0,1:T(2,128)S(1)}, f32[64,2]{0,1:T(2,128)S(1)}, u32[]{:S(2)}, u32[]{:S(2)}) collective-permute-start(f32[64,2]{0,1:T(2,128)S(1)} %pad_maximum_fusion.3), channel_id=1, source_target_pairs={{0,2},{1,3},{2,0},{3,1},{4,6},{5,7},{6,4},{7,5},{8,10},{9,11},{10,... | collective-permute-start | bytes 1544 | tf_op jit(solution)/shard_map/ppermute | solution.py:71
  47.7 1.5 collective-permute-start.11
  51.8 5.5 %fusion.25 = (f32[4,4,16]{2,1,0:T(4,128)S(1)}, f32[4,4,16,4096]{3,2,1,0:T(8,128)}) fusion(bf16[4096,512,1,1]{1,0,3,2:T(8,128)(2,1)} %bitcast.201, pred[4,512]{1,0:T(4,128)(4,1)S(1)} %iota_compare_fusion.1, bf16[4,16,512]{2,1,0:T(8,128)(2,1)S(1)} %convert_element_type.52, pred[16,4096]{1,0:T(8,128)(4,1)S(1)} %fusion.5), kind=kOutput, calls=%fused_computation.134 | convolution fusion | flops 1077018368 | bytes 8522752 | tf_op jit(solution)/shard_map/dot_general | solution.py:228
  57.5 3.4 %fusion.2 = (bf16[4,4,16,4096]{3,2,1,0:T(8,128)(2,1)S(1)}, f32[4,4,16]{2,1,0:T(4,128)S(1)}) fusion(f32[4,4,16,4096]{3,2,1,0:T(8,128)} %get-tuple-element.42, f32[4,4,16]{2,1,0:T(4,128)S(1)} %get-tuple-element.41, pred[16,4096]{1,0:T(8,128)(4,1)S(1)} %fusion.5), kind=kLoop, calls=%fused_computation.4 | loop fusion | flops 4194048 | bytes 6359040 | tf_op jit(solution)/shard_map/convert_element_type | solution.py:239
  60.9 1.2 convolution_bitcast_fusion
  64.0 6.7 %all-to-all-start = ((f32[32,1,1152]{2,1,0:T(1,128)}), f32[32,1,1152]{2,1,0:T(1,128)S(1)}, u32[]{:S(2)}, u32[]{:S(2)}) async-start(f32[32,1,1152]{2,1,0:T(1,128)} %reshape.343), calls=%async_computation | async-start | bytes 294912 | tf_op jit(solution)/shard_map/all_to_all | solution.py:256
  71.6 7.0 %all-to-all-done = f32[32,1,1152]{2,1,0:T(1,128)S(1)} async-done(((f32[32,1,1152]{2,1,0:T(1,128)}), f32[32,1,1152]{2,1,0:T(1,128)S(1)}, u32[]{:S(2)}, u32[]{:S(2)}) %all-to-all-start) | async-done | bytes 147488 | tf_op jit(solution)/shard_map/all_to_all | solution.py:256
  82.5 5.2 %collective-permute-start.13 = (bf16[64,16]{0,1:T(8,128)(2,1)S(1)}, bf16[64,16]{0,1:T(8,128)(2,1)S(1)}, u32[]{:S(2)}, u32[]{:S(2)}) collective-permute-start(bf16[64,16]{0,1:T(8,128)(2,1)S(1)} %copy.106), channel_id=1, source_target_pairs={{0,1},{1,33},{2,65},{3,97},{4,2},{5,34},{6,66},{7,98},{8,3},{9,35}... | collective-permute-start | bytes 6152 | tf_op jit(solution)/shard_map/ppermute | solution.py:294
  87.7 4.1 %collective-permute-start.14 = (bf16[64,16]{0,1:T(8,128)(2,1)S(1)}, bf16[64,16]{0,1:T(8,128)(2,1)S(1)}, u32[]{:S(2)}, u32[]{:S(2)}) collective-permute-start(bf16[64,16]{0,1:T(8,128)(2,1)S(1)} %copy.106), channel_id=1, source_target_pairs={{0,2},{1,34},{2,66},{3,98},{4,3},{5,35},{6,67},{7,99},{8,0},{9,32}... | collective-permute-start | bytes 6152 | tf_op jit(solution)/shard_map/ppermute | solution.py:294
  91.8 3.6 %collective-permute-start.15 = (bf16[64,16]{0,1:T(8,128)(2,1)S(1)}, bf16[64,16]{0,1:T(8,128)(2,1)S(1)}, u32[]{:S(2)}, u32[]{:S(2)}) collective-permute-start(bf16[64,16]{0,1:T(8,128)(2,1)S(1)} %copy.106), channel_id=1, source_target_pairs={{0,3},{1,35},{2,67},{3,99},{4,0},{5,32},{6,64},{7,96},{8,1},{9,33}... | collective-permute-start | bytes 6152 | tf_op jit(solution)/shard_map/ppermute | solution.py:294
  95.5 1.2 collective-permute-done.15
  96.9 2.8 %collective-permute-start.16 = (f32[64,256]{1,0:T(8,128)S(1)}, f32[64,256]{1,0:T(8,128)S(1)}, u32[]{:S(2)}, u32[]{:S(2)}) collective-permute-start(f32[64,256]{1,0:T(8,128)S(1)} %constant_dynamic-slice_fusion.9), channel_id=1, source_target_pairs={{0,4},{4,0},{8,12},{12,8},{16,20},{20,16},{24,28},{28,24},{32,36},... | collective-permute-start | bytes 196616 | tf_op jit(solution)/shard_map/ppermute | solution.py:83
  100.8 3.9 %collective-permute-start.18 = (f32[64,256]{1,0:T(8,128)S(1)}, f32[64,256]{1,0:T(8,128)S(1)}, u32[]{:S(2)}, u32[]{:S(2)}) collective-permute-start(f32[64,256]{1,0:T(8,128)S(1)} %get-tuple-element.10), channel_id=1, source_target_pairs={{0,16},{4,20},{8,24},{12,28},{16,0},{20,4},{24,8},{28,12},{32,48},... | collective-permute-start | bytes 196616 | tf_op jit(solution)/shard_map/ppermute | solution.py:71
  104.7 2.5 %collective-permute-start.19 = (f32[64,256]{1,0:T(8,128)S(1)}, f32[64,256]{1,0:T(8,128)S(1)}, u32[]{:S(2)}, u32[]{:S(2)}) collective-permute-start(f32[64,256]{1,0:T(8,128)S(1)} %get-tuple-element.10), channel_id=1, source_target_pairs={{0,24},{4,28},{8,0},{12,4},{16,8},{20,12},{24,16},{28,20},{32,56},... | collective-permute-start | bytes 196616 | tf_op jit(solution)/shard_map/ppermute | solution.py:71
  107.2 1.2 collective-permute-done.18
  109.2 2.4 %collective-permute-start.20 = (f32[64,256]{1,0:T(8,128)S(1)}, f32[64,256]{1,0:T(8,128)S(1)}, u32[]{:S(2)}, u32[]{:S(2)}) collective-permute-start(f32[64,256]{1,0:T(8,128)S(1)} %reduce_sum.162), channel_id=1, source_target_pairs={{0,32},{4,36},{8,40},{12,44},{16,48},{20,52},{24,56},{28,60},{32,6... | collective-permute-start | bytes 196616 | tf_op jit(solution)/shard_map/ppermute | solution.py:71
  111.6 5.3 %collective-permute-start.21 = (f32[64,256]{1,0:T(8,128)S(1)}, f32[64,256]{1,0:T(8,128)S(1)}, u32[]{:S(2)}, u32[]{:S(2)}) collective-permute-start(f32[64,256]{1,0:T(8,128)S(1)} %reduce_sum.162), channel_id=1, source_target_pairs={{0,64},{4,68},{8,72},{12,76},{16,80},{20,84},{24,88},{28,92},{32,9... | collective-permute-start | bytes 196616 | tf_op jit(solution)/shard_map/ppermute | solution.py:71
  116.9 2.5 %collective-permute-start.22 = (f32[64,256]{1,0:T(8,128)S(1)}, f32[64,256]{1,0:T(8,128)S(1)}, u32[]{:S(2)}, u32[]{:S(2)}) collective-permute-start(f32[64,256]{1,0:T(8,128)S(1)} %reduce_sum.162), channel_id=1, source_target_pairs={{0,96},{4,100},{8,104},{12,108},{16,112},{20,116},{24,120},{28,124... | collective-permute-start | bytes 196616 | tf_op jit(solution)/shard_map/ppermute | solution.py:71
  119.8 1.6 collective-permute-done.22
  121.5 1.2 collective-permute-done.23
  122.8 1.1 collective-permute-start.24
  124.0 3.8 %collective-permute-start.25 = (f32[64]{0:T(128)S(1)}, f32[64]{0:T(128)S(1)}, u32[]{:S(2)}, u32[]{:S(2)}) collective-permute-start(f32[64]{0:T(128)S(1)} %multiply_reduce_fusion.1), channel_id=1, source_target_pairs={{0,2},{1,3},{2,0},{3,1},{4,6},{5,7},{6,4},{7,5},{8,10},{9,11},{10,... | collective-permute-start | bytes 776 | tf_op jit(solution)/shard_map/ppermute | solution.py:71
  127.8 2.5 %collective-permute-start.26 = (f32[64]{0:T(128)S(1)}, f32[64]{0:T(128)S(1)}, u32[]{:S(2)}, u32[]{:S(2)}) collective-permute-start(f32[64]{0:T(128)S(1)} %multiply_reduce_fusion.1), channel_id=1, source_target_pairs={{0,3},{1,0},{2,1},{3,2},{4,7},{5,4},{6,5},{7,6},{8,11},{9,8},{10,9... | collective-permute-start | bytes 776 | tf_op jit(solution)/shard_map/ppermute | solution.py:71
  130.4 1.2 collective-permute-done.26
  133.4 1.4 stack_reshape.7
  134.8 3.6 %pad_maximum_fusion = f32[64,32,2,64]{3,2,1,0:T(2,128)S(1)} fusion(f32[64,32,1,64]{3,2,1,0:T(1,128)} %bitcast.168, f32[64,32,1,64]{3,2,1,0:T(1,128)S(1)} %bitcast.167), kind=kLoop, calls=%fused_computation.5 | loop fusion | flops 262144 | bytes 2097152 | tf_op jit(solution)/shard_map/stack | solution.py:122
  138.5 2.0 reshape.340
  140.6 1.8 collective-permute-done.28
  142.7 3.0 %collective-permute-start.30 = (f32[64,512]{1,0:T(8,128)S(1)}, f32[64,512]{1,0:T(8,128)S(1)}, u32[]{:S(2)}, u32[]{:S(2)}) collective-permute-start(f32[64,512]{1,0:T(8,128)S(1)} %get-tuple-element.19), channel_id=1, source_target_pairs={{0,16},{4,20},{8,24},{12,28},{16,0},{20,4},{24,8},{28,12},{32,48},... | collective-permute-start | bytes 393224 | tf_op jit(solution)/shard_map/ppermute | solution.py:83
  145.6 1.2 collective-permute-start.31
  146.8 5.4 %collective-permute-done.29 = f32[64,512]{1,0:T(8,128)S(1)} collective-permute-done((f32[64,512]{1,0:T(8,128)S(1)}, f32[64,512]{1,0:T(8,128)S(1)}, u32[]{:S(2)}, u32[]{:S(2)}) %collective-permute-start.29) | collective-permute-done | bytes 131104 | tf_op jit(solution)/shard_map/ppermute | solution.py:83
  152.9 7.2 %collective-permute-start.32 = (f32[64,128]{1,0:T(8,128)S(1)}, f32[64,128]{1,0:T(8,128)S(1)}, u32[]{:S(2)}, u32[]{:S(2)}) collective-permute-start(f32[64,128]{1,0:T(8,128)S(1)} %get-tuple-element.32), channel_id=1, source_target_pairs={{0,32},{4,36},{8,40},{12,44},{16,48},{20,52},{24,56},{28,60},{32,6... | collective-permute-start | bytes 98312 | tf_op jit(solution)/shard_map/ppermute | solution.py:83
  160.1 4.9 %collective-permute-start.33 = (f32[64,128]{1,0:T(8,128)S(1)}, f32[64,128]{1,0:T(8,128)S(1)}, u32[]{:S(2)}, u32[]{:S(2)}) collective-permute-start(f32[64,128]{1,0:T(8,128)S(1)} %get-tuple-element.34), channel_id=1, source_target_pairs={{0,64},{4,68},{8,72},{12,76},{16,80},{20,84},{24,88},{28,92},{32,9... | collective-permute-start | bytes 98312 | tf_op jit(solution)/shard_map/ppermute | solution.py:83
  165.6 1.6 collective-permute-done.33
  167.3 1.7 collective-permute-done.34
  169.1 3.1 %collective-permute-start.36 = (bf16[64,64]{1,0:T(8,128)(2,1)S(1)}, bf16[64,64]{1,0:T(8,128)(2,1)S(1)}, u32[]{:S(2)}, u32[]{:S(2)}) collective-permute-start(bf16[64,64]{1,0:T(8,128)(2,1)S(1)} %fusion.10), channel_id=1, source_target_pairs={{0,64},{4,68},{8,72},{12,76},{16,80},{20,84},{24,88},{28,92},{32,9... | collective-permute-start | bytes 24584 | tf_op jit(solution)/shard_map/ppermute | solution.py:94
  174.5 1.4 collective-permute-done.37
  177.2 4.0 %collective-permute-start.39 = (f32[64,256]{1,0:T(8,128)S(1)}, f32[64,256]{1,0:T(8,128)S(1)}, u32[]{:S(2)}, u32[]{:S(2)}) collective-permute-start(f32[64,256]{1,0:T(8,128)S(1)} %constant_dynamic-slice_fusion), channel_id=1, source_target_pairs={{0,4},{4,0},{8,12},{12,8},{16,20},{20,16},{24,28},{28,24},{32,36},... | collective-permute-start | bytes 196616 | tf_op jit(solution)/shard_map/ppermute | solution.py:83
  182.1 2.6 %collective-permute-start.40 = (f32[64,256]{1,0:T(8,128)S(1)}, f32[64,256]{1,0:T(8,128)S(1)}, u32[]{:S(2)}, u32[]{:S(2)}) collective-permute-start(f32[64,256]{1,0:T(8,128)S(1)} %get-tuple-element.8), channel_id=1, source_target_pairs={{0,8},{4,12},{8,16},{12,20},{16,24},{20,28},{24,0},{28,4},{32,40},... | collective-permute-start | bytes 196616 | tf_op jit(solution)/shard_map/ppermute | solution.py:71
  184.7 2.6 %collective-permute-start.41 = (f32[64,256]{1,0:T(8,128)S(1)}, f32[64,256]{1,0:T(8,128)S(1)}, u32[]{:S(2)}, u32[]{:S(2)}) collective-permute-start(f32[64,256]{1,0:T(8,128)S(1)} %get-tuple-element.8), channel_id=1, source_target_pairs={{0,16},{4,20},{8,24},{12,28},{16,0},{20,4},{24,8},{28,12},{32,48},... | collective-permute-start | bytes 196616 | tf_op jit(solution)/shard_map/ppermute | solution.py:71
  187.3 1.5 collective-permute-start.42
  188.9 2.1 collective-permute-done.41
  191.6 2.6 %collective-permute-start.43 = (f32[64,256]{1,0:T(8,128)S(1)}, f32[64,256]{1,0:T(8,128)S(1)}, u32[]{:S(2)}, u32[]{:S(2)}) collective-permute-start(f32[64,256]{1,0:T(8,128)S(1)} %reduce_sum.166), channel_id=1, source_target_pairs={{0,32},{4,36},{8,40},{12,44},{16,48},{20,52},{24,56},{28,60},{32,6... | collective-permute-start | bytes 196616 | tf_op jit(solution)/shard_map/ppermute | solution.py:71
  194.2 5.2 %collective-permute-start.44 = (f32[64,256]{1,0:T(8,128)S(1)}, f32[64,256]{1,0:T(8,128)S(1)}, u32[]{:S(2)}, u32[]{:S(2)}) collective-permute-start(f32[64,256]{1,0:T(8,128)S(1)} %reduce_sum.166), channel_id=1, source_target_pairs={{0,64},{4,68},{8,72},{12,76},{16,80},{20,84},{24,88},{28,92},{32,9... | collective-permute-start | bytes 196616 | tf_op jit(solution)/shard_map/ppermute | solution.py:71
  199.4 1.4 collective-permute-start.45
  200.9 1.4 collective-permute-done.44
  202.3 1.3 collective-permute-done.45
  203.8 1.2 collective-permute-done.46
  205.1 2.4 %collective-permute-start.47 = (f32[64]{0:T(128)S(1)}, f32[64]{0:T(128)S(1)}, u32[]{:S(2)}, u32[]{:S(2)}) collective-permute-start(f32[64]{0:T(128)S(1)} %multiply_reduce_fusion), channel_id=1, source_target_pairs={{0,1},{1,2},{2,3},{3,0},{4,5},{5,6},{6,7},{7,4},{8,9},{9,10},{10,1... | collective-permute-start | bytes 776 | tf_op jit(solution)/shard_map/ppermute | solution.py:71
  207.5 2.5 %collective-permute-start.48 = (f32[64]{0:T(128)S(1)}, f32[64]{0:T(128)S(1)}, u32[]{:S(2)}, u32[]{:S(2)}) collective-permute-start(f32[64]{0:T(128)S(1)} %multiply_reduce_fusion), channel_id=1, source_target_pairs={{0,2},{1,3},{2,0},{3,1},{4,6},{5,7},{6,4},{7,5},{8,10},{9,11},{10,... | collective-permute-start | bytes 776 | tf_op jit(solution)/shard_map/ppermute | solution.py:71
  210.4 2.2 %collective-permute-done.48 = f32[64]{0:T(128)S(1)} collective-permute-done((f32[64]{0:T(128)S(1)}, f32[64]{0:T(128)S(1)}, u32[]{:S(2)}, u32[]{:S(2)}) %collective-permute-start.48) | collective-permute-done | bytes 288 | tf_op jit(solution)/shard_map/ppermute | solution.py:71
  (236 shorter events, 31.0 us)
Async XLA Ops:
  0.0 132.5 %copy-start = (bf16[64,2048]{1,0:T(8,128)(2,1)S(1)}, bf16[64,2048]{1,0:T(8,128)(2,1)}, u32[]{:S(2)}) copy-start(bf16[64,2048]{1,0:T(8,128)(2,1)} %param.22) | copy-start | bytes 786436
  0.8 4.1 %collective-permute-start = (bf16[64,64]{1,0:T(8,128)(2,1)S(1)}, bf16[64,64]{1,0:T(8,128)(2,1)S(1)}, u32[]{:S(2)}, u32[]{:S(2)}) collective-permute-start(bf16[64,64]{1,0:T(8,128)(2,1)S(1)} %constant_dynamic-slice_fusion.13), channel_id=1, source_target_pairs={{0,0},{1,32},{2,64},{3,96},{4,4},{5,36},{6,68},{7,100},{8,8},{9,40... | collective-permute-start | bytes 24584 | tf_op jit(solution)/shard_map/ppermute | solution.py:47
  7.9 1.5 collective-permute-start.1
  9.5 41.8 %copy-start.5 = (f32[512]{0:T(512)S(1)}, f32[512]{0:T(512)}, u32[]{:S(2)}) copy-start(f32[512]{0:T(512)} %param.26) | copy-start | bytes 6148
  9.5 41.8 %copy-start.6 = (f32[512]{0:T(512)S(1)}, f32[512]{0:T(512)}, u32[]{:S(2)}) copy-start(f32[512]{0:T(512)} %param.25) | copy-start | bytes 6148
  9.6 8.2 %collective-permute-start.2 = (f32[64,768]{1,0:T(8,128)S(1)}, f32[64,768]{1,0:T(8,128)S(1)}, u32[]{:S(2)}, u32[]{:S(2)}) collective-permute-start(f32[64,768]{1,0:T(8,128)S(1)} %get-tuple-element.14), channel_id=1, source_target_pairs={{0,8},{4,12},{8,16},{12,20},{16,24},{20,28},{24,0},{28,4},{32,40},... | collective-permute-start | bytes 589832 | tf_op jit(solution)/shard_map/ppermute | solution.py:71
  11.3 11.9 %collective-permute-start.3 = (f32[64,768]{1,0:T(8,128)S(1)}, f32[64,768]{1,0:T(8,128)S(1)}, u32[]{:S(2)}, u32[]{:S(2)}) collective-permute-start(f32[64,768]{1,0:T(8,128)S(1)} %get-tuple-element.14), channel_id=1, source_target_pairs={{0,16},{4,20},{8,24},{12,28},{16,0},{20,4},{24,8},{28,12},{32,48},... | collective-permute-start | bytes 589832 | tf_op jit(solution)/shard_map/ppermute | solution.py:71
  14.0 9.1 %collective-permute-start.4 = (f32[64,768]{1,0:T(8,128)S(1)}, f32[64,768]{1,0:T(8,128)S(1)}, u32[]{:S(2)}, u32[]{:S(2)}) collective-permute-start(f32[64,768]{1,0:T(8,128)S(1)} %get-tuple-element.14), channel_id=1, source_target_pairs={{0,24},{4,28},{8,0},{12,4},{16,8},{20,12},{24,16},{28,20},{32,56},... | collective-permute-start | bytes 589832 | tf_op jit(solution)/shard_map/ppermute | solution.py:71
  23.2 12.9 %collective-permute-start.5 = (f32[64,768]{1,0:T(8,128)S(1)}, f32[64,768]{1,0:T(8,128)S(1)}, u32[]{:S(2)}, u32[]{:S(2)}) collective-permute-start(f32[64,768]{1,0:T(8,128)S(1)} %reduce_sum.153), channel_id=1, source_target_pairs={{0,32},{4,36},{8,40},{12,44},{16,48},{20,52},{24,56},{28,60},{32,6... | collective-permute-start | bytes 589832 | tf_op jit(solution)/shard_map/ppermute | solution.py:71
  27.9 13.1 %collective-permute-start.6 = (f32[64,768]{1,0:T(8,128)S(1)}, f32[64,768]{1,0:T(8,128)S(1)}, u32[]{:S(2)}, u32[]{:S(2)}) collective-permute-start(f32[64,768]{1,0:T(8,128)S(1)} %reduce_sum.153), channel_id=1, source_target_pairs={{0,64},{4,68},{8,72},{12,76},{16,80},{20,84},{24,88},{28,92},{32,9... | collective-permute-start | bytes 589832 | tf_op jit(solution)/shard_map/ppermute | solution.py:71
  32.7 8.3 %collective-permute-start.7 = (f32[64,768]{1,0:T(8,128)S(1)}, f32[64,768]{1,0:T(8,128)S(1)}, u32[]{:S(2)}, u32[]{:S(2)}) collective-permute-start(f32[64,768]{1,0:T(8,128)S(1)} %reduce_sum.153), channel_id=1, source_target_pairs={{0,96},{4,100},{8,104},{12,108},{16,112},{20,116},{24,120},{28,124... | collective-permute-start | bytes 589832 | tf_op jit(solution)/shard_map/ppermute | solution.py:71
  41.1 1.5 collective-permute-start.8
  42.8 6.8 %collective-permute-start.9 = (f32[64,2]{0,1:T(2,128)S(1)}, f32[64,2]{0,1:T(2,128)S(1)}, u32[]{:S(2)}, u32[]{:S(2)}) collective-permute-start(f32[64,2]{0,1:T(2,128)S(1)} %pad_maximum_fusion.3), channel_id=1, source_target_pairs={{0,1},{1,2},{2,3},{3,0},{4,5},{5,6},{6,7},{7,4},{8,9},{9,10},{10,1... | collective-permute-start | bytes 1544 | tf_op jit(solution)/shard_map/ppermute | solution.py:71
  45.3 5.1 %collective-permute-start.10 = (f32[64,2]{0,1:T(2,128)S(1)}, f32[64,2]{0,1:T(2,128)S(1)}, u32[]{:S(2)}, u32[]{:S(2)}) collective-permute-start(f32[64,2]{0,1:T(2,128)S(1)} %pad_maximum_fusion.3), channel_id=1, source_target_pairs={{0,2},{1,3},{2,0},{3,1},{4,6},{5,7},{6,4},{7,5},{8,10},{9,11},{10,... | collective-permute-start | bytes 1544 | tf_op jit(solution)/shard_map/ppermute | solution.py:71
  47.7 3.6 %collective-permute-start.11 = (f32[64,2]{0,1:T(2,128)S(1)}, f32[64,2]{0,1:T(2,128)S(1)}, u32[]{:S(2)}, u32[]{:S(2)}) collective-permute-start(f32[64,2]{0,1:T(2,128)S(1)} %pad_maximum_fusion.3), channel_id=1, source_target_pairs={{0,3},{1,0},{2,1},{3,2},{4,7},{5,4},{6,5},{7,6},{8,11},{9,8},{10,9... | collective-permute-start | bytes 1544 | tf_op jit(solution)/shard_map/ppermute | solution.py:71
  57.5 3.5 %copy-start.9 = (bf16[16,256,512]{2,1,0:T(8,128)(2,1)S(1)}, bf16[16,256,512]{2,1,0:T(8,128)(2,1)}, u32[]{:S(2)}) copy-start(bf16[16,256,512]{2,1,0:T(8,128)(2,1)} %param.30) | copy-start | bytes 12582916
  62.2 34.6 %copy-start.4 = (bf16[64,512]{1,0:T(8,128)(2,1)S(1)}, bf16[64,512]{1,0:T(8,128)(2,1)}, u32[]{:S(2)}) copy-start(bf16[64,512]{1,0:T(8,128)(2,1)} %param.21) | copy-start | bytes 196612
  63.0 68.7 %copy-start.3 = (bf16[4,16,512]{2,1,0:T(8,128)(2,1)S(1)}, bf16[4,16,512]{2,1,0:T(8,128)(2,1)}, u32[]{:S(2)}) copy-start(bf16[4,16,512]{2,1,0:T(8,128)(2,1)} %param.17) | copy-start | bytes 196612
  63.0 68.7 %copy-start.7 = (f32[512]{0:T(512)S(1)}, f32[512]{0:T(512)}, u32[]{:S(2)}) copy-start(f32[512]{0:T(512)} %param.27) | copy-start | bytes 6148
  64.0 14.7 %all-to-all-start = ((f32[32,1,1152]{2,1,0:T(1,128)}), f32[32,1,1152]{2,1,0:T(1,128)S(1)}, u32[]{:S(2)}, u32[]{:S(2)}) async-start(f32[32,1,1152]{2,1,0:T(1,128)} %reshape.343), calls=%async_computation | async-start | bytes 294912 | tf_op jit(solution)/shard_map/all_to_all | solution.py:256
  71.0 62.2 %copy-start.1 = (bf16[64,2048]{1,0:T(8,128)(2,1)S(1)}, bf16[64,2048]{1,0:T(8,128)(2,1)}, u32[]{:S(2)}) copy-start(bf16[64,2048]{1,0:T(8,128)(2,1)} %param.23) | copy-start | bytes 786436
  81.7 13.7 %collective-permute-start.12 = (bf16[64,16]{0,1:T(8,128)(2,1)S(1)}, bf16[64,16]{0,1:T(8,128)(2,1)S(1)}, u32[]{:S(2)}, u32[]{:S(2)}) collective-permute-start(bf16[64,16]{0,1:T(8,128)(2,1)S(1)} %copy.106), channel_id=1, source_target_pairs={{0,0},{1,32},{2,64},{3,96},{4,1},{5,33},{6,65},{7,97},{8,2},{9,34}... | collective-permute-start | bytes 6152 | tf_op jit(solution)/shard_map/ppermute | solution.py:294
  82.5 13.0 %collective-permute-start.13 = (bf16[64,16]{0,1:T(8,128)(2,1)S(1)}, bf16[64,16]{0,1:T(8,128)(2,1)S(1)}, u32[]{:S(2)}, u32[]{:S(2)}) collective-permute-start(bf16[64,16]{0,1:T(8,128)(2,1)S(1)} %copy.106), channel_id=1, source_target_pairs={{0,1},{1,33},{2,65},{3,97},{4,2},{5,34},{6,66},{7,98},{8,3},{9,35}... | collective-permute-start | bytes 6152 | tf_op jit(solution)/shard_map/ppermute | solution.py:294
  87.7 7.8 %collective-permute-start.14 = (bf16[64,16]{0,1:T(8,128)(2,1)S(1)}, bf16[64,16]{0,1:T(8,128)(2,1)S(1)}, u32[]{:S(2)}, u32[]{:S(2)}) collective-permute-start(bf16[64,16]{0,1:T(8,128)(2,1)S(1)} %copy.106), channel_id=1, source_target_pairs={{0,2},{1,34},{2,66},{3,98},{4,3},{5,35},{6,67},{7,99},{8,0},{9,32}... | collective-permute-start | bytes 6152 | tf_op jit(solution)/shard_map/ppermute | solution.py:294
  91.8 4.9 %collective-permute-start.15 = (bf16[64,16]{0,1:T(8,128)(2,1)S(1)}, bf16[64,16]{0,1:T(8,128)(2,1)S(1)}, u32[]{:S(2)}, u32[]{:S(2)}) collective-permute-start(bf16[64,16]{0,1:T(8,128)(2,1)S(1)} %copy.106), channel_id=1, source_target_pairs={{0,3},{1,35},{2,67},{3,99},{4,0},{5,32},{6,64},{7,96},{8,1},{9,33}... | collective-permute-start | bytes 6152 | tf_op jit(solution)/shard_map/ppermute | solution.py:294
  96.9 3.7 %collective-permute-start.16 = (f32[64,256]{1,0:T(8,128)S(1)}, f32[64,256]{1,0:T(8,128)S(1)}, u32[]{:S(2)}, u32[]{:S(2)}) collective-permute-start(f32[64,256]{1,0:T(8,128)S(1)} %constant_dynamic-slice_fusion.9), channel_id=1, source_target_pairs={{0,4},{4,0},{8,12},{12,8},{16,20},{20,16},{24,28},{28,24},{32,36},... | collective-permute-start | bytes 196616 | tf_op jit(solution)/shard_map/ppermute | solution.py:83
  100.7 6.6 %collective-permute-start.17 = (f32[64,256]{1,0:T(8,128)S(1)}, f32[64,256]{1,0:T(8,128)S(1)}, u32[]{:S(2)}, u32[]{:S(2)}) collective-permute-start(f32[64,256]{1,0:T(8,128)S(1)} %get-tuple-element.10), channel_id=1, source_target_pairs={{0,8},{4,12},{8,16},{12,20},{16,24},{20,28},{24,0},{28,4},{32,40},... | collective-permute-start | bytes 196616 | tf_op jit(solution)/shard_map/ppermute | solution.py:71
  100.8 7.7 %collective-permute-start.18 = (f32[64,256]{1,0:T(8,128)S(1)}, f32[64,256]{1,0:T(8,128)S(1)}, u32[]{:S(2)}, u32[]{:S(2)}) collective-permute-start(f32[64,256]{1,0:T(8,128)S(1)} %get-tuple-element.10), channel_id=1, source_target_pairs={{0,16},{4,20},{8,24},{12,28},{16,0},{20,4},{24,8},{28,12},{32,48},... | collective-permute-start | bytes 196616 | tf_op jit(solution)/shard_map/ppermute | solution.py:71
  104.7 4.4 %collective-permute-start.19 = (f32[64,256]{1,0:T(8,128)S(1)}, f32[64,256]{1,0:T(8,128)S(1)}, u32[]{:S(2)}, u32[]{:S(2)}) collective-permute-start(f32[64,256]{1,0:T(8,128)S(1)} %get-tuple-element.10), channel_id=1, source_target_pairs={{0,24},{4,28},{8,0},{12,4},{16,8},{20,12},{24,16},{28,20},{32,56},... | collective-permute-start | bytes 196616 | tf_op jit(solution)/shard_map/ppermute | solution.py:71
  109.2 10.3 %collective-permute-start.20 = (f32[64,256]{1,0:T(8,128)S(1)}, f32[64,256]{1,0:T(8,128)S(1)}, u32[]{:S(2)}, u32[]{:S(2)}) collective-permute-start(f32[64,256]{1,0:T(8,128)S(1)} %reduce_sum.162), channel_id=1, source_target_pairs={{0,32},{4,36},{8,40},{12,44},{16,48},{20,52},{24,56},{28,60},{32,6... | collective-permute-start | bytes 196616 | tf_op jit(solution)/shard_map/ppermute | solution.py:71
  111.6 8.2 %collective-permute-start.21 = (f32[64,256]{1,0:T(8,128)S(1)}, f32[64,256]{1,0:T(8,128)S(1)}, u32[]{:S(2)}, u32[]{:S(2)}) collective-permute-start(f32[64,256]{1,0:T(8,128)S(1)} %reduce_sum.162), channel_id=1, source_target_pairs={{0,64},{4,68},{8,72},{12,76},{16,80},{20,84},{24,88},{28,92},{32,9... | collective-permute-start | bytes 196616 | tf_op jit(solution)/shard_map/ppermute | solution.py:71
  116.9 4.4 %collective-permute-start.22 = (f32[64,256]{1,0:T(8,128)S(1)}, f32[64,256]{1,0:T(8,128)S(1)}, u32[]{:S(2)}, u32[]{:S(2)}) collective-permute-start(f32[64,256]{1,0:T(8,128)S(1)} %reduce_sum.162), channel_id=1, source_target_pairs={{0,96},{4,100},{8,104},{12,108},{16,112},{20,116},{24,120},{28,124... | collective-permute-start | bytes 196616 | tf_op jit(solution)/shard_map/ppermute | solution.py:71
  121.4 1.3 collective-permute-start.23
  122.8 7.5 %collective-permute-start.24 = (f32[64]{0:T(128)S(1)}, f32[64]{0:T(128)S(1)}, u32[]{:S(2)}, u32[]{:S(2)}) collective-permute-start(f32[64]{0:T(128)S(1)} %multiply_reduce_fusion.1), channel_id=1, source_target_pairs={{0,1},{1,2},{2,3},{3,0},{4,5},{5,6},{6,7},{7,4},{8,9},{9,10},{10,1... | collective-permute-start | bytes 776 | tf_op jit(solution)/shard_map/ppermute | solution.py:71
  124.0 6.4 %collective-permute-start.25 = (f32[64]{0:T(128)S(1)}, f32[64]{0:T(128)S(1)}, u32[]{:S(2)}, u32[]{:S(2)}) collective-permute-start(f32[64]{0:T(128)S(1)} %multiply_reduce_fusion.1), channel_id=1, source_target_pairs={{0,2},{1,3},{2,0},{3,1},{4,6},{5,7},{6,4},{7,5},{8,10},{9,11},{10,... | collective-permute-start | bytes 776 | tf_op jit(solution)/shard_map/ppermute | solution.py:71
  127.8 3.8 %collective-permute-start.26 = (f32[64]{0:T(128)S(1)}, f32[64]{0:T(128)S(1)}, u32[]{:S(2)}, u32[]{:S(2)}) collective-permute-start(f32[64]{0:T(128)S(1)} %multiply_reduce_fusion.1), channel_id=1, source_target_pairs={{0,3},{1,0},{2,1},{3,2},{4,7},{5,4},{6,5},{7,6},{8,11},{9,8},{10,9... | collective-permute-start | bytes 776 | tf_op jit(solution)/shard_map/ppermute | solution.py:71
  131.9 0.7 collective-permute-start.27
  140.4 36.5 %copy-start.2 = (bf16[256,512]{1,0:T(8,128)(2,1)S(1)}, bf16[256,512]{1,0:T(8,128)(2,1)}, u32[]{:S(2)}) copy-start(bf16[256,512]{1,0:T(8,128)(2,1)} %param.24) | copy-start | bytes 786436
  140.4 73.2 %copy-start.8 = (f32[512]{0:T(512)S(1)}, f32[512]{0:T(512)}, u32[]{:S(2)}) copy-start(f32[512]{0:T(512)} %param.28) | copy-start | bytes 6148
  140.5 2.0 collective-permute-start.28
  142.6 9.6 %collective-permute-start.29 = (f32[64,512]{1,0:T(8,128)S(1)}, f32[64,512]{1,0:T(8,128)S(1)}, u32[]{:S(2)}, u32[]{:S(2)}) collective-permute-start(f32[64,512]{1,0:T(8,128)S(1)} %get-tuple-element.17), channel_id=1, source_target_pairs={{0,8},{4,12},{8,16},{12,20},{16,24},{20,28},{24,0},{28,4},{32,40},... | collective-permute-start | bytes 393224 | tf_op jit(solution)/shard_map/ppermute | solution.py:83
  142.7 9.5 %collective-permute-start.30 = (f32[64,512]{1,0:T(8,128)S(1)}, f32[64,512]{1,0:T(8,128)S(1)}, u32[]{:S(2)}, u32[]{:S(2)}) collective-permute-start(f32[64,512]{1,0:T(8,128)S(1)} %get-tuple-element.19), channel_id=1, source_target_pairs={{0,16},{4,20},{8,24},{12,28},{16,0},{20,4},{24,8},{28,12},{32,48},... | collective-permute-start | bytes 393224 | tf_op jit(solution)/shard_map/ppermute | solution.py:83
  145.6 7.1 %collective-permute-start.31 = (f32[64,512]{1,0:T(8,128)S(1)}, f32[64,512]{1,0:T(8,128)S(1)}, u32[]{:S(2)}, u32[]{:S(2)}) collective-permute-start(f32[64,512]{1,0:T(8,128)S(1)} %get-tuple-element.18), channel_id=1, source_target_pairs={{0,24},{4,28},{8,0},{12,4},{16,8},{20,12},{24,16},{28,20},{32,56},... | collective-permute-start | bytes 393224 | tf_op jit(solution)/shard_map/ppermute | solution.py:83
  152.9 12.8 %collective-permute-start.32 = (f32[64,128]{1,0:T(8,128)S(1)}, f32[64,128]{1,0:T(8,128)S(1)}, u32[]{:S(2)}, u32[]{:S(2)}) collective-permute-start(f32[64,128]{1,0:T(8,128)S(1)} %get-tuple-element.32), channel_id=1, source_target_pairs={{0,32},{4,36},{8,40},{12,44},{16,48},{20,52},{24,56},{28,60},{32,6... | collective-permute-start | bytes 98312 | tf_op jit(solution)/shard_map/ppermute | solution.py:83
  160.1 7.2 %collective-permute-start.33 = (f32[64,128]{1,0:T(8,128)S(1)}, f32[64,128]{1,0:T(8,128)S(1)}, u32[]{:S(2)}, u32[]{:S(2)}) collective-permute-start(f32[64,128]{1,0:T(8,128)S(1)} %get-tuple-element.34), channel_id=1, source_target_pairs={{0,64},{4,68},{8,72},{12,76},{16,80},{20,84},{24,88},{28,92},{32,9... | collective-permute-start | bytes 98312 | tf_op jit(solution)/shard_map/ppermute | solution.py:83
  165.0 3.9 %collective-permute-start.34 = (f32[64,128]{1,0:T(8,128)S(1)}, f32[64,128]{1,0:T(8,128)S(1)}, u32[]{:S(2)}, u32[]{:S(2)}) collective-permute-start(f32[64,128]{1,0:T(8,128)S(1)} %get-tuple-element.33), channel_id=1, source_target_pairs={{0,96},{4,100},{8,104},{12,108},{16,112},{20,116},{24,120},{28,124... | collective-permute-start | bytes 98312 | tf_op jit(solution)/shard_map/ppermute | solution.py:83
  169.0 5.0 %collective-permute-start.35 = (bf16[64,64]{1,0:T(8,128)(2,1)S(1)}, bf16[64,64]{1,0:T(8,128)(2,1)S(1)}, u32[]{:S(2)}, u32[]{:S(2)}) collective-permute-start(bf16[64,64]{1,0:T(8,128)(2,1)S(1)} %fusion.10), channel_id=1, source_target_pairs={{0,32},{4,36},{8,40},{12,44},{16,48},{20,52},{24,56},{28,60},{32,6... | collective-permute-start | bytes 24584 | tf_op jit(solution)/shard_map/ppermute | solution.py:94
  169.1 5.3 %collective-permute-start.36 = (bf16[64,64]{1,0:T(8,128)(2,1)S(1)}, bf16[64,64]{1,0:T(8,128)(2,1)S(1)}, u32[]{:S(2)}, u32[]{:S(2)}) collective-permute-start(bf16[64,64]{1,0:T(8,128)(2,1)S(1)} %fusion.10), channel_id=1, source_target_pairs={{0,64},{4,68},{8,72},{12,76},{16,80},{20,84},{24,88},{28,92},{32,9... | collective-permute-start | bytes 24584 | tf_op jit(solution)/shard_map/ppermute | solution.py:94
  172.2 3.7 %collective-permute-start.37 = (bf16[64,64]{1,0:T(8,128)(2,1)S(1)}, bf16[64,64]{1,0:T(8,128)(2,1)S(1)}, u32[]{:S(2)}, u32[]{:S(2)}) collective-permute-start(bf16[64,64]{1,0:T(8,128)(2,1)S(1)} %fusion.10), channel_id=1, source_target_pairs={{0,96},{4,100},{8,104},{12,108},{16,112},{20,116},{24,120},{28,124... | collective-permute-start | bytes 24584 | tf_op jit(solution)/shard_map/ppermute | solution.py:94
  176.3 0.7 collective-permute-start.38
  177.2 4.9 %collective-permute-start.39 = (f32[64,256]{1,0:T(8,128)S(1)}, f32[64,256]{1,0:T(8,128)S(1)}, u32[]{:S(2)}, u32[]{:S(2)}) collective-permute-start(f32[64,256]{1,0:T(8,128)S(1)} %constant_dynamic-slice_fusion), channel_id=1, source_target_pairs={{0,4},{4,0},{8,12},{12,8},{16,20},{20,16},{24,28},{28,24},{32,36},... | collective-permute-start | bytes 196616 | tf_op jit(solution)/shard_map/ppermute | solution.py:83
  182.1 6.8 %collective-permute-start.40 = (f32[64,256]{1,0:T(8,128)S(1)}, f32[64,256]{1,0:T(8,128)S(1)}, u32[]{:S(2)}, u32[]{:S(2)}) collective-permute-start(f32[64,256]{1,0:T(8,128)S(1)} %get-tuple-element.8), channel_id=1, source_target_pairs={{0,8},{4,12},{8,16},{12,20},{16,24},{20,28},{24,0},{28,4},{32,40},... | collective-permute-start | bytes 196616 | tf_op jit(solution)/shard_map/ppermute | solution.py:71
  184.7 6.2 %collective-permute-start.41 = (f32[64,256]{1,0:T(8,128)S(1)}, f32[64,256]{1,0:T(8,128)S(1)}, u32[]{:S(2)}, u32[]{:S(2)}) collective-permute-start(f32[64,256]{1,0:T(8,128)S(1)} %get-tuple-element.8), channel_id=1, source_target_pairs={{0,16},{4,20},{8,24},{12,28},{16,0},{20,4},{24,8},{28,12},{32,48},... | collective-permute-start | bytes 196616 | tf_op jit(solution)/shard_map/ppermute | solution.py:71
  187.3 4.3 %collective-permute-start.42 = (f32[64,256]{1,0:T(8,128)S(1)}, f32[64,256]{1,0:T(8,128)S(1)}, u32[]{:S(2)}, u32[]{:S(2)}) collective-permute-start(f32[64,256]{1,0:T(8,128)S(1)} %get-tuple-element.8), channel_id=1, source_target_pairs={{0,24},{4,28},{8,0},{12,4},{16,8},{20,12},{24,16},{28,20},{32,56},... | collective-permute-start | bytes 196616 | tf_op jit(solution)/shard_map/ppermute | solution.py:71
  191.6 9.2 %collective-permute-start.43 = (f32[64,256]{1,0:T(8,128)S(1)}, f32[64,256]{1,0:T(8,128)S(1)}, u32[]{:S(2)}, u32[]{:S(2)}) collective-permute-start(f32[64,256]{1,0:T(8,128)S(1)} %reduce_sum.166), channel_id=1, source_target_pairs={{0,32},{4,36},{8,40},{12,44},{16,48},{20,52},{24,56},{28,60},{32,6... | collective-permute-start | bytes 196616 | tf_op jit(solution)/shard_map/ppermute | solution.py:71
  194.2 8.1 %collective-permute-start.44 = (f32[64,256]{1,0:T(8,128)S(1)}, f32[64,256]{1,0:T(8,128)S(1)}, u32[]{:S(2)}, u32[]{:S(2)}) collective-permute-start(f32[64,256]{1,0:T(8,128)S(1)} %reduce_sum.166), channel_id=1, source_target_pairs={{0,64},{4,68},{8,72},{12,76},{16,80},{20,84},{24,88},{28,92},{32,9... | collective-permute-start | bytes 196616 | tf_op jit(solution)/shard_map/ppermute | solution.py:71
  199.4 4.3 %collective-permute-start.45 = (f32[64,256]{1,0:T(8,128)S(1)}, f32[64,256]{1,0:T(8,128)S(1)}, u32[]{:S(2)}, u32[]{:S(2)}) collective-permute-start(f32[64,256]{1,0:T(8,128)S(1)} %reduce_sum.166), channel_id=1, source_target_pairs={{0,96},{4,100},{8,104},{12,108},{16,112},{20,116},{24,120},{28,124... | collective-permute-start | bytes 196616 | tf_op jit(solution)/shard_map/ppermute | solution.py:71
  203.7 1.3 collective-permute-start.46
  205.1 5.2 %collective-permute-start.47 = (f32[64]{0:T(128)S(1)}, f32[64]{0:T(128)S(1)}, u32[]{:S(2)}, u32[]{:S(2)}) collective-permute-start(f32[64]{0:T(128)S(1)} %multiply_reduce_fusion), channel_id=1, source_target_pairs={{0,1},{1,2},{2,3},{3,0},{4,5},{5,6},{6,7},{7,4},{8,9},{9,10},{10,1... | collective-permute-start | bytes 776 | tf_op jit(solution)/shard_map/ppermute | solution.py:71
  207.5 5.1 %collective-permute-start.48 = (f32[64]{0:T(128)S(1)}, f32[64]{0:T(128)S(1)}, u32[]{:S(2)}, u32[]{:S(2)}) collective-permute-start(f32[64]{0:T(128)S(1)} %multiply_reduce_fusion), channel_id=1, source_target_pairs={{0,2},{1,3},{2,0},{3,1},{4,6},{5,7},{6,4},{7,5},{8,10},{9,11},{10,... | collective-permute-start | bytes 776 | tf_op jit(solution)/shard_map/ppermute | solution.py:71
  210.0 3.6 %collective-permute-start.49 = (f32[64]{0:T(128)S(1)}, f32[64]{0:T(128)S(1)}, u32[]{:S(2)}, u32[]{:S(2)}) collective-permute-start(f32[64]{0:T(128)S(1)} %multiply_reduce_fusion), channel_id=1, source_target_pairs={{0,3},{1,0},{2,1},{3,2},{4,7},{5,4},{6,5},{7,6},{8,11},{9,8},{10,9... | collective-permute-start | bytes 776 | tf_op jit(solution)/shard_map/ppermute | solution.py:71

commit v5 on v4

--- a/solution.py
+++ b/solution.py
@@ -139,6 +139,33 @@
         for m in range(MP_SIZE):
             pairs.append((s * MP_SIZE + m, (m * per + lead) * MP_SIZE + last))
     return lax.ppermute(active, ("seq", "mp"), pairs)
+
+
+def deliver(piece, width, local_width):
+    slice_width = piece.shape[1]
+    per = local_width // width
+    holders = width // slice_width
+    assert holders == MP_SIZE
+    mp = lax.axis_index("mp")
+    result = jnp.zeros((piece.shape[0], width), piece.dtype)
+    for shift in range(MP_SIZE):
+        pairs = [
+            (s * MP_SIZE + m, (m * per + s // holders) * MP_SIZE + (s % holders + shift) % MP_SIZE)
+            for s in range(SEQ_SIZE)
+            for m in range(MP_SIZE)
+        ]
+        received = lax.ppermute(piece, ("seq", "mp"), pairs)
+        result = lax.dynamic_update_slice_in_dim(
+            result, received, ((mp - shift) % MP_SIZE) * slice_width, 1
+        )
+    return result
+
+
+def full_rows(weight):
+    rows, cols = weight.shape
+    block = cols // SEQ_SIZE
+    moved = lax.all_to_all(weight.reshape(rows, SEQ_SIZE, block), "seq", 1, 0, tiled=True)
+    return moved.reshape(rows * SEQ_SIZE, block)
 
 
 def merge_stack(stack):
@@ -280,21 +307,7 @@
     )
     attended = (final_running / final_totals[..., None]).astype(jnp.bfloat16).reshape(rows, slice_width)
 
-    width = output_weight.shape[0]
-    per = local_width // width
-    holders = width // slice_width
-    sliced = jnp.zeros((rows, width), jnp.bfloat16)
-    mp = lax.axis_index("mp")
-    for shift in range(MP_SIZE):
-        pairs = [
-            (s * MP_SIZE + m, (m * per + s // holders) * MP_SIZE + (s % holders + shift) % MP_SIZE)
-            for s in range(SEQ_SIZE)
-            for m in range(MP_SIZE)
-        ]
-        received = lax.ppermute(attended, ("seq", "mp"), pairs)
-        sliced = lax.dynamic_update_slice_in_dim(
-            sliced, received, ((mp - shift) % MP_SIZE) * slice_width, 1
-        )
+    sliced = deliver(attended, output_weight.shape[0], local_width)
     attention_out = seq_total(
         jnp.dot(sliced, output_weight, preferred_element_type=jnp.float32)
     )
@@ -303,11 +316,11 @@
         token_rows.astype(jnp.float32) + attention_out * inverse_rms(attention_squares) * attention_gain
     ).astype(jnp.bfloat16)
 
-    hidden_cols = seq_columns(hidden, gate_weight.shape[0])
-    active_cols = gate_up_active(
-        jnp.dot(hidden_cols, gate_weight, preferred_element_type=jnp.float32),
-        jnp.dot(hidden_cols, up_weight, preferred_element_type=jnp.float32),
-    )
+    hidden_all = lax.all_gather(hidden, "mp", axis=1, tiled=True)
+    gate = jnp.dot(hidden_all, full_rows(gate_weight), preferred_element_type=jnp.float32)
+    up_part = jnp.dot(hidden_all, full_rows(up_weight), preferred_element_type=jnp.float32)
+    active = (jax.nn.silu(gate) * up_part).astype(jnp.bfloat16)
+    active_cols = deliver(active, down_weight.shape[0], gate_weight.shape[1])
     mlp_out = seq_total(
         jnp.dot(active_cols, down_weight, preferred_element_type=jnp.float32)
     )

time: 215 us -> 212 us (0.986)
  blocking collectives: 0 us -> 12.3 us
  waiting for transfers between devices: 57.6 us -> 46.4 us
  other arithmetic: 13.3 us -> 9.51 us
  starting transfers between devices: 120 us -> 117 us
  local copies, waits for them, and re-layouts: 11.7 us -> 13.9 us
    ppermute x10 -> x3, starting transfers between devices: 23.8 us -> 3.39 us  [scatter_digit(): lax.ppermute(send, 'seq', digit_pairs(SEQ_SIZE, stride, size, shift))]
    ppermute x5 -> x8, starting transfers between devices: 14.2 us -> 28.4 us  [deliver(): received = lax.ppermute(piece, ('seq', 'mp'), pairs)]
    all_gather x0 -> x1, blocking collectives: none -> 12.3 us  [local(): hidden_all = lax.all_gather(hidden, 'mp', axis=1, tiled=True)]
    ppermute x10 -> x3, waiting for transfers between devices: 14.3 us -> 2.6 us  [scatter_digit(): lax.ppermute(send, 'seq', digit_pairs(SEQ_SIZE, stride, size, shift))]
    all_to_all x0 -> x2, starting transfers between devices: none -> 11.2 us  [full_rows(): lax.all_to_all(weight.reshape(rows, SEQ_SIZE, block), 'seq', 1, 0, tiled=...]
    unnamed x33 -> x37, local copies, waits for them, and re-layouts: 2.42 us -> 6.83 us
    ppermute x6 -> x3, starting transfers between devices: 4.41 us -> 0.26 us  [gather_digit(): lax.ppermute(current, 'seq', digit_pairs(SEQ_SIZE, stride, size, shift))]
    another operation x2 -> x1, other arithmetic: 3.8 us -> 0.17 us  [the longest x1 3.64 us: gate_up_active(): jnp.stack([gate_part.reshape(rows, SEQ_SIZE, unit_block), up_part.reshape...]
  transfers between devices with their start and end apart: 51 -> 45, of which waited for: 34 -> 26; matrix products, arithmetic and copies ran while one was open for 3% -> 7% of each run, Pallas kernels for 0% -> 0%
where the time goes in v5:
time: 212 us; the launch traced here: 211 us
  starting transfers between devices  117 us (55%)
  waiting for transfers between devices  46.4 us (22%)
  local copies, waits for them, and re-layouts  13.9 us (7%)
  blocking collectives  12.3 us (6%)
  matrix products  10.7 us (5%)
  other arithmetic  9.51 us (4%)
    ppermute x27, starting transfers between devices, exchange(): lax.ppermute(value, axis, digit_pairs(count, stride, size, shift))  66.5 us
    ppermute x8, starting transfers between devices, deliver(): received = lax.ppermute(piece, ('seq', 'mp'), pairs)  28.4 us
    ppermute x27, waiting for transfers between devices, exchange(): lax.ppermute(value, axis, digit_pairs(count, stride, size, shift))  27.8 us
    all_gather x1, blocking collectives, local(): hidden_all = lax.all_gather(hidden, 'mp', axis=1, tiled=True)  12.3 us
    all_to_all x2, starting transfers between devices, full_rows(): lax.all_to_all(weight.reshape(rows, SEQ_SIZE, block), 'seq', 1, 0, tiled=...  11.2 us
    all_to_all x1, waiting for transfers between devices, local(): sources = lax.all_to_all(send, 'seq', 0, 0, tiled=True)  7.06 us
    unnamed x37, local copies, waits for them, and re-layouts  6.83 us
    all_to_all x1, starting transfers between devices, local(): sources = lax.all_to_all(send, 'seq', 0, 0, tiled=True)  6.2 us
  transfers between devices with their start and end apart: 45, of which 26 were waited for; matrix products, arithmetic and copies ran while one was open for 7% of the time, Pallas kernels for 0%

profile of v5, /device:TPU:0, one launch (start us, length us, event | category | flops | bytes accessed | tf_op | source)
XLA Modules:
  0.0 211.0 jit_solution(8299345877803545577)
XLA Ops:
  4.9 1.2 copy.103
  6.1 1.1 reshape.361
  7.2 1.0 fusion.26
  8.2 1.0 fusion.27
  9.2 1.0 fusion.28
  10.5 1.2 collective-permute-done.1
  11.9 1.7 collective-permute-start.2
  13.6 2.7 %collective-permute-start.3 = (f32[64,768]{1,0:T(8,128)S(1)}, f32[64,768]{1,0:T(8,128)S(1)}, u32[]{:S(2)}, u32[]{:S(2)}) collective-permute-start(f32[64,768]{1,0:T(8,128)S(1)} %get-tuple-element.14), channel_id=1, source_target_pairs={{0,16},{4,20},{8,24},{12,28},{16,0},{20,4},{24,8},{28,12},{32,48},... | collective-permute-start | bytes 589832 | tf_op jit(solution)/shard_map/ppermute | solution.py:71
  16.3 1.4 collective-permute-start.4
  17.7 2.4 %collective-permute-done.2 = f32[64,768]{1,0:T(8,128)S(1)} collective-permute-done((f32[64,768]{1,0:T(8,128)S(1)}, f32[64,768]{1,0:T(8,128)S(1)}, u32[]{:S(2)}, u32[]{:S(2)}) %collective-permute-start.2) | collective-permute-done | bytes 196640 | tf_op jit(solution)/shard_map/ppermute | solution.py:71
  20.1 5.3 %collective-permute-done.3 = f32[64,768]{1,0:T(8,128)S(1)} collective-permute-done((f32[64,768]{1,0:T(8,128)S(1)}, f32[64,768]{1,0:T(8,128)S(1)}, u32[]{:S(2)}, u32[]{:S(2)}) %collective-permute-start.3) | collective-permute-done | bytes 196640 | tf_op jit(solution)/shard_map/ppermute | solution.py:71
  25.5 4.7 %collective-permute-start.5 = (f32[64,768]{1,0:T(8,128)S(1)}, f32[64,768]{1,0:T(8,128)S(1)}, u32[]{:S(2)}, u32[]{:S(2)}) collective-permute-start(f32[64,768]{1,0:T(8,128)S(1)} %reduce_sum.153), channel_id=1, source_target_pairs={{0,32},{4,36},{8,40},{12,44},{16,48},{20,52},{24,56},{28,60},{32,6... | collective-permute-start | bytes 589832 | tf_op jit(solution)/shard_map/ppermute | solution.py:71
  30.2 4.8 %collective-permute-start.6 = (f32[64,768]{1,0:T(8,128)S(1)}, f32[64,768]{1,0:T(8,128)S(1)}, u32[]{:S(2)}, u32[]{:S(2)}) collective-permute-start(f32[64,768]{1,0:T(8,128)S(1)} %reduce_sum.153), channel_id=1, source_target_pairs={{0,64},{4,68},{8,72},{12,76},{16,80},{20,84},{24,88},{28,92},{32,9... | collective-permute-start | bytes 589832 | tf_op jit(solution)/shard_map/ppermute | solution.py:71
  35.0 1.3 collective-permute-start.7
  36.4 2.0 collective-permute-done.5
  38.4 4.9 %collective-permute-done.6 = f32[64,768]{1,0:T(8,128)S(1)} collective-permute-done((f32[64,768]{1,0:T(8,128)S(1)}, f32[64,768]{1,0:T(8,128)S(1)}, u32[]{:S(2)}, u32[]{:S(2)}) %collective-permute-start.6) | collective-permute-done | bytes 196640 | tf_op jit(solution)/shard_map/ppermute | solution.py:71
  43.6 1.4 collective-permute-done.8
  45.1 1.9 collective-permute-start.9
  47.0 0.9 collective-permute-start.10
  47.9 1.9 collective-permute-start.11
  50.2 1.9 collective-permute-done.10
  52.7 5.5 %fusion.25 = (f32[4,4,16]{2,1,0:T(4,128)S(1)}, f32[4,4,16,4096]{3,2,1,0:T(8,128)}) fusion(bf16[4096,512,1,1]{1,0,3,2:T(8,128)(2,1)} %bitcast.223, pred[4,512]{1,0:T(4,128)(4,1)S(1)} %iota_compare_fusion.1, bf16[4,16,512]{2,1,0:T(8,128)(2,1)S(1)} %convert_element_type.52, pred[16,4096]{1,0:T(8,128)(4,1)S(1)} %fusion.6), kind=kOutput, calls=%fused_computation.122 | convolution fusion | flops 1077018368 | bytes 8522752 | tf_op jit(solution)/shard_map/dot_general | solution.py:255
  58.3 3.4 %fusion.2 = (bf16[4,4,16,4096]{3,2,1,0:T(8,128)(2,1)S(1)}, f32[4,4,16]{2,1,0:T(4,128)S(1)}) fusion(f32[4,4,16,4096]{3,2,1,0:T(8,128)} %get-tuple-element.36, f32[4,4,16]{2,1,0:T(4,128)S(1)} %get-tuple-element.35, pred[16,4096]{1,0:T(8,128)(4,1)S(1)} %fusion.6), kind=kLoop, calls=%fused_computation.4 | loop fusion | flops 4194048 | bytes 6359040 | tf_op jit(solution)/shard_map/convert_element_type | solution.py:266
  61.7 1.2 convolution_bitcast_fusion
  64.8 6.2 %all-to-all-start = ((f32[32,1,1152]{2,1,0:T(1,128)}), f32[32,1,1152]{2,1,0:T(1,128)S(1)}, u32[]{:S(2)}, u32[]{:S(2)}) async-start(f32[32,1,1152]{2,1,0:T(1,128)} %reshape.357), calls=%async_computation | async-start | bytes 294912 | tf_op jit(solution)/shard_map/all_to_all | solution.py:283
  71.8 7.1 %all-to-all-done = f32[32,1,1152]{2,1,0:T(1,128)S(1)} async-done(((f32[32,1,1152]{2,1,0:T(1,128)}), f32[32,1,1152]{2,1,0:T(1,128)S(1)}, u32[]{:S(2)}, u32[]{:S(2)}) %all-to-all-start) | async-done | bytes 147488 | tf_op jit(solution)/shard_map/all_to_all | solution.py:283
  78.9 4.0 %all-to-all-start.1 = ((bf16[32,2,2048]{2,1,0:T(2,128)(2,1)}), bf16[32,2,2048]{2,1,0:T(2,128)(2,1)S(1)}, u32[]{:S(2)}, u32[]{:S(2)}) async-start(bf16[32,2,2048]{2,1,0:T(2,128)(2,1)} %reshape.361), calls=%async_computation.1 | async-start | bytes 524288 | tf_op jit(solution)/shard_map/all_to_all | solution.py:167
  83.4 1.0 reduce.1
  87.0 1.1 reshape.359
  88.2 3.4 %all-to-all-done.1 = bf16[32,2,2048]{2,1,0:T(2,128)(2,1)S(1)} async-done(((bf16[32,2,2048]{2,1,0:T(2,128)(2,1)}), bf16[32,2,2048]{2,1,0:T(2,128)(2,1)S(1)}, u32[]{:S(2)}, u32[]{:S(2)}) %all-to-all-start.1) | async-done | bytes 262176 | tf_op jit(solution)/shard_map/all_to_all | solution.py:167
  91.5 7.2 %all-to-all-start.2 = ((bf16[32,2,2048]{2,1,0:T(2,128)(2,1)}), bf16[32,2,2048]{2,1,0:T(2,128)(2,1)S(1)}, u32[]{:S(2)}, u32[]{:S(2)}) async-start(bf16[32,2,2048]{2,1,0:T(2,128)(2,1)} %reshape.359), calls=%async_computation.2 | async-start | bytes 524288 | tf_op jit(solution)/shard_map/all_to_all | solution.py:167
  99.1 3.7 %collective-permute-start.13 = (bf16[64,16]{0,1:T(8,128)(2,1)S(1)}, bf16[64,16]{0,1:T(8,128)(2,1)S(1)}, u32[]{:S(2)}, u32[]{:S(2)}) collective-permute-start(bf16[64,16]{0,1:T(8,128)(2,1)S(1)} %copy.110), channel_id=1, source_target_pairs={{0,1},{1,33},{2,65},{3,97},{4,2},{5,34},{6,66},{7,98},{8,3},{9,35}... | collective-permute-start | bytes 6152 | tf_op jit(solution)/shard_map/ppermute | solution.py:157
  102.8 4.9 %collective-permute-start.14 = (bf16[64,16]{0,1:T(8,128)(2,1)S(1)}, bf16[64,16]{0,1:T(8,128)(2,1)S(1)}, u32[]{:S(2)}, u32[]{:S(2)}) collective-permute-start(bf16[64,16]{0,1:T(8,128)(2,1)S(1)} %copy.110), channel_id=1, source_target_pairs={{0,2},{1,34},{2,66},{3,98},{4,3},{5,35},{6,67},{7,99},{8,0},{9,32}... | collective-permute-start | bytes 6152 | tf_op jit(solution)/shard_map/ppermute | solution.py:157
  107.7 4.6 %collective-permute-start.15 = (bf16[64,16]{0,1:T(8,128)(2,1)S(1)}, bf16[64,16]{0,1:T(8,128)(2,1)S(1)}, u32[]{:S(2)}, u32[]{:S(2)}) collective-permute-start(bf16[64,16]{0,1:T(8,128)(2,1)S(1)} %copy.110), channel_id=1, source_target_pairs={{0,3},{1,35},{2,67},{3,99},{4,0},{5,32},{6,64},{7,96},{8,1},{9,33}... | collective-permute-start | bytes 6152 | tf_op jit(solution)/shard_map/ppermute | solution.py:157
  112.4 1.2 collective-permute-done.15
  115.2 1.0 collective-permute-start.17
  117.9 4.6 %collective-permute-start.18 = (f32[64,256]{1,0:T(8,128)S(1)}, f32[64,256]{1,0:T(8,128)S(1)}, u32[]{:S(2)}, u32[]{:S(2)}) collective-permute-start(f32[64,256]{1,0:T(8,128)S(1)} %get-tuple-element.10), channel_id=1, source_target_pairs={{0,16},{4,20},{8,24},{12,28},{16,0},{20,4},{24,8},{28,12},{32,48},... | collective-permute-start | bytes 196616 | tf_op jit(solution)/shard_map/ppermute | solution.py:71
  122.5 2.5 %collective-permute-start.19 = (f32[64,256]{1,0:T(8,128)S(1)}, f32[64,256]{1,0:T(8,128)S(1)}, u32[]{:S(2)}, u32[]{:S(2)}) collective-permute-start(f32[64,256]{1,0:T(8,128)S(1)} %get-tuple-element.10), channel_id=1, source_target_pairs={{0,24},{4,28},{8,0},{12,4},{16,8},{20,12},{24,16},{28,20},{32,56},... | collective-permute-start | bytes 196616 | tf_op jit(solution)/shard_map/ppermute | solution.py:71
  125.1 1.9 collective-permute-done.19
  127.8 6.9 %collective-permute-start.21 = (f32[64,256]{1,0:T(8,128)S(1)}, f32[64,256]{1,0:T(8,128)S(1)}, u32[]{:S(2)}, u32[]{:S(2)}) collective-permute-start(f32[64,256]{1,0:T(8,128)S(1)} %reduce_sum.162), channel_id=1, source_target_pairs={{0,64},{4,68},{8,72},{12,76},{16,80},{20,84},{24,88},{28,92},{32,9... | collective-permute-start | bytes 196616 | tf_op jit(solution)/shard_map/ppermute | solution.py:71
  134.7 2.5 %collective-permute-start.22 = (f32[64,256]{1,0:T(8,128)S(1)}, f32[64,256]{1,0:T(8,128)S(1)}, u32[]{:S(2)}, u32[]{:S(2)}) collective-permute-start(f32[64,256]{1,0:T(8,128)S(1)} %reduce_sum.162), channel_id=1, source_target_pairs={{0,96},{4,100},{8,104},{12,108},{16,112},{20,116},{24,120},{28,124... | collective-permute-start | bytes 196616 | tf_op jit(solution)/shard_map/ppermute | solution.py:71
  137.6 1.6 collective-permute-done.22
  139.3 1.2 collective-permute-done.23
  141.5 1.9 collective-permute-start.25
  143.4 2.1 collective-permute-start.26
  145.5 1.0 collective-permute-done.25
  147.1 12.3 %all_gather.3 = bf16[64,2048]{1,0:T(8,128)(2,1)S(1)} all-gather(bf16[64,512]{1,0:T(8,128)(2,1)S(1)} %add_convert_fusion.1), channel_id=1, replica_groups=mesh['seq'=32,'mp'=4] {'mp'}, dimensions={1}, use_global_device_ids=true | all-gather | bytes 327680 | tf_op jit(solution)/shard_map/all_gather | solution.py:319
  160.5 5.9 %collective-permute-start.28 = (bf16[64,64]{1,0:T(8,128)(2,1)S(1)}, bf16[64,64]{1,0:T(8,128)(2,1)S(1)}, u32[]{:S(2)}, u32[]{:S(2)}) collective-permute-start(bf16[64,64]{1,0:T(8,128)(2,1)S(1)} %fusion.3), channel_id=1, source_target_pairs={{0,1},{1,33},{2,65},{3,97},{4,2},{5,34},{6,66},{7,98},{8,3},{9,35}... | collective-permute-start | bytes 24584 | tf_op jit(solution)/shard_map/ppermute | solution.py:157
  166.5 4.6 %collective-permute-start.29 = (bf16[64,64]{1,0:T(8,128)(2,1)S(1)}, bf16[64,64]{1,0:T(8,128)(2,1)S(1)}, u32[]{:S(2)}, u32[]{:S(2)}) collective-permute-start(bf16[64,64]{1,0:T(8,128)(2,1)S(1)} %fusion.3), channel_id=1, source_target_pairs={{0,2},{1,34},{2,66},{3,98},{4,3},{5,35},{6,67},{7,99},{8,0},{9,32}... | collective-permute-start | bytes 24584 | tf_op jit(solution)/shard_map/ppermute | solution.py:157
  171.1 3.3 %collective-permute-start.30 = (bf16[64,64]{1,0:T(8,128)(2,1)S(1)}, bf16[64,64]{1,0:T(8,128)(2,1)S(1)}, u32[]{:S(2)}, u32[]{:S(2)}) collective-permute-start(bf16[64,64]{1,0:T(8,128)(2,1)S(1)} %fusion.3), channel_id=1, source_target_pairs={{0,3},{1,35},{2,67},{3,99},{4,0},{5,32},{6,64},{7,96},{8,1},{9,33}... | collective-permute-start | bytes 24584 | tf_op jit(solution)/shard_map/ppermute | solution.py:157
  176.4 2.8 %collective-permute-start.31 = (f32[64,256]{1,0:T(8,128)S(1)}, f32[64,256]{1,0:T(8,128)S(1)}, u32[]{:S(2)}, u32[]{:S(2)}) collective-permute-start(f32[64,256]{1,0:T(8,128)S(1)} %constant_dynamic-slice_fusion), channel_id=1, source_target_pairs={{0,4},{4,0},{8,12},{12,8},{16,20},{20,16},{24,28},{28,24},{32,36},... | collective-permute-start | bytes 196616 | tf_op jit(solution)/shard_map/ppermute | solution.py:83
  179.2 0.9 collective-permute-done.31
  180.8 5.6 %collective-permute-start.33 = (f32[64,256]{1,0:T(8,128)S(1)}, f32[64,256]{1,0:T(8,128)S(1)}, u32[]{:S(2)}, u32[]{:S(2)}) collective-permute-start(f32[64,256]{1,0:T(8,128)S(1)} %get-tuple-element.8), channel_id=1, source_target_pairs={{0,16},{4,20},{8,24},{12,28},{16,0},{20,4},{24,8},{28,12},{32,48},... | collective-permute-start | bytes 196616 | tf_op jit(solution)/shard_map/ppermute | solution.py:71
  186.4 2.0 collective-permute-start.34
  188.5 1.5 collective-permute-done.33
  190.7 0.9 collective-permute-start.35
  191.7 6.7 %collective-permute-start.36 = (f32[64,256]{1,0:T(8,128)S(1)}, f32[64,256]{1,0:T(8,128)S(1)}, u32[]{:S(2)}, u32[]{:S(2)}) collective-permute-start(f32[64,256]{1,0:T(8,128)S(1)} %reduce_sum.166), channel_id=1, source_target_pairs={{0,64},{4,68},{8,72},{12,76},{16,80},{20,84},{24,88},{28,92},{32,9... | collective-permute-start | bytes 196616 | tf_op jit(solution)/shard_map/ppermute | solution.py:71
  198.3 2.4 %collective-permute-start.37 = (f32[64,256]{1,0:T(8,128)S(1)}, f32[64,256]{1,0:T(8,128)S(1)}, u32[]{:S(2)}, u32[]{:S(2)}) collective-permute-start(f32[64,256]{1,0:T(8,128)S(1)} %reduce_sum.166), channel_id=1, source_target_pairs={{0,96},{4,100},{8,104},{12,108},{16,112},{20,116},{24,120},{28,124... | collective-permute-start | bytes 196616 | tf_op jit(solution)/shard_map/ppermute | solution.py:71
  201.3 1.4 collective-permute-done.37
  202.8 1.2 collective-permute-done.38
  204.2 0.9 collective-permute-start.39
  205.1 2.8 %collective-permute-start.41 = (f32[64]{0:T(128)S(1)}, f32[64]{0:T(128)S(1)}, u32[]{:S(2)}, u32[]{:S(2)}) collective-permute-start(f32[64]{0:T(128)S(1)} %multiply_reduce_fusion), channel_id=1, source_target_pairs={{0,3},{1,0},{2,1},{3,2},{4,7},{5,4},{6,5},{7,6},{8,11},{9,8},{10,9... | collective-permute-start | bytes 776 | tf_op jit(solution)/shard_map/ppermute | solution.py:71
  207.9 1.1 collective-permute-done.39
  209.0 1.1 collective-permute-done.40
  (223 shorter events, 24.6 us)
Async XLA Ops:
  0.0 176.2 %copy-start = (bf16[256,512]{1,0:T(8,128)(2,1)S(1)}, bf16[256,512]{1,0:T(8,128)(2,1)}, u32[]{:S(2)}) copy-start(bf16[256,512]{1,0:T(8,128)(2,1)} %param.24) | copy-start | bytes 786436
  0.8 6.4 %collective-permute-start = (bf16[64,64]{1,0:T(8,128)(2,1)S(1)}, bf16[64,64]{1,0:T(8,128)(2,1)S(1)}, u32[]{:S(2)}, u32[]{:S(2)}) collective-permute-start(bf16[64,64]{1,0:T(8,128)(2,1)S(1)} %constant_dynamic-slice_fusion.5), channel_id=1, source_target_pairs={{0,0},{1,32},{2,64},{3,96},{4,4},{5,36},{6,68},{7,100},{8,8},{9,40... | collective-permute-start | bytes 24584 | tf_op jit(solution)/shard_map/ppermute | solution.py:47
  10.2 1.5 collective-permute-start.1
  11.8 40.3 %copy-start.4 = (f32[512]{0:T(512)S(1)}, f32[512]{0:T(512)}, u32[]{:S(2)}) copy-start(f32[512]{0:T(512)} %param.26) | copy-start | bytes 6148
  11.8 40.3 %copy-start.5 = (f32[512]{0:T(512)S(1)}, f32[512]{0:T(512)}, u32[]{:S(2)}) copy-start(f32[512]{0:T(512)} %param.25) | copy-start | bytes 6148
  11.9 8.2 %collective-permute-start.2 = (f32[64,768]{1,0:T(8,128)S(1)}, f32[64,768]{1,0:T(8,128)S(1)}, u32[]{:S(2)}, u32[]{:S(2)}) collective-permute-start(f32[64,768]{1,0:T(8,128)S(1)} %get-tuple-element.14), channel_id=1, source_target_pairs={{0,8},{4,12},{8,16},{12,20},{16,24},{20,28},{24,0},{28,4},{32,40},... | collective-permute-start | bytes 589832 | tf_op jit(solution)/shard_map/ppermute | solution.py:71
  13.6 11.9 %collective-permute-start.3 = (f32[64,768]{1,0:T(8,128)S(1)}, f32[64,768]{1,0:T(8,128)S(1)}, u32[]{:S(2)}, u32[]{:S(2)}) collective-permute-start(f32[64,768]{1,0:T(8,128)S(1)} %get-tuple-element.14), channel_id=1, source_target_pairs={{0,16},{4,20},{8,24},{12,28},{16,0},{20,4},{24,8},{28,12},{32,48},... | collective-permute-start | bytes 589832 | tf_op jit(solution)/shard_map/ppermute | solution.py:71
  16.3 9.1 %collective-permute-start.4 = (f32[64,768]{1,0:T(8,128)S(1)}, f32[64,768]{1,0:T(8,128)S(1)}, u32[]{:S(2)}, u32[]{:S(2)}) collective-permute-start(f32[64,768]{1,0:T(8,128)S(1)} %get-tuple-element.14), channel_id=1, source_target_pairs={{0,24},{4,28},{8,0},{12,4},{16,8},{20,12},{24,16},{28,20},{32,56},... | collective-permute-start | bytes 589832 | tf_op jit(solution)/shard_map/ppermute | solution.py:71
  25.5 12.9 %collective-permute-start.5 = (f32[64,768]{1,0:T(8,128)S(1)}, f32[64,768]{1,0:T(8,128)S(1)}, u32[]{:S(2)}, u32[]{:S(2)}) collective-permute-start(f32[64,768]{1,0:T(8,128)S(1)} %reduce_sum.153), channel_id=1, source_target_pairs={{0,32},{4,36},{8,40},{12,44},{16,48},{20,52},{24,56},{28,60},{32,6... | collective-permute-start | bytes 589832 | tf_op jit(solution)/shard_map/ppermute | solution.py:71
  30.2 13.1 %collective-permute-start.6 = (f32[64,768]{1,0:T(8,128)S(1)}, f32[64,768]{1,0:T(8,128)S(1)}, u32[]{:S(2)}, u32[]{:S(2)}) collective-permute-start(f32[64,768]{1,0:T(8,128)S(1)} %reduce_sum.153), channel_id=1, source_target_pairs={{0,64},{4,68},{8,72},{12,76},{16,80},{20,84},{24,88},{28,92},{32,9... | collective-permute-start | bytes 589832 | tf_op jit(solution)/shard_map/ppermute | solution.py:71
  35.0 8.3 %collective-permute-start.7 = (f32[64,768]{1,0:T(8,128)S(1)}, f32[64,768]{1,0:T(8,128)S(1)}, u32[]{:S(2)}, u32[]{:S(2)}) collective-permute-start(f32[64,768]{1,0:T(8,128)S(1)} %reduce_sum.153), channel_id=1, source_target_pairs={{0,96},{4,100},{8,104},{12,108},{16,112},{20,116},{24,120},{28,124... | collective-permute-start | bytes 589832 | tf_op jit(solution)/shard_map/ppermute | solution.py:71
  43.4 1.5 collective-permute-start.8
  45.1 5.1 %collective-permute-start.9 = (f32[64,2]{0,1:T(2,128)S(1)}, f32[64,2]{0,1:T(2,128)S(1)}, u32[]{:S(2)}, u32[]{:S(2)}) collective-permute-start(f32[64,2]{0,1:T(2,128)S(1)} %pad_maximum_fusion.2), channel_id=1, source_target_pairs={{0,1},{1,2},{2,3},{3,0},{4,5},{5,6},{6,7},{7,4},{8,9},{9,10},{10,1... | collective-permute-start | bytes 1544 | tf_op jit(solution)/shard_map/ppermute | solution.py:71
  47.0 5.1 %collective-permute-start.10 = (f32[64,2]{0,1:T(2,128)S(1)}, f32[64,2]{0,1:T(2,128)S(1)}, u32[]{:S(2)}, u32[]{:S(2)}) collective-permute-start(f32[64,2]{0,1:T(2,128)S(1)} %pad_maximum_fusion.2), channel_id=1, source_target_pairs={{0,2},{1,3},{2,0},{3,1},{4,6},{5,7},{6,4},{7,5},{8,10},{9,11},{10,... | collective-permute-start | bytes 1544 | tf_op jit(solution)/shard_map/ppermute | solution.py:71
  47.9 4.2 %collective-permute-start.11 = (f32[64,2]{0,1:T(2,128)S(1)}, f32[64,2]{0,1:T(2,128)S(1)}, u32[]{:S(2)}, u32[]{:S(2)}) collective-permute-start(f32[64,2]{0,1:T(2,128)S(1)} %pad_maximum_fusion.2), channel_id=1, source_target_pairs={{0,3},{1,0},{2,1},{3,2},{4,7},{5,4},{6,5},{7,6},{8,11},{9,8},{10,9... | collective-permute-start | bytes 1544 | tf_op jit(solution)/shard_map/ppermute | solution.py:71
  58.3 3.5 %copy-start.8 = (bf16[16,256,512]{2,1,0:T(8,128)(2,1)S(1)}, bf16[16,256,512]{2,1,0:T(8,128)(2,1)}, u32[]{:S(2)}) copy-start(bf16[16,256,512]{2,1,0:T(8,128)(2,1)} %param.30) | copy-start | bytes 12582916
  63.0 23.8 %copy-start.1 = (bf16[64,2048]{1,0:T(8,128)(2,1)S(1)}, bf16[64,2048]{1,0:T(8,128)(2,1)}, u32[]{:S(2)}) copy-start(bf16[64,2048]{1,0:T(8,128)(2,1)} %param.23) | copy-start | bytes 786436
  63.8 49.8 %copy-start.3 = (bf16[64,512]{1,0:T(8,128)(2,1)S(1)}, bf16[64,512]{1,0:T(8,128)(2,1)}, u32[]{:S(2)}) copy-start(bf16[64,512]{1,0:T(8,128)(2,1)} %param.21) | copy-start | bytes 196612
  64.8 14.1 %all-to-all-start = ((f32[32,1,1152]{2,1,0:T(1,128)}), f32[32,1,1152]{2,1,0:T(1,128)S(1)}, u32[]{:S(2)}, u32[]{:S(2)}) async-start(f32[32,1,1152]{2,1,0:T(1,128)} %reshape.357), calls=%async_computation | async-start | bytes 294912 | tf_op jit(solution)/shard_map/all_to_all | solution.py:283
  78.9 12.7 %all-to-all-start.1 = ((bf16[32,2,2048]{2,1,0:T(2,128)(2,1)}), bf16[32,2,2048]{2,1,0:T(2,128)(2,1)S(1)}, u32[]{:S(2)}, u32[]{:S(2)}) async-start(bf16[32,2,2048]{2,1,0:T(2,128)(2,1)} %reshape.361), calls=%async_computation.1 | async-start | bytes 524288 | tf_op jit(solution)/shard_map/all_to_all | solution.py:167
  86.0 26.3 %collective-permute-start.12 = (bf16[64,16]{0,1:T(8,128)(2,1)S(1)}, bf16[64,16]{0,1:T(8,128)(2,1)S(1)}, u32[]{:S(2)}, u32[]{:S(2)}) collective-permute-start(bf16[64,16]{0,1:T(8,128)(2,1)S(1)} %copy.110), channel_id=1, source_target_pairs={{0,0},{1,32},{2,64},{3,96},{4,1},{5,33},{6,65},{7,97},{8,2},{9,34}... | collective-permute-start | bytes 6152 | tf_op jit(solution)/shard_map/ppermute | solution.py:157
  91.5 22.8 %all-to-all-start.2 = ((bf16[32,2,2048]{2,1,0:T(2,128)(2,1)}), bf16[32,2,2048]{2,1,0:T(2,128)(2,1)S(1)}, u32[]{:S(2)}, u32[]{:S(2)}) async-start(bf16[32,2,2048]{2,1,0:T(2,128)(2,1)} %reshape.359), calls=%async_computation.2 | async-start | bytes 524288 | tf_op jit(solution)/shard_map/all_to_all | solution.py:167
  99.1 13.2 %collective-permute-start.13 = (bf16[64,16]{0,1:T(8,128)(2,1)S(1)}, bf16[64,16]{0,1:T(8,128)(2,1)S(1)}, u32[]{:S(2)}, u32[]{:S(2)}) collective-permute-start(bf16[64,16]{0,1:T(8,128)(2,1)S(1)} %copy.110), channel_id=1, source_target_pairs={{0,1},{1,33},{2,65},{3,97},{4,2},{5,34},{6,66},{7,98},{8,3},{9,35}... | collective-permute-start | bytes 6152 | tf_op jit(solution)/shard_map/ppermute | solution.py:157
  102.8 9.6 %collective-permute-start.14 = (bf16[64,16]{0,1:T(8,128)(2,1)S(1)}, bf16[64,16]{0,1:T(8,128)(2,1)S(1)}, u32[]{:S(2)}, u32[]{:S(2)}) collective-permute-start(bf16[64,16]{0,1:T(8,128)(2,1)S(1)} %copy.110), channel_id=1, source_target_pairs={{0,2},{1,34},{2,66},{3,98},{4,3},{5,35},{6,67},{7,99},{8,0},{9,32}... | collective-permute-start | bytes 6152 | tf_op jit(solution)/shard_map/ppermute | solution.py:157
  107.7 5.9 %collective-permute-start.15 = (bf16[64,16]{0,1:T(8,128)(2,1)S(1)}, bf16[64,16]{0,1:T(8,128)(2,1)S(1)}, u32[]{:S(2)}, u32[]{:S(2)}) collective-permute-start(bf16[64,16]{0,1:T(8,128)(2,1)S(1)} %copy.110), channel_id=1, source_target_pairs={{0,3},{1,35},{2,67},{3,99},{4,0},{5,32},{6,64},{7,96},{8,1},{9,33}... | collective-permute-start | bytes 6152 | tf_op jit(solution)/shard_map/ppermute | solution.py:157
  113.8 1.4 collective-permute-start.16
  114.3 32.7 %copy-start.2 = (bf16[4,16,512]{2,1,0:T(8,128)(2,1)S(1)}, bf16[4,16,512]{2,1,0:T(8,128)(2,1)}, u32[]{:S(2)}) copy-start(bf16[4,16,512]{2,1,0:T(8,128)(2,1)} %param.17) | copy-start | bytes 196612
  114.3 32.6 %copy-start.6 = (f32[512]{0:T(512)S(1)}, f32[512]{0:T(512)}, u32[]{:S(2)}) copy-start(f32[512]{0:T(512)} %param.27) | copy-start | bytes 6148
  115.2 9.8 %collective-permute-start.17 = (f32[64,256]{1,0:T(8,128)S(1)}, f32[64,256]{1,0:T(8,128)S(1)}, u32[]{:S(2)}, u32[]{:S(2)}) collective-permute-start(f32[64,256]{1,0:T(8,128)S(1)} %get-tuple-element.10), channel_id=1, source_target_pairs={{0,8},{4,12},{8,16},{12,20},{16,24},{20,28},{24,0},{28,4},{32,40},... | collective-permute-start | bytes 196616 | tf_op jit(solution)/shard_map/ppermute | solution.py:71
  117.4 92.9 %copy-start.7 = (f32[512]{0:T(512)S(1)}, f32[512]{0:T(512)}, u32[]{:S(2)}) copy-start(f32[512]{0:T(512)} %param.28) | copy-start | bytes 6148
  117.9 7.2 %collective-permute-start.18 = (f32[64,256]{1,0:T(8,128)S(1)}, f32[64,256]{1,0:T(8,128)S(1)}, u32[]{:S(2)}, u32[]{:S(2)}) collective-permute-start(f32[64,256]{1,0:T(8,128)S(1)} %get-tuple-element.10), channel_id=1, source_target_pairs={{0,16},{4,20},{8,24},{12,28},{16,0},{20,4},{24,8},{28,12},{32,48},... | collective-permute-start | bytes 196616 | tf_op jit(solution)/shard_map/ppermute | solution.py:71
  122.5 4.5 %collective-permute-start.19 = (f32[64,256]{1,0:T(8,128)S(1)}, f32[64,256]{1,0:T(8,128)S(1)}, u32[]{:S(2)}, u32[]{:S(2)}) collective-permute-start(f32[64,256]{1,0:T(8,128)S(1)} %get-tuple-element.10), channel_id=1, source_target_pairs={{0,24},{4,28},{8,0},{12,4},{16,8},{20,12},{24,16},{28,20},{32,56},... | collective-permute-start | bytes 196616 | tf_op jit(solution)/shard_map/ppermute | solution.py:71
  127.0 10.3 %collective-permute-start.20 = (f32[64,256]{1,0:T(8,128)S(1)}, f32[64,256]{1,0:T(8,128)S(1)}, u32[]{:S(2)}, u32[]{:S(2)}) collective-permute-start(f32[64,256]{1,0:T(8,128)S(1)} %reduce_sum.162), channel_id=1, source_target_pairs={{0,32},{4,36},{8,40},{12,44},{16,48},{20,52},{24,56},{28,60},{32,6... | collective-permute-start | bytes 196616 | tf_op jit(solution)/shard_map/ppermute | solution.py:71
  127.8 9.7 %collective-permute-start.21 = (f32[64,256]{1,0:T(8,128)S(1)}, f32[64,256]{1,0:T(8,128)S(1)}, u32[]{:S(2)}, u32[]{:S(2)}) collective-permute-start(f32[64,256]{1,0:T(8,128)S(1)} %reduce_sum.162), channel_id=1, source_target_pairs={{0,64},{4,68},{8,72},{12,76},{16,80},{20,84},{24,88},{28,92},{32,9... | collective-permute-start | bytes 196616 | tf_op jit(solution)/shard_map/ppermute | solution.py:71
  134.7 4.4 %collective-permute-start.22 = (f32[64,256]{1,0:T(8,128)S(1)}, f32[64,256]{1,0:T(8,128)S(1)}, u32[]{:S(2)}, u32[]{:S(2)}) collective-permute-start(f32[64,256]{1,0:T(8,128)S(1)} %reduce_sum.162), channel_id=1, source_target_pairs={{0,96},{4,100},{8,104},{12,108},{16,112},{20,116},{24,120},{28,124... | collective-permute-start | bytes 196616 | tf_op jit(solution)/shard_map/ppermute | solution.py:71
  139.2 1.3 collective-permute-start.23
  140.6 4.8 %collective-permute-start.24 = (f32[64]{0:T(128)S(1)}, f32[64]{0:T(128)S(1)}, u32[]{:S(2)}, u32[]{:S(2)}) collective-permute-start(f32[64]{0:T(128)S(1)} %multiply_reduce_fusion.1), channel_id=1, source_target_pairs={{0,1},{1,2},{2,3},{3,0},{4,5},{5,6},{6,7},{7,4},{8,9},{9,10},{10,1... | collective-permute-start | bytes 776 | tf_op jit(solution)/shard_map/ppermute | solution.py:71
  141.5 5.1 %collective-permute-start.25 = (f32[64]{0:T(128)S(1)}, f32[64]{0:T(128)S(1)}, u32[]{:S(2)}, u32[]{:S(2)}) collective-permute-start(f32[64]{0:T(128)S(1)} %multiply_reduce_fusion.1), channel_id=1, source_target_pairs={{0,2},{1,3},{2,0},{3,1},{4,6},{5,7},{6,4},{7,5},{8,10},{9,11},{10,... | collective-permute-start | bytes 776 | tf_op jit(solution)/shard_map/ppermute | solution.py:71
  143.4 3.6 %collective-permute-start.26 = (f32[64]{0:T(128)S(1)}, f32[64]{0:T(128)S(1)}, u32[]{:S(2)}, u32[]{:S(2)}) collective-permute-start(f32[64]{0:T(128)S(1)} %multiply_reduce_fusion.1), channel_id=1, source_target_pairs={{0,3},{1,0},{2,1},{3,2},{4,7},{5,4},{6,5},{7,6},{8,11},{9,8},{10,9... | collective-permute-start | bytes 776 | tf_op jit(solution)/shard_map/ppermute | solution.py:71
  159.8 14.6 %collective-permute-start.27 = (bf16[64,64]{1,0:T(8,128)(2,1)S(1)}, bf16[64,64]{1,0:T(8,128)(2,1)S(1)}, u32[]{:S(2)}, u32[]{:S(2)}) collective-permute-start(bf16[64,64]{1,0:T(8,128)(2,1)S(1)} %fusion.3), channel_id=1, source_target_pairs={{0,0},{1,32},{2,64},{3,96},{4,1},{5,33},{6,65},{7,97},{8,2},{9,34}... | collective-permute-start | bytes 24584 | tf_op jit(solution)/shard_map/ppermute | solution.py:157
  160.5 14.2 %collective-permute-start.28 = (bf16[64,64]{1,0:T(8,128)(2,1)S(1)}, bf16[64,64]{1,0:T(8,128)(2,1)S(1)}, u32[]{:S(2)}, u32[]{:S(2)}) collective-permute-start(bf16[64,64]{1,0:T(8,128)(2,1)S(1)} %fusion.3), channel_id=1, source_target_pairs={{0,1},{1,33},{2,65},{3,97},{4,2},{5,34},{6,66},{7,98},{8,3},{9,35}... | collective-permute-start | bytes 24584 | tf_op jit(solution)/shard_map/ppermute | solution.py:157
  166.5 8.6 %collective-permute-start.29 = (bf16[64,64]{1,0:T(8,128)(2,1)S(1)}, bf16[64,64]{1,0:T(8,128)(2,1)S(1)}, u32[]{:S(2)}, u32[]{:S(2)}) collective-permute-start(bf16[64,64]{1,0:T(8,128)(2,1)S(1)} %fusion.3), channel_id=1, source_target_pairs={{0,2},{1,34},{2,66},{3,98},{4,3},{5,35},{6,67},{7,99},{8,0},{9,32}... | collective-permute-start | bytes 24584 | tf_op jit(solution)/shard_map/ppermute | solution.py:157
  171.1 4.8 %collective-permute-start.30 = (bf16[64,64]{1,0:T(8,128)(2,1)S(1)}, bf16[64,64]{1,0:T(8,128)(2,1)S(1)}, u32[]{:S(2)}, u32[]{:S(2)}) collective-permute-start(bf16[64,64]{1,0:T(8,128)(2,1)S(1)} %fusion.3), channel_id=1, source_target_pairs={{0,3},{1,35},{2,67},{3,99},{4,0},{5,32},{6,64},{7,96},{8,1},{9,33}... | collective-permute-start | bytes 24584 | tf_op jit(solution)/shard_map/ppermute | solution.py:157
  176.4 3.7 %collective-permute-start.31 = (f32[64,256]{1,0:T(8,128)S(1)}, f32[64,256]{1,0:T(8,128)S(1)}, u32[]{:S(2)}, u32[]{:S(2)}) collective-permute-start(f32[64,256]{1,0:T(8,128)S(1)} %constant_dynamic-slice_fusion), channel_id=1, source_target_pairs={{0,4},{4,0},{8,12},{12,8},{16,20},{20,16},{24,28},{28,24},{32,36},... | collective-permute-start | bytes 196616 | tf_op jit(solution)/shard_map/ppermute | solution.py:83
  180.2 8.3 %collective-permute-start.32 = (f32[64,256]{1,0:T(8,128)S(1)}, f32[64,256]{1,0:T(8,128)S(1)}, u32[]{:S(2)}, u32[]{:S(2)}) collective-permute-start(f32[64,256]{1,0:T(8,128)S(1)} %get-tuple-element.8), channel_id=1, source_target_pairs={{0,8},{4,12},{8,16},{12,20},{16,24},{20,28},{24,0},{28,4},{32,40},... | collective-permute-start | bytes 196616 | tf_op jit(solution)/shard_map/ppermute | solution.py:71
  180.8 9.2 %collective-permute-start.33 = (f32[64,256]{1,0:T(8,128)S(1)}, f32[64,256]{1,0:T(8,128)S(1)}, u32[]{:S(2)}, u32[]{:S(2)}) collective-permute-start(f32[64,256]{1,0:T(8,128)S(1)} %get-tuple-element.8), channel_id=1, source_target_pairs={{0,16},{4,20},{8,24},{12,28},{16,0},{20,4},{24,8},{28,12},{32,48},... | collective-permute-start | bytes 196616 | tf_op jit(solution)/shard_map/ppermute | solution.py:71
  186.4 4.3 %collective-permute-start.34 = (f32[64,256]{1,0:T(8,128)S(1)}, f32[64,256]{1,0:T(8,128)S(1)}, u32[]{:S(2)}, u32[]{:S(2)}) collective-permute-start(f32[64,256]{1,0:T(8,128)S(1)} %get-tuple-element.8), channel_id=1, source_target_pairs={{0,24},{4,28},{8,0},{12,4},{16,8},{20,12},{24,16},{28,20},{32,56},... | collective-permute-start | bytes 196616 | tf_op jit(solution)/shard_map/ppermute | solution.py:71
  190.7 10.1 %collective-permute-start.35 = (f32[64,256]{1,0:T(8,128)S(1)}, f32[64,256]{1,0:T(8,128)S(1)}, u32[]{:S(2)}, u32[]{:S(2)}) collective-permute-start(f32[64,256]{1,0:T(8,128)S(1)} %reduce_sum.166), channel_id=1, source_target_pairs={{0,32},{4,36},{8,40},{12,44},{16,48},{20,52},{24,56},{28,60},{32,6... | collective-permute-start | bytes 196616 | tf_op jit(solution)/shard_map/ppermute | solution.py:71
  191.7 9.6 %collective-permute-start.36 = (f32[64,256]{1,0:T(8,128)S(1)}, f32[64,256]{1,0:T(8,128)S(1)}, u32[]{:S(2)}, u32[]{:S(2)}) collective-permute-start(f32[64,256]{1,0:T(8,128)S(1)} %reduce_sum.166), channel_id=1, source_target_pairs={{0,64},{4,68},{8,72},{12,76},{16,80},{20,84},{24,88},{28,92},{32,9... | collective-permute-start | bytes 196616 | tf_op jit(solution)/shard_map/ppermute | solution.py:71
  198.3 4.3 %collective-permute-start.37 = (f32[64,256]{1,0:T(8,128)S(1)}, f32[64,256]{1,0:T(8,128)S(1)}, u32[]{:S(2)}, u32[]{:S(2)}) collective-permute-start(f32[64,256]{1,0:T(8,128)S(1)} %reduce_sum.166), channel_id=1, source_target_pairs={{0,96},{4,100},{8,104},{12,108},{16,112},{20,116},{24,120},{28,124... | collective-permute-start | bytes 196616 | tf_op jit(solution)/shard_map/ppermute | solution.py:71
  202.7 1.3 collective-permute-start.38
  204.2 4.8 %collective-permute-start.39 = (f32[64]{0:T(128)S(1)}, f32[64]{0:T(128)S(1)}, u32[]{:S(2)}, u32[]{:S(2)}) collective-permute-start(f32[64]{0:T(128)S(1)} %multiply_reduce_fusion), channel_id=1, source_target_pairs={{0,1},{1,2},{2,3},{3,0},{4,5},{5,6},{6,7},{7,4},{8,9},{9,10},{10,1... | collective-permute-start | bytes 776 | tf_op jit(solution)/shard_map/ppermute | solution.py:71
  205.1 5.1 %collective-permute-start.40 = (f32[64]{0:T(128)S(1)}, f32[64]{0:T(128)S(1)}, u32[]{:S(2)}, u32[]{:S(2)}) collective-permute-start(f32[64]{0:T(128)S(1)} %multiply_reduce_fusion), channel_id=1, source_target_pairs={{0,2},{1,3},{2,0},{3,1},{4,6},{5,7},{6,4},{7,5},{8,10},{9,11},{10,... | collective-permute-start | bytes 776 | tf_op jit(solution)/shard_map/ppermute | solution.py:71
  205.1 5.1 %collective-permute-start.41 = (f32[64]{0:T(128)S(1)}, f32[64]{0:T(128)S(1)}, u32[]{:S(2)}, u32[]{:S(2)}) collective-permute-start(f32[64]{0:T(128)S(1)} %multiply_reduce_fusion), channel_id=1, source_target_pairs={{0,3},{1,0},{2,1},{3,2},{4,7},{5,4},{6,5},{7,6},{8,11},{9,8},{10,9... | collective-permute-start | bytes 776 | tf_op jit(solution)/shard_map/ppermute | solution.py:71

commit v6 on v5

--- a/solution.py
+++ b/solution.py
@@ -316,9 +316,21 @@
         token_rows.astype(jnp.float32) + attention_out * inverse_rms(attention_squares) * attention_gain
     ).astype(jnp.bfloat16)
 
-    hidden_all = lax.all_gather(hidden, "mp", axis=1, tiled=True)
-    gate = jnp.dot(hidden_all, full_rows(gate_weight), preferred_element_type=jnp.float32)
-    up_part = jnp.dot(hidden_all, full_rows(up_weight), preferred_element_type=jnp.float32)
+    hidden_all = jnp.transpose(exchange(hidden, "mp", MP_SIZE, 1, MP_SIZE), (1, 0, 2)).reshape(
+        rows, MP_SIZE * local_width
+    )
+    units = gate_weight.shape[1] // SEQ_SIZE
+    both = full_rows(
+        jnp.concatenate(
+            [
+                gate_weight.reshape(-1, SEQ_SIZE, units),
+                up_weight.reshape(-1, SEQ_SIZE, units),
+            ],
+            axis=2,
+        ).reshape(gate_weight.shape[0], 2 * gate_weight.shape[1])
+    )
+    gate = jnp.dot(hidden_all, both[:, :units], preferred_element_type=jnp.float32)
+    up_part = jnp.dot(hidden_all, both[:, units:], preferred_element_type=jnp.float32)
     active = (jax.nn.silu(gate) * up_part).astype(jnp.bfloat16)
     active_cols = deliver(active, down_weight.shape[0], gate_weight.shape[1])
     mlp_out = seq_total(

time: 212 us -> 206 us (0.972)
  blocking collectives: 12.3 us -> 0 us
  waiting for transfers between devices: 46.4 us -> 50.4 us
    all_gather x1 -> x0, blocking collectives: 12.3 us -> none  [local(): hidden_all = lax.all_gather(hidden, 'mp', axis=1, tiled=True)]
    ppermute x27 -> x30, waiting for transfers between devices: 27.8 us -> 35.5 us  [exchange(): lax.ppermute(value, axis, digit_pairs(count, stride, size, shift))]
    unnamed x37 -> x34, local copies, waits for them, and re-layouts: 6.83 us -> 2.47 us
    dynamic_update_slice x27 -> x30, local copies, waits for them, and re-layouts: 0.44 us -> 3.84 us  [exchange(): lax.dynamic_update_index_in_dim(stack, received, (digit - shift) % size, 0)]
    all_to_all x2 -> x1, waiting for transfers between devices: 3.38 us -> 0.01 us  [full_rows(): lax.all_to_all(weight.reshape(rows, SEQ_SIZE, block), 'seq', 1, 0, tiled=...]
    ppermute x3, starting transfers between devices: 3.39 us -> 5.71 us  [scatter_digit(): lax.ppermute(send, 'seq', digit_pairs(SEQ_SIZE, stride, size, shift))]
    ppermute x27 -> x30, starting transfers between devices: 66.5 us -> 64.6 us  [exchange(): lax.ppermute(value, axis, digit_pairs(count, stride, size, shift))]
    all_to_all x2 -> x1, starting transfers between devices: 11.2 us -> 12.7 us  [full_rows(): lax.all_to_all(weight.reshape(rows, SEQ_SIZE, block), 'seq', 1, 0, tiled=...]
  transfers between devices with their start and end apart: 45 -> 47, of which waited for: 26 -> 28; matrix products, arithmetic and copies ran while one was open for 7% -> 7% of each run, Pallas kernels for 0% -> 0%
where the time goes in v6:
time: 206 us
  starting transfers between devices  118 us (57%)
  waiting for transfers between devices  50.4 us (24%)
  local copies, waits for them, and re-layouts  14.9 us (7%)
  matrix products  10.8 us (5%)
  other arithmetic  9.81 us (5%)
    ppermute x30, starting transfers between devices, exchange(): lax.ppermute(value, axis, digit_pairs(count, stride, size, shift))  64.6 us
    ppermute x30, waiting for transfers between devices, exchange(): lax.ppermute(value, axis, digit_pairs(count, stride, size, shift))  35.5 us
    ppermute x8, starting transfers between devices, deliver(): received = lax.ppermute(piece, ('seq', 'mp'), pairs)  27.4 us
    all_to_all x1, starting transfers between devices, full_rows(): lax.all_to_all(weight.reshape(rows, SEQ_SIZE, block), 'seq', 1, 0, tiled=...  12.7 us
    all_to_all x1, waiting for transfers between devices, local(): sources = lax.all_to_all(send, 'seq', 0, 0, tiled=True)  7.05 us
    all_to_all x1, starting transfers between devices, local(): sources = lax.all_to_all(send, 'seq', 0, 0, tiled=True)  6.74 us
    ppermute x3, starting transfers between devices, scatter_digit(): lax.ppermute(send, 'seq', digit_pairs(SEQ_SIZE, stride, size, shift))  5.71 us
    dot_general x1, matrix products, local(): lax.dot_general(block_queries, keys, (((1,), (1,)), ((), ())), preferred_...  5.51 us
  transfers between devices with their start and end apart: 47, of which 28 were waited for; matrix products, arithmetic and copies ran while one was open for 7% of the time, Pallas kernels for 0%

profile of v6, /device:TPU:0, one launch (start us, length us, event | category | flops | bytes accessed | tf_op | source)
XLA Modules:
  0.0 205.6 jit_solution(3092988747868010141)
XLA Ops:
  8.2 1.2 collective-permute-done.1
  9.6 1.7 collective-permute-start.2
  11.3 2.7 %collective-permute-start.3 = (f32[64,768]{1,0:T(8,128)S(1)}, f32[64,768]{1,0:T(8,128)S(1)}, u32[]{:S(2)}, u32[]{:S(2)}) collective-permute-start(f32[64,768]{1,0:T(8,128)S(1)} %get-tuple-element.14), channel_id=1, source_target_pairs={{0,16},{4,20},{8,24},{12,28},{16,0},{20,4},{24,8},{28,12},{32,48},... | collective-permute-start | bytes 589832 | tf_op jit(solution)/shard_map/ppermute | solution.py:71
  14.0 1.4 collective-permute-start.4
  15.4 2.4 %collective-permute-done.2 = f32[64,768]{1,0:T(8,128)S(1)} collective-permute-done((f32[64,768]{1,0:T(8,128)S(1)}, f32[64,768]{1,0:T(8,128)S(1)}, u32[]{:S(2)}, u32[]{:S(2)}) %collective-permute-start.2) | collective-permute-done | bytes 196640 | tf_op jit(solution)/shard_map/ppermute | solution.py:71
  17.8 5.3 %collective-permute-done.3 = f32[64,768]{1,0:T(8,128)S(1)} collective-permute-done((f32[64,768]{1,0:T(8,128)S(1)}, f32[64,768]{1,0:T(8,128)S(1)}, u32[]{:S(2)}, u32[]{:S(2)}) %collective-permute-start.3) | collective-permute-done | bytes 196640 | tf_op jit(solution)/shard_map/ppermute | solution.py:71
  23.2 4.7 %collective-permute-start.5 = (f32[64,768]{1,0:T(8,128)S(1)}, f32[64,768]{1,0:T(8,128)S(1)}, u32[]{:S(2)}, u32[]{:S(2)}) collective-permute-start(f32[64,768]{1,0:T(8,128)S(1)} %reduce_sum.153), channel_id=1, source_target_pairs={{0,32},{4,36},{8,40},{12,44},{16,48},{20,52},{24,56},{28,60},{32,6... | collective-permute-start | bytes 589832 | tf_op jit(solution)/shard_map/ppermute | solution.py:71
  27.9 4.8 %collective-permute-start.6 = (f32[64,768]{1,0:T(8,128)S(1)}, f32[64,768]{1,0:T(8,128)S(1)}, u32[]{:S(2)}, u32[]{:S(2)}) collective-permute-start(f32[64,768]{1,0:T(8,128)S(1)} %reduce_sum.153), channel_id=1, source_target_pairs={{0,64},{4,68},{8,72},{12,76},{16,80},{20,84},{24,88},{28,92},{32,9... | collective-permute-start | bytes 589832 | tf_op jit(solution)/shard_map/ppermute | solution.py:71
  32.7 1.9 collective-permute-start.7
  34.7 1.4 collective-permute-done.5
  36.1 4.9 %collective-permute-done.6 = f32[64,768]{1,0:T(8,128)S(1)} collective-permute-done((f32[64,768]{1,0:T(8,128)S(1)}, f32[64,768]{1,0:T(8,128)S(1)}, u32[]{:S(2)}, u32[]{:S(2)}) %collective-permute-start.6) | collective-permute-done | bytes 196640 | tf_op jit(solution)/shard_map/ppermute | solution.py:71
  41.3 1.4 collective-permute-done.8
  42.8 2.5 %collective-permute-start.9 = (f32[64,2]{0,1:T(2,128)S(1)}, f32[64,2]{0,1:T(2,128)S(1)}, u32[]{:S(2)}, u32[]{:S(2)}) collective-permute-start(f32[64,2]{0,1:T(2,128)S(1)} %pad_maximum_fusion.3), channel_id=1, source_target_pairs={{0,1},{1,2},{2,3},{3,0},{4,5},{5,6},{6,7},{7,4},{8,9},{9,10},{10,1... | collective-permute-start | bytes 1544 | tf_op jit(solution)/shard_map/ppermute | solution.py:71
  45.3 2.5 %collective-permute-start.10 = (f32[64,2]{0,1:T(2,128)S(1)}, f32[64,2]{0,1:T(2,128)S(1)}, u32[]{:S(2)}, u32[]{:S(2)}) collective-permute-start(f32[64,2]{0,1:T(2,128)S(1)} %pad_maximum_fusion.3), channel_id=1, source_target_pairs={{0,2},{1,3},{2,0},{3,1},{4,6},{5,7},{6,4},{7,5},{8,10},{9,11},{10,... | collective-permute-start | bytes 1544 | tf_op jit(solution)/shard_map/ppermute | solution.py:71
  47.7 1.5 collective-permute-start.11
  51.9 5.5 %fusion.28 = (f32[4,4,16]{2,1,0:T(4,128)S(1)}, f32[4,4,16,4096]{3,2,1,0:T(8,128)}) fusion(bf16[4096,512,1,1]{1,0,3,2:T(8,128)(2,1)} %bitcast.216, pred[4,512]{1,0:T(4,128)(4,1)S(1)} %iota_compare_fusion.1, bf16[4,16,512]{2,1,0:T(8,128)(2,1)S(1)} %convert_element_type.52, pred[16,4096]{1,0:T(8,128)(4,1)S(1)} %fusion.9), kind=kOutput, calls=%fused_computation.126 | convolution fusion | flops 1077018368 | bytes 8522752 | tf_op jit(solution)/shard_map/dot_general | solution.py:255
  57.4 3.4 %fusion.2 = (bf16[4,4,16,4096]{3,2,1,0:T(8,128)(2,1)S(1)}, f32[4,4,16]{2,1,0:T(4,128)S(1)}) fusion(f32[4,4,16,4096]{3,2,1,0:T(8,128)} %get-tuple-element.36, f32[4,4,16]{2,1,0:T(4,128)S(1)} %get-tuple-element.35, pred[16,4096]{1,0:T(8,128)(4,1)S(1)} %fusion.9), kind=kLoop, calls=%fused_computation.4 | loop fusion | flops 4194048 | bytes 6359040 | tf_op jit(solution)/shard_map/convert_element_type | solution.py:266
  60.9 1.2 convolution_bitcast_fusion
  64.0 6.7 %all-to-all-start = ((f32[32,1,1152]{2,1,0:T(1,128)}), f32[32,1,1152]{2,1,0:T(1,128)S(1)}, u32[]{:S(2)}, u32[]{:S(2)}) async-start(f32[32,1,1152]{2,1,0:T(1,128)} %reshape.356), calls=%async_computation | async-start | bytes 294912 | tf_op jit(solution)/shard_map/all_to_all | solution.py:283
  71.6 7.1 %all-to-all-done = f32[32,1,1152]{2,1,0:T(1,128)S(1)} async-done(((f32[32,1,1152]{2,1,0:T(1,128)}), f32[32,1,1152]{2,1,0:T(1,128)S(1)}, u32[]{:S(2)}, u32[]{:S(2)}) %all-to-all-start) | async-done | bytes 147488 | tf_op jit(solution)/shard_map/all_to_all | solution.py:283
  79.2 1.0 reduce.1
  82.5 5.2 %collective-permute-start.13 = (bf16[64,16]{0,1:T(8,128)(2,1)S(1)}, bf16[64,16]{0,1:T(8,128)(2,1)S(1)}, u32[]{:S(2)}, u32[]{:S(2)}) collective-permute-start(bf16[64,16]{0,1:T(8,128)(2,1)S(1)} %copy.116), channel_id=1, source_target_pairs={{0,1},{1,33},{2,65},{3,97},{4,2},{5,34},{6,66},{7,98},{8,3},{9,35}... | collective-permute-start | bytes 6152 | tf_op jit(solution)/shard_map/ppermute | solution.py:157
  87.7 4.1 %collective-permute-start.14 = (bf16[64,16]{0,1:T(8,128)(2,1)S(1)}, bf16[64,16]{0,1:T(8,128)(2,1)S(1)}, u32[]{:S(2)}, u32[]{:S(2)}) collective-permute-start(bf16[64,16]{0,1:T(8,128)(2,1)S(1)} %copy.116), channel_id=1, source_target_pairs={{0,2},{1,34},{2,66},{3,98},{4,3},{5,35},{6,67},{7,99},{8,0},{9,32}... | collective-permute-start | bytes 6152 | tf_op jit(solution)/shard_map/ppermute | solution.py:157
  91.8 3.6 %collective-permute-start.15 = (bf16[64,16]{0,1:T(8,128)(2,1)S(1)}, bf16[64,16]{0,1:T(8,128)(2,1)S(1)}, u32[]{:S(2)}, u32[]{:S(2)}) collective-permute-start(bf16[64,16]{0,1:T(8,128)(2,1)S(1)} %copy.116), channel_id=1, source_target_pairs={{0,3},{1,35},{2,67},{3,99},{4,0},{5,32},{6,64},{7,96},{8,1},{9,33}... | collective-permute-start | bytes 6152 | tf_op jit(solution)/shard_map/ppermute | solution.py:157
  95.5 1.2 collective-permute-done.15
  96.9 2.8 %collective-permute-start.16 = (f32[64,256]{1,0:T(8,128)S(1)}, f32[64,256]{1,0:T(8,128)S(1)}, u32[]{:S(2)}, u32[]{:S(2)}) collective-permute-start(f32[64,256]{1,0:T(8,128)S(1)} %constant_dynamic-slice_fusion.1), channel_id=1, source_target_pairs={{0,4},{4,0},{8,12},{12,8},{16,20},{20,16},{24,28},{28,24},{32,36},... | collective-permute-start | bytes 196616 | tf_op jit(solution)/shard_map/ppermute | solution.py:83
  101.3 1.0 copy.112
  102.3 12.7 %all-to-all-start.1 = ((bf16[64,32,128]{2,0,1:T(8,128)(2,1)}), bf16[64,32,128]{2,0,1:T(8,128)(2,1)S(1)}, u32[]{:S(2)}, u32[]{:S(2)}) async-start(bf16[64,32,128]{2,0,1:T(8,128)(2,1)} %copy.112), calls=%async_computation.1 | async-start | bytes 1048576 | tf_op jit(solution)/shard_map/all_to_all | solution.py:167
  115.0 3.4 %collective-permute-start.18 = (f32[64,256]{1,0:T(8,128)S(1)}, f32[64,256]{1,0:T(8,128)S(1)}, u32[]{:S(2)}, u32[]{:S(2)}) collective-permute-start(f32[64,256]{1,0:T(8,128)S(1)} %get-tuple-element.10), channel_id=1, source_target_pairs={{0,16},{4,20},{8,24},{12,28},{16,0},{20,4},{24,8},{28,12},{32,48},... | collective-permute-start | bytes 196616 | tf_op jit(solution)/shard_map/ppermute | solution.py:71
  118.4 1.2 collective-permute-start.19
  119.6 6.8 %collective-permute-done.18 = f32[64,256]{1,0:T(8,128)S(1)} collective-permute-done((f32[64,256]{1,0:T(8,128)S(1)}, f32[64,256]{1,0:T(8,128)S(1)}, u32[]{:S(2)}, u32[]{:S(2)}) %collective-permute-start.18) | collective-permute-done | bytes 65568 | tf_op jit(solution)/shard_map/ppermute | solution.py:71
  126.4 1.5 collective-permute-start.20
  128.0 2.7 %collective-permute-start.21 = (f32[64,256]{1,0:T(8,128)S(1)}, f32[64,256]{1,0:T(8,128)S(1)}, u32[]{:S(2)}, u32[]{:S(2)}) collective-permute-start(f32[64,256]{1,0:T(8,128)S(1)} %reduce_sum.162), channel_id=1, source_target_pairs={{0,64},{4,68},{8,72},{12,76},{16,80},{20,84},{24,88},{28,92},{32,9... | collective-permute-start | bytes 196616 | tf_op jit(solution)/shard_map/ppermute | solution.py:71
  130.7 1.4 collective-permute-start.22
  132.7 1.0 collective-permute-done.21
  133.8 1.2 collective-permute-done.22
  135.2 1.2 collective-permute-done.23
  136.5 1.2 collective-permute-start.24
  137.7 1.7 collective-permute-start.25
  139.4 2.5 %collective-permute-start.26 = (f32[64]{0:T(128)S(1)}, f32[64]{0:T(128)S(1)}, u32[]{:S(2)}, u32[]{:S(2)}) collective-permute-start(f32[64]{0:T(128)S(1)} %multiply_reduce_fusion.1), channel_id=1, source_target_pairs={{0,3},{1,0},{2,1},{3,2},{4,7},{5,4},{6,5},{7,6},{8,11},{9,8},{10,9... | collective-permute-start | bytes 776 | tf_op jit(solution)/shard_map/ppermute | solution.py:71
  143.4 1.2 collective-permute-start.27
  144.6 3.8 %collective-permute-start.28 = (bf16[64,512]{1,0:T(8,128)(2,1)S(1)}, bf16[64,512]{1,0:T(8,128)(2,1)S(1)}, u32[]{:S(2)}, u32[]{:S(2)}) collective-permute-start(bf16[64,512]{1,0:T(8,128)(2,1)S(1)} %add_convert_fusion.1), channel_id=1, source_target_pairs={{0,2},{1,3},{2,0},{3,1},{4,6},{5,7},{6,4},{7,5},{8,10},{9,11},{10,... | collective-permute-start | bytes 196616 | tf_op jit(solution)/shard_map/ppermute | solution.py:71
  148.6 1.1 dynamic_update_slice.199
  149.9 1.5 collective-permute-done.28
  151.5 1.2 collective-permute-done.29
  152.8 1.1 dynamic_update_slice.200
  153.9 1.1 dynamic_update_slice.201
  155.1 1.1 dynamic_update_slice.202
  157.5 5.2 %collective-permute-start.31 = (bf16[64,64]{1,0:T(8,128)(2,1)S(1)}, bf16[64,64]{1,0:T(8,128)(2,1)S(1)}, u32[]{:S(2)}, u32[]{:S(2)}) collective-permute-start(bf16[64,64]{1,0:T(8,128)(2,1)S(1)} %fusion.3), channel_id=1, source_target_pairs={{0,1},{1,33},{2,65},{3,97},{4,2},{5,34},{6,66},{7,98},{8,3},{9,35}... | collective-permute-start | bytes 24584 | tf_op jit(solution)/shard_map/ppermute | solution.py:157
  162.8 5.6 %collective-permute-start.32 = (bf16[64,64]{1,0:T(8,128)(2,1)S(1)}, bf16[64,64]{1,0:T(8,128)(2,1)S(1)}, u32[]{:S(2)}, u32[]{:S(2)}) collective-permute-start(bf16[64,64]{1,0:T(8,128)(2,1)S(1)} %fusion.3), channel_id=1, source_target_pairs={{0,2},{1,34},{2,66},{3,98},{4,3},{5,35},{6,67},{7,99},{8,0},{9,32}... | collective-permute-start | bytes 24584 | tf_op jit(solution)/shard_map/ppermute | solution.py:157
  168.4 2.3 %collective-permute-start.33 = (bf16[64,64]{1,0:T(8,128)(2,1)S(1)}, bf16[64,64]{1,0:T(8,128)(2,1)S(1)}, u32[]{:S(2)}, u32[]{:S(2)}) collective-permute-start(bf16[64,64]{1,0:T(8,128)(2,1)S(1)} %fusion.3), channel_id=1, source_target_pairs={{0,3},{1,35},{2,67},{3,99},{4,0},{5,32},{6,64},{7,96},{8,1},{9,33}... | collective-permute-start | bytes 24584 | tf_op jit(solution)/shard_map/ppermute | solution.py:157
  172.7 2.8 %collective-permute-start.34 = (f32[64,256]{1,0:T(8,128)S(1)}, f32[64,256]{1,0:T(8,128)S(1)}, u32[]{:S(2)}, u32[]{:S(2)}) collective-permute-start(f32[64,256]{1,0:T(8,128)S(1)} %constant_dynamic-slice_fusion), channel_id=1, source_target_pairs={{0,4},{4,0},{8,12},{12,8},{16,20},{20,16},{24,28},{28,24},{32,36},... | collective-permute-start | bytes 196616 | tf_op jit(solution)/shard_map/ppermute | solution.py:83
  176.8 5.0 %collective-permute-start.36 = (f32[64,256]{1,0:T(8,128)S(1)}, f32[64,256]{1,0:T(8,128)S(1)}, u32[]{:S(2)}, u32[]{:S(2)}) collective-permute-start(f32[64,256]{1,0:T(8,128)S(1)} %get-tuple-element.8), channel_id=1, source_target_pairs={{0,16},{4,20},{8,24},{12,28},{16,0},{20,4},{24,8},{28,12},{32,48},... | collective-permute-start | bytes 196616 | tf_op jit(solution)/shard_map/ppermute | solution.py:71
  181.8 2.3 %collective-permute-start.37 = (f32[64,256]{1,0:T(8,128)S(1)}, f32[64,256]{1,0:T(8,128)S(1)}, u32[]{:S(2)}, u32[]{:S(2)}) collective-permute-start(f32[64,256]{1,0:T(8,128)S(1)} %get-tuple-element.8), channel_id=1, source_target_pairs={{0,24},{4,28},{8,0},{12,4},{16,8},{20,12},{24,16},{28,20},{32,56},... | collective-permute-start | bytes 196616 | tf_op jit(solution)/shard_map/ppermute | solution.py:71
  184.1 1.2 collective-permute-done.36
  186.1 2.5 %collective-permute-start.38 = (f32[64,256]{1,0:T(8,128)S(1)}, f32[64,256]{1,0:T(8,128)S(1)}, u32[]{:S(2)}, u32[]{:S(2)}) collective-permute-start(f32[64,256]{1,0:T(8,128)S(1)} %reduce_sum.166), channel_id=1, source_target_pairs={{0,32},{4,36},{8,40},{12,44},{16,48},{20,52},{24,56},{28,60},{32,6... | collective-permute-start | bytes 196616 | tf_op jit(solution)/shard_map/ppermute | solution.py:71
  188.6 4.7 %collective-permute-start.39 = (f32[64,256]{1,0:T(8,128)S(1)}, f32[64,256]{1,0:T(8,128)S(1)}, u32[]{:S(2)}, u32[]{:S(2)}) collective-permute-start(f32[64,256]{1,0:T(8,128)S(1)} %reduce_sum.166), channel_id=1, source_target_pairs={{0,64},{4,68},{8,72},{12,76},{16,80},{20,84},{24,88},{28,92},{32,9... | collective-permute-start | bytes 196616 | tf_op jit(solution)/shard_map/ppermute | solution.py:71
  193.3 1.6 collective-permute-start.40
  194.9 1.3 collective-permute-done.39
  196.3 1.3 collective-permute-done.40
  197.7 1.2 collective-permute-done.41
  199.6 1.1 collective-permute-start.43
  200.7 2.1 %collective-permute-start.44 = (f32[64]{0:T(128)S(1)}, f32[64]{0:T(128)S(1)}, u32[]{:S(2)}, u32[]{:S(2)}) collective-permute-start(f32[64]{0:T(128)S(1)} %multiply_reduce_fusion), channel_id=1, source_target_pairs={{0,3},{1,0},{2,1},{3,2},{4,7},{5,4},{6,5},{7,6},{8,11},{9,8},{10,9... | collective-permute-start | bytes 776 | tf_op jit(solution)/shard_map/ppermute | solution.py:71
  202.9 1.0 collective-permute-done.42
  (230 shorter events, 28.7 us)
Async XLA Ops:
  0.0 172.5 %copy-start = (bf16[256,512]{1,0:T(8,128)(2,1)S(1)}, bf16[256,512]{1,0:T(8,128)(2,1)}, u32[]{:S(2)}) copy-start(bf16[256,512]{1,0:T(8,128)(2,1)} %param.24) | copy-start | bytes 786436
  0.8 4.1 %collective-permute-start = (bf16[64,64]{1,0:T(8,128)(2,1)S(1)}, bf16[64,64]{1,0:T(8,128)(2,1)S(1)}, u32[]{:S(2)}, u32[]{:S(2)}) collective-permute-start(bf16[64,64]{1,0:T(8,128)(2,1)S(1)} %constant_dynamic-slice_fusion.5), channel_id=1, source_target_pairs={{0,0},{1,32},{2,64},{3,96},{4,4},{5,36},{6,68},{7,100},{8,8},{9,40... | collective-permute-start | bytes 24584 | tf_op jit(solution)/shard_map/ppermute | solution.py:47
  7.9 1.5 collective-permute-start.1
  9.5 41.8 %copy-start.5 = (f32[512]{0:T(512)S(1)}, f32[512]{0:T(512)}, u32[]{:S(2)}) copy-start(f32[512]{0:T(512)} %param.26) | copy-start | bytes 6148
  9.5 41.8 %copy-start.6 = (f32[512]{0:T(512)S(1)}, f32[512]{0:T(512)}, u32[]{:S(2)}) copy-start(f32[512]{0:T(512)} %param.25) | copy-start | bytes 6148
  9.6 8.2 %collective-permute-start.2 = (f32[64,768]{1,0:T(8,128)S(1)}, f32[64,768]{1,0:T(8,128)S(1)}, u32[]{:S(2)}, u32[]{:S(2)}) collective-permute-start(f32[64,768]{1,0:T(8,128)S(1)} %get-tuple-element.14), channel_id=1, source_target_pairs={{0,8},{4,12},{8,16},{12,20},{16,24},{20,28},{24,0},{28,4},{32,40},... | collective-permute-start | bytes 589832 | tf_op jit(solution)/shard_map/ppermute | solution.py:71
  11.3 11.9 %collective-permute-start.3 = (f32[64,768]{1,0:T(8,128)S(1)}, f32[64,768]{1,0:T(8,128)S(1)}, u32[]{:S(2)}, u32[]{:S(2)}) collective-permute-start(f32[64,768]{1,0:T(8,128)S(1)} %get-tuple-element.14), channel_id=1, source_target_pairs={{0,16},{4,20},{8,24},{12,28},{16,0},{20,4},{24,8},{28,12},{32,48},... | collective-permute-start | bytes 589832 | tf_op jit(solution)/shard_map/ppermute | solution.py:71
  14.0 9.1 %collective-permute-start.4 = (f32[64,768]{1,0:T(8,128)S(1)}, f32[64,768]{1,0:T(8,128)S(1)}, u32[]{:S(2)}, u32[]{:S(2)}) collective-permute-start(f32[64,768]{1,0:T(8,128)S(1)} %get-tuple-element.14), channel_id=1, source_target_pairs={{0,24},{4,28},{8,0},{12,4},{16,8},{20,12},{24,16},{28,20},{32,56},... | collective-permute-start | bytes 589832 | tf_op jit(solution)/shard_map/ppermute | solution.py:71
  23.2 12.9 %collective-permute-start.5 = (f32[64,768]{1,0:T(8,128)S(1)}, f32[64,768]{1,0:T(8,128)S(1)}, u32[]{:S(2)}, u32[]{:S(2)}) collective-permute-start(f32[64,768]{1,0:T(8,128)S(1)} %reduce_sum.153), channel_id=1, source_target_pairs={{0,32},{4,36},{8,40},{12,44},{16,48},{20,52},{24,56},{28,60},{32,6... | collective-permute-start | bytes 589832 | tf_op jit(solution)/shard_map/ppermute | solution.py:71
  27.9 13.1 %collective-permute-start.6 = (f32[64,768]{1,0:T(8,128)S(1)}, f32[64,768]{1,0:T(8,128)S(1)}, u32[]{:S(2)}, u32[]{:S(2)}) collective-permute-start(f32[64,768]{1,0:T(8,128)S(1)} %reduce_sum.153), channel_id=1, source_target_pairs={{0,64},{4,68},{8,72},{12,76},{16,80},{20,84},{24,88},{28,92},{32,9... | collective-permute-start | bytes 589832 | tf_op jit(solution)/shard_map/ppermute | solution.py:71
  32.7 8.3 %collective-permute-start.7 = (f32[64,768]{1,0:T(8,128)S(1)}, f32[64,768]{1,0:T(8,128)S(1)}, u32[]{:S(2)}, u32[]{:S(2)}) collective-permute-start(f32[64,768]{1,0:T(8,128)S(1)} %reduce_sum.153), channel_id=1, source_target_pairs={{0,96},{4,100},{8,104},{12,108},{16,112},{20,116},{24,120},{28,124... | collective-permute-start | bytes 589832 | tf_op jit(solution)/shard_map/ppermute | solution.py:71
  41.1 1.5 collective-permute-start.8
  42.8 6.8 %collective-permute-start.9 = (f32[64,2]{0,1:T(2,128)S(1)}, f32[64,2]{0,1:T(2,128)S(1)}, u32[]{:S(2)}, u32[]{:S(2)}) collective-permute-start(f32[64,2]{0,1:T(2,128)S(1)} %pad_maximum_fusion.3), channel_id=1, source_target_pairs={{0,1},{1,2},{2,3},{3,0},{4,5},{5,6},{6,7},{7,4},{8,9},{9,10},{10,1... | collective-permute-start | bytes 1544 | tf_op jit(solution)/shard_map/ppermute | solution.py:71
  45.3 5.1 %collective-permute-start.10 = (f32[64,2]{0,1:T(2,128)S(1)}, f32[64,2]{0,1:T(2,128)S(1)}, u32[]{:S(2)}, u32[]{:S(2)}) collective-permute-start(f32[64,2]{0,1:T(2,128)S(1)} %pad_maximum_fusion.3), channel_id=1, source_target_pairs={{0,2},{1,3},{2,0},{3,1},{4,6},{5,7},{6,4},{7,5},{8,10},{9,11},{10,... | collective-permute-start | bytes 1544 | tf_op jit(solution)/shard_map/ppermute | solution.py:71
  47.7 3.6 %collective-permute-start.11 = (f32[64,2]{0,1:T(2,128)S(1)}, f32[64,2]{0,1:T(2,128)S(1)}, u32[]{:S(2)}, u32[]{:S(2)}) collective-permute-start(f32[64,2]{0,1:T(2,128)S(1)} %pad_maximum_fusion.3), channel_id=1, source_target_pairs={{0,3},{1,0},{2,1},{3,2},{4,7},{5,4},{6,5},{7,6},{8,11},{9,8},{10,9... | collective-permute-start | bytes 1544 | tf_op jit(solution)/shard_map/ppermute | solution.py:71
  57.4 3.5 %copy-start.9 = (bf16[16,256,512]{2,1,0:T(8,128)(2,1)S(1)}, bf16[16,256,512]{2,1,0:T(8,128)(2,1)}, u32[]{:S(2)}) copy-start(bf16[16,256,512]{2,1,0:T(8,128)(2,1)} %param.30) | copy-start | bytes 12582916
  62.1 34.6 %copy-start.4 = (bf16[64,512]{1,0:T(8,128)(2,1)S(1)}, bf16[64,512]{1,0:T(8,128)(2,1)}, u32[]{:S(2)}) copy-start(bf16[64,512]{1,0:T(8,128)(2,1)} %param.21) | copy-start | bytes 196612
  62.2 37.6 %copy-start.1 = (bf16[64,2048]{1,0:T(8,128)(2,1)S(1)}, bf16[64,2048]{1,0:T(8,128)(2,1)}, u32[]{:S(2)}) copy-start(bf16[64,2048]{1,0:T(8,128)(2,1)} %param.22) | copy-start | bytes 786436
  62.2 38.1 %copy-start.2 = (bf16[64,2048]{1,0:T(8,128)(2,1)S(1)}, bf16[64,2048]{1,0:T(8,128)(2,1)}, u32[]{:S(2)}) copy-start(bf16[64,2048]{1,0:T(8,128)(2,1)} %param.23) | copy-start | bytes 786436
  64.0 14.7 %all-to-all-start = ((f32[32,1,1152]{2,1,0:T(1,128)}), f32[32,1,1152]{2,1,0:T(1,128)S(1)}, u32[]{:S(2)}, u32[]{:S(2)}) async-start(f32[32,1,1152]{2,1,0:T(1,128)} %reshape.356), calls=%async_computation | async-start | bytes 294912 | tf_op jit(solution)/shard_map/all_to_all | solution.py:283
  81.7 13.7 %collective-permute-start.12 = (bf16[64,16]{0,1:T(8,128)(2,1)S(1)}, bf16[64,16]{0,1:T(8,128)(2,1)S(1)}, u32[]{:S(2)}, u32[]{:S(2)}) collective-permute-start(bf16[64,16]{0,1:T(8,128)(2,1)S(1)} %copy.116), channel_id=1, source_target_pairs={{0,0},{1,32},{2,64},{3,96},{4,1},{5,33},{6,65},{7,97},{8,2},{9,34}... | collective-permute-start | bytes 6152 | tf_op jit(solution)/shard_map/ppermute | solution.py:157
  82.5 13.0 %collective-permute-start.13 = (bf16[64,16]{0,1:T(8,128)(2,1)S(1)}, bf16[64,16]{0,1:T(8,128)(2,1)S(1)}, u32[]{:S(2)}, u32[]{:S(2)}) collective-permute-start(bf16[64,16]{0,1:T(8,128)(2,1)S(1)} %copy.116), channel_id=1, source_target_pairs={{0,1},{1,33},{2,65},{3,97},{4,2},{5,34},{6,66},{7,98},{8,3},{9,35}... | collective-permute-start | bytes 6152 | tf_op jit(solution)/shard_map/ppermute | solution.py:157
  87.7 7.8 %collective-permute-start.14 = (bf16[64,16]{0,1:T(8,128)(2,1)S(1)}, bf16[64,16]{0,1:T(8,128)(2,1)S(1)}, u32[]{:S(2)}, u32[]{:S(2)}) collective-permute-start(bf16[64,16]{0,1:T(8,128)(2,1)S(1)} %copy.116), channel_id=1, source_target_pairs={{0,2},{1,34},{2,66},{3,98},{4,3},{5,35},{6,67},{7,99},{8,0},{9,32}... | collective-permute-start | bytes 6152 | tf_op jit(solution)/shard_map/ppermute | solution.py:157
  91.8 4.9 %collective-permute-start.15 = (bf16[64,16]{0,1:T(8,128)(2,1)S(1)}, bf16[64,16]{0,1:T(8,128)(2,1)S(1)}, u32[]{:S(2)}, u32[]{:S(2)}) collective-permute-start(bf16[64,16]{0,1:T(8,128)(2,1)S(1)} %copy.116), channel_id=1, source_target_pairs={{0,3},{1,35},{2,67},{3,99},{4,0},{5,32},{6,64},{7,96},{8,1},{9,33}... | collective-permute-start | bytes 6152 | tf_op jit(solution)/shard_map/ppermute | solution.py:157
  96.9 46.4 %copy-start.3 = (bf16[4,16,512]{2,1,0:T(8,128)(2,1)S(1)}, bf16[4,16,512]{2,1,0:T(8,128)(2,1)}, u32[]{:S(2)}) copy-start(bf16[4,16,512]{2,1,0:T(8,128)(2,1)} %param.17) | copy-start | bytes 196612
  96.9 46.4 %copy-start.7 = (f32[512]{0:T(512)S(1)}, f32[512]{0:T(512)}, u32[]{:S(2)}) copy-start(f32[512]{0:T(512)} %param.27) | copy-start | bytes 6148
  96.9 3.9 %collective-permute-start.16 = (f32[64,256]{1,0:T(8,128)S(1)}, f32[64,256]{1,0:T(8,128)S(1)}, u32[]{:S(2)}, u32[]{:S(2)}) collective-permute-start(f32[64,256]{1,0:T(8,128)S(1)} %constant_dynamic-slice_fusion.1), channel_id=1, source_target_pairs={{0,4},{4,0},{8,12},{12,8},{16,20},{20,16},{24,28},{28,24},{32,36},... | collective-permute-start | bytes 196616 | tf_op jit(solution)/shard_map/ppermute | solution.py:83
  100.9 18.7 %collective-permute-start.17 = (f32[64,256]{1,0:T(8,128)S(1)}, f32[64,256]{1,0:T(8,128)S(1)}, u32[]{:S(2)}, u32[]{:S(2)}) collective-permute-start(f32[64,256]{1,0:T(8,128)S(1)} %get-tuple-element.10), channel_id=1, source_target_pairs={{0,8},{4,12},{8,16},{12,20},{16,24},{20,28},{24,0},{28,4},{32,40},... | collective-permute-start | bytes 196616 | tf_op jit(solution)/shard_map/ppermute | solution.py:71
  102.3 54.0 %all-to-all-start.1 = ((bf16[64,32,128]{2,0,1:T(8,128)(2,1)}), bf16[64,32,128]{2,0,1:T(8,128)(2,1)S(1)}, u32[]{:S(2)}, u32[]{:S(2)}) async-start(bf16[64,32,128]{2,0,1:T(8,128)(2,1)} %copy.112), calls=%async_computation.1 | async-start | bytes 1048576 | tf_op jit(solution)/shard_map/all_to_all | solution.py:167
  115.0 11.4 %collective-permute-start.18 = (f32[64,256]{1,0:T(8,128)S(1)}, f32[64,256]{1,0:T(8,128)S(1)}, u32[]{:S(2)}, u32[]{:S(2)}) collective-permute-start(f32[64,256]{1,0:T(8,128)S(1)} %get-tuple-element.10), channel_id=1, source_target_pairs={{0,16},{4,20},{8,24},{12,28},{16,0},{20,4},{24,8},{28,12},{32,48},... | collective-permute-start | bytes 196616 | tf_op jit(solution)/shard_map/ppermute | solution.py:71
  118.4 8.0 %collective-permute-start.19 = (f32[64,256]{1,0:T(8,128)S(1)}, f32[64,256]{1,0:T(8,128)S(1)}, u32[]{:S(2)}, u32[]{:S(2)}) collective-permute-start(f32[64,256]{1,0:T(8,128)S(1)} %get-tuple-element.10), channel_id=1, source_target_pairs={{0,24},{4,28},{8,0},{12,4},{16,8},{20,12},{24,16},{28,20},{32,56},... | collective-permute-start | bytes 196616 | tf_op jit(solution)/shard_map/ppermute | solution.py:71
  126.4 6.2 %collective-permute-start.20 = (f32[64,256]{1,0:T(8,128)S(1)}, f32[64,256]{1,0:T(8,128)S(1)}, u32[]{:S(2)}, u32[]{:S(2)}) collective-permute-start(f32[64,256]{1,0:T(8,128)S(1)} %reduce_sum.162), channel_id=1, source_target_pairs={{0,32},{4,36},{8,40},{12,44},{16,48},{20,52},{24,56},{28,60},{32,6... | collective-permute-start | bytes 196616 | tf_op jit(solution)/shard_map/ppermute | solution.py:71
  128.0 5.8 %collective-permute-start.21 = (f32[64,256]{1,0:T(8,128)S(1)}, f32[64,256]{1,0:T(8,128)S(1)}, u32[]{:S(2)}, u32[]{:S(2)}) collective-permute-start(f32[64,256]{1,0:T(8,128)S(1)} %reduce_sum.162), channel_id=1, source_target_pairs={{0,64},{4,68},{8,72},{12,76},{16,80},{20,84},{24,88},{28,92},{32,9... | collective-permute-start | bytes 196616 | tf_op jit(solution)/shard_map/ppermute | solution.py:71
  130.7 4.3 %collective-permute-start.22 = (f32[64,256]{1,0:T(8,128)S(1)}, f32[64,256]{1,0:T(8,128)S(1)}, u32[]{:S(2)}, u32[]{:S(2)}) collective-permute-start(f32[64,256]{1,0:T(8,128)S(1)} %reduce_sum.162), channel_id=1, source_target_pairs={{0,96},{4,100},{8,104},{12,108},{16,112},{20,116},{24,120},{28,124... | collective-permute-start | bytes 196616 | tf_op jit(solution)/shard_map/ppermute | solution.py:71
  135.0 1.3 collective-permute-start.23
  136.5 68.4 %copy-start.8 = (f32[512]{0:T(512)S(1)}, f32[512]{0:T(512)}, u32[]{:S(2)}) copy-start(f32[512]{0:T(512)} %param.28) | copy-start | bytes 6148
  136.5 5.5 %collective-permute-start.24 = (f32[64]{0:T(128)S(1)}, f32[64]{0:T(128)S(1)}, u32[]{:S(2)}, u32[]{:S(2)}) collective-permute-start(f32[64]{0:T(128)S(1)} %multiply_reduce_fusion.1), channel_id=1, source_target_pairs={{0,1},{1,2},{2,3},{3,0},{4,5},{5,6},{6,7},{7,4},{8,9},{9,10},{10,1... | collective-permute-start | bytes 776 | tf_op jit(solution)/shard_map/ppermute | solution.py:71
  137.7 5.1 %collective-permute-start.25 = (f32[64]{0:T(128)S(1)}, f32[64]{0:T(128)S(1)}, u32[]{:S(2)}, u32[]{:S(2)}) collective-permute-start(f32[64]{0:T(128)S(1)} %multiply_reduce_fusion.1), channel_id=1, source_target_pairs={{0,2},{1,3},{2,0},{3,1},{4,6},{5,7},{6,4},{7,5},{8,10},{9,11},{10,... | collective-permute-start | bytes 776 | tf_op jit(solution)/shard_map/ppermute | solution.py:71
  139.4 3.8 %collective-permute-start.26 = (f32[64]{0:T(128)S(1)}, f32[64]{0:T(128)S(1)}, u32[]{:S(2)}, u32[]{:S(2)}) collective-permute-start(f32[64]{0:T(128)S(1)} %multiply_reduce_fusion.1), channel_id=1, source_target_pairs={{0,3},{1,0},{2,1},{3,2},{4,7},{5,4},{6,5},{7,6},{8,11},{9,8},{10,9... | collective-permute-start | bytes 776 | tf_op jit(solution)/shard_map/ppermute | solution.py:71
  143.4 6.3 %collective-permute-start.27 = (bf16[64,512]{1,0:T(8,128)(2,1)S(1)}, bf16[64,512]{1,0:T(8,128)(2,1)S(1)}, u32[]{:S(2)}, u32[]{:S(2)}) collective-permute-start(bf16[64,512]{1,0:T(8,128)(2,1)S(1)} %add_convert_fusion.1), channel_id=1, source_target_pairs={{0,1},{1,2},{2,3},{3,0},{4,5},{5,6},{6,7},{7,4},{8,9},{9,10},{10,1... | collective-permute-start | bytes 196616 | tf_op jit(solution)/shard_map/ppermute | solution.py:71
  144.6 6.7 %collective-permute-start.28 = (bf16[64,512]{1,0:T(8,128)(2,1)S(1)}, bf16[64,512]{1,0:T(8,128)(2,1)S(1)}, u32[]{:S(2)}, u32[]{:S(2)}) collective-permute-start(bf16[64,512]{1,0:T(8,128)(2,1)S(1)} %add_convert_fusion.1), channel_id=1, source_target_pairs={{0,2},{1,3},{2,0},{3,1},{4,6},{5,7},{6,4},{7,5},{8,10},{9,11},{10,... | collective-permute-start | bytes 196616 | tf_op jit(solution)/shard_map/ppermute | solution.py:71
  148.4 4.3 %collective-permute-start.29 = (bf16[64,512]{1,0:T(8,128)(2,1)S(1)}, bf16[64,512]{1,0:T(8,128)(2,1)S(1)}, u32[]{:S(2)}, u32[]{:S(2)}) collective-permute-start(bf16[64,512]{1,0:T(8,128)(2,1)S(1)} %add_convert_fusion.1), channel_id=1, source_target_pairs={{0,3},{1,0},{2,1},{3,2},{4,7},{5,4},{6,5},{7,6},{8,11},{9,8},{10,9... | collective-permute-start | bytes 196616 | tf_op jit(solution)/shard_map/ppermute | solution.py:71
  156.9 13.9 %collective-permute-start.30 = (bf16[64,64]{1,0:T(8,128)(2,1)S(1)}, bf16[64,64]{1,0:T(8,128)(2,1)S(1)}, u32[]{:S(2)}, u32[]{:S(2)}) collective-permute-start(bf16[64,64]{1,0:T(8,128)(2,1)S(1)} %fusion.3), channel_id=1, source_target_pairs={{0,0},{1,32},{2,64},{3,96},{4,1},{5,33},{6,65},{7,97},{8,2},{9,34}... | collective-permute-start | bytes 24584 | tf_op jit(solution)/shard_map/ppermute | solution.py:157
  157.5 13.4 %collective-permute-start.31 = (bf16[64,64]{1,0:T(8,128)(2,1)S(1)}, bf16[64,64]{1,0:T(8,128)(2,1)S(1)}, u32[]{:S(2)}, u32[]{:S(2)}) collective-permute-start(bf16[64,64]{1,0:T(8,128)(2,1)S(1)} %fusion.3), channel_id=1, source_target_pairs={{0,1},{1,33},{2,65},{3,97},{4,2},{5,34},{6,66},{7,98},{8,3},{9,35}... | collective-permute-start | bytes 24584 | tf_op jit(solution)/shard_map/ppermute | solution.py:157
  162.8 8.6 %collective-permute-start.32 = (bf16[64,64]{1,0:T(8,128)(2,1)S(1)}, bf16[64,64]{1,0:T(8,128)(2,1)S(1)}, u32[]{:S(2)}, u32[]{:S(2)}) collective-permute-start(bf16[64,64]{1,0:T(8,128)(2,1)S(1)} %fusion.3), channel_id=1, source_target_pairs={{0,2},{1,34},{2,66},{3,98},{4,3},{5,35},{6,67},{7,99},{8,0},{9,32}... | collective-permute-start | bytes 24584 | tf_op jit(solution)/shard_map/ppermute | solution.py:157
  168.4 3.8 %collective-permute-start.33 = (bf16[64,64]{1,0:T(8,128)(2,1)S(1)}, bf16[64,64]{1,0:T(8,128)(2,1)S(1)}, u32[]{:S(2)}, u32[]{:S(2)}) collective-permute-start(bf16[64,64]{1,0:T(8,128)(2,1)S(1)} %fusion.3), channel_id=1, source_target_pairs={{0,3},{1,35},{2,67},{3,99},{4,0},{5,32},{6,64},{7,96},{8,1},{9,33}... | collective-permute-start | bytes 24584 | tf_op jit(solution)/shard_map/ppermute | solution.py:157
  172.7 3.7 %collective-permute-start.34 = (f32[64,256]{1,0:T(8,128)S(1)}, f32[64,256]{1,0:T(8,128)S(1)}, u32[]{:S(2)}, u32[]{:S(2)}) collective-permute-start(f32[64,256]{1,0:T(8,128)S(1)} %constant_dynamic-slice_fusion), channel_id=1, source_target_pairs={{0,4},{4,0},{8,12},{12,8},{16,20},{20,16},{24,28},{28,24},{32,36},... | collective-permute-start | bytes 196616 | tf_op jit(solution)/shard_map/ppermute | solution.py:83
  176.4 7.7 %collective-permute-start.35 = (f32[64,256]{1,0:T(8,128)S(1)}, f32[64,256]{1,0:T(8,128)S(1)}, u32[]{:S(2)}, u32[]{:S(2)}) collective-permute-start(f32[64,256]{1,0:T(8,128)S(1)} %get-tuple-element.8), channel_id=1, source_target_pairs={{0,8},{4,12},{8,16},{12,20},{16,24},{20,28},{24,0},{28,4},{32,40},... | collective-permute-start | bytes 196616 | tf_op jit(solution)/shard_map/ppermute | solution.py:71
  176.8 8.5 %collective-permute-start.36 = (f32[64,256]{1,0:T(8,128)S(1)}, f32[64,256]{1,0:T(8,128)S(1)}, u32[]{:S(2)}, u32[]{:S(2)}) collective-permute-start(f32[64,256]{1,0:T(8,128)S(1)} %get-tuple-element.8), channel_id=1, source_target_pairs={{0,16},{4,20},{8,24},{12,28},{16,0},{20,4},{24,8},{28,12},{32,48},... | collective-permute-start | bytes 196616 | tf_op jit(solution)/shard_map/ppermute | solution.py:71
  181.8 4.3 %collective-permute-start.37 = (f32[64,256]{1,0:T(8,128)S(1)}, f32[64,256]{1,0:T(8,128)S(1)}, u32[]{:S(2)}, u32[]{:S(2)}) collective-permute-start(f32[64,256]{1,0:T(8,128)S(1)} %get-tuple-element.8), channel_id=1, source_target_pairs={{0,24},{4,28},{8,0},{12,4},{16,8},{20,12},{24,16},{28,20},{32,56},... | collective-permute-start | bytes 196616 | tf_op jit(solution)/shard_map/ppermute | solution.py:71
  186.1 8.8 %collective-permute-start.38 = (f32[64,256]{1,0:T(8,128)S(1)}, f32[64,256]{1,0:T(8,128)S(1)}, u32[]{:S(2)}, u32[]{:S(2)}) collective-permute-start(f32[64,256]{1,0:T(8,128)S(1)} %reduce_sum.166), channel_id=1, source_target_pairs={{0,32},{4,36},{8,40},{12,44},{16,48},{20,52},{24,56},{28,60},{32,6... | collective-permute-start | bytes 196616 | tf_op jit(solution)/shard_map/ppermute | solution.py:71
  188.6 7.7 %collective-permute-start.39 = (f32[64,256]{1,0:T(8,128)S(1)}, f32[64,256]{1,0:T(8,128)S(1)}, u32[]{:S(2)}, u32[]{:S(2)}) collective-permute-start(f32[64,256]{1,0:T(8,128)S(1)} %reduce_sum.166), channel_id=1, source_target_pairs={{0,64},{4,68},{8,72},{12,76},{16,80},{20,84},{24,88},{28,92},{32,9... | collective-permute-start | bytes 196616 | tf_op jit(solution)/shard_map/ppermute | solution.py:71
  193.3 4.3 %collective-permute-start.40 = (f32[64,256]{1,0:T(8,128)S(1)}, f32[64,256]{1,0:T(8,128)S(1)}, u32[]{:S(2)}, u32[]{:S(2)}) collective-permute-start(f32[64,256]{1,0:T(8,128)S(1)} %reduce_sum.166), channel_id=1, source_target_pairs={{0,96},{4,100},{8,104},{12,108},{16,112},{20,116},{24,120},{28,124... | collective-permute-start | bytes 196616 | tf_op jit(solution)/shard_map/ppermute | solution.py:71
  197.6 1.3 collective-permute-start.41
  199.1 4.8 %collective-permute-start.42 = (f32[64]{0:T(128)S(1)}, f32[64]{0:T(128)S(1)}, u32[]{:S(2)}, u32[]{:S(2)}) collective-permute-start(f32[64]{0:T(128)S(1)} %multiply_reduce_fusion), channel_id=1, source_target_pairs={{0,1},{1,2},{2,3},{3,0},{4,5},{5,6},{6,7},{7,4},{8,9},{9,10},{10,1... | collective-permute-start | bytes 776 | tf_op jit(solution)/shard_map/ppermute | solution.py:71
  199.6 5.1 %collective-permute-start.43 = (f32[64]{0:T(128)S(1)}, f32[64]{0:T(128)S(1)}, u32[]{:S(2)}, u32[]{:S(2)}) collective-permute-start(f32[64]{0:T(128)S(1)} %multiply_reduce_fusion), channel_id=1, source_target_pairs={{0,2},{1,3},{2,0},{3,1},{4,6},{5,7},{6,4},{7,5},{8,10},{9,11},{10,... | collective-permute-start | bytes 776 | tf_op jit(solution)/shard_map/ppermute | solution.py:71
  200.7 4.1 %collective-permute-start.44 = (f32[64]{0:T(128)S(1)}, f32[64]{0:T(128)S(1)}, u32[]{:S(2)}, u32[]{:S(2)}) collective-permute-start(f32[64]{0:T(128)S(1)} %multiply_reduce_fusion), channel_id=1, source_target_pairs={{0,3},{1,0},{2,1},{3,2},{4,7},{5,4},{6,5},{7,6},{8,11},{9,8},{10,9... | collective-permute-start | bytes 776 | tf_op jit(solution)/shard_map/ppermute | solution.py:71

commit v7 on v6

--- a/solution.py
+++ b/solution.py
@@ -211,20 +211,22 @@
     token_rows = states.reshape(rows, local_width)
     positions = (lengths[None, :] + jnp.arange(STEPS, dtype=jnp.int32)[:, None]).reshape(rows)
 
-    sliced = seq_columns(token_rows, query_weight.shape[0])
-    summed = seq_total(
+    block = local_width // SEQ_SIZE
+    qkv_weight = full_rows(
         jnp.concatenate(
-            [
-                jnp.dot(sliced, query_weight, preferred_element_type=jnp.float32),
-                jnp.dot(sliced, key_weight, preferred_element_type=jnp.float32),
-                jnp.dot(sliced, value_weight, preferred_element_type=jnp.float32),
-            ],
-            axis=1,
-        )
-    )
-    query_raw = summed[:, :local_width]
-    key_raw = summed[:, local_width : 2 * local_width]
-    value_raw = summed[:, 2 * local_width :]
+            [w.reshape(-1, SEQ_SIZE, block) for w in (query_weight, key_weight, value_weight)], axis=2
+        ).reshape(query_weight.shape[0], 3 * local_width)
+    )
+    states_all = jnp.transpose(exchange(token_rows, "mp", MP_SIZE, 1, MP_SIZE), (1, 0, 2)).reshape(
+        rows, MP_SIZE * local_width
+    )
+    own = jnp.dot(states_all, qkv_weight, preferred_element_type=jnp.float32)
+    for stride, size in seq_groups():
+        own = gather_digit(own, stride, size)
+    gathered = own.reshape(rows, SEQ_SIZE, 3, block)
+    query_raw = gathered[:, :, 0].reshape(rows, local_width)
+    key_raw = gathered[:, :, 1].reshape(rows, local_width)
+    value_raw = gathered[:, :, 2].reshape(rows, local_width)
     squares = feature_sums(
         jnp.stack([jnp.sum(query_raw * query_raw, axis=1), jnp.sum(key_raw * key_raw, axis=1)], axis=1)
     )

time: 206 us -> 211 us (1.024)
  local copies, waits for them, and re-layouts: 14.9 us -> 24.4 us
  waiting for transfers between devices: 50.4 us -> 44.2 us
  starting transfers between devices: 118 us -> 122 us
  matrix products: 10.8 us -> 8.13 us
    ppermute x30 -> x27, starting transfers between devices: 64.6 us -> 49.7 us  [exchange(): lax.ppermute(value, axis, digit_pairs(count, stride, size, shift))]
    ppermute x30 -> x27, waiting for transfers between devices: 35.5 us -> 22.3 us  [exchange(): lax.ppermute(value, axis, digit_pairs(count, stride, size, shift))]
    ppermute x3 -> x9, starting transfers between devices: 0.26 us -> 12.1 us  [gather_digit(): lax.ppermute(current, 'seq', digit_pairs(SEQ_SIZE, stride, size, shift))]
    all_to_all x1 -> x2, starting transfers between devices: 12.7 us -> 21.6 us  [full_rows(): lax.all_to_all(weight.reshape(rows, SEQ_SIZE, block), 'seq', 1, 0, tiled=...]
    ppermute x3 -> x9, waiting for transfers between devices: 3.76 us -> 12.1 us  [gather_digit(): lax.ppermute(current, 'seq', digit_pairs(SEQ_SIZE, stride, size, shift))]
    unnamed x34 -> x38, local copies, waits for them, and re-layouts: 2.47 us -> 6.57 us
    dynamic_update_slice x30 -> x27, local copies, waits for them, and re-layouts: 3.84 us -> 7.13 us  [exchange(): lax.dynamic_update_index_in_dim(stack, received, (digit - shift) % size, 0)]
    dot_general x3 -> x1, matrix products: 2.91 us -> 0.21 us  [local(): own = jnp.dot(states_all, qkv_weight, preferred_element_type=jnp.float32)]
  transfers between devices with their start and end apart: 47 -> 49, of which waited for: 28 -> 28; matrix products, arithmetic and copies ran while one was open for 7% -> 11% of each run, Pallas kernels for 0% -> 0%
where the time goes in v7:
time: 211 us; the launch traced here: 210 us
  starting transfers between devices  122 us (58%)
  waiting for transfers between devices  44.2 us (21%)
  local copies, waits for them, and re-layouts  24.4 us (12%)
  other arithmetic  9.4 us (4%)
  matrix products  8.13 us (4%)
    ppermute x27, starting transfers between devices, exchange(): lax.ppermute(value, axis, digit_pairs(count, stride, size, shift))  49.7 us
    ppermute x8, starting transfers between devices, deliver(): received = lax.ppermute(piece, ('seq', 'mp'), pairs)  27.2 us
    ppermute x27, waiting for transfers between devices, exchange(): lax.ppermute(value, axis, digit_pairs(count, stride, size, shift))  22.3 us
    all_to_all x2, starting transfers between devices, full_rows(): lax.all_to_all(weight.reshape(rows, SEQ_SIZE, block), 'seq', 1, 0, tiled=...  21.6 us
    ppermute x9, starting transfers between devices, gather_digit(): lax.ppermute(current, 'seq', digit_pairs(SEQ_SIZE, stride, size, shift))  12.1 us
    ppermute x9, waiting for transfers between devices, gather_digit(): lax.ppermute(current, 'seq', digit_pairs(SEQ_SIZE, stride, size, shift))  12.1 us
    dynamic_update_slice x27, local copies, waits for them, and re-layouts, exchange(): lax.dynamic_update_index_in_dim(stack, received, (digit - shift) % size, 0)  7.13 us
    all_to_all x1, waiting for transfers between devices, local(): sources = lax.all_to_all(send, 'seq', 0, 0, tiled=True)  7.05 us
  transfers between devices with their start and end apart: 49, of which 28 were waited for; matrix products, arithmetic and copies ran while one was open for 11% of the time, Pallas kernels for 0%

profile of v7, /device:TPU:0, one launch (start us, length us, event | category | flops | bytes accessed | tf_op | source)
XLA Modules:
  0.0 210.0 jit_solution(7416129367501999832)
XLA Ops:
  0.0 2.0 collective-permute-start
  2.0 3.6 %collective-permute-start.1 = (bf16[64,512]{1,0:T(8,128)(2,1)}, bf16[64,512]{1,0:T(8,128)(2,1)S(1)}, u32[]{:S(2)}, u32[]{:S(2)}) collective-permute-start(bf16[64,512]{1,0:T(8,128)(2,1)} %bitcast.202), channel_id=1, source_target_pairs={{0,2},{1,3},{2,0},{3,1},{4,6},{5,7},{6,4},{7,5},{8,10},{9,11},{10,... | collective-permute-start | bytes 196616 | tf_op jit(solution)/shard_map/ppermute | solution.py:71
  10.5 7.3 %all-to-all-start = ((bf16[32,2,1536]{2,1,0:T(2,128)(2,1)}), bf16[32,2,1536]{2,1,0:T(2,128)(2,1)S(1)}, u32[]{:S(2)}, u32[]{:S(2)}) async-start(bf16[32,2,1536]{2,1,0:T(2,128)(2,1)} %reshape.397), calls=%async_computation | async-start | bytes 393216 | tf_op jit(solution)/shard_map/all_to_all | solution.py:167
  22.3 1.1 dynamic_update_slice.178
  23.8 1.1 dynamic_update_slice.179
  24.9 1.1 dynamic_update_slice.180
  26.1 1.1 dynamic_update_slice.181
  29.6 1.8 collective-permute-start.4
  31.4 2.7 %collective-permute-start.5 = (f32[64,96]{0,1:T(8,128)S(1)}, f32[64,96]{0,1:T(8,128)S(1)}, u32[]{:S(2)}, u32[]{:S(2)}) collective-permute-start(f32[64,96]{0,1:T(8,128)S(1)} %constant_dynamic-update-slice_fusion.20), channel_id=1, source_target_pairs={{0,16},{4,20},{8,24},{12,28},{16,0},{20,4},{24,8},{28,12},{32,48},... | collective-permute-start | bytes 73736 | tf_op jit(solution)/shard_map/ppermute | solution.py:94
  34.0 1.5 collective-permute-start.6
  35.6 1.4 collective-permute-done.5
  37.0 1.2 collective-permute-done.6
  38.1 1.5 collective-permute-start.7
  39.6 2.8 %collective-permute-start.8 = (f32[64,384]{0,1:T(8,128)S(1)}, f32[64,384]{0,1:T(8,128)S(1)}, u32[]{:S(2)}, u32[]{:S(2)}) collective-permute-start(f32[64,384]{0,1:T(8,128)S(1)} %constant_dynamic-update-slice_fusion.16), channel_id=1, source_target_pairs={{0,64},{4,68},{8,72},{12,76},{16,80},{20,84},{24,88},{28,92},{32,9... | collective-permute-start | bytes 294920 | tf_op jit(solution)/shard_map/ppermute | solution.py:94
  42.4 1.4 collective-permute-start.9
  43.9 2.5 %collective-permute-done.7 = f32[64,384]{0,1:T(8,128)S(1)} collective-permute-done((f32[64,384]{0,1:T(8,128)S(1)}, f32[64,384]{0,1:T(8,128)S(1)}, u32[]{:S(2)}, u32[]{:S(2)}) %collective-permute-start.7) | collective-permute-done | bytes 98336 | tf_op jit(solution)/shard_map/ppermute | solution.py:94
  46.4 3.7 %collective-permute-done.8 = f32[64,384]{0,1:T(8,128)S(1)} collective-permute-done((f32[64,384]{0,1:T(8,128)S(1)}, f32[64,384]{0,1:T(8,128)S(1)}, u32[]{:S(2)}, u32[]{:S(2)}) %collective-permute-start.8) | collective-permute-done | bytes 98336 | tf_op jit(solution)/shard_map/ppermute | solution.py:94
  50.3 1.1 collective-permute-start.10
  51.8 2.3 %collective-permute-start.12 = (f32[64,2]{0,1:T(2,128)S(1)}, f32[64,2]{0,1:T(2,128)S(1)}, u32[]{:S(2)}, u32[]{:S(2)}) collective-permute-start(f32[64,2]{0,1:T(2,128)S(1)} %pad_maximum_fusion.3), channel_id=1, source_target_pairs={{0,3},{1,0},{2,1},{3,2},{4,7},{5,4},{6,5},{7,6},{8,11},{9,8},{10,9... | collective-permute-start | bytes 1544 | tf_op jit(solution)/shard_map/ppermute | solution.py:71
  55.1 1.3 collective-permute-done.11
  56.9 5.5 %fusion.28 = (f32[4,4,16]{2,1,0:T(4,128)S(1)}, f32[4,4,16,4096]{3,2,1,0:T(8,128)}) fusion(bf16[4096,512,1,1]{1,0,3,2:T(8,128)(2,1)} %bitcast.240, pred[4,512]{1,0:T(4,128)(4,1)S(1)} %iota_compare_fusion.1, bf16[4,16,512]{2,1,0:T(8,128)(2,1)S(1)} %convert_element_type.56, pred[16,4096]{1,0:T(8,128)(4,1)S(1)} %fusion.9), kind=kOutput, calls=%fused_computation.123 | convolution fusion | flops 1077018368 | bytes 8522752 | tf_op jit(solution)/shard_map/dot_general | solution.py:257
  62.5 3.4 %fusion.2 = (bf16[4,4,16,4096]{3,2,1,0:T(8,128)(2,1)S(1)}, f32[4,4,16]{2,1,0:T(4,128)S(1)}) fusion(f32[4,4,16,4096]{3,2,1,0:T(8,128)} %get-tuple-element.36, f32[4,4,16]{2,1,0:T(4,128)S(1)} %get-tuple-element.35, pred[16,4096]{1,0:T(8,128)(4,1)S(1)} %fusion.9), kind=kLoop, calls=%fused_computation.4 | loop fusion | flops 4194048 | bytes 6359040 | tf_op jit(solution)/shard_map/convert_element_type | solution.py:268
  65.9 1.2 convolution_bitcast_fusion
  69.0 6.1 %all-to-all-start.1 = ((f32[32,1,1152]{2,1,0:T(1,128)}), f32[32,1,1152]{2,1,0:T(1,128)S(1)}, u32[]{:S(2)}, u32[]{:S(2)}) async-start(f32[32,1,1152]{2,1,0:T(1,128)} %reshape.399), calls=%async_computation.1 | async-start | bytes 294912 | tf_op jit(solution)/shard_map/all_to_all | solution.py:285
  75.9 7.1 %all-to-all-done.1 = f32[32,1,1152]{2,1,0:T(1,128)S(1)} async-done(((f32[32,1,1152]{2,1,0:T(1,128)}), f32[32,1,1152]{2,1,0:T(1,128)S(1)}, u32[]{:S(2)}, u32[]{:S(2)}) %all-to-all-start.1) | async-done | bytes 147488 | tf_op jit(solution)/shard_map/all_to_all | solution.py:285
  86.8 5.2 %collective-permute-start.14 = (bf16[64,16]{0,1:T(8,128)(2,1)S(1)}, bf16[64,16]{0,1:T(8,128)(2,1)S(1)}, u32[]{:S(2)}, u32[]{:S(2)}) collective-permute-start(bf16[64,16]{0,1:T(8,128)(2,1)S(1)} %copy.157), channel_id=1, source_target_pairs={{0,1},{1,33},{2,65},{3,97},{4,2},{5,34},{6,66},{7,98},{8,3},{9,35}... | collective-permute-start | bytes 6152 | tf_op jit(solution)/shard_map/ppermute | solution.py:157
  92.0 4.1 %collective-permute-start.15 = (bf16[64,16]{0,1:T(8,128)(2,1)S(1)}, bf16[64,16]{0,1:T(8,128)(2,1)S(1)}, u32[]{:S(2)}, u32[]{:S(2)}) collective-permute-start(bf16[64,16]{0,1:T(8,128)(2,1)S(1)} %copy.157), channel_id=1, source_target_pairs={{0,2},{1,34},{2,66},{3,98},{4,3},{5,35},{6,67},{7,99},{8,0},{9,32}... | collective-permute-start | bytes 6152 | tf_op jit(solution)/shard_map/ppermute | solution.py:157
  96.1 3.4 %collective-permute-start.16 = (bf16[64,16]{0,1:T(8,128)(2,1)S(1)}, bf16[64,16]{0,1:T(8,128)(2,1)S(1)}, u32[]{:S(2)}, u32[]{:S(2)}) collective-permute-start(bf16[64,16]{0,1:T(8,128)(2,1)S(1)} %copy.157), channel_id=1, source_target_pairs={{0,3},{1,35},{2,67},{3,99},{4,0},{5,32},{6,64},{7,96},{8,1},{9,33}... | collective-permute-start | bytes 6152 | tf_op jit(solution)/shard_map/ppermute | solution.py:157
  99.6 1.2 collective-permute-done.16
  101.1 2.8 %collective-permute-start.17 = (f32[64,256]{1,0:T(8,128)S(1)}, f32[64,256]{1,0:T(8,128)S(1)}, u32[]{:S(2)}, u32[]{:S(2)}) collective-permute-start(f32[64,256]{1,0:T(8,128)S(1)} %constant_dynamic-slice_fusion.1), channel_id=1, source_target_pairs={{0,4},{4,0},{8,12},{12,8},{16,20},{20,16},{24,28},{28,24},{32,36},... | collective-permute-start | bytes 196616 | tf_op jit(solution)/shard_map/ppermute | solution.py:83
  106.4 14.3 %all-to-all-start.2 = ((bf16[64,32,128]{2,0,1:T(8,128)(2,1)}), bf16[64,32,128]{2,0,1:T(8,128)(2,1)S(1)}, u32[]{:S(2)}, u32[]{:S(2)}) async-start(bf16[64,32,128]{2,0,1:T(8,128)(2,1)} %copy.153), calls=%async_computation.2 | async-start | bytes 1048576 | tf_op jit(solution)/shard_map/all_to_all | solution.py:167
  120.8 3.4 %collective-permute-start.19 = (f32[64,256]{1,0:T(8,128)S(1)}, f32[64,256]{1,0:T(8,128)S(1)}, u32[]{:S(2)}, u32[]{:S(2)}) collective-permute-start(f32[64,256]{1,0:T(8,128)S(1)} %get-tuple-element.10), channel_id=1, source_target_pairs={{0,16},{4,20},{8,24},{12,28},{16,0},{20,4},{24,8},{28,12},{32,48},... | collective-permute-start | bytes 196616 | tf_op jit(solution)/shard_map/ppermute | solution.py:71
  124.2 1.2 collective-permute-start.20
  125.3 6.8 %collective-permute-done.19 = f32[64,256]{1,0:T(8,128)S(1)} collective-permute-done((f32[64,256]{1,0:T(8,128)S(1)}, f32[64,256]{1,0:T(8,128)S(1)}, u32[]{:S(2)}, u32[]{:S(2)}) %collective-permute-start.19) | collective-permute-done | bytes 65568 | tf_op jit(solution)/shard_map/ppermute | solution.py:71
  132.2 1.5 collective-permute-start.21
  133.7 2.7 %collective-permute-start.22 = (f32[64,256]{1,0:T(8,128)S(1)}, f32[64,256]{1,0:T(8,128)S(1)}, u32[]{:S(2)}, u32[]{:S(2)}) collective-permute-start(f32[64,256]{1,0:T(8,128)S(1)} %reduce_sum.142), channel_id=1, source_target_pairs={{0,64},{4,68},{8,72},{12,76},{16,80},{20,84},{24,88},{28,92},{32,9... | collective-permute-start | bytes 196616 | tf_op jit(solution)/shard_map/ppermute | solution.py:71
  136.4 1.4 collective-permute-start.23
  138.4 1.0 collective-permute-done.22
  139.5 1.2 collective-permute-done.23
  140.9 1.2 collective-permute-done.24
  142.3 1.4 collective-permute-start.26
  143.7 2.3 %collective-permute-start.27 = (f32[64]{0:T(128)S(1)}, f32[64]{0:T(128)S(1)}, u32[]{:S(2)}, u32[]{:S(2)}) collective-permute-start(f32[64]{0:T(128)S(1)} %multiply_reduce_fusion.3), channel_id=1, source_target_pairs={{0,3},{1,0},{2,1},{3,2},{4,7},{5,4},{6,5},{7,6},{8,11},{9,8},{10,9... | collective-permute-start | bytes 776 | tf_op jit(solution)/shard_map/ppermute | solution.py:71
  148.1 2.1 collective-permute-start.28
  150.2 2.3 %collective-permute-start.29 = (bf16[64,512]{1,0:T(8,128)(2,1)S(1)}, bf16[64,512]{1,0:T(8,128)(2,1)S(1)}, u32[]{:S(2)}, u32[]{:S(2)}) collective-permute-start(bf16[64,512]{1,0:T(8,128)(2,1)S(1)} %add_convert_fusion.1), channel_id=1, source_target_pairs={{0,2},{1,3},{2,0},{3,1},{4,6},{5,7},{6,4},{7,5},{8,10},{9,11},{10,... | collective-permute-start | bytes 196616 | tf_op jit(solution)/shard_map/ppermute | solution.py:71
  153.1 1.1 dynamic_update_slice.214
  154.4 1.6 collective-permute-done.29
  156.9 1.1 dynamic_update_slice.215
  158.0 1.1 dynamic_update_slice.216
  159.2 1.1 dynamic_update_slice.217
  161.7 5.2 %collective-permute-start.32 = (bf16[64,64]{1,0:T(8,128)(2,1)S(1)}, bf16[64,64]{1,0:T(8,128)(2,1)S(1)}, u32[]{:S(2)}, u32[]{:S(2)}) collective-permute-start(bf16[64,64]{1,0:T(8,128)(2,1)S(1)} %fusion.3), channel_id=1, source_target_pairs={{0,1},{1,33},{2,65},{3,97},{4,2},{5,34},{6,66},{7,98},{8,3},{9,35}... | collective-permute-start | bytes 24584 | tf_op jit(solution)/shard_map/ppermute | solution.py:157
  166.9 5.6 %collective-permute-start.33 = (bf16[64,64]{1,0:T(8,128)(2,1)S(1)}, bf16[64,64]{1,0:T(8,128)(2,1)S(1)}, u32[]{:S(2)}, u32[]{:S(2)}) collective-permute-start(bf16[64,64]{1,0:T(8,128)(2,1)S(1)} %fusion.3), channel_id=1, source_target_pairs={{0,2},{1,34},{2,66},{3,98},{4,3},{5,35},{6,67},{7,99},{8,0},{9,32}... | collective-permute-start | bytes 24584 | tf_op jit(solution)/shard_map/ppermute | solution.py:157
  172.5 2.3 %collective-permute-start.34 = (bf16[64,64]{1,0:T(8,128)(2,1)S(1)}, bf16[64,64]{1,0:T(8,128)(2,1)S(1)}, u32[]{:S(2)}, u32[]{:S(2)}) collective-permute-start(bf16[64,64]{1,0:T(8,128)(2,1)S(1)} %fusion.3), channel_id=1, source_target_pairs={{0,3},{1,35},{2,67},{3,99},{4,0},{5,32},{6,64},{7,96},{8,1},{9,33}... | collective-permute-start | bytes 24584 | tf_op jit(solution)/shard_map/ppermute | solution.py:157
  176.8 2.8 %collective-permute-start.35 = (f32[64,256]{1,0:T(8,128)S(1)}, f32[64,256]{1,0:T(8,128)S(1)}, u32[]{:S(2)}, u32[]{:S(2)}) collective-permute-start(f32[64,256]{1,0:T(8,128)S(1)} %constant_dynamic-slice_fusion), channel_id=1, source_target_pairs={{0,4},{4,0},{8,12},{12,8},{16,20},{20,16},{24,28},{28,24},{32,36},... | collective-permute-start | bytes 196616 | tf_op jit(solution)/shard_map/ppermute | solution.py:83
  180.9 4.8 %collective-permute-start.37 = (f32[64,256]{1,0:T(8,128)S(1)}, f32[64,256]{1,0:T(8,128)S(1)}, u32[]{:S(2)}, u32[]{:S(2)}) collective-permute-start(f32[64,256]{1,0:T(8,128)S(1)} %get-tuple-element.8), channel_id=1, source_target_pairs={{0,16},{4,20},{8,24},{12,28},{16,0},{20,4},{24,8},{28,12},{32,48},... | collective-permute-start | bytes 196616 | tf_op jit(solution)/shard_map/ppermute | solution.py:71
  185.7 2.5 %collective-permute-start.38 = (f32[64,256]{1,0:T(8,128)S(1)}, f32[64,256]{1,0:T(8,128)S(1)}, u32[]{:S(2)}, u32[]{:S(2)}) collective-permute-start(f32[64,256]{1,0:T(8,128)S(1)} %get-tuple-element.8), channel_id=1, source_target_pairs={{0,24},{4,28},{8,0},{12,4},{16,8},{20,12},{24,16},{28,20},{32,56},... | collective-permute-start | bytes 196616 | tf_op jit(solution)/shard_map/ppermute | solution.py:71
  188.2 1.2 collective-permute-done.37
  190.2 2.5 %collective-permute-start.39 = (f32[64,256]{1,0:T(8,128)S(1)}, f32[64,256]{1,0:T(8,128)S(1)}, u32[]{:S(2)}, u32[]{:S(2)}) collective-permute-start(f32[64,256]{1,0:T(8,128)S(1)} %reduce_sum.146), channel_id=1, source_target_pairs={{0,32},{4,36},{8,40},{12,44},{16,48},{20,52},{24,56},{28,60},{32,6... | collective-permute-start | bytes 196616 | tf_op jit(solution)/shard_map/ppermute | solution.py:71
  192.7 5.0 %collective-permute-start.40 = (f32[64,256]{1,0:T(8,128)S(1)}, f32[64,256]{1,0:T(8,128)S(1)}, u32[]{:S(2)}, u32[]{:S(2)}) collective-permute-start(f32[64,256]{1,0:T(8,128)S(1)} %reduce_sum.146), channel_id=1, source_target_pairs={{0,64},{4,68},{8,72},{12,76},{16,80},{20,84},{24,88},{28,92},{32,9... | collective-permute-start | bytes 196616 | tf_op jit(solution)/shard_map/ppermute | solution.py:71
  197.7 1.6 collective-permute-start.41
  199.4 1.3 collective-permute-done.40
  200.7 1.3 collective-permute-done.41
  202.1 1.2 collective-permute-done.42
  205.1 1.9 collective-permute-start.45
  207.0 1.3 collective-permute-done.43
  (244 shorter events, 36.4 us)
Async XLA Ops:
  0.0 176.6 %copy-start = (bf16[256,512]{1,0:T(8,128)(2,1)S(1)}, bf16[256,512]{1,0:T(8,128)(2,1)}, u32[]{:S(2)}) copy-start(bf16[256,512]{1,0:T(8,128)(2,1)} %param.24) | copy-start | bytes 786436
  0.0 23.4 %collective-permute-start = (bf16[64,512]{1,0:T(8,128)(2,1)}, bf16[64,512]{1,0:T(8,128)(2,1)S(1)}, u32[]{:S(2)}, u32[]{:S(2)}) collective-permute-start(bf16[64,512]{1,0:T(8,128)(2,1)} %bitcast.201), channel_id=1, source_target_pairs={{0,1},{1,2},{2,3},{3,0},{4,5},{5,6},{6,7},{7,4},{8,9},{9,10},{10,1... | collective-permute-start | bytes 196616 | tf_op jit(solution)/shard_map/ppermute | solution.py:71
  2.0 21.5 %collective-permute-start.1 = (bf16[64,512]{1,0:T(8,128)(2,1)}, bf16[64,512]{1,0:T(8,128)(2,1)S(1)}, u32[]{:S(2)}, u32[]{:S(2)}) collective-permute-start(bf16[64,512]{1,0:T(8,128)(2,1)} %bitcast.202), channel_id=1, source_target_pairs={{0,2},{1,3},{2,0},{3,1},{4,6},{5,7},{6,4},{7,5},{8,10},{9,11},{10,... | collective-permute-start | bytes 196616 | tf_op jit(solution)/shard_map/ppermute | solution.py:71
  5.6 18.0 %collective-permute-start.2 = (bf16[64,512]{1,0:T(8,128)(2,1)}, bf16[64,512]{1,0:T(8,128)(2,1)S(1)}, u32[]{:S(2)}, u32[]{:S(2)}) collective-permute-start(bf16[64,512]{1,0:T(8,128)(2,1)} %bitcast.203), channel_id=1, source_target_pairs={{0,3},{1,0},{2,1},{3,2},{4,7},{5,4},{6,5},{7,6},{8,11},{9,8},{10,9... | collective-permute-start | bytes 196616 | tf_op jit(solution)/shard_map/ppermute | solution.py:71
  10.5 16.7 %all-to-all-start = ((bf16[32,2,1536]{2,1,0:T(2,128)(2,1)}), bf16[32,2,1536]{2,1,0:T(2,128)(2,1)S(1)}, u32[]{:S(2)}, u32[]{:S(2)}) async-start(bf16[32,2,1536]{2,1,0:T(2,128)(2,1)} %reshape.397), calls=%async_computation | async-start | bytes 393216 | tf_op jit(solution)/shard_map/all_to_all | solution.py:167
  27.3 29.2 %copy-start.5 = (f32[512]{0:T(512)S(1)}, f32[512]{0:T(512)}, u32[]{:S(2)}) copy-start(f32[512]{0:T(512)} %param.25) | copy-start | bytes 6148
  28.3 1.3 collective-permute-start.3
  29.6 6.0 %collective-permute-start.4 = (f32[64,96]{0,1:T(8,128)S(1)}, f32[64,96]{0,1:T(8,128)S(1)}, u32[]{:S(2)}, u32[]{:S(2)}) collective-permute-start(f32[64,96]{0,1:T(8,128)S(1)} %constant_dynamic-update-slice_fusion.20), channel_id=1, source_target_pairs={{0,8},{4,12},{8,16},{12,20},{16,24},{20,28},{24,0},{28,4},{32,40},... | collective-permute-start | bytes 73736 | tf_op jit(solution)/shard_map/ppermute | solution.py:94
  31.4 5.6 %collective-permute-start.5 = (f32[64,96]{0,1:T(8,128)S(1)}, f32[64,96]{0,1:T(8,128)S(1)}, u32[]{:S(2)}, u32[]{:S(2)}) collective-permute-start(f32[64,96]{0,1:T(8,128)S(1)} %constant_dynamic-update-slice_fusion.20), channel_id=1, source_target_pairs={{0,16},{4,20},{8,24},{12,28},{16,0},{20,4},{24,8},{28,12},{32,48},... | collective-permute-start | bytes 73736 | tf_op jit(solution)/shard_map/ppermute | solution.py:94
  34.0 4.1 %collective-permute-start.6 = (f32[64,96]{0,1:T(8,128)S(1)}, f32[64,96]{0,1:T(8,128)S(1)}, u32[]{:S(2)}, u32[]{:S(2)}) collective-permute-start(f32[64,96]{0,1:T(8,128)S(1)} %constant_dynamic-update-slice_fusion.20), channel_id=1, source_target_pairs={{0,24},{4,28},{8,0},{12,4},{16,8},{20,12},{24,16},{28,20},{32,56},... | collective-permute-start | bytes 73736 | tf_op jit(solution)/shard_map/ppermute | solution.py:94
  38.1 8.2 %collective-permute-start.7 = (f32[64,384]{0,1:T(8,128)S(1)}, f32[64,384]{0,1:T(8,128)S(1)}, u32[]{:S(2)}, u32[]{:S(2)}) collective-permute-start(f32[64,384]{0,1:T(8,128)S(1)} %constant_dynamic-update-slice_fusion.16), channel_id=1, source_target_pairs={{0,32},{4,36},{8,40},{12,44},{16,48},{20,52},{24,56},{28,60},{32,6... | collective-permute-start | bytes 294920 | tf_op jit(solution)/shard_map/ppermute | solution.py:94
  39.6 10.5 %collective-permute-start.8 = (f32[64,384]{0,1:T(8,128)S(1)}, f32[64,384]{0,1:T(8,128)S(1)}, u32[]{:S(2)}, u32[]{:S(2)}) collective-permute-start(f32[64,384]{0,1:T(8,128)S(1)} %constant_dynamic-update-slice_fusion.16), channel_id=1, source_target_pairs={{0,64},{4,68},{8,72},{12,76},{16,80},{20,84},{24,88},{28,92},{32,9... | collective-permute-start | bytes 294920 | tf_op jit(solution)/shard_map/ppermute | solution.py:94
  42.4 7.8 %collective-permute-start.9 = (f32[64,384]{0,1:T(8,128)S(1)}, f32[64,384]{0,1:T(8,128)S(1)}, u32[]{:S(2)}, u32[]{:S(2)}) collective-permute-start(f32[64,384]{0,1:T(8,128)S(1)} %constant_dynamic-update-slice_fusion.16), channel_id=1, source_target_pairs={{0,96},{4,100},{8,104},{12,108},{16,112},{20,116},{24,120},{28,124... | collective-permute-start | bytes 294920 | tf_op jit(solution)/shard_map/ppermute | solution.py:94
  50.3 4.8 %collective-permute-start.10 = (f32[64,2]{0,1:T(2,128)S(1)}, f32[64,2]{0,1:T(2,128)S(1)}, u32[]{:S(2)}, u32[]{:S(2)}) collective-permute-start(f32[64,2]{0,1:T(2,128)S(1)} %pad_maximum_fusion.3), channel_id=1, source_target_pairs={{0,1},{1,2},{2,3},{3,0},{4,5},{5,6},{6,7},{7,4},{8,9},{9,10},{10,1... | collective-permute-start | bytes 1544 | tf_op jit(solution)/shard_map/ppermute | solution.py:71
  51.4 5.1 %collective-permute-start.11 = (f32[64,2]{0,1:T(2,128)S(1)}, f32[64,2]{0,1:T(2,128)S(1)}, u32[]{:S(2)}, u32[]{:S(2)}) collective-permute-start(f32[64,2]{0,1:T(2,128)S(1)} %pad_maximum_fusion.3), channel_id=1, source_target_pairs={{0,2},{1,3},{2,0},{3,1},{4,6},{5,7},{6,4},{7,5},{8,10},{9,11},{10,... | collective-permute-start | bytes 1544 | tf_op jit(solution)/shard_map/ppermute | solution.py:71
  51.8 4.6 %collective-permute-start.12 = (f32[64,2]{0,1:T(2,128)S(1)}, f32[64,2]{0,1:T(2,128)S(1)}, u32[]{:S(2)}, u32[]{:S(2)}) collective-permute-start(f32[64,2]{0,1:T(2,128)S(1)} %pad_maximum_fusion.3), channel_id=1, source_target_pairs={{0,3},{1,0},{2,1},{3,2},{4,7},{5,4},{6,5},{7,6},{8,11},{9,8},{10,9... | collective-permute-start | bytes 1544 | tf_op jit(solution)/shard_map/ppermute | solution.py:71
  62.5 3.5 %copy-start.9 = (bf16[16,256,512]{2,1,0:T(8,128)(2,1)S(1)}, bf16[16,256,512]{2,1,0:T(8,128)(2,1)}, u32[]{:S(2)}) copy-start(bf16[16,256,512]{2,1,0:T(8,128)(2,1)} %param.30) | copy-start | bytes 12582916
  65.9 9.2 %copy-start.6 = (f32[512]{0:T(512)S(1)}, f32[512]{0:T(512)}, u32[]{:S(2)}) copy-start(f32[512]{0:T(512)} %param.26) | copy-start | bytes 6148
  67.2 33.7 %copy-start.4 = (bf16[64,512]{1,0:T(8,128)(2,1)S(1)}, bf16[64,512]{1,0:T(8,128)(2,1)}, u32[]{:S(2)}) copy-start(bf16[64,512]{1,0:T(8,128)(2,1)} %param.21) | copy-start | bytes 196612
  67.2 36.7 %copy-start.1 = (bf16[64,2048]{1,0:T(8,128)(2,1)S(1)}, bf16[64,2048]{1,0:T(8,128)(2,1)}, u32[]{:S(2)}) copy-start(bf16[64,2048]{1,0:T(8,128)(2,1)} %param.22) | copy-start | bytes 786436
  67.2 37.2 %copy-start.2 = (bf16[64,2048]{1,0:T(8,128)(2,1)S(1)}, bf16[64,2048]{1,0:T(8,128)(2,1)}, u32[]{:S(2)}) copy-start(bf16[64,2048]{1,0:T(8,128)(2,1)} %param.23) | copy-start | bytes 786436
  69.0 14.0 %all-to-all-start.1 = ((f32[32,1,1152]{2,1,0:T(1,128)}), f32[32,1,1152]{2,1,0:T(1,128)S(1)}, u32[]{:S(2)}, u32[]{:S(2)}) async-start(f32[32,1,1152]{2,1,0:T(1,128)} %reshape.399), calls=%async_computation.1 | async-start | bytes 294912 | tf_op jit(solution)/shard_map/all_to_all | solution.py:285
  86.1 13.5 %collective-permute-start.13 = (bf16[64,16]{0,1:T(8,128)(2,1)S(1)}, bf16[64,16]{0,1:T(8,128)(2,1)S(1)}, u32[]{:S(2)}, u32[]{:S(2)}) collective-permute-start(bf16[64,16]{0,1:T(8,128)(2,1)S(1)} %copy.157), channel_id=1, source_target_pairs={{0,0},{1,32},{2,64},{3,96},{4,1},{5,33},{6,65},{7,97},{8,2},{9,34}... | collective-permute-start | bytes 6152 | tf_op jit(solution)/shard_map/ppermute | solution.py:157
  86.8 12.8 %collective-permute-start.14 = (bf16[64,16]{0,1:T(8,128)(2,1)S(1)}, bf16[64,16]{0,1:T(8,128)(2,1)S(1)}, u32[]{:S(2)}, u32[]{:S(2)}) collective-permute-start(bf16[64,16]{0,1:T(8,128)(2,1)S(1)} %copy.157), channel_id=1, source_target_pairs={{0,1},{1,33},{2,65},{3,97},{4,2},{5,34},{6,66},{7,98},{8,3},{9,35}... | collective-permute-start | bytes 6152 | tf_op jit(solution)/shard_map/ppermute | solution.py:157
  92.0 7.6 %collective-permute-start.15 = (bf16[64,16]{0,1:T(8,128)(2,1)S(1)}, bf16[64,16]{0,1:T(8,128)(2,1)S(1)}, u32[]{:S(2)}, u32[]{:S(2)}) collective-permute-start(bf16[64,16]{0,1:T(8,128)(2,1)S(1)} %copy.157), channel_id=1, source_target_pairs={{0,2},{1,34},{2,66},{3,98},{4,3},{5,35},{6,67},{7,99},{8,0},{9,32}... | collective-permute-start | bytes 6152 | tf_op jit(solution)/shard_map/ppermute | solution.py:157
  96.1 4.7 %collective-permute-start.16 = (bf16[64,16]{0,1:T(8,128)(2,1)S(1)}, bf16[64,16]{0,1:T(8,128)(2,1)S(1)}, u32[]{:S(2)}, u32[]{:S(2)}) collective-permute-start(bf16[64,16]{0,1:T(8,128)(2,1)S(1)} %copy.157), channel_id=1, source_target_pairs={{0,3},{1,35},{2,67},{3,99},{4,0},{5,32},{6,64},{7,96},{8,1},{9,33}... | collective-permute-start | bytes 6152 | tf_op jit(solution)/shard_map/ppermute | solution.py:157
  101.0 47.0 %copy-start.3 = (bf16[4,16,512]{2,1,0:T(8,128)(2,1)S(1)}, bf16[4,16,512]{2,1,0:T(8,128)(2,1)}, u32[]{:S(2)}) copy-start(bf16[4,16,512]{2,1,0:T(8,128)(2,1)} %param.17) | copy-start | bytes 196612
  101.0 47.0 %copy-start.7 = (f32[512]{0:T(512)S(1)}, f32[512]{0:T(512)}, u32[]{:S(2)}) copy-start(f32[512]{0:T(512)} %param.27) | copy-start | bytes 6148
  101.1 3.9 %collective-permute-start.17 = (f32[64,256]{1,0:T(8,128)S(1)}, f32[64,256]{1,0:T(8,128)S(1)}, u32[]{:S(2)}, u32[]{:S(2)}) collective-permute-start(f32[64,256]{1,0:T(8,128)S(1)} %constant_dynamic-slice_fusion.1), channel_id=1, source_target_pairs={{0,4},{4,0},{8,12},{12,8},{16,20},{20,16},{24,28},{28,24},{32,36},... | collective-permute-start | bytes 196616 | tf_op jit(solution)/shard_map/ppermute | solution.py:83
  105.0 20.3 %collective-permute-start.18 = (f32[64,256]{1,0:T(8,128)S(1)}, f32[64,256]{1,0:T(8,128)S(1)}, u32[]{:S(2)}, u32[]{:S(2)}) collective-permute-start(f32[64,256]{1,0:T(8,128)S(1)} %get-tuple-element.10), channel_id=1, source_target_pairs={{0,8},{4,12},{8,16},{12,20},{16,24},{20,28},{24,0},{28,4},{32,40},... | collective-permute-start | bytes 196616 | tf_op jit(solution)/shard_map/ppermute | solution.py:71
  106.4 54.0 %all-to-all-start.2 = ((bf16[64,32,128]{2,0,1:T(8,128)(2,1)}), bf16[64,32,128]{2,0,1:T(8,128)(2,1)S(1)}, u32[]{:S(2)}, u32[]{:S(2)}) async-start(bf16[64,32,128]{2,0,1:T(8,128)(2,1)} %copy.153), calls=%async_computation.2 | async-start | bytes 1048576 | tf_op jit(solution)/shard_map/all_to_all | solution.py:167
  120.8 11.3 %collective-permute-start.19 = (f32[64,256]{1,0:T(8,128)S(1)}, f32[64,256]{1,0:T(8,128)S(1)}, u32[]{:S(2)}, u32[]{:S(2)}) collective-permute-start(f32[64,256]{1,0:T(8,128)S(1)} %get-tuple-element.10), channel_id=1, source_target_pairs={{0,16},{4,20},{8,24},{12,28},{16,0},{20,4},{24,8},{28,12},{32,48},... | collective-permute-start | bytes 196616 | tf_op jit(solution)/shard_map/ppermute | solution.py:71
  124.2 8.0 %collective-permute-start.20 = (f32[64,256]{1,0:T(8,128)S(1)}, f32[64,256]{1,0:T(8,128)S(1)}, u32[]{:S(2)}, u32[]{:S(2)}) collective-permute-start(f32[64,256]{1,0:T(8,128)S(1)} %get-tuple-element.10), channel_id=1, source_target_pairs={{0,24},{4,28},{8,0},{12,4},{16,8},{20,12},{24,16},{28,20},{32,56},... | collective-permute-start | bytes 196616 | tf_op jit(solution)/shard_map/ppermute | solution.py:71
  132.2 6.2 %collective-permute-start.21 = (f32[64,256]{1,0:T(8,128)S(1)}, f32[64,256]{1,0:T(8,128)S(1)}, u32[]{:S(2)}, u32[]{:S(2)}) collective-permute-start(f32[64,256]{1,0:T(8,128)S(1)} %reduce_sum.142), channel_id=1, source_target_pairs={{0,32},{4,36},{8,40},{12,44},{16,48},{20,52},{24,56},{28,60},{32,6... | collective-permute-start | bytes 196616 | tf_op jit(solution)/shard_map/ppermute | solution.py:71
  133.7 5.8 %collective-permute-start.22 = (f32[64,256]{1,0:T(8,128)S(1)}, f32[64,256]{1,0:T(8,128)S(1)}, u32[]{:S(2)}, u32[]{:S(2)}) collective-permute-start(f32[64,256]{1,0:T(8,128)S(1)} %reduce_sum.142), channel_id=1, source_target_pairs={{0,64},{4,68},{8,72},{12,76},{16,80},{20,84},{24,88},{28,92},{32,9... | collective-permute-start | bytes 196616 | tf_op jit(solution)/shard_map/ppermute | solution.py:71
  136.4 4.3 %collective-permute-start.23 = (f32[64,256]{1,0:T(8,128)S(1)}, f32[64,256]{1,0:T(8,128)S(1)}, u32[]{:S(2)}, u32[]{:S(2)}) collective-permute-start(f32[64,256]{1,0:T(8,128)S(1)} %reduce_sum.142), channel_id=1, source_target_pairs={{0,96},{4,100},{8,104},{12,108},{16,112},{20,116},{24,120},{28,124... | collective-permute-start | bytes 196616 | tf_op jit(solution)/shard_map/ppermute | solution.py:71
  140.7 1.3 collective-permute-start.24
  142.2 67.1 %copy-start.8 = (f32[512]{0:T(512)S(1)}, f32[512]{0:T(512)}, u32[]{:S(2)}) copy-start(f32[512]{0:T(512)} %param.28) | copy-start | bytes 6148
  142.2 4.8 %collective-permute-start.25 = (f32[64]{0:T(128)S(1)}, f32[64]{0:T(128)S(1)}, u32[]{:S(2)}, u32[]{:S(2)}) collective-permute-start(f32[64]{0:T(128)S(1)} %multiply_reduce_fusion.3), channel_id=1, source_target_pairs={{0,1},{1,2},{2,3},{3,0},{4,5},{5,6},{6,7},{7,4},{8,9},{9,10},{10,1... | collective-permute-start | bytes 776 | tf_op jit(solution)/shard_map/ppermute | solution.py:71
  142.3 5.4 %collective-permute-start.26 = (f32[64]{0:T(128)S(1)}, f32[64]{0:T(128)S(1)}, u32[]{:S(2)}, u32[]{:S(2)}) collective-permute-start(f32[64]{0:T(128)S(1)} %multiply_reduce_fusion.3), channel_id=1, source_target_pairs={{0,2},{1,3},{2,0},{3,1},{4,6},{5,7},{6,4},{7,5},{8,10},{9,11},{10,... | collective-permute-start | bytes 776 | tf_op jit(solution)/shard_map/ppermute | solution.py:71
  143.7 4.2 %collective-permute-start.27 = (f32[64]{0:T(128)S(1)}, f32[64]{0:T(128)S(1)}, u32[]{:S(2)}, u32[]{:S(2)}) collective-permute-start(f32[64]{0:T(128)S(1)} %multiply_reduce_fusion.3), channel_id=1, source_target_pairs={{0,3},{1,0},{2,1},{3,2},{4,7},{5,4},{6,5},{7,6},{8,11},{9,8},{10,9... | collective-permute-start | bytes 776 | tf_op jit(solution)/shard_map/ppermute | solution.py:71
  148.1 6.2 %collective-permute-start.28 = (bf16[64,512]{1,0:T(8,128)(2,1)S(1)}, bf16[64,512]{1,0:T(8,128)(2,1)S(1)}, u32[]{:S(2)}, u32[]{:S(2)}) collective-permute-start(bf16[64,512]{1,0:T(8,128)(2,1)S(1)} %add_convert_fusion.1), channel_id=1, source_target_pairs={{0,1},{1,2},{2,3},{3,0},{4,5},{5,6},{6,7},{7,4},{8,9},{9,10},{10,1... | collective-permute-start | bytes 196616 | tf_op jit(solution)/shard_map/ppermute | solution.py:71
  150.2 5.8 %collective-permute-start.29 = (bf16[64,512]{1,0:T(8,128)(2,1)S(1)}, bf16[64,512]{1,0:T(8,128)(2,1)S(1)}, u32[]{:S(2)}, u32[]{:S(2)}) collective-permute-start(bf16[64,512]{1,0:T(8,128)(2,1)S(1)} %add_convert_fusion.1), channel_id=1, source_target_pairs={{0,2},{1,3},{2,0},{3,1},{4,6},{5,7},{6,4},{7,5},{8,10},{9,11},{10,... | collective-permute-start | bytes 196616 | tf_op jit(solution)/shard_map/ppermute | solution.py:71
  152.5 4.3 %collective-permute-start.30 = (bf16[64,512]{1,0:T(8,128)(2,1)S(1)}, bf16[64,512]{1,0:T(8,128)(2,1)S(1)}, u32[]{:S(2)}, u32[]{:S(2)}) collective-permute-start(bf16[64,512]{1,0:T(8,128)(2,1)S(1)} %add_convert_fusion.1), channel_id=1, source_target_pairs={{0,3},{1,0},{2,1},{3,2},{4,7},{5,4},{6,5},{7,6},{8,11},{9,8},{10,9... | collective-permute-start | bytes 196616 | tf_op jit(solution)/shard_map/ppermute | solution.py:71
  161.0 13.9 %collective-permute-start.31 = (bf16[64,64]{1,0:T(8,128)(2,1)S(1)}, bf16[64,64]{1,0:T(8,128)(2,1)S(1)}, u32[]{:S(2)}, u32[]{:S(2)}) collective-permute-start(bf16[64,64]{1,0:T(8,128)(2,1)S(1)} %fusion.3), channel_id=1, source_target_pairs={{0,0},{1,32},{2,64},{3,96},{4,1},{5,33},{6,65},{7,97},{8,2},{9,34}... | collective-permute-start | bytes 24584 | tf_op jit(solution)/shard_map/ppermute | solution.py:157
  161.7 13.4 %collective-permute-start.32 = (bf16[64,64]{1,0:T(8,128)(2,1)S(1)}, bf16[64,64]{1,0:T(8,128)(2,1)S(1)}, u32[]{:S(2)}, u32[]{:S(2)}) collective-permute-start(bf16[64,64]{1,0:T(8,128)(2,1)S(1)} %fusion.3), channel_id=1, source_target_pairs={{0,1},{1,33},{2,65},{3,97},{4,2},{5,34},{6,66},{7,98},{8,3},{9,35}... | collective-permute-start | bytes 24584 | tf_op jit(solution)/shard_map/ppermute | solution.py:157
  166.9 8.6 %collective-permute-start.33 = (bf16[64,64]{1,0:T(8,128)(2,1)S(1)}, bf16[64,64]{1,0:T(8,128)(2,1)S(1)}, u32[]{:S(2)}, u32[]{:S(2)}) collective-permute-start(bf16[64,64]{1,0:T(8,128)(2,1)S(1)} %fusion.3), channel_id=1, source_target_pairs={{0,2},{1,34},{2,66},{3,98},{4,3},{5,35},{6,67},{7,99},{8,0},{9,32}... | collective-permute-start | bytes 24584 | tf_op jit(solution)/shard_map/ppermute | solution.py:157
  172.5 3.8 %collective-permute-start.34 = (bf16[64,64]{1,0:T(8,128)(2,1)S(1)}, bf16[64,64]{1,0:T(8,128)(2,1)S(1)}, u32[]{:S(2)}, u32[]{:S(2)}) collective-permute-start(bf16[64,64]{1,0:T(8,128)(2,1)S(1)} %fusion.3), channel_id=1, source_target_pairs={{0,3},{1,35},{2,67},{3,99},{4,0},{5,32},{6,64},{7,96},{8,1},{9,33}... | collective-permute-start | bytes 24584 | tf_op jit(solution)/shard_map/ppermute | solution.py:157
  176.8 3.7 %collective-permute-start.35 = (f32[64,256]{1,0:T(8,128)S(1)}, f32[64,256]{1,0:T(8,128)S(1)}, u32[]{:S(2)}, u32[]{:S(2)}) collective-permute-start(f32[64,256]{1,0:T(8,128)S(1)} %constant_dynamic-slice_fusion), channel_id=1, source_target_pairs={{0,4},{4,0},{8,12},{12,8},{16,20},{20,16},{24,28},{28,24},{32,36},... | collective-permute-start | bytes 196616 | tf_op jit(solution)/shard_map/ppermute | solution.py:83
  180.6 7.7 %collective-permute-start.36 = (f32[64,256]{1,0:T(8,128)S(1)}, f32[64,256]{1,0:T(8,128)S(1)}, u32[]{:S(2)}, u32[]{:S(2)}) collective-permute-start(f32[64,256]{1,0:T(8,128)S(1)} %get-tuple-element.8), channel_id=1, source_target_pairs={{0,8},{4,12},{8,16},{12,20},{16,24},{20,28},{24,0},{28,4},{32,40},... | collective-permute-start | bytes 196616 | tf_op jit(solution)/shard_map/ppermute | solution.py:71
  180.9 8.5 %collective-permute-start.37 = (f32[64,256]{1,0:T(8,128)S(1)}, f32[64,256]{1,0:T(8,128)S(1)}, u32[]{:S(2)}, u32[]{:S(2)}) collective-permute-start(f32[64,256]{1,0:T(8,128)S(1)} %get-tuple-element.8), channel_id=1, source_target_pairs={{0,16},{4,20},{8,24},{12,28},{16,0},{20,4},{24,8},{28,12},{32,48},... | collective-permute-start | bytes 196616 | tf_op jit(solution)/shard_map/ppermute | solution.py:71
  185.7 4.4 %collective-permute-start.38 = (f32[64,256]{1,0:T(8,128)S(1)}, f32[64,256]{1,0:T(8,128)S(1)}, u32[]{:S(2)}, u32[]{:S(2)}) collective-permute-start(f32[64,256]{1,0:T(8,128)S(1)} %get-tuple-element.8), channel_id=1, source_target_pairs={{0,24},{4,28},{8,0},{12,4},{16,8},{20,12},{24,16},{28,20},{32,56},... | collective-permute-start | bytes 196616 | tf_op jit(solution)/shard_map/ppermute | solution.py:71
  190.2 9.2 %collective-permute-start.39 = (f32[64,256]{1,0:T(8,128)S(1)}, f32[64,256]{1,0:T(8,128)S(1)}, u32[]{:S(2)}, u32[]{:S(2)}) collective-permute-start(f32[64,256]{1,0:T(8,128)S(1)} %reduce_sum.146), channel_id=1, source_target_pairs={{0,32},{4,36},{8,40},{12,44},{16,48},{20,52},{24,56},{28,60},{32,6... | collective-permute-start | bytes 196616 | tf_op jit(solution)/shard_map/ppermute | solution.py:71
  192.7 8.0 %collective-permute-start.40 = (f32[64,256]{1,0:T(8,128)S(1)}, f32[64,256]{1,0:T(8,128)S(1)}, u32[]{:S(2)}, u32[]{:S(2)}) collective-permute-start(f32[64,256]{1,0:T(8,128)S(1)} %reduce_sum.146), channel_id=1, source_target_pairs={{0,64},{4,68},{8,72},{12,76},{16,80},{20,84},{24,88},{28,92},{32,9... | collective-permute-start | bytes 196616 | tf_op jit(solution)/shard_map/ppermute | solution.py:71
  197.7 4.3 %collective-permute-start.41 = (f32[64,256]{1,0:T(8,128)S(1)}, f32[64,256]{1,0:T(8,128)S(1)}, u32[]{:S(2)}, u32[]{:S(2)}) collective-permute-start(f32[64,256]{1,0:T(8,128)S(1)} %reduce_sum.146), channel_id=1, source_target_pairs={{0,96},{4,100},{8,104},{12,108},{16,112},{20,116},{24,120},{28,124... | collective-permute-start | bytes 196616 | tf_op jit(solution)/shard_map/ppermute | solution.py:71
  202.0 1.3 collective-permute-start.42
  203.5 4.8 %collective-permute-start.43 = (f32[64]{0:T(128)S(1)}, f32[64]{0:T(128)S(1)}, u32[]{:S(2)}, u32[]{:S(2)}) collective-permute-start(f32[64]{0:T(128)S(1)} %multiply_reduce_fusion.2), channel_id=1, source_target_pairs={{0,1},{1,2},{2,3},{3,0},{4,5},{5,6},{6,7},{7,4},{8,9},{9,10},{10,1... | collective-permute-start | bytes 776 | tf_op jit(solution)/shard_map/ppermute | solution.py:71
  204.1 5.1 %collective-permute-start.44 = (f32[64]{0:T(128)S(1)}, f32[64]{0:T(128)S(1)}, u32[]{:S(2)}, u32[]{:S(2)}) collective-permute-start(f32[64]{0:T(128)S(1)} %multiply_reduce_fusion.2), channel_id=1, source_target_pairs={{0,2},{1,3},{2,0},{3,1},{4,6},{5,7},{6,4},{7,5},{8,10},{9,11},{10,... | collective-permute-start | bytes 776 | tf_op jit(solution)/shard_map/ppermute | solution.py:71
  205.1 4.1 %collective-permute-start.45 = (f32[64]{0:T(128)S(1)}, f32[64]{0:T(128)S(1)}, u32[]{:S(2)}, u32[]{:S(2)}) collective-permute-start(f32[64]{0:T(128)S(1)} %multiply_reduce_fusion.2), channel_id=1, source_target_pairs={{0,3},{1,0},{2,1},{3,2},{4,7},{5,4},{6,5},{7,6},{8,11},{9,8},{10,9... | collective-permute-start | bytes 776 | tf_op jit(solution)/shard_map/ppermute | solution.py:71

commit v8 on v6

--- a/solution.py
+++ b/solution.py
@@ -65,12 +65,17 @@
 
 def exchange(value, axis, count, stride, size):
     digit = (lax.axis_index(axis) // stride) % size
-    stack = jnp.zeros((size,) + value.shape, value.dtype)
-    stack = lax.dynamic_update_index_in_dim(stack, value, digit, 0)
-    for shift in range(1, size):
-        received = lax.ppermute(value, axis, digit_pairs(count, stride, size, shift))
-        stack = lax.dynamic_update_index_in_dim(stack, received, (digit - shift) % size, 0)
-    return stack
+    pieces = [value] + [
+        lax.ppermute(value, axis, digit_pairs(count, stride, size, shift)) for shift in range(1, size)
+    ]
+    return jnp.stack([pick(pieces, (digit - slot) % size) for slot in range(size)])
+
+
+def pick(pieces, index):
+    chosen = pieces[0]
+    for k in range(1, len(pieces)):
+        chosen = jnp.where(index == k, pieces[k], chosen)
+    return chosen
 
 
 def scatter_digit(current, stride, size):
@@ -147,18 +152,15 @@
     holders = width // slice_width
     assert holders == MP_SIZE
     mp = lax.axis_index("mp")
-    result = jnp.zeros((piece.shape[0], width), piece.dtype)
+    received = []
     for shift in range(MP_SIZE):
         pairs = [
             (s * MP_SIZE + m, (m * per + s // holders) * MP_SIZE + (s % holders + shift) % MP_SIZE)
             for s in range(SEQ_SIZE)
             for m in range(MP_SIZE)
         ]
-        received = lax.ppermute(piece, ("seq", "mp"), pairs)
-        result = lax.dynamic_update_slice_in_dim(
-            result, received, ((mp - shift) % MP_SIZE) * slice_width, 1
-        )
-    return result
+        received.append(lax.ppermute(piece, ("seq", "mp"), pairs))
+    return jnp.concatenate([pick(received, (mp - slot) % MP_SIZE) for slot in range(MP_SIZE)], axis=1)
 
 
 def full_rows(weight):

time: 206 us -> 204 us (level)
  waiting for transfers between devices: 50.4 us -> 72.8 us
  starting transfers between devices: 118 us -> 98.7 us
  local copies, waits for them, and re-layouts: 14.9 us -> 7.86 us
  matrix products: 10.8 us -> 13.1 us
    ppermute x30, waiting for transfers between devices: 35.5 us -> 54.5 us  [exchange(): lax.ppermute(value, axis, digit_pairs(count, stride, size, shift))]
    ppermute x8, starting transfers between devices: 27.4 us -> 16 us  [deliver(): received.append(lax.ppermute(piece, ('seq', 'mp'), pairs))]
    all_to_all x1, starting transfers between devices: 12.7 us -> 3.89 us  [full_rows(): lax.all_to_all(weight.reshape(rows, SEQ_SIZE, block), 'seq', 1, 0, tiled=...]
    dynamic_update_slice x47 -> x0, local copies, waits for them, and re-layouts: 6.19 us -> none  [the longest x30 3.84 us: exchange(): lax.dynamic_update_index_in_dim(stack, received, (digit - shift) % size, 0)]
    ppermute x3, starting transfers between devices: 5.71 us -> 11 us  [scatter_digit(): lax.ppermute(send, 'seq', digit_pairs(SEQ_SIZE, stride, size, shift))]
    all_to_all x1, starting transfers between devices: 6.74 us -> 3.86 us  [local(): sources = lax.all_to_all(send, 'seq', 0, 0, tiled=True)]
    ppermute x8, waiting for transfers between devices: 1.86 us -> 4.7 us  [deliver(): received.append(lax.ppermute(piece, ('seq', 'mp'), pairs))]
    dot_general x1, matrix products: 1.24 us -> 3.43 us  [local(): lax.dot_general(values, weights.astype(jnp.bfloat16).reshape(local_heads...]
  transfers between devices with their start and end apart: 47 -> 47, of which waited for: 28 -> 33; matrix products, arithmetic and copies ran while one was open for 7% -> 3% of each run, Pallas kernels for 0% -> 0%
where the time goes in v8:
time: 204 us; the launch traced here: 203 us
  starting transfers between devices  98.7 us (48%)
  waiting for transfers between devices  72.8 us (36%)
  matrix products  13.1 us (6%)
  other arithmetic  9.88 us (5%)
  local copies, waits for them, and re-layouts  7.86 us (4%)
    ppermute x30, starting transfers between devices, exchange(): lax.ppermute(value, axis, digit_pairs(count, stride, size, shift))  63.1 us
    ppermute x30, waiting for transfers between devices, exchange(): lax.ppermute(value, axis, digit_pairs(count, stride, size, shift))  54.5 us
    ppermute x8, starting transfers between devices, deliver(): received.append(lax.ppermute(piece, ('seq', 'mp'), pairs))  16 us
    ppermute x3, starting transfers between devices, scatter_digit(): lax.ppermute(send, 'seq', digit_pairs(SEQ_SIZE, stride, size, shift))  11 us
    all_to_all x1, waiting for transfers between devices, local(): sources = lax.all_to_all(send, 'seq', 0, 0, tiled=True)  7.06 us
    dot_general x1, matrix products, local(): lax.dot_general(block_queries, keys, (((1,), (1,)), ((), ())), preferred_...  5.53 us
    ppermute x8, waiting for transfers between devices, deliver(): received.append(lax.ppermute(piece, ('seq', 'mp'), pairs))  4.7 us
  transfers between devices with their start and end apart: 47, of which 33 were waited for; matrix products, arithmetic and copies ran while one was open for 3% of the time, Pallas kernels for 0%

profile of v8, /device:TPU:0, one launch (start us, length us, event | category | flops | bytes accessed | tf_op | source)
XLA Modules:
  0.0 203.3 jit_solution(6514165270749880219)
XLA Ops:
  3.8 1.0 fusion.55
  4.8 1.0 fusion.54
  5.8 1.0 fusion.53
  8.4 3.0 %collective-permute-start.2 = (f32[64,768]{1,0:T(8,128)S(1)}, f32[64,768]{1,0:T(8,128)S(1)}, u32[]{:S(2)}, u32[]{:S(2)}) collective-permute-start(f32[64,768]{1,0:T(8,128)S(1)} %dynamic-slice_add_fusion), channel_id=1, source_target_pairs={{0,24},{4,28},{8,0},{12,4},{16,8},{20,12},{24,16},{28,20},{32,56},... | collective-permute-start | bytes 589832 | tf_op jit(solution)/shard_map/ppermute | solution.py:69
  12.1 0.9 collective-permute-start.4
  13.0 7.0 %collective-permute-done.2 = f32[64,768]{1,0:T(8,128)S(1)} collective-permute-done((f32[64,768]{1,0:T(8,128)S(1)}, f32[64,768]{1,0:T(8,128)S(1)}, u32[]{:S(2)}, u32[]{:S(2)}) %collective-permute-start.2) | collective-permute-done | bytes 196640 | tf_op jit(solution)/shard_map/ppermute | solution.py:69
  20.7 3.1 %collective-permute-done.4 = f32[64,768]{1,0:T(8,128)S(1)} collective-permute-done((f32[64,768]{1,0:T(8,128)S(1)}, f32[64,768]{1,0:T(8,128)S(1)}, u32[]{:S(2)}, u32[]{:S(2)}) %collective-permute-start.4) | collective-permute-done | bytes 196640 | tf_op jit(solution)/shard_map/ppermute | solution.py:69
  23.8 9.1 %collective-permute-start.5 = (f32[64,768]{1,0:T(8,128)S(1)}, f32[64,768]{1,0:T(8,128)S(1)}, u32[]{:S(2)}, u32[]{:S(2)}) collective-permute-start(f32[64,768]{1,0:T(8,128)S(1)} %select_add_fusion.1), channel_id=1, source_target_pairs={{0,96},{4,100},{8,104},{12,108},{16,112},{20,116},{24,120},{28,124... | collective-permute-start | bytes 589832 | tf_op jit(solution)/shard_map/ppermute | solution.py:69
  32.9 0.9 collective-permute-start.6
  33.7 1.3 collective-permute-start.7
  35.3 6.2 %collective-permute-done.5 = f32[64,768]{1,0:T(8,128)S(1)} collective-permute-done((f32[64,768]{1,0:T(8,128)S(1)}, f32[64,768]{1,0:T(8,128)S(1)}, u32[]{:S(2)}, u32[]{:S(2)}) %collective-permute-start.5) | collective-permute-done | bytes 196640 | tf_op jit(solution)/shard_map/ppermute | solution.py:69
  42.2 2.9 %collective-permute-done.7 = f32[64,768]{1,0:T(8,128)S(1)} collective-permute-done((f32[64,768]{1,0:T(8,128)S(1)}, f32[64,768]{1,0:T(8,128)S(1)}, u32[]{:S(2)}, u32[]{:S(2)}) %collective-permute-start.7) | collective-permute-done | bytes 196640 | tf_op jit(solution)/shard_map/ppermute | solution.py:69
  45.4 1.4 collective-permute-done.8
  47.0 2.1 %collective-permute-start.9 = (f32[64,2]{0,1:T(2,128)S(1)}, f32[64,2]{0,1:T(2,128)S(1)}, u32[]{:S(2)}, u32[]{:S(2)}) collective-permute-start(f32[64,2]{0,1:T(2,128)S(1)} %pad_maximum_fusion.3), channel_id=1, source_target_pairs={{0,3},{1,0},{2,1},{3,2},{4,7},{5,4},{6,5},{7,6},{8,11},{9,8},{10,9... | collective-permute-start | bytes 1544 | tf_op jit(solution)/shard_map/ppermute | solution.py:69
  49.1 2.3 %collective-permute-start.10 = (f32[64,2]{0,1:T(2,128)S(1)}, f32[64,2]{0,1:T(2,128)S(1)}, u32[]{:S(2)}, u32[]{:S(2)}) collective-permute-start(f32[64,2]{0,1:T(2,128)S(1)} %pad_maximum_fusion.3), channel_id=1, source_target_pairs={{0,2},{1,3},{2,0},{3,1},{4,6},{5,7},{6,4},{7,5},{8,10},{9,11},{10,... | collective-permute-start | bytes 1544 | tf_op jit(solution)/shard_map/ppermute | solution.py:69
  51.7 2.5 %collective-permute-done.10 = f32[64,2]{0,1:T(2,128)S(1)} collective-permute-done((f32[64,2]{0,1:T(2,128)S(1)}, f32[64,2]{0,1:T(2,128)S(1)}, u32[]{:S(2)}, u32[]{:S(2)}) %collective-permute-start.10) | collective-permute-done | bytes 544 | tf_op jit(solution)/shard_map/ppermute | solution.py:69
  54.1 2.0 collective-permute-done.11
  56.7 5.5 %fusion.52 = (f32[4,4,16]{2,1,0:T(4,128)S(1)}, f32[4,4,16,4096]{3,2,1,0:T(8,128)}) fusion(bf16[4096,512,1,1]{1,0,3,2:T(8,128)(2,1)} %bitcast.142, pred[4,512]{1,0:T(4,128)(4,1)S(1)} %iota_compare_fusion.1, bf16[4,16,512]{2,1,0:T(8,128)(2,1)S(1)} %convert_element_type.52, pred[16,4096]{1,0:T(8,128)(4,1)S(1)} %fusion.9), kind=kOutput, calls=%fused_computation.162 | convolution fusion | flops 1077018368 | bytes 8522752 | tf_op jit(solution)/shard_map/dot_general | solution.py:257
  62.3 3.2 %fusion.2 = (bf16[4,4,16,4096]{3,2,1,0:T(8,128)(2,1)S(1)}, f32[4,4,16]{2,1,0:T(4,128)S(1)}) fusion(f32[4,4,16,4096]{3,2,1,0:T(8,128)} %get-tuple-element.48, f32[4,4,16]{2,1,0:T(4,128)S(1)} %get-tuple-element.47, pred[16,4096]{1,0:T(8,128)(4,1)S(1)} %fusion.9), kind=kLoop, calls=%fused_computation.4 | loop fusion | flops 4194048 | bytes 6359040 | tf_op jit(solution)/shard_map/convert_element_type | solution.py:268
  65.6 3.4 %convolution_bitcast_fusion = f32[512,256]{0,1:T(8,128)S(1)} fusion(bf16[256,4096]{1,0:T(8,128)(2,1)S(1)} %bitcast.114, bf16[4096,512]{1,0:T(8,128)(2,1)} %bitcast.143), kind=kOutput, calls=%fused_computation.5 | convolution fusion | flops 1073741824 | bytes 6815744 | tf_op jit(solution)/shard_map/dot_general | solution.py:266
  70.8 3.9 %all-to-all-start = ((f32[32,1,1152]{2,1,0:T(1,128)}), f32[32,1,1152]{2,1,0:T(1,128)S(1)}, u32[]{:S(2)}, u32[]{:S(2)}) async-start(f32[32,1,1152]{2,1,0:T(1,128)} %reshape.432), calls=%async_computation | async-start | bytes 294912 | tf_op jit(solution)/shard_map/all_to_all | solution.py:285
  75.5 7.1 %all-to-all-done = f32[32,1,1152]{2,1,0:T(1,128)S(1)} async-done(((f32[32,1,1152]{2,1,0:T(1,128)}), f32[32,1,1152]{2,1,0:T(1,128)S(1)}, u32[]{:S(2)}, u32[]{:S(2)}) %all-to-all-start) | async-done | bytes 147488 | tf_op jit(solution)/shard_map/all_to_all | solution.py:285
  83.0 1.0 reduce.37
  85.6 1.9 collective-permute-start.12
  87.6 1.9 collective-permute-start.13
  89.5 1.9 collective-permute-start.14
  92.2 2.2 %collective-permute-done.14 = bf16[64,16]{0,1:T(8,128)(2,1)S(1)} collective-permute-done((bf16[64,16]{0,1:T(8,128)(2,1)S(1)}, bf16[64,16]{0,1:T(8,128)(2,1)S(1)}, u32[]{:S(2)}, u32[]{:S(2)}) %collective-permute-start.14) | collective-permute-done | bytes 2080 | tf_op jit(solution)/shard_map/ppermute | solution.py:162
  94.7 5.6 %collective-permute-start.16 = (f32[64,256]{1,0:T(8,128)S(1)}, f32[64,256]{1,0:T(8,128)S(1)}, u32[]{:S(2)}, u32[]{:S(2)}) collective-permute-start(f32[64,256]{1,0:T(8,128)S(1)} %constant_dynamic-slice_fusion.1), channel_id=1, source_target_pairs={{0,4},{4,0},{8,12},{12,8},{16,20},{20,16},{24,28},{28,24},{32,36},... | collective-permute-start | bytes 196616 | tf_op jit(solution)/shard_map/ppermute | solution.py:88
  100.2 0.9 collective-permute-done.16
  101.2 5.2 %collective-permute-start.17 = (f32[64,256]{1,0:T(8,128)S(1)}, f32[64,256]{1,0:T(8,128)S(1)}, u32[]{:S(2)}, u32[]{:S(2)}) collective-permute-start(f32[64,256]{1,0:T(8,128)S(1)} %dynamic-slice_add_fusion.2), channel_id=1, source_target_pairs={{0,24},{4,28},{8,0},{12,4},{16,8},{20,12},{24,16},{28,20},{32,56},... | collective-permute-start | bytes 196616 | tf_op jit(solution)/shard_map/ppermute | solution.py:69
  106.4 1.4 collective-permute-start.18
  107.8 1.3 collective-permute-start.19
  109.1 3.4 %collective-permute-done.18 = f32[64,256]{1,0:T(8,128)S(1)} collective-permute-done((f32[64,256]{1,0:T(8,128)S(1)}, f32[64,256]{1,0:T(8,128)S(1)}, u32[]{:S(2)}, u32[]{:S(2)}) %collective-permute-start.18) | collective-permute-done | bytes 65568 | tf_op jit(solution)/shard_map/ppermute | solution.py:69
  112.5 1.0 collective-permute-done.19
  113.6 7.4 %collective-permute-start.20 = (f32[64,256]{1,0:T(8,128)S(1)}, f32[64,256]{1,0:T(8,128)S(1)}, u32[]{:S(2)}, u32[]{:S(2)}) collective-permute-start(f32[64,256]{1,0:T(8,128)S(1)} %select_add_fusion.5), channel_id=1, source_target_pairs={{0,96},{4,100},{8,104},{12,108},{16,112},{20,116},{24,120},{28,124... | collective-permute-start | bytes 196616 | tf_op jit(solution)/shard_map/ppermute | solution.py:69
  121.0 0.9 collective-permute-start.22
  122.0 1.6 collective-permute-done.20
  123.5 3.3 %collective-permute-done.21 = f32[64,256]{1,0:T(8,128)S(1)} collective-permute-done((f32[64,256]{1,0:T(8,128)S(1)}, f32[64,256]{1,0:T(8,128)S(1)}, u32[]{:S(2)}, u32[]{:S(2)}) %collective-permute-start.21) | collective-permute-done | bytes 65568 | tf_op jit(solution)/shard_map/ppermute | solution.py:69
  128.8 3.0 %collective-permute-start.25 = (f32[64]{0:T(128)S(1)}, f32[64]{0:T(128)S(1)}, u32[]{:S(2)}, u32[]{:S(2)}) collective-permute-start(f32[64]{0:T(128)S(1)} %multiply_reduce_fusion.1), channel_id=1, source_target_pairs={{0,2},{1,3},{2,0},{3,1},{4,6},{5,7},{6,4},{7,5},{8,10},{9,11},{10,... | collective-permute-start | bytes 776 | tf_op jit(solution)/shard_map/ppermute | solution.py:69
  132.1 1.0 copy.107
  133.1 3.9 %all-to-all-start.1 = ((bf16[64,32,128]{2,0,1:T(8,128)(2,1)}), bf16[64,32,128]{2,0,1:T(8,128)(2,1)S(1)}, u32[]{:S(2)}, u32[]{:S(2)}) async-start(bf16[64,32,128]{2,0,1:T(8,128)(2,1)} %copy.107), calls=%async_computation.1 | async-start | bytes 1048576 | tf_op jit(solution)/shard_map/all_to_all | solution.py:169
  137.1 3.3 %collective-permute-start.27 = (bf16[64,512]{1,0:T(8,128)(2,1)S(1)}, bf16[64,512]{1,0:T(8,128)(2,1)S(1)}, u32[]{:S(2)}, u32[]{:S(2)}) collective-permute-start(bf16[64,512]{1,0:T(8,128)(2,1)S(1)} %add_convert_fusion.1), channel_id=1, source_target_pairs={{0,3},{1,0},{2,1},{3,2},{4,7},{5,4},{6,5},{7,6},{8,11},{9,8},{10,9... | collective-permute-start | bytes 196616 | tf_op jit(solution)/shard_map/ppermute | solution.py:69
  140.6 1.3 collective-permute-start.29
  141.9 1.7 collective-permute-done.27
  143.6 2.9 %collective-permute-done.28 = bf16[64,512]{1,0:T(8,128)(2,1)S(1)} collective-permute-done((bf16[64,512]{1,0:T(8,128)(2,1)S(1)}, bf16[64,512]{1,0:T(8,128)(2,1)S(1)}, u32[]{:S(2)}, u32[]{:S(2)}) %collective-permute-start.28) | collective-permute-done | bytes 65568 | tf_op jit(solution)/shard_map/ppermute | solution.py:69
  147.3 1.2 all-to-all-done.1
  149.1 5.1 %collective-permute-start.30 = (bf16[64,64]{1,0:T(8,128)(2,1)S(1)}, bf16[64,64]{1,0:T(8,128)(2,1)S(1)}, u32[]{:S(2)}, u32[]{:S(2)}) collective-permute-start(bf16[64,64]{1,0:T(8,128)(2,1)S(1)} %fusion.3), channel_id=1, source_target_pairs={{0,3},{1,35},{2,67},{3,99},{4,0},{5,32},{6,64},{7,96},{8,1},{9,33}... | collective-permute-start | bytes 24584 | tf_op jit(solution)/shard_map/ppermute | solution.py:162
  154.3 1.9 collective-permute-start.31
  156.1 1.9 collective-permute-start.32
  158.8 2.4 %collective-permute-done.32 = bf16[64,64]{1,0:T(8,128)(2,1)S(1)} collective-permute-done((bf16[64,64]{1,0:T(8,128)(2,1)S(1)}, bf16[64,64]{1,0:T(8,128)(2,1)S(1)}, u32[]{:S(2)}, u32[]{:S(2)}) %collective-permute-start.32) | collective-permute-done | bytes 8224 | tf_op jit(solution)/shard_map/ppermute | solution.py:162
  161.5 5.3 %collective-permute-start.34 = (f32[64,256]{1,0:T(8,128)S(1)}, f32[64,256]{1,0:T(8,128)S(1)}, u32[]{:S(2)}, u32[]{:S(2)}) collective-permute-start(f32[64,256]{1,0:T(8,128)S(1)} %constant_dynamic-slice_fusion), channel_id=1, source_target_pairs={{0,4},{4,0},{8,12},{12,8},{16,20},{20,16},{24,28},{28,24},{32,36},... | collective-permute-start | bytes 196616 | tf_op jit(solution)/shard_map/ppermute | solution.py:88
  166.8 0.9 collective-permute-done.34
  167.7 3.6 %collective-permute-start.35 = (f32[64,256]{1,0:T(8,128)S(1)}, f32[64,256]{1,0:T(8,128)S(1)}, u32[]{:S(2)}, u32[]{:S(2)}) collective-permute-start(f32[64,256]{1,0:T(8,128)S(1)} %dynamic-slice_add_fusion.1), channel_id=1, source_target_pairs={{0,24},{4,28},{8,0},{12,4},{16,8},{20,12},{24,16},{28,20},{32,56},... | collective-permute-start | bytes 196616 | tf_op jit(solution)/shard_map/ppermute | solution.py:69
  171.3 0.9 collective-permute-start.36
  172.2 1.3 collective-permute-start.37
  173.6 3.8 %collective-permute-done.36 = f32[64,256]{1,0:T(8,128)S(1)} collective-permute-done((f32[64,256]{1,0:T(8,128)S(1)}, f32[64,256]{1,0:T(8,128)S(1)}, u32[]{:S(2)}, u32[]{:S(2)}) %collective-permute-start.36) | collective-permute-done | bytes 65568 | tf_op jit(solution)/shard_map/ppermute | solution.py:69
  178.1 7.0 %collective-permute-start.38 = (f32[64,256]{1,0:T(8,128)S(1)}, f32[64,256]{1,0:T(8,128)S(1)}, u32[]{:S(2)}, u32[]{:S(2)}) collective-permute-start(f32[64,256]{1,0:T(8,128)S(1)} %select_add_fusion.3), channel_id=1, source_target_pairs={{0,96},{4,100},{8,104},{12,108},{16,112},{20,116},{24,120},{28,124... | collective-permute-start | bytes 196616 | tf_op jit(solution)/shard_map/ppermute | solution.py:69
  185.1 2.4 %collective-permute-start.39 = (f32[64,256]{1,0:T(8,128)S(1)}, f32[64,256]{1,0:T(8,128)S(1)}, u32[]{:S(2)}, u32[]{:S(2)}) collective-permute-start(f32[64,256]{1,0:T(8,128)S(1)} %select_add_fusion.3), channel_id=1, source_target_pairs={{0,64},{4,68},{8,72},{12,76},{16,80},{20,84},{24,88},{28,92},{32,9... | collective-permute-start | bytes 196616 | tf_op jit(solution)/shard_map/ppermute | solution.py:69
  187.7 3.5 %collective-permute-done.39 = f32[64,256]{1,0:T(8,128)S(1)} collective-permute-done((f32[64,256]{1,0:T(8,128)S(1)}, f32[64,256]{1,0:T(8,128)S(1)}, u32[]{:S(2)}, u32[]{:S(2)}) %collective-permute-start.39) | collective-permute-done | bytes 65568 | tf_op jit(solution)/shard_map/ppermute | solution.py:69
  191.2 1.8 collective-permute-done.40
  193.2 1.2 collective-permute-done.41
  194.6 3.1 %collective-permute-start.43 = (f32[64]{0:T(128)S(1)}, f32[64]{0:T(128)S(1)}, u32[]{:S(2)}, u32[]{:S(2)}) collective-permute-start(f32[64]{0:T(128)S(1)} %multiply_reduce_fusion), channel_id=1, source_target_pairs={{0,2},{1,3},{2,0},{3,1},{4,6},{5,7},{6,4},{7,5},{8,10},{9,11},{10,... | collective-permute-start | bytes 776 | tf_op jit(solution)/shard_map/ppermute | solution.py:69
  198.2 1.6 collective-permute-done.43
  199.8 2.8 %collective-permute-done.44 = f32[64]{0:T(128)S(1)} collective-permute-done((f32[64]{0:T(128)S(1)}, f32[64]{0:T(128)S(1)}, u32[]{:S(2)}, u32[]{:S(2)}) %collective-permute-start.44) | collective-permute-done | bytes 288 | tf_op jit(solution)/shard_map/ppermute | solution.py:69
  (166 shorter events, 21.9 us)
Async XLA Ops:
  0.0 161.2 %copy-start = (bf16[256,512]{1,0:T(8,128)(2,1)S(1)}, bf16[256,512]{1,0:T(8,128)(2,1)}, u32[]{:S(2)}) copy-start(bf16[256,512]{1,0:T(8,128)(2,1)} %param.24) | copy-start | bytes 786436
  0.0 56.1 %copy-start.5 = (f32[512]{0:T(512)S(1)}, f32[512]{0:T(512)}, u32[]{:S(2)}) copy-start(f32[512]{0:T(512)} %param.26) | copy-start | bytes 6148
  0.0 56.2 %copy-start.6 = (f32[512]{0:T(512)S(1)}, f32[512]{0:T(512)}, u32[]{:S(2)}) copy-start(f32[512]{0:T(512)} %param.25) | copy-start | bytes 6148
  0.8 3.0 %collective-permute-start = (bf16[64,64]{1,0:T(8,128)(2,1)S(1)}, bf16[64,64]{1,0:T(8,128)(2,1)S(1)}, u32[]{:S(2)}, u32[]{:S(2)}) collective-permute-start(bf16[64,64]{1,0:T(8,128)(2,1)S(1)} %constant_dynamic-slice_fusion.5), channel_id=1, source_target_pairs={{0,0},{1,32},{2,64},{3,96},{4,4},{5,36},{6,68},{7,100},{8,8},{9,40... | collective-permute-start | bytes 24584 | tf_op jit(solution)/shard_map/ppermute | solution.py:47
  6.8 1.5 collective-permute-start.1
  8.4 11.6 %collective-permute-start.2 = (f32[64,768]{1,0:T(8,128)S(1)}, f32[64,768]{1,0:T(8,128)S(1)}, u32[]{:S(2)}, u32[]{:S(2)}) collective-permute-start(f32[64,768]{1,0:T(8,128)S(1)} %dynamic-slice_add_fusion), channel_id=1, source_target_pairs={{0,24},{4,28},{8,0},{12,4},{16,8},{20,12},{24,16},{28,20},{32,56},... | collective-permute-start | bytes 589832 | tf_op jit(solution)/shard_map/ppermute | solution.py:69
  11.3 9.3 %collective-permute-start.3 = (f32[64,768]{1,0:T(8,128)S(1)}, f32[64,768]{1,0:T(8,128)S(1)}, u32[]{:S(2)}, u32[]{:S(2)}) collective-permute-start(f32[64,768]{1,0:T(8,128)S(1)} %dynamic-slice_add_fusion), channel_id=1, source_target_pairs={{0,16},{4,20},{8,24},{12,28},{16,0},{20,4},{24,8},{28,12},{32,48},... | collective-permute-start | bytes 589832 | tf_op jit(solution)/shard_map/ppermute | solution.py:69
  12.1 11.6 %collective-permute-start.4 = (f32[64,768]{1,0:T(8,128)S(1)}, f32[64,768]{1,0:T(8,128)S(1)}, u32[]{:S(2)}, u32[]{:S(2)}) collective-permute-start(f32[64,768]{1,0:T(8,128)S(1)} %dynamic-slice_add_fusion), channel_id=1, source_target_pairs={{0,8},{4,12},{8,16},{12,20},{16,24},{20,28},{24,0},{28,4},{32,40},... | collective-permute-start | bytes 589832 | tf_op jit(solution)/shard_map/ppermute | solution.py:69
  23.8 17.6 %collective-permute-start.5 = (f32[64,768]{1,0:T(8,128)S(1)}, f32[64,768]{1,0:T(8,128)S(1)}, u32[]{:S(2)}, u32[]{:S(2)}) collective-permute-start(f32[64,768]{1,0:T(8,128)S(1)} %select_add_fusion.1), channel_id=1, source_target_pairs={{0,96},{4,100},{8,104},{12,108},{16,112},{20,116},{24,120},{28,124... | collective-permute-start | bytes 589832 | tf_op jit(solution)/shard_map/ppermute | solution.py:69
  32.9 9.3 %collective-permute-start.6 = (f32[64,768]{1,0:T(8,128)S(1)}, f32[64,768]{1,0:T(8,128)S(1)}, u32[]{:S(2)}, u32[]{:S(2)}) collective-permute-start(f32[64,768]{1,0:T(8,128)S(1)} %select_add_fusion.1), channel_id=1, source_target_pairs={{0,64},{4,68},{8,72},{12,76},{16,80},{20,84},{24,88},{28,92},{32,9... | collective-permute-start | bytes 589832 | tf_op jit(solution)/shard_map/ppermute | solution.py:69
  33.7 11.4 %collective-permute-start.7 = (f32[64,768]{1,0:T(8,128)S(1)}, f32[64,768]{1,0:T(8,128)S(1)}, u32[]{:S(2)}, u32[]{:S(2)}) collective-permute-start(f32[64,768]{1,0:T(8,128)S(1)} %select_add_fusion.1), channel_id=1, source_target_pairs={{0,32},{4,36},{8,40},{12,44},{16,48},{20,52},{24,56},{28,60},{32,6... | collective-permute-start | bytes 589832 | tf_op jit(solution)/shard_map/ppermute | solution.py:69
  45.3 1.5 collective-permute-start.8
  47.0 4.7 %collective-permute-start.9 = (f32[64,2]{0,1:T(2,128)S(1)}, f32[64,2]{0,1:T(2,128)S(1)}, u32[]{:S(2)}, u32[]{:S(2)}) collective-permute-start(f32[64,2]{0,1:T(2,128)S(1)} %pad_maximum_fusion.3), channel_id=1, source_target_pairs={{0,3},{1,0},{2,1},{3,2},{4,7},{5,4},{6,5},{7,6},{8,11},{9,8},{10,9... | collective-permute-start | bytes 1544 | tf_op jit(solution)/shard_map/ppermute | solution.py:69
  49.1 5.1 %collective-permute-start.10 = (f32[64,2]{0,1:T(2,128)S(1)}, f32[64,2]{0,1:T(2,128)S(1)}, u32[]{:S(2)}, u32[]{:S(2)}) collective-permute-start(f32[64,2]{0,1:T(2,128)S(1)} %pad_maximum_fusion.3), channel_id=1, source_target_pairs={{0,2},{1,3},{2,0},{3,1},{4,6},{5,7},{6,4},{7,5},{8,10},{9,11},{10,... | collective-permute-start | bytes 1544 | tf_op jit(solution)/shard_map/ppermute | solution.py:69
  51.3 4.8 %collective-permute-start.11 = (f32[64,2]{0,1:T(2,128)S(1)}, f32[64,2]{0,1:T(2,128)S(1)}, u32[]{:S(2)}, u32[]{:S(2)}) collective-permute-start(f32[64,2]{0,1:T(2,128)S(1)} %pad_maximum_fusion.3), channel_id=1, source_target_pairs={{0,1},{1,2},{2,3},{3,0},{4,5},{5,6},{6,7},{7,4},{8,9},{9,10},{10,1... | collective-permute-start | bytes 1544 | tf_op jit(solution)/shard_map/ppermute | solution.py:69
  69.0 25.4 %copy-start.4 = (bf16[64,512]{1,0:T(8,128)(2,1)S(1)}, bf16[64,512]{1,0:T(8,128)(2,1)}, u32[]{:S(2)}) copy-start(bf16[64,512]{1,0:T(8,128)(2,1)} %param.21) | copy-start | bytes 196612
  69.0 58.3 %copy-start.1 = (bf16[64,2048]{1,0:T(8,128)(2,1)S(1)}, bf16[64,2048]{1,0:T(8,128)(2,1)}, u32[]{:S(2)}) copy-start(bf16[64,2048]{1,0:T(8,128)(2,1)} %param.23) | copy-start | bytes 786436
  69.2 58.7 %copy-start.2 = (bf16[64,2048]{1,0:T(8,128)(2,1)S(1)}, bf16[64,2048]{1,0:T(8,128)(2,1)}, u32[]{:S(2)}) copy-start(bf16[64,2048]{1,0:T(8,128)(2,1)} %param.22) | copy-start | bytes 786436
  70.8 11.8 %all-to-all-start = ((f32[32,1,1152]{2,1,0:T(1,128)}), f32[32,1,1152]{2,1,0:T(1,128)S(1)}, u32[]{:S(2)}, u32[]{:S(2)}) async-start(f32[32,1,1152]{2,1,0:T(1,128)} %reshape.432), calls=%async_computation | async-start | bytes 294912 | tf_op jit(solution)/shard_map/all_to_all | solution.py:285
  84.0 53.0 %copy-start.3 = (bf16[4,16,512]{2,1,0:T(8,128)(2,1)S(1)}, bf16[4,16,512]{2,1,0:T(8,128)(2,1)}, u32[]{:S(2)}) copy-start(bf16[4,16,512]{2,1,0:T(8,128)(2,1)} %param.17) | copy-start | bytes 196612
  84.0 53.0 %copy-start.7 = (f32[512]{0:T(512)S(1)}, f32[512]{0:T(512)}, u32[]{:S(2)}) copy-start(f32[512]{0:T(512)} %param.27) | copy-start | bytes 6148
  85.6 6.5 %collective-permute-start.12 = (bf16[64,16]{0,1:T(8,128)(2,1)S(1)}, bf16[64,16]{0,1:T(8,128)(2,1)S(1)}, u32[]{:S(2)}, u32[]{:S(2)}) collective-permute-start(bf16[64,16]{0,1:T(8,128)(2,1)S(1)} %copy.111), channel_id=1, source_target_pairs={{0,3},{1,35},{2,67},{3,99},{4,0},{5,32},{6,64},{7,96},{8,1},{9,33}... | collective-permute-start | bytes 6152 | tf_op jit(solution)/shard_map/ppermute | solution.py:162
  87.6 4.6 %collective-permute-start.13 = (bf16[64,16]{0,1:T(8,128)(2,1)S(1)}, bf16[64,16]{0,1:T(8,128)(2,1)S(1)}, u32[]{:S(2)}, u32[]{:S(2)}) collective-permute-start(bf16[64,16]{0,1:T(8,128)(2,1)S(1)} %copy.111), channel_id=1, source_target_pairs={{0,2},{1,34},{2,66},{3,98},{4,3},{5,35},{6,67},{7,99},{8,0},{9,32}... | collective-permute-start | bytes 6152 | tf_op jit(solution)/shard_map/ppermute | solution.py:162
  89.5 4.9 %collective-permute-start.14 = (bf16[64,16]{0,1:T(8,128)(2,1)S(1)}, bf16[64,16]{0,1:T(8,128)(2,1)S(1)}, u32[]{:S(2)}, u32[]{:S(2)}) collective-permute-start(bf16[64,16]{0,1:T(8,128)(2,1)S(1)} %copy.111), channel_id=1, source_target_pairs={{0,1},{1,33},{2,65},{3,97},{4,2},{5,34},{6,66},{7,98},{8,3},{9,35}... | collective-permute-start | bytes 6152 | tf_op jit(solution)/shard_map/ppermute | solution.py:162
  91.4 3.0 %collective-permute-start.15 = (bf16[64,16]{0,1:T(8,128)(2,1)S(1)}, bf16[64,16]{0,1:T(8,128)(2,1)S(1)}, u32[]{:S(2)}, u32[]{:S(2)}) collective-permute-start(bf16[64,16]{0,1:T(8,128)(2,1)S(1)} %copy.111), channel_id=1, source_target_pairs={{0,0},{1,32},{2,64},{3,96},{4,1},{5,33},{6,65},{7,97},{8,2},{9,34}... | collective-permute-start | bytes 6152 | tf_op jit(solution)/shard_map/ppermute | solution.py:162
  94.7 6.5 %collective-permute-start.16 = (f32[64,256]{1,0:T(8,128)S(1)}, f32[64,256]{1,0:T(8,128)S(1)}, u32[]{:S(2)}, u32[]{:S(2)}) collective-permute-start(f32[64,256]{1,0:T(8,128)S(1)} %constant_dynamic-slice_fusion.1), channel_id=1, source_target_pairs={{0,4},{4,0},{8,12},{12,8},{16,20},{20,16},{24,28},{28,24},{32,36},... | collective-permute-start | bytes 196616 | tf_op jit(solution)/shard_map/ppermute | solution.py:88
  101.2 8.0 %collective-permute-start.17 = (f32[64,256]{1,0:T(8,128)S(1)}, f32[64,256]{1,0:T(8,128)S(1)}, u32[]{:S(2)}, u32[]{:S(2)}) collective-permute-start(f32[64,256]{1,0:T(8,128)S(1)} %dynamic-slice_add_fusion.2), channel_id=1, source_target_pairs={{0,24},{4,28},{8,0},{12,4},{16,8},{20,12},{24,16},{28,20},{32,56},... | collective-permute-start | bytes 196616 | tf_op jit(solution)/shard_map/ppermute | solution.py:69
  106.4 6.2 %collective-permute-start.18 = (f32[64,256]{1,0:T(8,128)S(1)}, f32[64,256]{1,0:T(8,128)S(1)}, u32[]{:S(2)}, u32[]{:S(2)}) collective-permute-start(f32[64,256]{1,0:T(8,128)S(1)} %dynamic-slice_add_fusion.2), channel_id=1, source_target_pairs={{0,16},{4,20},{8,24},{12,28},{16,0},{20,4},{24,8},{28,12},{32,48},... | collective-permute-start | bytes 196616 | tf_op jit(solution)/shard_map/ppermute | solution.py:69
  107.8 5.8 %collective-permute-start.19 = (f32[64,256]{1,0:T(8,128)S(1)}, f32[64,256]{1,0:T(8,128)S(1)}, u32[]{:S(2)}, u32[]{:S(2)}) collective-permute-start(f32[64,256]{1,0:T(8,128)S(1)} %dynamic-slice_add_fusion.2), channel_id=1, source_target_pairs={{0,8},{4,12},{8,16},{12,20},{16,24},{20,28},{24,0},{28,4},{32,40},... | collective-permute-start | bytes 196616 | tf_op jit(solution)/shard_map/ppermute | solution.py:69
  113.6 9.9 %collective-permute-start.20 = (f32[64,256]{1,0:T(8,128)S(1)}, f32[64,256]{1,0:T(8,128)S(1)}, u32[]{:S(2)}, u32[]{:S(2)}) collective-permute-start(f32[64,256]{1,0:T(8,128)S(1)} %select_add_fusion.5), channel_id=1, source_target_pairs={{0,96},{4,100},{8,104},{12,108},{16,112},{20,116},{24,120},{28,124... | collective-permute-start | bytes 196616 | tf_op jit(solution)/shard_map/ppermute | solution.py:69
  121.0 5.9 %collective-permute-start.21 = (f32[64,256]{1,0:T(8,128)S(1)}, f32[64,256]{1,0:T(8,128)S(1)}, u32[]{:S(2)}, u32[]{:S(2)}) collective-permute-start(f32[64,256]{1,0:T(8,128)S(1)} %select_add_fusion.5), channel_id=1, source_target_pairs={{0,64},{4,68},{8,72},{12,76},{16,80},{20,84},{24,88},{28,92},{32,9... | collective-permute-start | bytes 196616 | tf_op jit(solution)/shard_map/ppermute | solution.py:69
  121.0 6.2 %collective-permute-start.22 = (f32[64,256]{1,0:T(8,128)S(1)}, f32[64,256]{1,0:T(8,128)S(1)}, u32[]{:S(2)}, u32[]{:S(2)}) collective-permute-start(f32[64,256]{1,0:T(8,128)S(1)} %select_add_fusion.5), channel_id=1, source_target_pairs={{0,32},{4,36},{8,40},{12,44},{16,48},{20,52},{24,56},{28,60},{32,6... | collective-permute-start | bytes 196616 | tf_op jit(solution)/shard_map/ppermute | solution.py:69
  127.3 1.3 collective-permute-start.23
  128.7 8.2 %collective-permute-start.24 = (f32[64]{0:T(128)S(1)}, f32[64]{0:T(128)S(1)}, u32[]{:S(2)}, u32[]{:S(2)}) collective-permute-start(f32[64]{0:T(128)S(1)} %multiply_reduce_fusion.1), channel_id=1, source_target_pairs={{0,3},{1,0},{2,1},{3,2},{4,7},{5,4},{6,5},{7,6},{8,11},{9,8},{10,9... | collective-permute-start | bytes 776 | tf_op jit(solution)/shard_map/ppermute | solution.py:69
  128.8 8.2 %collective-permute-start.25 = (f32[64]{0:T(128)S(1)}, f32[64]{0:T(128)S(1)}, u32[]{:S(2)}, u32[]{:S(2)}) collective-permute-start(f32[64]{0:T(128)S(1)} %multiply_reduce_fusion.1), channel_id=1, source_target_pairs={{0,2},{1,3},{2,0},{3,1},{4,6},{5,7},{6,4},{7,5},{8,10},{9,11},{10,... | collective-permute-start | bytes 776 | tf_op jit(solution)/shard_map/ppermute | solution.py:69
  131.8 5.2 %collective-permute-start.26 = (f32[64]{0:T(128)S(1)}, f32[64]{0:T(128)S(1)}, u32[]{:S(2)}, u32[]{:S(2)}) collective-permute-start(f32[64]{0:T(128)S(1)} %multiply_reduce_fusion.1), channel_id=1, source_target_pairs={{0,1},{1,2},{2,3},{3,0},{4,5},{5,6},{6,7},{7,4},{8,9},{9,10},{10,1... | collective-permute-start | bytes 776 | tf_op jit(solution)/shard_map/ppermute | solution.py:69
  132.1 70.5 %copy-start.8 = (f32[512]{0:T(512)S(1)}, f32[512]{0:T(512)}, u32[]{:S(2)}) copy-start(f32[512]{0:T(512)} %param.28) | copy-start | bytes 6148
  133.1 15.5 %all-to-all-start.1 = ((bf16[64,32,128]{2,0,1:T(8,128)(2,1)}), bf16[64,32,128]{2,0,1:T(8,128)(2,1)S(1)}, u32[]{:S(2)}, u32[]{:S(2)}) async-start(bf16[64,32,128]{2,0,1:T(8,128)(2,1)} %copy.107), calls=%async_computation.1 | async-start | bytes 1048576 | tf_op jit(solution)/shard_map/all_to_all | solution.py:169
  137.1 6.5 %collective-permute-start.27 = (bf16[64,512]{1,0:T(8,128)(2,1)S(1)}, bf16[64,512]{1,0:T(8,128)(2,1)S(1)}, u32[]{:S(2)}, u32[]{:S(2)}) collective-permute-start(bf16[64,512]{1,0:T(8,128)(2,1)S(1)} %add_convert_fusion.1), channel_id=1, source_target_pairs={{0,3},{1,0},{2,1},{3,2},{4,7},{5,4},{6,5},{7,6},{8,11},{9,8},{10,9... | collective-permute-start | bytes 196616 | tf_op jit(solution)/shard_map/ppermute | solution.py:69
  140.4 6.1 %collective-permute-start.28 = (bf16[64,512]{1,0:T(8,128)(2,1)S(1)}, bf16[64,512]{1,0:T(8,128)(2,1)S(1)}, u32[]{:S(2)}, u32[]{:S(2)}) collective-permute-start(bf16[64,512]{1,0:T(8,128)(2,1)S(1)} %add_convert_fusion.1), channel_id=1, source_target_pairs={{0,2},{1,3},{2,0},{3,1},{4,6},{5,7},{6,4},{7,5},{8,10},{9,11},{10,... | collective-permute-start | bytes 196616 | tf_op jit(solution)/shard_map/ppermute | solution.py:69
  140.6 6.6 %collective-permute-start.29 = (bf16[64,512]{1,0:T(8,128)(2,1)S(1)}, bf16[64,512]{1,0:T(8,128)(2,1)S(1)}, u32[]{:S(2)}, u32[]{:S(2)}) collective-permute-start(bf16[64,512]{1,0:T(8,128)(2,1)S(1)} %add_convert_fusion.1), channel_id=1, source_target_pairs={{0,1},{1,2},{2,3},{3,0},{4,5},{5,6},{6,7},{7,4},{8,9},{9,10},{10,1... | collective-permute-start | bytes 196616 | tf_op jit(solution)/shard_map/ppermute | solution.py:69
  149.1 9.6 %collective-permute-start.30 = (bf16[64,64]{1,0:T(8,128)(2,1)S(1)}, bf16[64,64]{1,0:T(8,128)(2,1)S(1)}, u32[]{:S(2)}, u32[]{:S(2)}) collective-permute-start(bf16[64,64]{1,0:T(8,128)(2,1)S(1)} %fusion.3), channel_id=1, source_target_pairs={{0,3},{1,35},{2,67},{3,99},{4,0},{5,32},{6,64},{7,96},{8,1},{9,33}... | collective-permute-start | bytes 24584 | tf_op jit(solution)/shard_map/ppermute | solution.py:162
  154.3 4.5 %collective-permute-start.31 = (bf16[64,64]{1,0:T(8,128)(2,1)S(1)}, bf16[64,64]{1,0:T(8,128)(2,1)S(1)}, u32[]{:S(2)}, u32[]{:S(2)}) collective-permute-start(bf16[64,64]{1,0:T(8,128)(2,1)S(1)} %fusion.3), channel_id=1, source_target_pairs={{0,2},{1,34},{2,66},{3,98},{4,3},{5,35},{6,67},{7,99},{8,0},{9,32}... | collective-permute-start | bytes 24584 | tf_op jit(solution)/shard_map/ppermute | solution.py:162
  156.1 5.0 %collective-permute-start.32 = (bf16[64,64]{1,0:T(8,128)(2,1)S(1)}, bf16[64,64]{1,0:T(8,128)(2,1)S(1)}, u32[]{:S(2)}, u32[]{:S(2)}) collective-permute-start(bf16[64,64]{1,0:T(8,128)(2,1)S(1)} %fusion.3), channel_id=1, source_target_pairs={{0,1},{1,33},{2,65},{3,97},{4,2},{5,34},{6,66},{7,98},{8,3},{9,35}... | collective-permute-start | bytes 24584 | tf_op jit(solution)/shard_map/ppermute | solution.py:162
  158.1 3.1 %collective-permute-start.33 = (bf16[64,64]{1,0:T(8,128)(2,1)S(1)}, bf16[64,64]{1,0:T(8,128)(2,1)S(1)}, u32[]{:S(2)}, u32[]{:S(2)}) collective-permute-start(bf16[64,64]{1,0:T(8,128)(2,1)S(1)} %fusion.3), channel_id=1, source_target_pairs={{0,0},{1,32},{2,64},{3,96},{4,1},{5,33},{6,65},{7,97},{8,2},{9,34}... | collective-permute-start | bytes 24584 | tf_op jit(solution)/shard_map/ppermute | solution.py:162
  161.5 6.2 %collective-permute-start.34 = (f32[64,256]{1,0:T(8,128)S(1)}, f32[64,256]{1,0:T(8,128)S(1)}, u32[]{:S(2)}, u32[]{:S(2)}) collective-permute-start(f32[64,256]{1,0:T(8,128)S(1)} %constant_dynamic-slice_fusion), channel_id=1, source_target_pairs={{0,4},{4,0},{8,12},{12,8},{16,20},{20,16},{24,28},{28,24},{32,36},... | collective-permute-start | bytes 196616 | tf_op jit(solution)/shard_map/ppermute | solution.py:88
  167.7 5.9 %collective-permute-start.35 = (f32[64,256]{1,0:T(8,128)S(1)}, f32[64,256]{1,0:T(8,128)S(1)}, u32[]{:S(2)}, u32[]{:S(2)}) collective-permute-start(f32[64,256]{1,0:T(8,128)S(1)} %dynamic-slice_add_fusion.1), channel_id=1, source_target_pairs={{0,24},{4,28},{8,0},{12,4},{16,8},{20,12},{24,16},{28,20},{32,56},... | collective-permute-start | bytes 196616 | tf_op jit(solution)/shard_map/ppermute | solution.py:69
  171.3 6.1 %collective-permute-start.36 = (f32[64,256]{1,0:T(8,128)S(1)}, f32[64,256]{1,0:T(8,128)S(1)}, u32[]{:S(2)}, u32[]{:S(2)}) collective-permute-start(f32[64,256]{1,0:T(8,128)S(1)} %dynamic-slice_add_fusion.1), channel_id=1, source_target_pairs={{0,16},{4,20},{8,24},{12,28},{16,0},{20,4},{24,8},{28,12},{32,48},... | collective-permute-start | bytes 196616 | tf_op jit(solution)/shard_map/ppermute | solution.py:69
  172.2 5.8 %collective-permute-start.37 = (f32[64,256]{1,0:T(8,128)S(1)}, f32[64,256]{1,0:T(8,128)S(1)}, u32[]{:S(2)}, u32[]{:S(2)}) collective-permute-start(f32[64,256]{1,0:T(8,128)S(1)} %dynamic-slice_add_fusion.1), channel_id=1, source_target_pairs={{0,8},{4,12},{8,16},{12,20},{16,24},{20,28},{24,0},{28,4},{32,40},... | collective-permute-start | bytes 196616 | tf_op jit(solution)/shard_map/ppermute | solution.py:69
  178.1 9.6 %collective-permute-start.38 = (f32[64,256]{1,0:T(8,128)S(1)}, f32[64,256]{1,0:T(8,128)S(1)}, u32[]{:S(2)}, u32[]{:S(2)}) collective-permute-start(f32[64,256]{1,0:T(8,128)S(1)} %select_add_fusion.3), channel_id=1, source_target_pairs={{0,96},{4,100},{8,104},{12,108},{16,112},{20,116},{24,120},{28,124... | collective-permute-start | bytes 196616 | tf_op jit(solution)/shard_map/ppermute | solution.py:69
  185.1 6.1 %collective-permute-start.39 = (f32[64,256]{1,0:T(8,128)S(1)}, f32[64,256]{1,0:T(8,128)S(1)}, u32[]{:S(2)}, u32[]{:S(2)}) collective-permute-start(f32[64,256]{1,0:T(8,128)S(1)} %select_add_fusion.3), channel_id=1, source_target_pairs={{0,64},{4,68},{8,72},{12,76},{16,80},{20,84},{24,88},{28,92},{32,9... | collective-permute-start | bytes 196616 | tf_op jit(solution)/shard_map/ppermute | solution.py:69
  187.5 5.5 %collective-permute-start.40 = (f32[64,256]{1,0:T(8,128)S(1)}, f32[64,256]{1,0:T(8,128)S(1)}, u32[]{:S(2)}, u32[]{:S(2)}) collective-permute-start(f32[64,256]{1,0:T(8,128)S(1)} %select_add_fusion.3), channel_id=1, source_target_pairs={{0,32},{4,36},{8,40},{12,44},{16,48},{20,52},{24,56},{28,60},{32,6... | collective-permute-start | bytes 196616 | tf_op jit(solution)/shard_map/ppermute | solution.py:69
  193.1 1.3 collective-permute-start.41
  194.5 3.6 %collective-permute-start.42 = (f32[64]{0:T(128)S(1)}, f32[64]{0:T(128)S(1)}, u32[]{:S(2)}, u32[]{:S(2)}) collective-permute-start(f32[64]{0:T(128)S(1)} %multiply_reduce_fusion), channel_id=1, source_target_pairs={{0,3},{1,0},{2,1},{3,2},{4,7},{5,4},{6,5},{7,6},{8,11},{9,8},{10,9... | collective-permute-start | bytes 776 | tf_op jit(solution)/shard_map/ppermute | solution.py:69
  194.6 5.2 %collective-permute-start.43 = (f32[64]{0:T(128)S(1)}, f32[64]{0:T(128)S(1)}, u32[]{:S(2)}, u32[]{:S(2)}) collective-permute-start(f32[64]{0:T(128)S(1)} %multiply_reduce_fusion), channel_id=1, source_target_pairs={{0,2},{1,3},{2,0},{3,1},{4,6},{5,7},{6,4},{7,5},{8,10},{9,11},{10,... | collective-permute-start | bytes 776 | tf_op jit(solution)/shard_map/ppermute | solution.py:69
  197.7 4.8 %collective-permute-start.44 = (f32[64]{0:T(128)S(1)}, f32[64]{0:T(128)S(1)}, u32[]{:S(2)}, u32[]{:S(2)}) collective-permute-start(f32[64]{0:T(128)S(1)} %multiply_reduce_fusion), channel_id=1, source_target_pairs={{0,1},{1,2},{2,3},{3,0},{4,5},{5,6},{6,7},{7,4},{8,9},{9,10},{10,1... | collective-permute-start | bytes 776 | tf_op jit(solution)/shard_map/ppermute | solution.py:69

commit v9 on v8

--- a/solution.py
+++ b/solution.py
@@ -38,7 +38,7 @@
 def seq_columns(block, width):
     per = block.shape[1] // width
     seq = lax.axis_index("seq")
-    piece = lax.dynamic_slice_in_dim(block, (seq % per) * width, width, 1)
+    piece = pick([block[:, k * width : (k + 1) * width] for k in range(per)], seq % per)
     pairs = [
         (s * MP_SIZE + m, (m * per + s % per) * MP_SIZE + s // per)
         for s in range(SEQ_SIZE)
@@ -82,9 +82,10 @@
     me = lax.axis_index("seq")
     digit = (me // stride) % size
     part = current.shape[1] // size
-    total = lax.dynamic_slice_in_dim(current, digit * part, part, 1)
+    parts = [current[:, p * part : (p + 1) * part] for p in range(size)]
+    total = pick(parts, digit)
     for shift in range(1, size):
-        send = lax.dynamic_slice_in_dim(current, ((digit + shift) % size) * part, part, 1)
+        send = pick(parts, (digit + shift) % size)
         total = total + lax.ppermute(send, "seq", digit_pairs(SEQ_SIZE, stride, size, shift))
     return total
 
@@ -92,13 +93,11 @@
 def gather_digit(current, stride, size):
     me = lax.axis_index("seq")
     digit = (me // stride) % size
-    part = current.shape[1]
-    whole = jnp.zeros((current.shape[0], part * size), current.dtype)
-    whole = lax.dynamic_update_slice_in_dim(whole, current, digit * part, 1)
-    for shift in range(1, size):
-        received = lax.ppermute(current, "seq", digit_pairs(SEQ_SIZE, stride, size, shift))
-        whole = lax.dynamic_update_slice_in_dim(whole, received, ((digit - shift) % size) * part, 1)
-    return whole
+    pieces = [current] + [
+        lax.ppermute(current, "seq", digit_pairs(SEQ_SIZE, stride, size, shift))
+        for shift in range(1, size)
+    ]
+    return jnp.concatenate([pick(pieces, (digit - slot) % size) for slot in range(size)], axis=1)
 
 
 def seq_total(partial_value, ladder=False, butterfly=False):

time: 204 us -> 204 us (level)
  no operation moved by 1% of the time
where the time goes in v9:
time: 204 us; the launch traced here: 203 us
  starting transfers between devices  98.8 us (48%)
  waiting for transfers between devices  72.8 us (36%)
  matrix products  13.1 us (6%)
  other arithmetic  10.5 us (5%)
  local copies, waits for them, and re-layouts  7.36 us (4%)
    ppermute x30, starting transfers between devices, exchange(): lax.ppermute(value, axis, digit_pairs(count, stride, size, shift))  63.1 us
    ppermute x30, waiting for transfers between devices, exchange(): lax.ppermute(value, axis, digit_pairs(count, stride, size, shift))  54.4 us
    ppermute x8, starting transfers between devices, deliver(): received.append(lax.ppermute(piece, ('seq', 'mp'), pairs))  16 us
    ppermute x3, starting transfers between devices, scatter_digit(): lax.ppermute(send, 'seq', digit_pairs(SEQ_SIZE, stride, size, shift))  11 us
    all_to_all x1, waiting for transfers between devices, local(): sources = lax.all_to_all(send, 'seq', 0, 0, tiled=True)  7.15 us
    dot_general x1, matrix products, local(): lax.dot_general(block_queries, keys, (((1,), (1,)), ((), ())), preferred_...  5.54 us
    ppermute x8, waiting for transfers between devices, deliver(): received.append(lax.ppermute(piece, ('seq', 'mp'), pairs))  4.7 us
  transfers between devices with their start and end apart: 47, of which 33 were waited for; matrix products, arithmetic and copies ran while one was open for 3% of the time, Pallas kernels for 0%

profile of v9, /device:TPU:0, one launch (start us, length us, event | category | flops | bytes accessed | tf_op | source)
XLA Modules:
  0.0 203.4 jit_solution(8115708595128826896)
XLA Ops:
  0.0 0.9 fusion.37
  3.9 1.0 fusion.70
  4.9 1.0 fusion.69
  5.9 1.0 fusion.71
  8.5 3.0 %collective-permute-start.2 = (f32[64,768]{1,0:T(8,128)S(1)}, f32[64,768]{1,0:T(8,128)S(1)}, u32[]{:S(2)}, u32[]{:S(2)}) collective-permute-start(f32[64,768]{1,0:T(8,128)S(1)} %select_add_fusion.2), channel_id=1, source_target_pairs={{0,24},{4,28},{8,0},{12,4},{16,8},{20,12},{24,16},{28,20},{32,56},... | collective-permute-start | bytes 589832 | tf_op jit(solution)/shard_map/ppermute | solution.py:69
  12.2 0.9 collective-permute-start.4
  13.1 7.0 %collective-permute-done.2 = f32[64,768]{1,0:T(8,128)S(1)} collective-permute-done((f32[64,768]{1,0:T(8,128)S(1)}, f32[64,768]{1,0:T(8,128)S(1)}, u32[]{:S(2)}, u32[]{:S(2)}) %collective-permute-start.2) | collective-permute-done | bytes 196640 | tf_op jit(solution)/shard_map/ppermute | solution.py:69
  20.7 3.1 %collective-permute-done.4 = f32[64,768]{1,0:T(8,128)S(1)} collective-permute-done((f32[64,768]{1,0:T(8,128)S(1)}, f32[64,768]{1,0:T(8,128)S(1)}, u32[]{:S(2)}, u32[]{:S(2)}) %collective-permute-start.4) | collective-permute-done | bytes 196640 | tf_op jit(solution)/shard_map/ppermute | solution.py:69
  23.9 9.1 %collective-permute-start.5 = (f32[64,768]{1,0:T(8,128)S(1)}, f32[64,768]{1,0:T(8,128)S(1)}, u32[]{:S(2)}, u32[]{:S(2)}) collective-permute-start(f32[64,768]{1,0:T(8,128)S(1)} %select_add_fusion.1), channel_id=1, source_target_pairs={{0,96},{4,100},{8,104},{12,108},{16,112},{20,116},{24,120},{28,124... | collective-permute-start | bytes 589832 | tf_op jit(solution)/shard_map/ppermute | solution.py:69
  33.8 1.3 collective-permute-start.7
  35.4 6.2 %collective-permute-done.5 = f32[64,768]{1,0:T(8,128)S(1)} collective-permute-done((f32[64,768]{1,0:T(8,128)S(1)}, f32[64,768]{1,0:T(8,128)S(1)}, u32[]{:S(2)}, u32[]{:S(2)}) %collective-permute-start.5) | collective-permute-done | bytes 196640 | tf_op jit(solution)/shard_map/ppermute | solution.py:69
  42.3 2.9 %collective-permute-done.7 = f32[64,768]{1,0:T(8,128)S(1)} collective-permute-done((f32[64,768]{1,0:T(8,128)S(1)}, f32[64,768]{1,0:T(8,128)S(1)}, u32[]{:S(2)}, u32[]{:S(2)}) %collective-permute-start.7) | collective-permute-done | bytes 196640 | tf_op jit(solution)/shard_map/ppermute | solution.py:69
  45.4 1.4 collective-permute-done.8
  47.0 2.1 %collective-permute-start.9 = (f32[64,2]{0,1:T(2,128)S(1)}, f32[64,2]{0,1:T(2,128)S(1)}, u32[]{:S(2)}, u32[]{:S(2)}) collective-permute-start(f32[64,2]{0,1:T(2,128)S(1)} %pad_maximum_fusion.6), channel_id=1, source_target_pairs={{0,3},{1,0},{2,1},{3,2},{4,7},{5,4},{6,5},{7,6},{8,11},{9,8},{10,9... | collective-permute-start | bytes 1544 | tf_op jit(solution)/shard_map/ppermute | solution.py:69
  49.1 2.3 %collective-permute-start.10 = (f32[64,2]{0,1:T(2,128)S(1)}, f32[64,2]{0,1:T(2,128)S(1)}, u32[]{:S(2)}, u32[]{:S(2)}) collective-permute-start(f32[64,2]{0,1:T(2,128)S(1)} %pad_maximum_fusion.6), channel_id=1, source_target_pairs={{0,2},{1,3},{2,0},{3,1},{4,6},{5,7},{6,4},{7,5},{8,10},{9,11},{10,... | collective-permute-start | bytes 1544 | tf_op jit(solution)/shard_map/ppermute | solution.py:69
  51.7 2.5 %collective-permute-done.10 = f32[64,2]{0,1:T(2,128)S(1)} collective-permute-done((f32[64,2]{0,1:T(2,128)S(1)}, f32[64,2]{0,1:T(2,128)S(1)}, u32[]{:S(2)}, u32[]{:S(2)}) %collective-permute-start.10) | collective-permute-done | bytes 544 | tf_op jit(solution)/shard_map/ppermute | solution.py:69
  54.2 2.0 collective-permute-done.11
  56.8 5.5 %fusion.68 = (f32[4,4,16]{2,1,0:T(4,128)S(1)}, f32[4,4,16,4096]{3,2,1,0:T(8,128)}) fusion(bf16[4096,512,1,1]{1,0,3,2:T(8,128)(2,1)} %bitcast.149, pred[4,512]{1,0:T(4,128)(4,1)S(1)} %iota_compare_fusion.1, bf16[4,16,512]{2,1,0:T(8,128)(2,1)S(1)} %convert_element_type.60, pred[16,4096]{1,0:T(8,128)(4,1)S(1)} %fusion.9), kind=kOutput, calls=%fused_computation.181 | convolution fusion | flops 1077018368 | bytes 8522752 | tf_op jit(solution)/shard_map/dot_general | solution.py:256
  62.4 3.2 %fusion.2 = (bf16[4,4,16,4096]{3,2,1,0:T(8,128)(2,1)S(1)}, f32[4,4,16]{2,1,0:T(4,128)S(1)}) fusion(f32[4,4,16,4096]{3,2,1,0:T(8,128)} %get-tuple-element.52, f32[4,4,16]{2,1,0:T(4,128)S(1)} %get-tuple-element.51, pred[16,4096]{1,0:T(8,128)(4,1)S(1)} %fusion.9), kind=kLoop, calls=%fused_computation.4 | loop fusion | flops 4194048 | bytes 6359040 | tf_op jit(solution)/shard_map/convert_element_type | solution.py:267
  65.7 3.4 %convolution_bitcast_fusion = f32[512,256]{0,1:T(8,128)S(1)} fusion(bf16[256,4096]{1,0:T(8,128)(2,1)S(1)} %bitcast.117, bf16[4096,512]{1,0:T(8,128)(2,1)} %bitcast.150), kind=kOutput, calls=%fused_computation.5 | convolution fusion | flops 1073741824 | bytes 6815744 | tf_op jit(solution)/shard_map/dot_general | solution.py:265
  70.9 3.9 %all-to-all-start = ((f32[32,1,1152]{2,1,0:T(1,128)}), f32[32,1,1152]{2,1,0:T(1,128)S(1)}, u32[]{:S(2)}, u32[]{:S(2)}) async-start(f32[32,1,1152]{2,1,0:T(1,128)} %reshape.454), calls=%async_computation | async-start | bytes 294912 | tf_op jit(solution)/shard_map/all_to_all | solution.py:284
  75.5 7.2 %all-to-all-done = f32[32,1,1152]{2,1,0:T(1,128)S(1)} async-done(((f32[32,1,1152]{2,1,0:T(1,128)}), f32[32,1,1152]{2,1,0:T(1,128)S(1)}, u32[]{:S(2)}, u32[]{:S(2)}) %all-to-all-start) | async-done | bytes 147488 | tf_op jit(solution)/shard_map/all_to_all | solution.py:284
  83.2 1.0 reduce.37
  85.8 1.9 collective-permute-start.12
  87.7 1.9 collective-permute-start.13
  89.6 1.9 collective-permute-start.14
  92.3 2.2 %collective-permute-done.14 = bf16[64,16]{0,1:T(8,128)(2,1)S(1)} collective-permute-done((bf16[64,16]{0,1:T(8,128)(2,1)S(1)}, bf16[64,16]{0,1:T(8,128)(2,1)S(1)}, u32[]{:S(2)}, u32[]{:S(2)}) %collective-permute-start.14) | collective-permute-done | bytes 2080 | tf_op jit(solution)/shard_map/ppermute | solution.py:161
  94.8 5.6 %collective-permute-start.16 = (f32[64,256]{1,0:T(8,128)S(1)}, f32[64,256]{1,0:T(8,128)S(1)}, u32[]{:S(2)}, u32[]{:S(2)}) collective-permute-start(f32[64,256]{1,0:T(8,128)S(1)} %slice_select_fusion.1), channel_id=1, source_target_pairs={{0,4},{4,0},{8,12},{12,8},{16,20},{20,16},{24,28},{28,24},{32,36},... | collective-permute-start | bytes 196616 | tf_op jit(solution)/shard_map/ppermute | solution.py:89
  100.4 0.9 collective-permute-done.16
  101.3 5.2 %collective-permute-start.17 = (f32[64,256]{1,0:T(8,128)S(1)}, f32[64,256]{1,0:T(8,128)S(1)}, u32[]{:S(2)}, u32[]{:S(2)}) collective-permute-start(f32[64,256]{1,0:T(8,128)S(1)} %select_add_fusion.8), channel_id=1, source_target_pairs={{0,24},{4,28},{8,0},{12,4},{16,8},{20,12},{24,16},{28,20},{32,56},... | collective-permute-start | bytes 196616 | tf_op jit(solution)/shard_map/ppermute | solution.py:69
  106.5 1.4 collective-permute-start.18
  107.9 1.3 collective-permute-start.19
  109.2 3.4 %collective-permute-done.18 = f32[64,256]{1,0:T(8,128)S(1)} collective-permute-done((f32[64,256]{1,0:T(8,128)S(1)}, f32[64,256]{1,0:T(8,128)S(1)}, u32[]{:S(2)}, u32[]{:S(2)}) %collective-permute-start.18) | collective-permute-done | bytes 65568 | tf_op jit(solution)/shard_map/ppermute | solution.py:69
  112.7 1.0 collective-permute-done.19
  113.7 7.4 %collective-permute-start.20 = (f32[64,256]{1,0:T(8,128)S(1)}, f32[64,256]{1,0:T(8,128)S(1)}, u32[]{:S(2)}, u32[]{:S(2)}) collective-permute-start(f32[64,256]{1,0:T(8,128)S(1)} %select_add_fusion.7), channel_id=1, source_target_pairs={{0,96},{4,100},{8,104},{12,108},{16,112},{20,116},{24,120},{28,124... | collective-permute-start | bytes 196616 | tf_op jit(solution)/shard_map/ppermute | solution.py:69
  121.1 0.9 collective-permute-start.22
  122.1 1.6 collective-permute-done.20
  123.7 3.3 %collective-permute-done.21 = f32[64,256]{1,0:T(8,128)S(1)} collective-permute-done((f32[64,256]{1,0:T(8,128)S(1)}, f32[64,256]{1,0:T(8,128)S(1)}, u32[]{:S(2)}, u32[]{:S(2)}) %collective-permute-start.21) | collective-permute-done | bytes 65568 | tf_op jit(solution)/shard_map/ppermute | solution.py:69
  128.9 3.0 %collective-permute-start.25 = (f32[64]{0:T(128)S(1)}, f32[64]{0:T(128)S(1)}, u32[]{:S(2)}, u32[]{:S(2)}) collective-permute-start(f32[64]{0:T(128)S(1)} %multiply_reduce_fusion), channel_id=1, source_target_pairs={{0,2},{1,3},{2,0},{3,1},{4,6},{5,7},{6,4},{7,5},{8,10},{9,11},{10,... | collective-permute-start | bytes 776 | tf_op jit(solution)/shard_map/ppermute | solution.py:69
  132.2 1.0 copy.121
  133.2 3.9 %all-to-all-start.1 = ((bf16[64,32,128]{2,0,1:T(8,128)(2,1)}), bf16[64,32,128]{2,0,1:T(8,128)(2,1)S(1)}, u32[]{:S(2)}, u32[]{:S(2)}) async-start(bf16[64,32,128]{2,0,1:T(8,128)(2,1)} %copy.121), calls=%async_computation.1 | async-start | bytes 1048576 | tf_op jit(solution)/shard_map/all_to_all | solution.py:168
  137.2 3.3 %collective-permute-start.27 = (bf16[64,512]{1,0:T(8,128)(2,1)S(1)}, bf16[64,512]{1,0:T(8,128)(2,1)S(1)}, u32[]{:S(2)}, u32[]{:S(2)}) collective-permute-start(bf16[64,512]{1,0:T(8,128)(2,1)S(1)} %add_convert_fusion), channel_id=1, source_target_pairs={{0,3},{1,0},{2,1},{3,2},{4,7},{5,4},{6,5},{7,6},{8,11},{9,8},{10,9... | collective-permute-start | bytes 196616 | tf_op jit(solution)/shard_map/ppermute | solution.py:69
  140.7 1.3 collective-permute-start.29
  142.0 1.7 collective-permute-done.27
  143.7 2.9 %collective-permute-done.28 = bf16[64,512]{1,0:T(8,128)(2,1)S(1)} collective-permute-done((bf16[64,512]{1,0:T(8,128)(2,1)S(1)}, bf16[64,512]{1,0:T(8,128)(2,1)S(1)}, u32[]{:S(2)}, u32[]{:S(2)}) %collective-permute-start.28) | collective-permute-done | bytes 65568 | tf_op jit(solution)/shard_map/ppermute | solution.py:69
  147.4 1.2 all-to-all-done.1
  149.2 5.1 %collective-permute-start.30 = (bf16[64,64]{1,0:T(8,128)(2,1)S(1)}, bf16[64,64]{1,0:T(8,128)(2,1)S(1)}, u32[]{:S(2)}, u32[]{:S(2)}) collective-permute-start(bf16[64,64]{1,0:T(8,128)(2,1)S(1)} %fusion.3), channel_id=1, source_target_pairs={{0,3},{1,35},{2,67},{3,99},{4,0},{5,32},{6,64},{7,96},{8,1},{9,33}... | collective-permute-start | bytes 24584 | tf_op jit(solution)/shard_map/ppermute | solution.py:161
  154.4 1.8 collective-permute-start.31
  156.2 1.9 collective-permute-start.32
  158.8 2.4 %collective-permute-done.32 = bf16[64,64]{1,0:T(8,128)(2,1)S(1)} collective-permute-done((bf16[64,64]{1,0:T(8,128)(2,1)S(1)}, bf16[64,64]{1,0:T(8,128)(2,1)S(1)}, u32[]{:S(2)}, u32[]{:S(2)}) %collective-permute-start.32) | collective-permute-done | bytes 8224 | tf_op jit(solution)/shard_map/ppermute | solution.py:161
  161.5 5.3 %collective-permute-start.34 = (f32[64,256]{1,0:T(8,128)S(1)}, f32[64,256]{1,0:T(8,128)S(1)}, u32[]{:S(2)}, u32[]{:S(2)}) collective-permute-start(f32[64,256]{1,0:T(8,128)S(1)} %slice_select_fusion), channel_id=1, source_target_pairs={{0,4},{4,0},{8,12},{12,8},{16,20},{20,16},{24,28},{28,24},{32,36},... | collective-permute-start | bytes 196616 | tf_op jit(solution)/shard_map/ppermute | solution.py:89
  166.9 0.9 collective-permute-done.34
  167.8 3.6 %collective-permute-start.35 = (f32[64,256]{1,0:T(8,128)S(1)}, f32[64,256]{1,0:T(8,128)S(1)}, u32[]{:S(2)}, u32[]{:S(2)}) collective-permute-start(f32[64,256]{1,0:T(8,128)S(1)} %select_add_fusion.5), channel_id=1, source_target_pairs={{0,24},{4,28},{8,0},{12,4},{16,8},{20,12},{24,16},{28,20},{32,56},... | collective-permute-start | bytes 196616 | tf_op jit(solution)/shard_map/ppermute | solution.py:69
  171.4 0.9 collective-permute-start.36
  172.3 1.3 collective-permute-start.37
  173.7 3.8 %collective-permute-done.36 = f32[64,256]{1,0:T(8,128)S(1)} collective-permute-done((f32[64,256]{1,0:T(8,128)S(1)}, f32[64,256]{1,0:T(8,128)S(1)}, u32[]{:S(2)}, u32[]{:S(2)}) %collective-permute-start.36) | collective-permute-done | bytes 65568 | tf_op jit(solution)/shard_map/ppermute | solution.py:69
  178.2 7.0 %collective-permute-start.38 = (f32[64,256]{1,0:T(8,128)S(1)}, f32[64,256]{1,0:T(8,128)S(1)}, u32[]{:S(2)}, u32[]{:S(2)}) collective-permute-start(f32[64,256]{1,0:T(8,128)S(1)} %select_add_fusion.4), channel_id=1, source_target_pairs={{0,96},{4,100},{8,104},{12,108},{16,112},{20,116},{24,120},{28,124... | collective-permute-start | bytes 196616 | tf_op jit(solution)/shard_map/ppermute | solution.py:69
  185.2 2.4 %collective-permute-start.39 = (f32[64,256]{1,0:T(8,128)S(1)}, f32[64,256]{1,0:T(8,128)S(1)}, u32[]{:S(2)}, u32[]{:S(2)}) collective-permute-start(f32[64,256]{1,0:T(8,128)S(1)} %select_add_fusion.4), channel_id=1, source_target_pairs={{0,64},{4,68},{8,72},{12,76},{16,80},{20,84},{24,88},{28,92},{32,9... | collective-permute-start | bytes 196616 | tf_op jit(solution)/shard_map/ppermute | solution.py:69
  187.8 3.5 %collective-permute-done.39 = f32[64,256]{1,0:T(8,128)S(1)} collective-permute-done((f32[64,256]{1,0:T(8,128)S(1)}, f32[64,256]{1,0:T(8,128)S(1)}, u32[]{:S(2)}, u32[]{:S(2)}) %collective-permute-start.39) | collective-permute-done | bytes 65568 | tf_op jit(solution)/shard_map/ppermute | solution.py:69
  191.3 1.8 collective-permute-done.40
  193.2 1.2 collective-permute-done.41
  194.7 3.1 %collective-permute-start.43 = (f32[64]{0:T(128)S(1)}, f32[64]{0:T(128)S(1)}, u32[]{:S(2)}, u32[]{:S(2)}) collective-permute-start(f32[64]{0:T(128)S(1)} %fusion.17), channel_id=1, source_target_pairs={{0,2},{1,3},{2,0},{3,1},{4,6},{5,7},{6,4},{7,5},{8,10},{9,11},{10,... | collective-permute-start | bytes 776 | tf_op jit(solution)/shard_map/ppermute | solution.py:69
  198.2 1.6 collective-permute-done.43
  199.8 2.8 %collective-permute-done.44 = f32[64]{0:T(128)S(1)} collective-permute-done((f32[64]{0:T(128)S(1)}, f32[64]{0:T(128)S(1)}, u32[]{:S(2)}, u32[]{:S(2)}) %collective-permute-start.44) | collective-permute-done | bytes 288 | tf_op jit(solution)/shard_map/ppermute | solution.py:69
  (165 shorter events, 21.9 us)
Async XLA Ops:
  0.0 161.3 %copy-start = (bf16[256,512]{1,0:T(8,128)(2,1)S(1)}, bf16[256,512]{1,0:T(8,128)(2,1)}, u32[]{:S(2)}) copy-start(bf16[256,512]{1,0:T(8,128)(2,1)} %param.24) | copy-start | bytes 786436
  0.0 56.2 %copy-start.6 = (f32[512]{0:T(512)S(1)}, f32[512]{0:T(512)}, u32[]{:S(2)}) copy-start(f32[512]{0:T(512)} %param.26) | copy-start | bytes 6148
  0.0 56.2 %copy-start.7 = (f32[512]{0:T(512)S(1)}, f32[512]{0:T(512)}, u32[]{:S(2)}) copy-start(f32[512]{0:T(512)} %param.25) | copy-start | bytes 6148
  1.0 3.0 %collective-permute-start = (bf16[64,64]{1,0:T(8,128)(2,1)S(1)}, bf16[64,64]{1,0:T(8,128)(2,1)S(1)}, u32[]{:S(2)}, u32[]{:S(2)}) collective-permute-start(bf16[64,64]{1,0:T(8,128)(2,1)S(1)} %fusion.37), channel_id=1, source_target_pairs={{0,0},{1,32},{2,64},{3,96},{4,4},{5,36},{6,68},{7,100},{8,8},{9,40... | collective-permute-start | bytes 24584 | tf_op jit(solution)/shard_map/ppermute | solution.py:47
  6.9 1.5 collective-permute-start.1
  8.5 11.6 %collective-permute-start.2 = (f32[64,768]{1,0:T(8,128)S(1)}, f32[64,768]{1,0:T(8,128)S(1)}, u32[]{:S(2)}, u32[]{:S(2)}) collective-permute-start(f32[64,768]{1,0:T(8,128)S(1)} %select_add_fusion.2), channel_id=1, source_target_pairs={{0,24},{4,28},{8,0},{12,4},{16,8},{20,12},{24,16},{28,20},{32,56},... | collective-permute-start | bytes 589832 | tf_op jit(solution)/shard_map/ppermute | solution.py:69
  11.4 9.3 %collective-permute-start.3 = (f32[64,768]{1,0:T(8,128)S(1)}, f32[64,768]{1,0:T(8,128)S(1)}, u32[]{:S(2)}, u32[]{:S(2)}) collective-permute-start(f32[64,768]{1,0:T(8,128)S(1)} %select_add_fusion.2), channel_id=1, source_target_pairs={{0,16},{4,20},{8,24},{12,28},{16,0},{20,4},{24,8},{28,12},{32,48},... | collective-permute-start | bytes 589832 | tf_op jit(solution)/shard_map/ppermute | solution.py:69
  12.2 11.6 %collective-permute-start.4 = (f32[64,768]{1,0:T(8,128)S(1)}, f32[64,768]{1,0:T(8,128)S(1)}, u32[]{:S(2)}, u32[]{:S(2)}) collective-permute-start(f32[64,768]{1,0:T(8,128)S(1)} %select_add_fusion.2), channel_id=1, source_target_pairs={{0,8},{4,12},{8,16},{12,20},{16,24},{20,28},{24,0},{28,4},{32,40},... | collective-permute-start | bytes 589832 | tf_op jit(solution)/shard_map/ppermute | solution.py:69
  23.9 17.6 %collective-permute-start.5 = (f32[64,768]{1,0:T(8,128)S(1)}, f32[64,768]{1,0:T(8,128)S(1)}, u32[]{:S(2)}, u32[]{:S(2)}) collective-permute-start(f32[64,768]{1,0:T(8,128)S(1)} %select_add_fusion.1), channel_id=1, source_target_pairs={{0,96},{4,100},{8,104},{12,108},{16,112},{20,116},{24,120},{28,124... | collective-permute-start | bytes 589832 | tf_op jit(solution)/shard_map/ppermute | solution.py:69
  33.0 9.3 %collective-permute-start.6 = (f32[64,768]{1,0:T(8,128)S(1)}, f32[64,768]{1,0:T(8,128)S(1)}, u32[]{:S(2)}, u32[]{:S(2)}) collective-permute-start(f32[64,768]{1,0:T(8,128)S(1)} %select_add_fusion.1), channel_id=1, source_target_pairs={{0,64},{4,68},{8,72},{12,76},{16,80},{20,84},{24,88},{28,92},{32,9... | collective-permute-start | bytes 589832 | tf_op jit(solution)/shard_map/ppermute | solution.py:69
  33.8 11.4 %collective-permute-start.7 = (f32[64,768]{1,0:T(8,128)S(1)}, f32[64,768]{1,0:T(8,128)S(1)}, u32[]{:S(2)}, u32[]{:S(2)}) collective-permute-start(f32[64,768]{1,0:T(8,128)S(1)} %select_add_fusion.1), channel_id=1, source_target_pairs={{0,32},{4,36},{8,40},{12,44},{16,48},{20,52},{24,56},{28,60},{32,6... | collective-permute-start | bytes 589832 | tf_op jit(solution)/shard_map/ppermute | solution.py:69
  45.3 1.5 collective-permute-start.8
  47.0 4.7 %collective-permute-start.9 = (f32[64,2]{0,1:T(2,128)S(1)}, f32[64,2]{0,1:T(2,128)S(1)}, u32[]{:S(2)}, u32[]{:S(2)}) collective-permute-start(f32[64,2]{0,1:T(2,128)S(1)} %pad_maximum_fusion.6), channel_id=1, source_target_pairs={{0,3},{1,0},{2,1},{3,2},{4,7},{5,4},{6,5},{7,6},{8,11},{9,8},{10,9... | collective-permute-start | bytes 1544 | tf_op jit(solution)/shard_map/ppermute | solution.py:69
  49.1 5.1 %collective-permute-start.10 = (f32[64,2]{0,1:T(2,128)S(1)}, f32[64,2]{0,1:T(2,128)S(1)}, u32[]{:S(2)}, u32[]{:S(2)}) collective-permute-start(f32[64,2]{0,1:T(2,128)S(1)} %pad_maximum_fusion.6), channel_id=1, source_target_pairs={{0,2},{1,3},{2,0},{3,1},{4,6},{5,7},{6,4},{7,5},{8,10},{9,11},{10,... | collective-permute-start | bytes 1544 | tf_op jit(solution)/shard_map/ppermute | solution.py:69
  51.4 4.8 %collective-permute-start.11 = (f32[64,2]{0,1:T(2,128)S(1)}, f32[64,2]{0,1:T(2,128)S(1)}, u32[]{:S(2)}, u32[]{:S(2)}) collective-permute-start(f32[64,2]{0,1:T(2,128)S(1)} %pad_maximum_fusion.6), channel_id=1, source_target_pairs={{0,1},{1,2},{2,3},{3,0},{4,5},{5,6},{6,7},{7,4},{8,9},{9,10},{10,1... | collective-permute-start | bytes 1544 | tf_op jit(solution)/shard_map/ppermute | solution.py:69
  69.1 25.5 %copy-start.4 = (bf16[64,512]{1,0:T(8,128)(2,1)S(1)}, bf16[64,512]{1,0:T(8,128)(2,1)}, u32[]{:S(2)}) copy-start(bf16[64,512]{1,0:T(8,128)(2,1)} %param.21) | copy-start | bytes 196612
  69.1 58.3 %copy-start.2 = (bf16[64,2048]{1,0:T(8,128)(2,1)S(1)}, bf16[64,2048]{1,0:T(8,128)(2,1)}, u32[]{:S(2)}) copy-start(bf16[64,2048]{1,0:T(8,128)(2,1)} %param.23) | copy-start | bytes 786436
  69.3 58.6 %copy-start.3 = (bf16[64,2048]{1,0:T(8,128)(2,1)S(1)}, bf16[64,2048]{1,0:T(8,128)(2,1)}, u32[]{:S(2)}) copy-start(bf16[64,2048]{1,0:T(8,128)(2,1)} %param.22) | copy-start | bytes 786436
  70.9 11.8 %all-to-all-start = ((f32[32,1,1152]{2,1,0:T(1,128)}), f32[32,1,1152]{2,1,0:T(1,128)S(1)}, u32[]{:S(2)}, u32[]{:S(2)}) async-start(f32[32,1,1152]{2,1,0:T(1,128)} %reshape.454), calls=%async_computation | async-start | bytes 294912 | tf_op jit(solution)/shard_map/all_to_all | solution.py:284
  84.2 53.0 %copy-start.1 = (bf16[4,16,512]{2,1,0:T(8,128)(2,1)S(1)}, bf16[4,16,512]{2,1,0:T(8,128)(2,1)}, u32[]{:S(2)}) copy-start(bf16[4,16,512]{2,1,0:T(8,128)(2,1)} %param.17) | copy-start | bytes 196612
  84.2 53.0 %copy-start.5 = (f32[512]{0:T(512)S(1)}, f32[512]{0:T(512)}, u32[]{:S(2)}) copy-start(f32[512]{0:T(512)} %param.27) | copy-start | bytes 6148
  85.8 6.5 %collective-permute-start.12 = (bf16[64,16]{0,1:T(8,128)(2,1)S(1)}, bf16[64,16]{0,1:T(8,128)(2,1)S(1)}, u32[]{:S(2)}, u32[]{:S(2)}) collective-permute-start(bf16[64,16]{0,1:T(8,128)(2,1)S(1)} %copy.126), channel_id=1, source_target_pairs={{0,3},{1,35},{2,67},{3,99},{4,0},{5,32},{6,64},{7,96},{8,1},{9,33}... | collective-permute-start | bytes 6152 | tf_op jit(solution)/shard_map/ppermute | solution.py:161
  87.7 4.6 %collective-permute-start.13 = (bf16[64,16]{0,1:T(8,128)(2,1)S(1)}, bf16[64,16]{0,1:T(8,128)(2,1)S(1)}, u32[]{:S(2)}, u32[]{:S(2)}) collective-permute-start(bf16[64,16]{0,1:T(8,128)(2,1)S(1)} %copy.126), channel_id=1, source_target_pairs={{0,2},{1,34},{2,66},{3,98},{4,3},{5,35},{6,67},{7,99},{8,0},{9,32}... | collective-permute-start | bytes 6152 | tf_op jit(solution)/shard_map/ppermute | solution.py:161
  89.6 4.9 %collective-permute-start.14 = (bf16[64,16]{0,1:T(8,128)(2,1)S(1)}, bf16[64,16]{0,1:T(8,128)(2,1)S(1)}, u32[]{:S(2)}, u32[]{:S(2)}) collective-permute-start(bf16[64,16]{0,1:T(8,128)(2,1)S(1)} %copy.126), channel_id=1, source_target_pairs={{0,1},{1,33},{2,65},{3,97},{4,2},{5,34},{6,66},{7,98},{8,3},{9,35}... | collective-permute-start | bytes 6152 | tf_op jit(solution)/shard_map/ppermute | solution.py:161
  91.6 3.0 %collective-permute-start.15 = (bf16[64,16]{0,1:T(8,128)(2,1)S(1)}, bf16[64,16]{0,1:T(8,128)(2,1)S(1)}, u32[]{:S(2)}, u32[]{:S(2)}) collective-permute-start(bf16[64,16]{0,1:T(8,128)(2,1)S(1)} %copy.126), channel_id=1, source_target_pairs={{0,0},{1,32},{2,64},{3,96},{4,1},{5,33},{6,65},{7,97},{8,2},{9,34}... | collective-permute-start | bytes 6152 | tf_op jit(solution)/shard_map/ppermute | solution.py:161
  94.8 6.5 %collective-permute-start.16 = (f32[64,256]{1,0:T(8,128)S(1)}, f32[64,256]{1,0:T(8,128)S(1)}, u32[]{:S(2)}, u32[]{:S(2)}) collective-permute-start(f32[64,256]{1,0:T(8,128)S(1)} %slice_select_fusion.1), channel_id=1, source_target_pairs={{0,4},{4,0},{8,12},{12,8},{16,20},{20,16},{24,28},{28,24},{32,36},... | collective-permute-start | bytes 196616 | tf_op jit(solution)/shard_map/ppermute | solution.py:89
  101.3 8.0 %collective-permute-start.17 = (f32[64,256]{1,0:T(8,128)S(1)}, f32[64,256]{1,0:T(8,128)S(1)}, u32[]{:S(2)}, u32[]{:S(2)}) collective-permute-start(f32[64,256]{1,0:T(8,128)S(1)} %select_add_fusion.8), channel_id=1, source_target_pairs={{0,24},{4,28},{8,0},{12,4},{16,8},{20,12},{24,16},{28,20},{32,56},... | collective-permute-start | bytes 196616 | tf_op jit(solution)/shard_map/ppermute | solution.py:69
  106.5 6.2 %collective-permute-start.18 = (f32[64,256]{1,0:T(8,128)S(1)}, f32[64,256]{1,0:T(8,128)S(1)}, u32[]{:S(2)}, u32[]{:S(2)}) collective-permute-start(f32[64,256]{1,0:T(8,128)S(1)} %select_add_fusion.8), channel_id=1, source_target_pairs={{0,16},{4,20},{8,24},{12,28},{16,0},{20,4},{24,8},{28,12},{32,48},... | collective-permute-start | bytes 196616 | tf_op jit(solution)/shard_map/ppermute | solution.py:69
  107.9 5.8 %collective-permute-start.19 = (f32[64,256]{1,0:T(8,128)S(1)}, f32[64,256]{1,0:T(8,128)S(1)}, u32[]{:S(2)}, u32[]{:S(2)}) collective-permute-start(f32[64,256]{1,0:T(8,128)S(1)} %select_add_fusion.8), channel_id=1, source_target_pairs={{0,8},{4,12},{8,16},{12,20},{16,24},{20,28},{24,0},{28,4},{32,40},... | collective-permute-start | bytes 196616 | tf_op jit(solution)/shard_map/ppermute | solution.py:69
  113.7 9.9 %collective-permute-start.20 = (f32[64,256]{1,0:T(8,128)S(1)}, f32[64,256]{1,0:T(8,128)S(1)}, u32[]{:S(2)}, u32[]{:S(2)}) collective-permute-start(f32[64,256]{1,0:T(8,128)S(1)} %select_add_fusion.7), channel_id=1, source_target_pairs={{0,96},{4,100},{8,104},{12,108},{16,112},{20,116},{24,120},{28,124... | collective-permute-start | bytes 196616 | tf_op jit(solution)/shard_map/ppermute | solution.py:69
  121.1 5.9 %collective-permute-start.21 = (f32[64,256]{1,0:T(8,128)S(1)}, f32[64,256]{1,0:T(8,128)S(1)}, u32[]{:S(2)}, u32[]{:S(2)}) collective-permute-start(f32[64,256]{1,0:T(8,128)S(1)} %select_add_fusion.7), channel_id=1, source_target_pairs={{0,64},{4,68},{8,72},{12,76},{16,80},{20,84},{24,88},{28,92},{32,9... | collective-permute-start | bytes 196616 | tf_op jit(solution)/shard_map/ppermute | solution.py:69
  121.1 6.2 %collective-permute-start.22 = (f32[64,256]{1,0:T(8,128)S(1)}, f32[64,256]{1,0:T(8,128)S(1)}, u32[]{:S(2)}, u32[]{:S(2)}) collective-permute-start(f32[64,256]{1,0:T(8,128)S(1)} %select_add_fusion.7), channel_id=1, source_target_pairs={{0,32},{4,36},{8,40},{12,44},{16,48},{20,52},{24,56},{28,60},{32,6... | collective-permute-start | bytes 196616 | tf_op jit(solution)/shard_map/ppermute | solution.py:69
  127.4 1.3 collective-permute-start.23
  128.8 8.2 %collective-permute-start.24 = (f32[64]{0:T(128)S(1)}, f32[64]{0:T(128)S(1)}, u32[]{:S(2)}, u32[]{:S(2)}) collective-permute-start(f32[64]{0:T(128)S(1)} %multiply_reduce_fusion), channel_id=1, source_target_pairs={{0,3},{1,0},{2,1},{3,2},{4,7},{5,4},{6,5},{7,6},{8,11},{9,8},{10,9... | collective-permute-start | bytes 776 | tf_op jit(solution)/shard_map/ppermute | solution.py:69
  128.9 8.2 %collective-permute-start.25 = (f32[64]{0:T(128)S(1)}, f32[64]{0:T(128)S(1)}, u32[]{:S(2)}, u32[]{:S(2)}) collective-permute-start(f32[64]{0:T(128)S(1)} %multiply_reduce_fusion), channel_id=1, source_target_pairs={{0,2},{1,3},{2,0},{3,1},{4,6},{5,7},{6,4},{7,5},{8,10},{9,11},{10,... | collective-permute-start | bytes 776 | tf_op jit(solution)/shard_map/ppermute | solution.py:69
  131.9 5.2 %collective-permute-start.26 = (f32[64]{0:T(128)S(1)}, f32[64]{0:T(128)S(1)}, u32[]{:S(2)}, u32[]{:S(2)}) collective-permute-start(f32[64]{0:T(128)S(1)} %multiply_reduce_fusion), channel_id=1, source_target_pairs={{0,1},{1,2},{2,3},{3,0},{4,5},{5,6},{6,7},{7,4},{8,9},{9,10},{10,1... | collective-permute-start | bytes 776 | tf_op jit(solution)/shard_map/ppermute | solution.py:69
  132.2 70.6 %copy-start.8 = (f32[512]{0:T(512)S(1)}, f32[512]{0:T(512)}, u32[]{:S(2)}) copy-start(f32[512]{0:T(512)} %param.28) | copy-start | bytes 6148
  133.2 15.5 %all-to-all-start.1 = ((bf16[64,32,128]{2,0,1:T(8,128)(2,1)}), bf16[64,32,128]{2,0,1:T(8,128)(2,1)S(1)}, u32[]{:S(2)}, u32[]{:S(2)}) async-start(bf16[64,32,128]{2,0,1:T(8,128)(2,1)} %copy.121), calls=%async_computation.1 | async-start | bytes 1048576 | tf_op jit(solution)/shard_map/all_to_all | solution.py:168
  137.2 6.5 %collective-permute-start.27 = (bf16[64,512]{1,0:T(8,128)(2,1)S(1)}, bf16[64,512]{1,0:T(8,128)(2,1)S(1)}, u32[]{:S(2)}, u32[]{:S(2)}) collective-permute-start(bf16[64,512]{1,0:T(8,128)(2,1)S(1)} %add_convert_fusion), channel_id=1, source_target_pairs={{0,3},{1,0},{2,1},{3,2},{4,7},{5,4},{6,5},{7,6},{8,11},{9,8},{10,9... | collective-permute-start | bytes 196616 | tf_op jit(solution)/shard_map/ppermute | solution.py:69
  140.5 6.1 %collective-permute-start.28 = (bf16[64,512]{1,0:T(8,128)(2,1)S(1)}, bf16[64,512]{1,0:T(8,128)(2,1)S(1)}, u32[]{:S(2)}, u32[]{:S(2)}) collective-permute-start(bf16[64,512]{1,0:T(8,128)(2,1)S(1)} %add_convert_fusion), channel_id=1, source_target_pairs={{0,2},{1,3},{2,0},{3,1},{4,6},{5,7},{6,4},{7,5},{8,10},{9,11},{10,... | collective-permute-start | bytes 196616 | tf_op jit(solution)/shard_map/ppermute | solution.py:69
  140.7 6.6 %collective-permute-start.29 = (bf16[64,512]{1,0:T(8,128)(2,1)S(1)}, bf16[64,512]{1,0:T(8,128)(2,1)S(1)}, u32[]{:S(2)}, u32[]{:S(2)}) collective-permute-start(bf16[64,512]{1,0:T(8,128)(2,1)S(1)} %add_convert_fusion), channel_id=1, source_target_pairs={{0,1},{1,2},{2,3},{3,0},{4,5},{5,6},{6,7},{7,4},{8,9},{9,10},{10,1... | collective-permute-start | bytes 196616 | tf_op jit(solution)/shard_map/ppermute | solution.py:69
  149.2 9.6 %collective-permute-start.30 = (bf16[64,64]{1,0:T(8,128)(2,1)S(1)}, bf16[64,64]{1,0:T(8,128)(2,1)S(1)}, u32[]{:S(2)}, u32[]{:S(2)}) collective-permute-start(bf16[64,64]{1,0:T(8,128)(2,1)S(1)} %fusion.3), channel_id=1, source_target_pairs={{0,3},{1,35},{2,67},{3,99},{4,0},{5,32},{6,64},{7,96},{8,1},{9,33}... | collective-permute-start | bytes 24584 | tf_op jit(solution)/shard_map/ppermute | solution.py:161
  154.4 4.4 %collective-permute-start.31 = (bf16[64,64]{1,0:T(8,128)(2,1)S(1)}, bf16[64,64]{1,0:T(8,128)(2,1)S(1)}, u32[]{:S(2)}, u32[]{:S(2)}) collective-permute-start(bf16[64,64]{1,0:T(8,128)(2,1)S(1)} %fusion.3), channel_id=1, source_target_pairs={{0,2},{1,34},{2,66},{3,98},{4,3},{5,35},{6,67},{7,99},{8,0},{9,32}... | collective-permute-start | bytes 24584 | tf_op jit(solution)/shard_map/ppermute | solution.py:161
  156.2 5.0 %collective-permute-start.32 = (bf16[64,64]{1,0:T(8,128)(2,1)S(1)}, bf16[64,64]{1,0:T(8,128)(2,1)S(1)}, u32[]{:S(2)}, u32[]{:S(2)}) collective-permute-start(bf16[64,64]{1,0:T(8,128)(2,1)S(1)} %fusion.3), channel_id=1, source_target_pairs={{0,1},{1,33},{2,65},{3,97},{4,2},{5,34},{6,66},{7,98},{8,3},{9,35}... | collective-permute-start | bytes 24584 | tf_op jit(solution)/shard_map/ppermute | solution.py:161
  158.2 3.1 %collective-permute-start.33 = (bf16[64,64]{1,0:T(8,128)(2,1)S(1)}, bf16[64,64]{1,0:T(8,128)(2,1)S(1)}, u32[]{:S(2)}, u32[]{:S(2)}) collective-permute-start(bf16[64,64]{1,0:T(8,128)(2,1)S(1)} %fusion.3), channel_id=1, source_target_pairs={{0,0},{1,32},{2,64},{3,96},{4,1},{5,33},{6,65},{7,97},{8,2},{9,34}... | collective-permute-start | bytes 24584 | tf_op jit(solution)/shard_map/ppermute | solution.py:161
  161.5 6.2 %collective-permute-start.34 = (f32[64,256]{1,0:T(8,128)S(1)}, f32[64,256]{1,0:T(8,128)S(1)}, u32[]{:S(2)}, u32[]{:S(2)}) collective-permute-start(f32[64,256]{1,0:T(8,128)S(1)} %slice_select_fusion), channel_id=1, source_target_pairs={{0,4},{4,0},{8,12},{12,8},{16,20},{20,16},{24,28},{28,24},{32,36},... | collective-permute-start | bytes 196616 | tf_op jit(solution)/shard_map/ppermute | solution.py:89
  167.8 5.9 %collective-permute-start.35 = (f32[64,256]{1,0:T(8,128)S(1)}, f32[64,256]{1,0:T(8,128)S(1)}, u32[]{:S(2)}, u32[]{:S(2)}) collective-permute-start(f32[64,256]{1,0:T(8,128)S(1)} %select_add_fusion.5), channel_id=1, source_target_pairs={{0,24},{4,28},{8,0},{12,4},{16,8},{20,12},{24,16},{28,20},{32,56},... | collective-permute-start | bytes 196616 | tf_op jit(solution)/shard_map/ppermute | solution.py:69
  171.4 6.1 %collective-permute-start.36 = (f32[64,256]{1,0:T(8,128)S(1)}, f32[64,256]{1,0:T(8,128)S(1)}, u32[]{:S(2)}, u32[]{:S(2)}) collective-permute-start(f32[64,256]{1,0:T(8,128)S(1)} %select_add_fusion.5), channel_id=1, source_target_pairs={{0,16},{4,20},{8,24},{12,28},{16,0},{20,4},{24,8},{28,12},{32,48},... | collective-permute-start | bytes 196616 | tf_op jit(solution)/shard_map/ppermute | solution.py:69
  172.3 5.8 %collective-permute-start.37 = (f32[64,256]{1,0:T(8,128)S(1)}, f32[64,256]{1,0:T(8,128)S(1)}, u32[]{:S(2)}, u32[]{:S(2)}) collective-permute-start(f32[64,256]{1,0:T(8,128)S(1)} %select_add_fusion.5), channel_id=1, source_target_pairs={{0,8},{4,12},{8,16},{12,20},{16,24},{20,28},{24,0},{28,4},{32,40},... | collective-permute-start | bytes 196616 | tf_op jit(solution)/shard_map/ppermute | solution.py:69
  178.2 9.6 %collective-permute-start.38 = (f32[64,256]{1,0:T(8,128)S(1)}, f32[64,256]{1,0:T(8,128)S(1)}, u32[]{:S(2)}, u32[]{:S(2)}) collective-permute-start(f32[64,256]{1,0:T(8,128)S(1)} %select_add_fusion.4), channel_id=1, source_target_pairs={{0,96},{4,100},{8,104},{12,108},{16,112},{20,116},{24,120},{28,124... | collective-permute-start | bytes 196616 | tf_op jit(solution)/shard_map/ppermute | solution.py:69
  185.2 6.1 %collective-permute-start.39 = (f32[64,256]{1,0:T(8,128)S(1)}, f32[64,256]{1,0:T(8,128)S(1)}, u32[]{:S(2)}, u32[]{:S(2)}) collective-permute-start(f32[64,256]{1,0:T(8,128)S(1)} %select_add_fusion.4), channel_id=1, source_target_pairs={{0,64},{4,68},{8,72},{12,76},{16,80},{20,84},{24,88},{28,92},{32,9... | collective-permute-start | bytes 196616 | tf_op jit(solution)/shard_map/ppermute | solution.py:69
  187.6 5.5 %collective-permute-start.40 = (f32[64,256]{1,0:T(8,128)S(1)}, f32[64,256]{1,0:T(8,128)S(1)}, u32[]{:S(2)}, u32[]{:S(2)}) collective-permute-start(f32[64,256]{1,0:T(8,128)S(1)} %select_add_fusion.4), channel_id=1, source_target_pairs={{0,32},{4,36},{8,40},{12,44},{16,48},{20,52},{24,56},{28,60},{32,6... | collective-permute-start | bytes 196616 | tf_op jit(solution)/shard_map/ppermute | solution.py:69
  193.1 1.3 collective-permute-start.41
  194.6 3.6 %collective-permute-start.42 = (f32[64]{0:T(128)S(1)}, f32[64]{0:T(128)S(1)}, u32[]{:S(2)}, u32[]{:S(2)}) collective-permute-start(f32[64]{0:T(128)S(1)} %fusion.17), channel_id=1, source_target_pairs={{0,3},{1,0},{2,1},{3,2},{4,7},{5,4},{6,5},{7,6},{8,11},{9,8},{10,9... | collective-permute-start | bytes 776 | tf_op jit(solution)/shard_map/ppermute | solution.py:69
  194.7 5.2 %collective-permute-start.43 = (f32[64]{0:T(128)S(1)}, f32[64]{0:T(128)S(1)}, u32[]{:S(2)}, u32[]{:S(2)}) collective-permute-start(f32[64]{0:T(128)S(1)} %fusion.17), channel_id=1, source_target_pairs={{0,2},{1,3},{2,0},{3,1},{4,6},{5,7},{6,4},{7,5},{8,10},{9,11},{10,... | collective-permute-start | bytes 776 | tf_op jit(solution)/shard_map/ppermute | solution.py:69
  197.8 4.8 %collective-permute-start.44 = (f32[64]{0:T(128)S(1)}, f32[64]{0:T(128)S(1)}, u32[]{:S(2)}, u32[]{:S(2)}) collective-permute-start(f32[64]{0:T(128)S(1)} %fusion.17), channel_id=1, source_target_pairs={{0,1},{1,2},{2,3},{3,0},{4,5},{5,6},{6,7},{7,4},{8,9},{9,10},{10,1... | collective-permute-start | bytes 776 | tf_op jit(solution)/shard_map/ppermute | solution.py:69

commit v10 on v8

--- a/solution.py
+++ b/solution.py
@@ -168,6 +168,19 @@
     block = cols // SEQ_SIZE
     moved = lax.all_to_all(weight.reshape(rows, SEQ_SIZE, block), "seq", 1, 0, tiled=True)
     return moved.reshape(rows * SEQ_SIZE, block)
+
+
+def seq_total_and_squares(partial_value):
+    groups = seq_groups()
+    stride, size = groups[0]
+    current = scatter_digit(partial_value, stride, size)
+    for other_stride, other_size in groups[1:]:
+        current = jnp.sum(exchange(current, "seq", SEQ_SIZE, other_stride, other_size), axis=0)
+    half_squares = jnp.sum(current * current, axis=1)
+    squares = jnp.sum(
+        exchange(half_squares, ("seq", "mp"), SEQ_SIZE * MP_SIZE, 1, size * MP_SIZE), axis=0
+    )
+    return gather_digit(current, stride, size), squares
 
 
 def merge_stack(stack):
@@ -310,10 +323,9 @@
     attended = (final_running / final_totals[..., None]).astype(jnp.bfloat16).reshape(rows, slice_width)
 
     sliced = deliver(attended, output_weight.shape[0], local_width)
-    attention_out = seq_total(
+    attention_out, attention_squares = seq_total_and_squares(
         jnp.dot(sliced, output_weight, preferred_element_type=jnp.float32)
     )
-    attention_squares = feature_sums(jnp.sum(attention_out * attention_out, axis=1))
     hidden = (
         token_rows.astype(jnp.float32) + attention_out * inverse_rms(attention_squares) * attention_gain
     ).astype(jnp.bfloat16)
@@ -335,10 +347,9 @@
     up_part = jnp.dot(hidden_all, both[:, units:], preferred_element_type=jnp.float32)
     active = (jax.nn.silu(gate) * up_part).astype(jnp.bfloat16)
     active_cols = deliver(active, down_weight.shape[0], gate_weight.shape[1])
-    mlp_out = seq_total(
+    mlp_out, mlp_squares = seq_total_and_squares(
         jnp.dot(active_cols, down_weight, preferred_element_type=jnp.float32)
     )
-    mlp_squares = feature_sums(jnp.sum(mlp_out * mlp_out, axis=1))
     decoded = (
         hidden.astype(jnp.float32) + mlp_out * inverse_rms(mlp_squares) * feedforward_gain
     ).astype(jnp.bfloat16)

time: 204 us -> 206 us (level)
  starting transfers between devices: 98.7 us -> 108 us
  waiting for transfers between devices: 72.8 us -> 64.7 us
    ppermute x30 -> x38, starting transfers between devices: 63.1 us -> 69.6 us  [exchange(): lax.ppermute(value, axis, digit_pairs(count, stride, size, shift))]
    ppermute x30 -> x38, waiting for transfers between devices: 54.5 us -> 49.3 us  [exchange(): lax.ppermute(value, axis, digit_pairs(count, stride, size, shift))]
  transfers between devices with their start and end apart: 47 -> 55, of which waited for: 33 -> 29; matrix products, arithmetic and copies ran while one was open for 3% -> 3% of each run, Pallas kernels for 0% -> 0%
where the time goes in v10:
time: 206 us; the launch traced here: 205 us
  starting transfers between devices  108 us (52%)
  waiting for transfers between devices  64.7 us (31%)
  matrix products  13.1 us (6%)
  other arithmetic  9.91 us (5%)
  local copies, waits for them, and re-layouts  7.91 us (4%)
    ppermute x38, starting transfers between devices, exchange(): lax.ppermute(value, axis, digit_pairs(count, stride, size, shift))  69.6 us
    ppermute x38, waiting for transfers between devices, exchange(): lax.ppermute(value, axis, digit_pairs(count, stride, size, shift))  49.3 us
    ppermute x8, starting transfers between devices, deliver(): received.append(lax.ppermute(piece, ('seq', 'mp'), pairs))  16.4 us
    ppermute x3, starting transfers between devices, scatter_digit(): lax.ppermute(send, 'seq', digit_pairs(SEQ_SIZE, stride, size, shift))  12.2 us
    all_to_all x1, waiting for transfers between devices, local(): sources = lax.all_to_all(send, 'seq', 0, 0, tiled=True)  7.06 us
    dot_general x1, matrix products, local(): lax.dot_general(block_queries, keys, (((1,), (1,)), ((), ())), preferred_...  5.52 us
    all_to_all x1, starting transfers between devices, full_rows(): lax.all_to_all(weight.reshape(rows, SEQ_SIZE, block), 'seq', 1, 0, tiled=...  5 us
    ppermute x8, waiting for transfers between devices, deliver(): received.append(lax.ppermute(piece, ('seq', 'mp'), pairs))  4.46 us
  transfers between devices with their start and end apart: 55, of which 29 were waited for; matrix products, arithmetic and copies ran while one was open for 3% of the time, Pallas kernels for 0%

profile of v10, /device:TPU:0, one launch (start us, length us, event | category | flops | bytes accessed | tf_op | source)
XLA Modules:
  0.0 204.6 jit_solution(15811810469078466330)
XLA Ops:
  3.8 1.0 fusion.65
  4.8 1.0 fusion.64
  5.8 1.0 fusion.63
  8.4 3.0 %collective-permute-start.2 = (f32[64,768]{1,0:T(8,128)S(1)}, f32[64,768]{1,0:T(8,128)S(1)}, u32[]{:S(2)}, u32[]{:S(2)}) collective-permute-start(f32[64,768]{1,0:T(8,128)S(1)} %dynamic-slice_add_fusion), channel_id=1, source_target_pairs={{0,24},{4,28},{8,0},{12,4},{16,8},{20,12},{24,16},{28,20},{32,56},... | collective-permute-start | bytes 589832 | tf_op jit(solution)/shard_map/ppermute | solution.py:69
  12.1 0.9 collective-permute-start.4
  13.0 7.0 %collective-permute-done.2 = f32[64,768]{1,0:T(8,128)S(1)} collective-permute-done((f32[64,768]{1,0:T(8,128)S(1)}, f32[64,768]{1,0:T(8,128)S(1)}, u32[]{:S(2)}, u32[]{:S(2)}) %collective-permute-start.2) | collective-permute-done | bytes 196640 | tf_op jit(solution)/shard_map/ppermute | solution.py:69
  20.7 3.1 %collective-permute-done.4 = f32[64,768]{1,0:T(8,128)S(1)} collective-permute-done((f32[64,768]{1,0:T(8,128)S(1)}, f32[64,768]{1,0:T(8,128)S(1)}, u32[]{:S(2)}, u32[]{:S(2)}) %collective-permute-start.4) | collective-permute-done | bytes 196640 | tf_op jit(solution)/shard_map/ppermute | solution.py:69
  23.8 9.1 %collective-permute-start.5 = (f32[64,768]{1,0:T(8,128)S(1)}, f32[64,768]{1,0:T(8,128)S(1)}, u32[]{:S(2)}, u32[]{:S(2)}) collective-permute-start(f32[64,768]{1,0:T(8,128)S(1)} %select_add_fusion.1), channel_id=1, source_target_pairs={{0,96},{4,100},{8,104},{12,108},{16,112},{20,116},{24,120},{28,124... | collective-permute-start | bytes 589832 | tf_op jit(solution)/shard_map/ppermute | solution.py:69
  33.7 1.3 collective-permute-start.7
  35.3 6.2 %collective-permute-done.5 = f32[64,768]{1,0:T(8,128)S(1)} collective-permute-done((f32[64,768]{1,0:T(8,128)S(1)}, f32[64,768]{1,0:T(8,128)S(1)}, u32[]{:S(2)}, u32[]{:S(2)}) %collective-permute-start.5) | collective-permute-done | bytes 196640 | tf_op jit(solution)/shard_map/ppermute | solution.py:69
  42.2 2.9 %collective-permute-done.7 = f32[64,768]{1,0:T(8,128)S(1)} collective-permute-done((f32[64,768]{1,0:T(8,128)S(1)}, f32[64,768]{1,0:T(8,128)S(1)}, u32[]{:S(2)}, u32[]{:S(2)}) %collective-permute-start.7) | collective-permute-done | bytes 196640 | tf_op jit(solution)/shard_map/ppermute | solution.py:69
  45.4 1.4 collective-permute-done.8
  47.0 2.1 %collective-permute-start.9 = (f32[64,2]{0,1:T(2,128)S(1)}, f32[64,2]{0,1:T(2,128)S(1)}, u32[]{:S(2)}, u32[]{:S(2)}) collective-permute-start(f32[64,2]{0,1:T(2,128)S(1)} %pad_maximum_fusion.3), channel_id=1, source_target_pairs={{0,3},{1,0},{2,1},{3,2},{4,7},{5,4},{6,5},{7,6},{8,11},{9,8},{10,9... | collective-permute-start | bytes 1544 | tf_op jit(solution)/shard_map/ppermute | solution.py:69
  49.1 2.3 %collective-permute-start.10 = (f32[64,2]{0,1:T(2,128)S(1)}, f32[64,2]{0,1:T(2,128)S(1)}, u32[]{:S(2)}, u32[]{:S(2)}) collective-permute-start(f32[64,2]{0,1:T(2,128)S(1)} %pad_maximum_fusion.3), channel_id=1, source_target_pairs={{0,2},{1,3},{2,0},{3,1},{4,6},{5,7},{6,4},{7,5},{8,10},{9,11},{10,... | collective-permute-start | bytes 1544 | tf_op jit(solution)/shard_map/ppermute | solution.py:69
  51.7 2.5 %collective-permute-done.10 = f32[64,2]{0,1:T(2,128)S(1)} collective-permute-done((f32[64,2]{0,1:T(2,128)S(1)}, f32[64,2]{0,1:T(2,128)S(1)}, u32[]{:S(2)}, u32[]{:S(2)}) %collective-permute-start.10) | collective-permute-done | bytes 544 | tf_op jit(solution)/shard_map/ppermute | solution.py:69
  54.1 2.0 collective-permute-done.11
  56.7 5.5 %fusion.62 = (f32[4,4,16]{2,1,0:T(4,128)S(1)}, f32[4,4,16,4096]{3,2,1,0:T(8,128)}) fusion(bf16[4096,512,1,1]{1,0,3,2:T(8,128)(2,1)} %bitcast.142, pred[4,512]{1,0:T(4,128)(4,1)S(1)} %iota_compare_fusion.1, bf16[4,16,512]{2,1,0:T(8,128)(2,1)S(1)} %convert_element_type.52, pred[16,4096]{1,0:T(8,128)(4,1)S(1)} %fusion.9), kind=kOutput, calls=%fused_computation.260 | convolution fusion | flops 1077018368 | bytes 8522752 | tf_op jit(solution)/shard_map/dot_general | solution.py:270
  62.3 3.2 %fusion.2 = (bf16[4,4,16,4096]{3,2,1,0:T(8,128)(2,1)S(1)}, f32[4,4,16]{2,1,0:T(4,128)S(1)}) fusion(f32[4,4,16,4096]{3,2,1,0:T(8,128)} %get-tuple-element.48, f32[4,4,16]{2,1,0:T(4,128)S(1)} %get-tuple-element.47, pred[16,4096]{1,0:T(8,128)(4,1)S(1)} %fusion.9), kind=kLoop, calls=%fused_computation.4 | loop fusion | flops 4194048 | bytes 6359040 | tf_op jit(solution)/shard_map/convert_element_type | solution.py:281
  65.6 3.4 %convolution_bitcast_fusion = f32[512,256]{0,1:T(8,128)S(1)} fusion(bf16[256,4096]{1,0:T(8,128)(2,1)S(1)} %bitcast.114, bf16[4096,512]{1,0:T(8,128)(2,1)} %bitcast.143), kind=kOutput, calls=%fused_computation.5 | convolution fusion | flops 1073741824 | bytes 6815744 | tf_op jit(solution)/shard_map/dot_general | solution.py:279
  70.7 3.9 %all-to-all-start = ((f32[32,1,1152]{2,1,0:T(1,128)}), f32[32,1,1152]{2,1,0:T(1,128)S(1)}, u32[]{:S(2)}, u32[]{:S(2)}) async-start(f32[32,1,1152]{2,1,0:T(1,128)} %reshape.456), calls=%async_computation | async-start | bytes 294912 | tf_op jit(solution)/shard_map/all_to_all | solution.py:298
  75.5 7.1 %all-to-all-done = f32[32,1,1152]{2,1,0:T(1,128)S(1)} async-done(((f32[32,1,1152]{2,1,0:T(1,128)}), f32[32,1,1152]{2,1,0:T(1,128)S(1)}, u32[]{:S(2)}, u32[]{:S(2)}) %all-to-all-start) | async-done | bytes 147488 | tf_op jit(solution)/shard_map/all_to_all | solution.py:298
  83.0 1.0 reduce.45
  85.6 1.9 collective-permute-start.12
  87.6 1.9 collective-permute-start.13
  89.5 1.9 collective-permute-start.14
  92.2 2.2 %collective-permute-done.14 = bf16[64,16]{0,1:T(8,128)(2,1)S(1)} collective-permute-done((bf16[64,16]{0,1:T(8,128)(2,1)S(1)}, bf16[64,16]{0,1:T(8,128)(2,1)S(1)}, u32[]{:S(2)}, u32[]{:S(2)}) %collective-permute-start.14) | collective-permute-done | bytes 2080 | tf_op jit(solution)/shard_map/ppermute | solution.py:162
  94.7 5.6 %collective-permute-start.16 = (f32[64,256]{1,0:T(8,128)S(1)}, f32[64,256]{1,0:T(8,128)S(1)}, u32[]{:S(2)}, u32[]{:S(2)}) collective-permute-start(f32[64,256]{1,0:T(8,128)S(1)} %constant_dynamic-slice_fusion.1), channel_id=1, source_target_pairs={{0,4},{4,0},{8,12},{12,8},{16,20},{20,16},{24,28},{28,24},{32,36},... | collective-permute-start | bytes 196616 | tf_op jit(solution)/shard_map/ppermute | solution.py:88
  100.2 0.9 collective-permute-done.16
  101.1 5.2 %collective-permute-start.17 = (f32[64,256]{1,0:T(8,128)S(1)}, f32[64,256]{1,0:T(8,128)S(1)}, u32[]{:S(2)}, u32[]{:S(2)}) collective-permute-start(f32[64,256]{1,0:T(8,128)S(1)} %dynamic-slice_add_fusion.2), channel_id=1, source_target_pairs={{0,24},{4,28},{8,0},{12,4},{16,8},{20,12},{24,16},{28,20},{32,56},... | collective-permute-start | bytes 196616 | tf_op jit(solution)/shard_map/ppermute | solution.py:69
  106.3 1.4 collective-permute-start.18
  107.8 1.3 collective-permute-start.19
  110.2 2.4 %collective-permute-done.18 = f32[64,256]{1,0:T(8,128)S(1)} collective-permute-done((f32[64,256]{1,0:T(8,128)S(1)}, f32[64,256]{1,0:T(8,128)S(1)}, u32[]{:S(2)}, u32[]{:S(2)}) %collective-permute-start.18) | collective-permute-done | bytes 65568 | tf_op jit(solution)/shard_map/ppermute | solution.py:69
  112.5 1.0 collective-permute-done.19
  113.6 7.4 %collective-permute-start.20 = (f32[64,256]{1,0:T(8,128)S(1)}, f32[64,256]{1,0:T(8,128)S(1)}, u32[]{:S(2)}, u32[]{:S(2)}) collective-permute-start(f32[64,256]{1,0:T(8,128)S(1)} %select_add_fusion.5), channel_id=1, source_target_pairs={{0,96},{4,100},{8,104},{12,108},{16,112},{20,116},{24,120},{28,124... | collective-permute-start | bytes 196616 | tf_op jit(solution)/shard_map/ppermute | solution.py:69
  121.0 0.9 collective-permute-start.22
  122.3 1.0 copy.107
  123.3 5.0 %all-to-all-start.1 = ((bf16[64,32,128]{2,0,1:T(8,128)(2,1)}), bf16[64,32,128]{2,0,1:T(8,128)(2,1)S(1)}, u32[]{:S(2)}, u32[]{:S(2)}) async-start(bf16[64,32,128]{2,0,1:T(8,128)(2,1)} %copy.107), calls=%async_computation.1 | async-start | bytes 1048576 | tf_op jit(solution)/shard_map/all_to_all | solution.py:169
  129.2 1.4 collective-permute-start.25
  131.2 3.0 %collective-permute-start.28 = (f32[64]{0:T(128)S(1)}, f32[64]{0:T(128)S(1)}, u32[]{:S(2)}, u32[]{:S(2)}) collective-permute-start(f32[64]{0:T(128)S(1)} %get-tuple-element.9), channel_id=1, source_target_pairs={{0,3},{1,4},{2,5},{3,6},{4,7},{5,0},{6,1},{7,2},{8,11},{9,12},{10,... | collective-permute-start | bytes 776 | tf_op jit(solution)/shard_map/ppermute | solution.py:69
  134.2 1.0 collective-permute-start.29
  135.2 1.0 collective-permute-start.30
  136.2 2.5 %collective-permute-done.29 = f32[64]{0:T(128)S(1)} collective-permute-done((f32[64]{0:T(128)S(1)}, f32[64]{0:T(128)S(1)}, u32[]{:S(2)}, u32[]{:S(2)}) %collective-permute-start.29) | collective-permute-done | bytes 288 | tf_op jit(solution)/shard_map/ppermute | solution.py:69
  139.6 1.1 collective-permute-start.31
  140.7 1.4 collective-permute-start.32
  142.6 1.8 collective-permute-done.31
  144.4 2.7 %collective-permute-done.32 = bf16[64,512]{1,0:T(8,128)(2,1)S(1)} collective-permute-done((bf16[64,512]{1,0:T(8,128)(2,1)S(1)}, bf16[64,512]{1,0:T(8,128)(2,1)S(1)}, u32[]{:S(2)}, u32[]{:S(2)}) %collective-permute-start.32) | collective-permute-done | bytes 65568 | tf_op jit(solution)/shard_map/ppermute | solution.py:69
  148.4 2.8 %collective-permute-start.34 = (bf16[64,64]{1,0:T(8,128)(2,1)S(1)}, bf16[64,64]{1,0:T(8,128)(2,1)S(1)}, u32[]{:S(2)}, u32[]{:S(2)}) collective-permute-start(bf16[64,64]{1,0:T(8,128)(2,1)S(1)} %fusion.3), channel_id=1, source_target_pairs={{0,3},{1,35},{2,67},{3,99},{4,0},{5,32},{6,64},{7,96},{8,1},{9,33}... | collective-permute-start | bytes 24584 | tf_op jit(solution)/shard_map/ppermute | solution.py:162
  151.3 4.3 %collective-permute-start.35 = (bf16[64,64]{1,0:T(8,128)(2,1)S(1)}, bf16[64,64]{1,0:T(8,128)(2,1)S(1)}, u32[]{:S(2)}, u32[]{:S(2)}) collective-permute-start(bf16[64,64]{1,0:T(8,128)(2,1)S(1)} %fusion.3), channel_id=1, source_target_pairs={{0,2},{1,34},{2,66},{3,98},{4,3},{5,35},{6,67},{7,99},{8,0},{9,32}... | collective-permute-start | bytes 24584 | tf_op jit(solution)/shard_map/ppermute | solution.py:162
  155.5 2.1 %collective-permute-start.36 = (bf16[64,64]{1,0:T(8,128)(2,1)S(1)}, bf16[64,64]{1,0:T(8,128)(2,1)S(1)}, u32[]{:S(2)}, u32[]{:S(2)}) collective-permute-start(bf16[64,64]{1,0:T(8,128)(2,1)S(1)} %fusion.3), channel_id=1, source_target_pairs={{0,1},{1,33},{2,65},{3,97},{4,2},{5,34},{6,66},{7,98},{8,3},{9,35}... | collective-permute-start | bytes 24584 | tf_op jit(solution)/shard_map/ppermute | solution.py:162
  158.4 2.2 %collective-permute-done.36 = bf16[64,64]{1,0:T(8,128)(2,1)S(1)} collective-permute-done((bf16[64,64]{1,0:T(8,128)(2,1)S(1)}, bf16[64,64]{1,0:T(8,128)(2,1)S(1)}, u32[]{:S(2)}, u32[]{:S(2)}) %collective-permute-start.36) | collective-permute-done | bytes 8224 | tf_op jit(solution)/shard_map/ppermute | solution.py:162
  160.8 6.6 %collective-permute-start.38 = (f32[64,256]{1,0:T(8,128)S(1)}, f32[64,256]{1,0:T(8,128)S(1)}, u32[]{:S(2)}, u32[]{:S(2)}) collective-permute-start(f32[64,256]{1,0:T(8,128)S(1)} %constant_dynamic-slice_fusion), channel_id=1, source_target_pairs={{0,4},{4,0},{8,12},{12,8},{16,20},{20,16},{24,28},{28,24},{32,36},... | collective-permute-start | bytes 196616 | tf_op jit(solution)/shard_map/ppermute | solution.py:88
  167.4 0.9 collective-permute-done.38
  168.3 3.8 %collective-permute-start.39 = (f32[64,256]{1,0:T(8,128)S(1)}, f32[64,256]{1,0:T(8,128)S(1)}, u32[]{:S(2)}, u32[]{:S(2)}) collective-permute-start(f32[64,256]{1,0:T(8,128)S(1)} %dynamic-slice_add_fusion.1), channel_id=1, source_target_pairs={{0,24},{4,28},{8,0},{12,4},{16,8},{20,12},{24,16},{28,20},{32,56},... | collective-permute-start | bytes 196616 | tf_op jit(solution)/shard_map/ppermute | solution.py:69
  172.7 1.3 collective-permute-start.41
  174.6 3.6 %collective-permute-done.40 = f32[64,256]{1,0:T(8,128)S(1)} collective-permute-done((f32[64,256]{1,0:T(8,128)S(1)}, f32[64,256]{1,0:T(8,128)S(1)}, u32[]{:S(2)}, u32[]{:S(2)}) %collective-permute-start.40) | collective-permute-done | bytes 65568 | tf_op jit(solution)/shard_map/ppermute | solution.py:69
  178.9 6.8 %collective-permute-start.42 = (f32[64,256]{1,0:T(8,128)S(1)}, f32[64,256]{1,0:T(8,128)S(1)}, u32[]{:S(2)}, u32[]{:S(2)}) collective-permute-start(f32[64,256]{1,0:T(8,128)S(1)} %select_add_fusion.3), channel_id=1, source_target_pairs={{0,96},{4,100},{8,104},{12,108},{16,112},{20,116},{24,120},{28,124... | collective-permute-start | bytes 196616 | tf_op jit(solution)/shard_map/ppermute | solution.py:69
  185.7 1.8 collective-permute-start.43
  188.3 3.2 %collective-permute-done.43 = f32[64,256]{1,0:T(8,128)S(1)} collective-permute-done((f32[64,256]{1,0:T(8,128)S(1)}, f32[64,256]{1,0:T(8,128)S(1)}, u32[]{:S(2)}, u32[]{:S(2)}) %collective-permute-start.43) | collective-permute-done | bytes 65568 | tf_op jit(solution)/shard_map/ppermute | solution.py:69
  191.6 1.4 collective-permute-done.44
  193.7 1.8 collective-permute-start.49
  195.6 3.0 %collective-permute-start.50 = (f32[64]{0:T(128)S(1)}, f32[64]{0:T(128)S(1)}, u32[]{:S(2)}, u32[]{:S(2)}) collective-permute-start(f32[64]{0:T(128)S(1)} %get-tuple-element.7), channel_id=1, source_target_pairs={{0,3},{1,4},{2,5},{3,6},{4,7},{5,0},{6,1},{7,2},{8,11},{9,12},{10,... | collective-permute-start | bytes 776 | tf_op jit(solution)/shard_map/ppermute | solution.py:69
  198.6 1.0 collective-permute-start.51
  199.6 1.0 collective-permute-start.52
  200.6 2.5 %collective-permute-done.51 = f32[64]{0:T(128)S(1)} collective-permute-done((f32[64]{0:T(128)S(1)}, f32[64]{0:T(128)S(1)}, u32[]{:S(2)}, u32[]{:S(2)}) %collective-permute-start.51) | collective-permute-done | bytes 288 | tf_op jit(solution)/shard_map/ppermute | solution.py:69
  (182 shorter events, 26.6 us)
Async XLA Ops:
  0.0 160.6 %copy-start = (bf16[256,512]{1,0:T(8,128)(2,1)S(1)}, bf16[256,512]{1,0:T(8,128)(2,1)}, u32[]{:S(2)}) copy-start(bf16[256,512]{1,0:T(8,128)(2,1)} %param.24) | copy-start | bytes 786436
  0.0 56.1 %copy-start.5 = (f32[512]{0:T(512)S(1)}, f32[512]{0:T(512)}, u32[]{:S(2)}) copy-start(f32[512]{0:T(512)} %param.26) | copy-start | bytes 6148
  0.0 56.2 %copy-start.6 = (f32[512]{0:T(512)S(1)}, f32[512]{0:T(512)}, u32[]{:S(2)}) copy-start(f32[512]{0:T(512)} %param.25) | copy-start | bytes 6148
  0.8 3.0 %collective-permute-start = (bf16[64,64]{1,0:T(8,128)(2,1)S(1)}, bf16[64,64]{1,0:T(8,128)(2,1)S(1)}, u32[]{:S(2)}, u32[]{:S(2)}) collective-permute-start(bf16[64,64]{1,0:T(8,128)(2,1)S(1)} %constant_dynamic-slice_fusion.5), channel_id=1, source_target_pairs={{0,0},{1,32},{2,64},{3,96},{4,4},{5,36},{6,68},{7,100},{8,8},{9,40... | collective-permute-start | bytes 24584 | tf_op jit(solution)/shard_map/ppermute | solution.py:47
  6.8 1.5 collective-permute-start.1
  8.4 11.6 %collective-permute-start.2 = (f32[64,768]{1,0:T(8,128)S(1)}, f32[64,768]{1,0:T(8,128)S(1)}, u32[]{:S(2)}, u32[]{:S(2)}) collective-permute-start(f32[64,768]{1,0:T(8,128)S(1)} %dynamic-slice_add_fusion), channel_id=1, source_target_pairs={{0,24},{4,28},{8,0},{12,4},{16,8},{20,12},{24,16},{28,20},{32,56},... | collective-permute-start | bytes 589832 | tf_op jit(solution)/shard_map/ppermute | solution.py:69
  11.3 9.3 %collective-permute-start.3 = (f32[64,768]{1,0:T(8,128)S(1)}, f32[64,768]{1,0:T(8,128)S(1)}, u32[]{:S(2)}, u32[]{:S(2)}) collective-permute-start(f32[64,768]{1,0:T(8,128)S(1)} %dynamic-slice_add_fusion), channel_id=1, source_target_pairs={{0,16},{4,20},{8,24},{12,28},{16,0},{20,4},{24,8},{28,12},{32,48},... | collective-permute-start | bytes 589832 | tf_op jit(solution)/shard_map/ppermute | solution.py:69
  12.1 11.6 %collective-permute-start.4 = (f32[64,768]{1,0:T(8,128)S(1)}, f32[64,768]{1,0:T(8,128)S(1)}, u32[]{:S(2)}, u32[]{:S(2)}) collective-permute-start(f32[64,768]{1,0:T(8,128)S(1)} %dynamic-slice_add_fusion), channel_id=1, source_target_pairs={{0,8},{4,12},{8,16},{12,20},{16,24},{20,28},{24,0},{28,4},{32,40},... | collective-permute-start | bytes 589832 | tf_op jit(solution)/shard_map/ppermute | solution.py:69
  23.8 17.6 %collective-permute-start.5 = (f32[64,768]{1,0:T(8,128)S(1)}, f32[64,768]{1,0:T(8,128)S(1)}, u32[]{:S(2)}, u32[]{:S(2)}) collective-permute-start(f32[64,768]{1,0:T(8,128)S(1)} %select_add_fusion.1), channel_id=1, source_target_pairs={{0,96},{4,100},{8,104},{12,108},{16,112},{20,116},{24,120},{28,124... | collective-permute-start | bytes 589832 | tf_op jit(solution)/shard_map/ppermute | solution.py:69
  32.9 9.3 %collective-permute-start.6 = (f32[64,768]{1,0:T(8,128)S(1)}, f32[64,768]{1,0:T(8,128)S(1)}, u32[]{:S(2)}, u32[]{:S(2)}) collective-permute-start(f32[64,768]{1,0:T(8,128)S(1)} %select_add_fusion.1), channel_id=1, source_target_pairs={{0,64},{4,68},{8,72},{12,76},{16,80},{20,84},{24,88},{28,92},{32,9... | collective-permute-start | bytes 589832 | tf_op jit(solution)/shard_map/ppermute | solution.py:69
  33.7 11.4 %collective-permute-start.7 = (f32[64,768]{1,0:T(8,128)S(1)}, f32[64,768]{1,0:T(8,128)S(1)}, u32[]{:S(2)}, u32[]{:S(2)}) collective-permute-start(f32[64,768]{1,0:T(8,128)S(1)} %select_add_fusion.1), channel_id=1, source_target_pairs={{0,32},{4,36},{8,40},{12,44},{16,48},{20,52},{24,56},{28,60},{32,6... | collective-permute-start | bytes 589832 | tf_op jit(solution)/shard_map/ppermute | solution.py:69
  45.3 1.5 collective-permute-start.8
  47.0 4.7 %collective-permute-start.9 = (f32[64,2]{0,1:T(2,128)S(1)}, f32[64,2]{0,1:T(2,128)S(1)}, u32[]{:S(2)}, u32[]{:S(2)}) collective-permute-start(f32[64,2]{0,1:T(2,128)S(1)} %pad_maximum_fusion.3), channel_id=1, source_target_pairs={{0,3},{1,0},{2,1},{3,2},{4,7},{5,4},{6,5},{7,6},{8,11},{9,8},{10,9... | collective-permute-start | bytes 1544 | tf_op jit(solution)/shard_map/ppermute | solution.py:69
  49.1 5.1 %collective-permute-start.10 = (f32[64,2]{0,1:T(2,128)S(1)}, f32[64,2]{0,1:T(2,128)S(1)}, u32[]{:S(2)}, u32[]{:S(2)}) collective-permute-start(f32[64,2]{0,1:T(2,128)S(1)} %pad_maximum_fusion.3), channel_id=1, source_target_pairs={{0,2},{1,3},{2,0},{3,1},{4,6},{5,7},{6,4},{7,5},{8,10},{9,11},{10,... | collective-permute-start | bytes 1544 | tf_op jit(solution)/shard_map/ppermute | solution.py:69
  51.3 4.8 %collective-permute-start.11 = (f32[64,2]{0,1:T(2,128)S(1)}, f32[64,2]{0,1:T(2,128)S(1)}, u32[]{:S(2)}, u32[]{:S(2)}) collective-permute-start(f32[64,2]{0,1:T(2,128)S(1)} %pad_maximum_fusion.3), channel_id=1, source_target_pairs={{0,1},{1,2},{2,3},{3,0},{4,5},{5,6},{6,7},{7,4},{8,9},{9,10},{10,1... | collective-permute-start | bytes 1544 | tf_op jit(solution)/shard_map/ppermute | solution.py:69
  69.0 25.5 %copy-start.4 = (bf16[64,512]{1,0:T(8,128)(2,1)S(1)}, bf16[64,512]{1,0:T(8,128)(2,1)}, u32[]{:S(2)}) copy-start(bf16[64,512]{1,0:T(8,128)(2,1)} %param.21) | copy-start | bytes 196612
  69.0 40.1 %copy-start.1 = (bf16[64,2048]{1,0:T(8,128)(2,1)S(1)}, bf16[64,2048]{1,0:T(8,128)(2,1)}, u32[]{:S(2)}) copy-start(bf16[64,2048]{1,0:T(8,128)(2,1)} %param.23) | copy-start | bytes 786436
  69.0 40.6 %copy-start.2 = (bf16[64,2048]{1,0:T(8,128)(2,1)S(1)}, bf16[64,2048]{1,0:T(8,128)(2,1)}, u32[]{:S(2)}) copy-start(bf16[64,2048]{1,0:T(8,128)(2,1)} %param.22) | copy-start | bytes 786436
  70.7 11.8 %all-to-all-start = ((f32[32,1,1152]{2,1,0:T(1,128)}), f32[32,1,1152]{2,1,0:T(1,128)S(1)}, u32[]{:S(2)}, u32[]{:S(2)}) async-start(f32[32,1,1152]{2,1,0:T(1,128)} %reshape.456), calls=%async_computation | async-start | bytes 294912 | tf_op jit(solution)/shard_map/all_to_all | solution.py:298
  84.1 55.3 %copy-start.3 = (bf16[4,16,512]{2,1,0:T(8,128)(2,1)S(1)}, bf16[4,16,512]{2,1,0:T(8,128)(2,1)}, u32[]{:S(2)}) copy-start(bf16[4,16,512]{2,1,0:T(8,128)(2,1)} %param.17) | copy-start | bytes 196612
  84.1 55.3 %copy-start.7 = (f32[512]{0:T(512)S(1)}, f32[512]{0:T(512)}, u32[]{:S(2)}) copy-start(f32[512]{0:T(512)} %param.27) | copy-start | bytes 6148
  85.6 6.5 %collective-permute-start.12 = (bf16[64,16]{0,1:T(8,128)(2,1)S(1)}, bf16[64,16]{0,1:T(8,128)(2,1)S(1)}, u32[]{:S(2)}, u32[]{:S(2)}) collective-permute-start(bf16[64,16]{0,1:T(8,128)(2,1)S(1)} %copy.111), channel_id=1, source_target_pairs={{0,3},{1,35},{2,67},{3,99},{4,0},{5,32},{6,64},{7,96},{8,1},{9,33}... | collective-permute-start | bytes 6152 | tf_op jit(solution)/shard_map/ppermute | solution.py:162
  87.6 4.6 %collective-permute-start.13 = (bf16[64,16]{0,1:T(8,128)(2,1)S(1)}, bf16[64,16]{0,1:T(8,128)(2,1)S(1)}, u32[]{:S(2)}, u32[]{:S(2)}) collective-permute-start(bf16[64,16]{0,1:T(8,128)(2,1)S(1)} %copy.111), channel_id=1, source_target_pairs={{0,2},{1,34},{2,66},{3,98},{4,3},{5,35},{6,67},{7,99},{8,0},{9,32}... | collective-permute-start | bytes 6152 | tf_op jit(solution)/shard_map/ppermute | solution.py:162
  89.5 4.9 %collective-permute-start.14 = (bf16[64,16]{0,1:T(8,128)(2,1)S(1)}, bf16[64,16]{0,1:T(8,128)(2,1)S(1)}, u32[]{:S(2)}, u32[]{:S(2)}) collective-permute-start(bf16[64,16]{0,1:T(8,128)(2,1)S(1)} %copy.111), channel_id=1, source_target_pairs={{0,1},{1,33},{2,65},{3,97},{4,2},{5,34},{6,66},{7,98},{8,3},{9,35}... | collective-permute-start | bytes 6152 | tf_op jit(solution)/shard_map/ppermute | solution.py:162
  91.4 3.0 %collective-permute-start.15 = (bf16[64,16]{0,1:T(8,128)(2,1)S(1)}, bf16[64,16]{0,1:T(8,128)(2,1)S(1)}, u32[]{:S(2)}, u32[]{:S(2)}) collective-permute-start(bf16[64,16]{0,1:T(8,128)(2,1)S(1)} %copy.111), channel_id=1, source_target_pairs={{0,0},{1,32},{2,64},{3,96},{4,1},{5,33},{6,65},{7,97},{8,2},{9,34}... | collective-permute-start | bytes 6152 | tf_op jit(solution)/shard_map/ppermute | solution.py:162
  94.7 6.5 %collective-permute-start.16 = (f32[64,256]{1,0:T(8,128)S(1)}, f32[64,256]{1,0:T(8,128)S(1)}, u32[]{:S(2)}, u32[]{:S(2)}) collective-permute-start(f32[64,256]{1,0:T(8,128)S(1)} %constant_dynamic-slice_fusion.1), channel_id=1, source_target_pairs={{0,4},{4,0},{8,12},{12,8},{16,20},{20,16},{24,28},{28,24},{32,36},... | collective-permute-start | bytes 196616 | tf_op jit(solution)/shard_map/ppermute | solution.py:88
  101.1 9.0 %collective-permute-start.17 = (f32[64,256]{1,0:T(8,128)S(1)}, f32[64,256]{1,0:T(8,128)S(1)}, u32[]{:S(2)}, u32[]{:S(2)}) collective-permute-start(f32[64,256]{1,0:T(8,128)S(1)} %dynamic-slice_add_fusion.2), channel_id=1, source_target_pairs={{0,24},{4,28},{8,0},{12,4},{16,8},{20,12},{24,16},{28,20},{32,56},... | collective-permute-start | bytes 196616 | tf_op jit(solution)/shard_map/ppermute | solution.py:69
  106.3 6.2 %collective-permute-start.18 = (f32[64,256]{1,0:T(8,128)S(1)}, f32[64,256]{1,0:T(8,128)S(1)}, u32[]{:S(2)}, u32[]{:S(2)}) collective-permute-start(f32[64,256]{1,0:T(8,128)S(1)} %dynamic-slice_add_fusion.2), channel_id=1, source_target_pairs={{0,16},{4,20},{8,24},{12,28},{16,0},{20,4},{24,8},{28,12},{32,48},... | collective-permute-start | bytes 196616 | tf_op jit(solution)/shard_map/ppermute | solution.py:69
  107.8 5.8 %collective-permute-start.19 = (f32[64,256]{1,0:T(8,128)S(1)}, f32[64,256]{1,0:T(8,128)S(1)}, u32[]{:S(2)}, u32[]{:S(2)}) collective-permute-start(f32[64,256]{1,0:T(8,128)S(1)} %dynamic-slice_add_fusion.2), channel_id=1, source_target_pairs={{0,8},{4,12},{8,16},{12,20},{16,24},{20,28},{24,0},{28,4},{32,40},... | collective-permute-start | bytes 196616 | tf_op jit(solution)/shard_map/ppermute | solution.py:69
  113.6 15.0 %collective-permute-start.20 = (f32[64,256]{1,0:T(8,128)S(1)}, f32[64,256]{1,0:T(8,128)S(1)}, u32[]{:S(2)}, u32[]{:S(2)}) collective-permute-start(f32[64,256]{1,0:T(8,128)S(1)} %select_add_fusion.5), channel_id=1, source_target_pairs={{0,96},{4,100},{8,104},{12,108},{16,112},{20,116},{24,120},{28,124... | collective-permute-start | bytes 196616 | tf_op jit(solution)/shard_map/ppermute | solution.py:69
  121.0 7.6 %collective-permute-start.21 = (f32[64,256]{1,0:T(8,128)S(1)}, f32[64,256]{1,0:T(8,128)S(1)}, u32[]{:S(2)}, u32[]{:S(2)}) collective-permute-start(f32[64,256]{1,0:T(8,128)S(1)} %select_add_fusion.5), channel_id=1, source_target_pairs={{0,64},{4,68},{8,72},{12,76},{16,80},{20,84},{24,88},{28,92},{32,9... | collective-permute-start | bytes 196616 | tf_op jit(solution)/shard_map/ppermute | solution.py:69
  121.0 7.6 %collective-permute-start.22 = (f32[64,256]{1,0:T(8,128)S(1)}, f32[64,256]{1,0:T(8,128)S(1)}, u32[]{:S(2)}, u32[]{:S(2)}) collective-permute-start(f32[64,256]{1,0:T(8,128)S(1)} %select_add_fusion.5), channel_id=1, source_target_pairs={{0,32},{4,36},{8,40},{12,44},{16,48},{20,52},{24,56},{28,60},{32,6... | collective-permute-start | bytes 196616 | tf_op jit(solution)/shard_map/ppermute | solution.py:69
  122.2 81.6 %copy-start.8 = (f32[512]{0:T(512)S(1)}, f32[512]{0:T(512)}, u32[]{:S(2)}) copy-start(f32[512]{0:T(512)} %param.28) | copy-start | bytes 6148
  123.3 24.5 %all-to-all-start.1 = ((bf16[64,32,128]{2,0,1:T(8,128)(2,1)}), bf16[64,32,128]{2,0,1:T(8,128)(2,1)S(1)}, u32[]{:S(2)}, u32[]{:S(2)}) async-start(bf16[64,32,128]{2,0,1:T(8,128)(2,1)} %copy.107), calls=%async_computation.1 | async-start | bytes 1048576 | tf_op jit(solution)/shard_map/all_to_all | solution.py:169
  128.7 5.4 %collective-permute-start.24 = (f32[64]{0:T(128)S(1)}, f32[64]{0:T(128)S(1)}, u32[]{:S(2)}, u32[]{:S(2)}) collective-permute-start(f32[64]{0:T(128)S(1)} %get-tuple-element.9), channel_id=1, source_target_pairs={{0,7},{1,0},{2,1},{3,2},{4,3},{5,4},{6,5},{7,6},{8,15},{9,8},{10,9... | collective-permute-start | bytes 776 | tf_op jit(solution)/shard_map/ppermute | solution.py:69
  129.2 6.0 %collective-permute-start.25 = (f32[64]{0:T(128)S(1)}, f32[64]{0:T(128)S(1)}, u32[]{:S(2)}, u32[]{:S(2)}) collective-permute-start(f32[64]{0:T(128)S(1)} %get-tuple-element.9), channel_id=1, source_target_pairs={{0,6},{1,7},{2,0},{3,1},{4,2},{5,3},{6,4},{7,5},{8,14},{9,15},{10,... | collective-permute-start | bytes 776 | tf_op jit(solution)/shard_map/ppermute | solution.py:69
  130.6 5.6 %collective-permute-start.26 = (f32[64]{0:T(128)S(1)}, f32[64]{0:T(128)S(1)}, u32[]{:S(2)}, u32[]{:S(2)}) collective-permute-start(f32[64]{0:T(128)S(1)} %get-tuple-element.9), channel_id=1, source_target_pairs={{0,5},{1,6},{2,7},{3,0},{4,1},{5,2},{6,3},{7,4},{8,13},{9,14},{10,... | collective-permute-start | bytes 776 | tf_op jit(solution)/shard_map/ppermute | solution.py:69
  131.1 5.1 %collective-permute-start.27 = (f32[64]{0:T(128)S(1)}, f32[64]{0:T(128)S(1)}, u32[]{:S(2)}, u32[]{:S(2)}) collective-permute-start(f32[64]{0:T(128)S(1)} %get-tuple-element.9), channel_id=1, source_target_pairs={{0,4},{1,5},{2,6},{3,7},{4,0},{5,1},{6,2},{7,3},{8,12},{9,13},{10,... | collective-permute-start | bytes 776 | tf_op jit(solution)/shard_map/ppermute | solution.py:69
  131.2 5.1 %collective-permute-start.28 = (f32[64]{0:T(128)S(1)}, f32[64]{0:T(128)S(1)}, u32[]{:S(2)}, u32[]{:S(2)}) collective-permute-start(f32[64]{0:T(128)S(1)} %get-tuple-element.9), channel_id=1, source_target_pairs={{0,3},{1,4},{2,5},{3,6},{4,7},{5,0},{6,1},{7,2},{8,11},{9,12},{10,... | collective-permute-start | bytes 776 | tf_op jit(solution)/shard_map/ppermute | solution.py:69
  134.2 4.6 %collective-permute-start.29 = (f32[64]{0:T(128)S(1)}, f32[64]{0:T(128)S(1)}, u32[]{:S(2)}, u32[]{:S(2)}) collective-permute-start(f32[64]{0:T(128)S(1)} %get-tuple-element.9), channel_id=1, source_target_pairs={{0,2},{1,3},{2,4},{3,5},{4,6},{5,7},{6,0},{7,1},{8,10},{9,11},{10,... | collective-permute-start | bytes 776 | tf_op jit(solution)/shard_map/ppermute | solution.py:69
  135.2 4.2 %collective-permute-start.30 = (f32[64]{0:T(128)S(1)}, f32[64]{0:T(128)S(1)}, u32[]{:S(2)}, u32[]{:S(2)}) collective-permute-start(f32[64]{0:T(128)S(1)} %get-tuple-element.9), channel_id=1, source_target_pairs={{0,1},{1,2},{2,3},{3,4},{4,5},{5,6},{6,7},{7,0},{8,9},{9,10},{10,1... | collective-permute-start | bytes 776 | tf_op jit(solution)/shard_map/ppermute | solution.py:69
  136.2 3.2 %collective-permute-start.23 = (f32[64,256]{1,0:T(8,128)S(1)}, f32[64,256]{1,0:T(8,128)S(1)}, u32[]{:S(2)}, u32[]{:S(2)}) collective-permute-start(f32[64,256]{1,0:T(8,128)S(1)} %get-tuple-element.10), channel_id=1, source_target_pairs={{0,4},{4,0},{8,12},{12,8},{16,20},{20,16},{24,28},{28,24},{32,36},... | collective-permute-start | bytes 196616 | tf_op jit(solution)/shard_map/ppermute | solution.py:99
  139.6 4.8 %collective-permute-start.31 = (bf16[64,512]{1,0:T(8,128)(2,1)S(1)}, bf16[64,512]{1,0:T(8,128)(2,1)S(1)}, u32[]{:S(2)}, u32[]{:S(2)}) collective-permute-start(bf16[64,512]{1,0:T(8,128)(2,1)S(1)} %add_convert_fusion.1), channel_id=1, source_target_pairs={{0,3},{1,0},{2,1},{3,2},{4,7},{5,4},{6,5},{7,6},{8,11},{9,8},{10,9... | collective-permute-start | bytes 196616 | tf_op jit(solution)/shard_map/ppermute | solution.py:69
  140.7 6.4 %collective-permute-start.32 = (bf16[64,512]{1,0:T(8,128)(2,1)S(1)}, bf16[64,512]{1,0:T(8,128)(2,1)S(1)}, u32[]{:S(2)}, u32[]{:S(2)}) collective-permute-start(bf16[64,512]{1,0:T(8,128)(2,1)S(1)} %add_convert_fusion.1), channel_id=1, source_target_pairs={{0,2},{1,3},{2,0},{3,1},{4,6},{5,7},{6,4},{7,5},{8,10},{9,11},{10,... | collective-permute-start | bytes 196616 | tf_op jit(solution)/shard_map/ppermute | solution.py:69
  142.1 5.6 %collective-permute-start.33 = (bf16[64,512]{1,0:T(8,128)(2,1)S(1)}, bf16[64,512]{1,0:T(8,128)(2,1)S(1)}, u32[]{:S(2)}, u32[]{:S(2)}) collective-permute-start(bf16[64,512]{1,0:T(8,128)(2,1)S(1)} %add_convert_fusion.1), channel_id=1, source_target_pairs={{0,1},{1,2},{2,3},{3,0},{4,5},{5,6},{6,7},{7,4},{8,9},{9,10},{10,1... | collective-permute-start | bytes 196616 | tf_op jit(solution)/shard_map/ppermute | solution.py:69
  148.4 10.0 %collective-permute-start.34 = (bf16[64,64]{1,0:T(8,128)(2,1)S(1)}, bf16[64,64]{1,0:T(8,128)(2,1)S(1)}, u32[]{:S(2)}, u32[]{:S(2)}) collective-permute-start(bf16[64,64]{1,0:T(8,128)(2,1)S(1)} %fusion.3), channel_id=1, source_target_pairs={{0,3},{1,35},{2,67},{3,99},{4,0},{5,32},{6,64},{7,96},{8,1},{9,33}... | collective-permute-start | bytes 24584 | tf_op jit(solution)/shard_map/ppermute | solution.py:162
  151.3 7.1 %collective-permute-start.35 = (bf16[64,64]{1,0:T(8,128)(2,1)S(1)}, bf16[64,64]{1,0:T(8,128)(2,1)S(1)}, u32[]{:S(2)}, u32[]{:S(2)}) collective-permute-start(bf16[64,64]{1,0:T(8,128)(2,1)S(1)} %fusion.3), channel_id=1, source_target_pairs={{0,2},{1,34},{2,66},{3,98},{4,3},{5,35},{6,67},{7,99},{8,0},{9,32}... | collective-permute-start | bytes 24584 | tf_op jit(solution)/shard_map/ppermute | solution.py:162
  155.5 5.0 %collective-permute-start.36 = (bf16[64,64]{1,0:T(8,128)(2,1)S(1)}, bf16[64,64]{1,0:T(8,128)(2,1)S(1)}, u32[]{:S(2)}, u32[]{:S(2)}) collective-permute-start(bf16[64,64]{1,0:T(8,128)(2,1)S(1)} %fusion.3), channel_id=1, source_target_pairs={{0,1},{1,33},{2,65},{3,97},{4,2},{5,34},{6,66},{7,98},{8,3},{9,35}... | collective-permute-start | bytes 24584 | tf_op jit(solution)/shard_map/ppermute | solution.py:162
  157.7 2.9 %collective-permute-start.37 = (bf16[64,64]{1,0:T(8,128)(2,1)S(1)}, bf16[64,64]{1,0:T(8,128)(2,1)S(1)}, u32[]{:S(2)}, u32[]{:S(2)}) collective-permute-start(bf16[64,64]{1,0:T(8,128)(2,1)S(1)} %fusion.3), channel_id=1, source_target_pairs={{0,0},{1,32},{2,64},{3,96},{4,1},{5,33},{6,65},{7,97},{8,2},{9,34}... | collective-permute-start | bytes 24584 | tf_op jit(solution)/shard_map/ppermute | solution.py:162
  160.8 7.5 %collective-permute-start.38 = (f32[64,256]{1,0:T(8,128)S(1)}, f32[64,256]{1,0:T(8,128)S(1)}, u32[]{:S(2)}, u32[]{:S(2)}) collective-permute-start(f32[64,256]{1,0:T(8,128)S(1)} %constant_dynamic-slice_fusion), channel_id=1, source_target_pairs={{0,4},{4,0},{8,12},{12,8},{16,20},{20,16},{24,28},{28,24},{32,36},... | collective-permute-start | bytes 196616 | tf_op jit(solution)/shard_map/ppermute | solution.py:88
  168.3 6.3 %collective-permute-start.39 = (f32[64,256]{1,0:T(8,128)S(1)}, f32[64,256]{1,0:T(8,128)S(1)}, u32[]{:S(2)}, u32[]{:S(2)}) collective-permute-start(f32[64,256]{1,0:T(8,128)S(1)} %dynamic-slice_add_fusion.1), channel_id=1, source_target_pairs={{0,24},{4,28},{8,0},{12,4},{16,8},{20,12},{24,16},{28,20},{32,56},... | collective-permute-start | bytes 196616 | tf_op jit(solution)/shard_map/ppermute | solution.py:69
  172.1 6.1 %collective-permute-start.40 = (f32[64,256]{1,0:T(8,128)S(1)}, f32[64,256]{1,0:T(8,128)S(1)}, u32[]{:S(2)}, u32[]{:S(2)}) collective-permute-start(f32[64,256]{1,0:T(8,128)S(1)} %dynamic-slice_add_fusion.1), channel_id=1, source_target_pairs={{0,16},{4,20},{8,24},{12,28},{16,0},{20,4},{24,8},{28,12},{32,48},... | collective-permute-start | bytes 196616 | tf_op jit(solution)/shard_map/ppermute | solution.py:69
  172.7 6.1 %collective-permute-start.41 = (f32[64,256]{1,0:T(8,128)S(1)}, f32[64,256]{1,0:T(8,128)S(1)}, u32[]{:S(2)}, u32[]{:S(2)}) collective-permute-start(f32[64,256]{1,0:T(8,128)S(1)} %dynamic-slice_add_fusion.1), channel_id=1, source_target_pairs={{0,8},{4,12},{8,16},{12,20},{16,24},{20,28},{24,0},{28,4},{32,40},... | collective-permute-start | bytes 196616 | tf_op jit(solution)/shard_map/ppermute | solution.py:69
  178.9 9.4 %collective-permute-start.42 = (f32[64,256]{1,0:T(8,128)S(1)}, f32[64,256]{1,0:T(8,128)S(1)}, u32[]{:S(2)}, u32[]{:S(2)}) collective-permute-start(f32[64,256]{1,0:T(8,128)S(1)} %select_add_fusion.3), channel_id=1, source_target_pairs={{0,96},{4,100},{8,104},{12,108},{16,112},{20,116},{24,120},{28,124... | collective-permute-start | bytes 196616 | tf_op jit(solution)/shard_map/ppermute | solution.py:69
  185.7 5.9 %collective-permute-start.43 = (f32[64,256]{1,0:T(8,128)S(1)}, f32[64,256]{1,0:T(8,128)S(1)}, u32[]{:S(2)}, u32[]{:S(2)}) collective-permute-start(f32[64,256]{1,0:T(8,128)S(1)} %select_add_fusion.3), channel_id=1, source_target_pairs={{0,64},{4,68},{8,72},{12,76},{16,80},{20,84},{24,88},{28,92},{32,9... | collective-permute-start | bytes 196616 | tf_op jit(solution)/shard_map/ppermute | solution.py:69
  187.5 5.5 %collective-permute-start.44 = (f32[64,256]{1,0:T(8,128)S(1)}, f32[64,256]{1,0:T(8,128)S(1)}, u32[]{:S(2)}, u32[]{:S(2)}) collective-permute-start(f32[64,256]{1,0:T(8,128)S(1)} %select_add_fusion.3), channel_id=1, source_target_pairs={{0,32},{4,36},{8,40},{12,44},{16,48},{20,52},{24,56},{28,60},{32,6... | collective-permute-start | bytes 196616 | tf_op jit(solution)/shard_map/ppermute | solution.py:69
  193.1 5.5 %collective-permute-start.46 = (f32[64]{0:T(128)S(1)}, f32[64]{0:T(128)S(1)}, u32[]{:S(2)}, u32[]{:S(2)}) collective-permute-start(f32[64]{0:T(128)S(1)} %get-tuple-element.7), channel_id=1, source_target_pairs={{0,7},{1,0},{2,1},{3,2},{4,3},{5,4},{6,5},{7,6},{8,15},{9,8},{10,9... | collective-permute-start | bytes 776 | tf_op jit(solution)/shard_map/ppermute | solution.py:69
  193.2 6.4 %collective-permute-start.47 = (f32[64]{0:T(128)S(1)}, f32[64]{0:T(128)S(1)}, u32[]{:S(2)}, u32[]{:S(2)}) collective-permute-start(f32[64]{0:T(128)S(1)} %get-tuple-element.7), channel_id=1, source_target_pairs={{0,6},{1,7},{2,0},{3,1},{4,2},{5,3},{6,4},{7,5},{8,14},{9,15},{10,... | collective-permute-start | bytes 776 | tf_op jit(solution)/shard_map/ppermute | solution.py:69
  193.3 7.3 %collective-permute-start.48 = (f32[64]{0:T(128)S(1)}, f32[64]{0:T(128)S(1)}, u32[]{:S(2)}, u32[]{:S(2)}) collective-permute-start(f32[64]{0:T(128)S(1)} %get-tuple-element.7), channel_id=1, source_target_pairs={{0,5},{1,6},{2,7},{3,0},{4,1},{5,2},{6,3},{7,4},{8,13},{9,14},{10,... | collective-permute-start | bytes 776 | tf_op jit(solution)/shard_map/ppermute | solution.py:69
  193.7 6.9 %collective-permute-start.49 = (f32[64]{0:T(128)S(1)}, f32[64]{0:T(128)S(1)}, u32[]{:S(2)}, u32[]{:S(2)}) collective-permute-start(f32[64]{0:T(128)S(1)} %get-tuple-element.7), channel_id=1, source_target_pairs={{0,4},{1,5},{2,6},{3,7},{4,0},{5,1},{6,2},{7,3},{8,12},{9,13},{10,... | collective-permute-start | bytes 776 | tf_op jit(solution)/shard_map/ppermute | solution.py:69
  195.6 5.0 %collective-permute-start.50 = (f32[64]{0:T(128)S(1)}, f32[64]{0:T(128)S(1)}, u32[]{:S(2)}, u32[]{:S(2)}) collective-permute-start(f32[64]{0:T(128)S(1)} %get-tuple-element.7), channel_id=1, source_target_pairs={{0,3},{1,4},{2,5},{3,6},{4,7},{5,0},{6,1},{7,2},{8,11},{9,12},{10,... | collective-permute-start | bytes 776 | tf_op jit(solution)/shard_map/ppermute | solution.py:69
  198.6 4.6 %collective-permute-start.51 = (f32[64]{0:T(128)S(1)}, f32[64]{0:T(128)S(1)}, u32[]{:S(2)}, u32[]{:S(2)}) collective-permute-start(f32[64]{0:T(128)S(1)} %get-tuple-element.7), channel_id=1, source_target_pairs={{0,2},{1,3},{2,4},{3,5},{4,6},{5,7},{6,0},{7,1},{8,10},{9,11},{10,... | collective-permute-start | bytes 776 | tf_op jit(solution)/shard_map/ppermute | solution.py:69
  199.6 4.2 %collective-permute-start.52 = (f32[64]{0:T(128)S(1)}, f32[64]{0:T(128)S(1)}, u32[]{:S(2)}, u32[]{:S(2)}) collective-permute-start(f32[64]{0:T(128)S(1)} %get-tuple-element.7), channel_id=1, source_target_pairs={{0,1},{1,2},{2,3},{3,4},{4,5},{5,6},{6,7},{7,0},{8,9},{9,10},{10,1... | collective-permute-start | bytes 776 | tf_op jit(solution)/shard_map/ppermute | solution.py:69
  200.6 3.2 %collective-permute-start.45 = (f32[64,256]{1,0:T(8,128)S(1)}, f32[64,256]{1,0:T(8,128)S(1)}, u32[]{:S(2)}, u32[]{:S(2)}) collective-permute-start(f32[64,256]{1,0:T(8,128)S(1)} %get-tuple-element.8), channel_id=1, source_target_pairs={{0,4},{4,0},{8,12},{12,8},{16,20},{20,16},{24,28},{28,24},{32,36},... | collective-permute-start | bytes 196616 | tf_op jit(solution)/shard_map/ppermute | solution.py:99
